TPU v7x, 32 devices: a whole 2x2x4 slice. The times are simulated.
32 devices in a mesh: lvl: 4 (over y, x), prow: 4 (over z), pcol: 2 (over core).
Axes of the slice: x: 2, y: 2, z: 4, core: 2. Of those that a mesh axis runs over, the one named last changes fastest.
Arguments:
- rhs: float32 [4, 2, 1024, 256], P('lvl', 'pcol'), may hold values from -6 to 6
- diag_inverse: bfloat16 [4, 2, 1024, 1024], P('lvl', 'pcol', 'prow'), may hold values from -0.1875 to 0.1875
- off_tiles: bfloat16 [4, 2, 32, 32, 1024], P('lvl', 'pcol', 'prow'), may hold values from -0.625 to 0.625
- panel_super: int32 [4, 2, 8], P('lvl', 'pcol'), may hold values from 0 to 7, as said below
- off_device: int32 [4, 2, 32], P('lvl', 'pcol', 'prow'), may hold values from 0 to 7, as said below
- off_block: int32 [4, 2, 32], P('lvl', 'pcol', 'prow'), may hold values from 0 to 47, as said below
- offdiag_block_panel: int32 [4, 2, 32], P('lvl', 'pcol', 'prow'), may hold values from 0 to 7
Outputs:
- solution: float32 [4, 2, 1024, 256], P('lvl', 'pcol', 'prow')
- outer: float32 [4, 2, 512, 256], P('lvl', 'pcol')
Inputs may be any that keep to these rules, and one draw needn't show every extreme that they name: `panel_super`: within a group ids start at 0 and rise by 0 or 1 from panel to panel; panels of one id form one supernode. `off_device`: one device sends at most 2 block rows to any one target group; some group receives 2 from every device. `off_block`: A block under 1024 / 32 (a window row) goes only to a group on a higher level than the sender's; the others are rows above the window.
All inputs are finite; a program needn't handle non-finite values.
Results may differ from a plain program's by a relative error of at most 0.0055.
Values may be sent and summed in bfloat16 or wider, within the bound.
No kernel may reach another device: no remote copies, remote signals or barrier semaphores. Data moves between devices by JAX's collectives and lax.ppermute only.
A program may use at most 64 MiB of HBM per device.

v0:
```python
import jax
import jax.numpy as jnp
from jax import lax
from jax.sharding import PartitionSpec as P

CAP = 2
ABOVE = 512
NT = 48


def per_device(
    rhs, diag_inverse, off_tiles, panel_super, off_device, off_block, offdiag_block_panel
):
    levels = lax.axis_size("lvl")
    col_groups = lax.axis_size("pcol")
    groups = levels * col_groups
    level_index = lax.axis_index("lvl")
    row_index = lax.axis_index("prow")
    width = rhs.shape[2]
    columns_all = rhs.shape[3]
    row_count = diag_inverse.shape[2]
    tile_count = off_tiles.shape[2]
    block_rows = off_tiles.shape[3]
    panels = panel_super[0, 0]
    panel_cols = width // panels.shape[0]
    col_super = jnp.repeat(panels, panel_cols)
    row_ids = row_index * row_count + jnp.arange(row_count, dtype=jnp.int32)
    row_super = jnp.take(col_super, row_ids)
    inverse = jnp.where(
        row_super[:, None] == col_super[None, :], diag_inverse[0, 0], jnp.zeros((), jnp.bfloat16)
    )
    tile_supernode = jnp.take(panels, offdiag_block_panel[0, 0])
    tiles_used = jnp.where(
        col_super[None, None, :] == tile_supernode[:, None, None],
        off_tiles[0, 0],
        jnp.zeros((), jnp.bfloat16),
    )
    tiles_used = tiles_used.reshape(tile_count * block_rows, width)
    target = off_device[0, 0]
    target_block = off_block[0, 0]
    tile_ids = jnp.arange(tile_count, dtype=jnp.int32)
    earlier = (target[:, None] == target[None, :]) & (tile_ids[:, None] > tile_ids[None, :])
    position = jnp.sum(earlier.astype(jnp.int32), axis=1)
    slot_index = target * CAP + position
    slot_total = groups * CAP
    match = slot_index[None, :] == jnp.arange(slot_total, dtype=jnp.int32)[:, None]
    filled = jnp.any(match, axis=1)
    chosen = jnp.sum(jnp.where(match, tile_ids[None, :], 0), axis=1)
    slot_block = jnp.where(filled, jnp.take(target_block, chosen), -1)
    slot_level = jnp.arange(slot_total, dtype=jnp.int32) // (col_groups * CAP)
    col_blocks = 1
    block_cols = columns_all // col_blocks
    right = rhs[0, 0]
    solved = jnp.zeros((row_count, columns_all), jnp.float32)
    outer = jnp.zeros((ABOVE, columns_all), jnp.float32)
    block_numbers = jnp.arange(NT, dtype=jnp.int32)
    for section in range(levels + col_blocks - 1):
        my_block = section - level_index
        active = (my_block >= 0) & (my_block < col_blocks)
        right_part = right
        solved_rows = jnp.dot(
            inverse, right_part.astype(jnp.bfloat16), preferred_element_type=jnp.float32
        )
        previous = solved
        solved = jnp.where(active, solved_rows, previous)
        updates = jnp.dot(
            tiles_used,
            lax.all_gather(solved_rows.astype(jnp.bfloat16), "prow", axis=0, tiled=True),
            preferred_element_type=jnp.float32,
        )
        updates = updates.astype(jnp.bfloat16).reshape(tile_count, block_rows, block_cols)
        padded = jnp.concatenate(
            [updates, jnp.zeros((1, block_rows, block_cols), jnp.bfloat16)], axis=0
        )
        sending = jnp.take(padded, jnp.where(filled & active, chosen, tile_count), axis=0)
        send_block = jnp.where(active, slot_block, -1)
        incoming_block_rows, received_block = (
            lax.all_to_all(sending, ("lvl", "pcol"), split_axis=0, concat_axis=0, tiled=True),
            lax.all_to_all(send_block, ("lvl", "pcol"), split_axis=0, concat_axis=0, tiled=True),
        )
        from_level = slot_level == section
        choosing_mask = (
            (received_block[:, None] == block_numbers[None, :]) & from_level[:, None]
        ).astype(jnp.bfloat16)
        block_fragments = jnp.einsum(
            "at,apz->tpz", choosing_mask, incoming_block_rows, preferred_element_type=jnp.float32
        )
        summed = block_fragments
        summed = summed.reshape(NT * block_rows, columns_all)
        summed = lax.psum(summed, "prow")
        right = right - summed[:width]
        outer = outer + summed[width:]
    return (solved[None, None], outer[None, None])


def solution(mesh):
    placed = (
        P("lvl", "pcol", None, None),
        P("lvl", "pcol", "prow", None),
        P("lvl", "pcol", "prow", None, None),
        P("lvl", "pcol", None),
        P("lvl", "pcol", "prow"),
        P("lvl", "pcol", "prow"),
        P("lvl", "pcol", "prow"),
    )
    return jax.shard_map(
        per_device,
        mesh=mesh,
        in_specs=placed,
        out_specs=(P("lvl", "pcol", "prow", None), P("lvl", "pcol", None, None)),
        check_vma=False,
    )
```

profile of v0, /device:TPU:0, one launch (start us, length us, event | category | flops | bytes accessed | tf_op | source)
XLA Modules:
  0.0 433.2 jit_solution(8528554265465169059)
XLA Ops:
  7.2 1.0 convert_reduce_fusion
  8.2 0.7 multiply_add_fusion
  8.8 0.1 select_reduce_fusion
  8.9 0.1 fusion.40
  9.1 0.1 reduce_or.12
  9.2 1.3 gather_fusion.1
  10.5 0.1 gather.19
  10.6 0.6 broadcast_select_fusion.4
  11.2 0.6 broadcast_select_fusion.5
  11.8 5.2 %all-to-all-start = ((s32[8,2,1]{1,2,0:T(1,128)}), s32[8,2,1]{1,2,0:T(1,128)S(1)}, u32[]{:S(2)}, u32[]{:S(2)}) async-start(s32[8,2,1]{1,2,0:T(1,128)} %bitcast.9), calls=%async_computation | async-start | bytes 8192 | tf_op jit(solution)/shard_map/all_to_all | solution.py:79
  17.0 0.7 fusion.47
  17.8 0.6 gather_fusion.2
  18.4 0.7 and_select_fusion.4
  19.1 1.4 gather_fusion
  20.6 1.1 fusion.50
  21.7 16.6 %all_gather.12 = bf16[1024,256]{1,0:T(8,128)(2,1)S(1)} all-gather(bf16[256,256]{1,0:T(8,128)(2,1)S(1)} %get-tuple-element.24), channel_id=1, replica_groups=mesh['lvl'=4,'prow'=4,'pcol'=2] {'prow'}, dimensions={0}, use_global_device_ids=true | all-gather | bytes 655360 | tf_op jit(solution)/shard_map/all_gather | solution.py:68
  38.2 0.1 bitcast_select_fusion
  38.3 0.3 convolution_convert_fusion.3
  38.6 0.6 gather_fusion.3
  39.2 0.8 broadcast_select_fusion.3
  40.0 3.8 all-to-all-start.1
  43.9 0.5 broadcast.584
  44.4 0.6 reduce.12
  45.1 5.6 %all-to-all-done.1 = bf16[16,32,256]{2,1,0:T(8,128)(2,1)S(1)} async-done(((bf16[16,32,256]{2,1,0:T(8,128)(2,1)}), bf16[16,32,256]{2,1,0:T(8,128)(2,1)S(1)}, u32[]{:S(2)}, u32[]{:S(2)}) %all-to-all-start.1) | async-done | bytes 262176 | tf_op jit(solution)/shard_map/all_to_all | solution.py:78
  50.7 0.5 fusion.21
  51.2 2.1 copy.31
  53.3 3.3 all-to-all-start.2
  56.6 65.5 %all-reduce.9.cloned.1.call-done = f32[1536,256]{1,0:T(8,128)} async-done(((f32[1536,256]{1,0:T(8,128)}), f32[1536,256]{1,0:T(8,128)}) %all-reduce.9.cloned.1.call-update) | async-done | bytes 1572880 | tf_op jit(solution)/shard_map/psum | solution.py:90
  122.2 2.3 fusion.51
  124.5 15.8 %all_gather.13 = bf16[1024,256]{1,0:T(8,128)(2,1)S(1)} all-gather(bf16[256,256]{1,0:T(8,128)(2,1)S(1)} %get-tuple-element.26), channel_id=1, replica_groups=mesh['lvl'=4,'prow'=4,'pcol'=2] {'prow'}, dimensions={0}, use_global_device_ids=true | all-gather | bytes 655360 | tf_op jit(solution)/shard_map/all_gather | solution.py:68
  140.3 0.3 convolution_convert_fusion.2
  140.7 0.6 gather_fusion.4
  141.2 0.8 broadcast_select_fusion.2
  142.0 3.4 all-to-all-start.3
  145.5 0.6 reduce.13
  146.2 6.1 %all-to-all-done.3 = bf16[16,32,256]{2,1,0:T(8,128)(2,1)S(1)} async-done(((bf16[16,32,256]{2,1,0:T(8,128)(2,1)}), bf16[16,32,256]{2,1,0:T(8,128)(2,1)S(1)}, u32[]{:S(2)}, u32[]{:S(2)}) %all-to-all-start.3) | async-done | bytes 262176 | tf_op jit(solution)/shard_map/all_to_all | solution.py:78
  152.3 0.5 fusion.19
  152.8 2.1 copy.34
  154.9 3.5 all-to-all-start.4
  158.4 63.7 %all-reduce.11.cloned.1.call-done = f32[1536,256]{1,0:T(8,128)} async-done(((f32[1536,256]{1,0:T(8,128)}), f32[1536,256]{1,0:T(8,128)}) %all-reduce.11.cloned.1.call-update) | async-done | bytes 1572880 | tf_op jit(solution)/shard_map/psum | solution.py:90
  222.0 2.6 fusion.52
  224.6 15.8 %all_gather.14 = bf16[1024,256]{1,0:T(8,128)(2,1)S(1)} all-gather(bf16[256,256]{1,0:T(8,128)(2,1)S(1)} %get-tuple-element.28), channel_id=1, replica_groups=mesh['lvl'=4,'prow'=4,'pcol'=2] {'prow'}, dimensions={0}, use_global_device_ids=true | all-gather | bytes 655360 | tf_op jit(solution)/shard_map/all_gather | solution.py:68
  240.5 0.3 convolution_convert_fusion.1
  240.8 1.3 gather_fusion.5
  242.1 1.7 broadcast_select_fusion.1
  243.8 3.4 all-to-all-start.5
  247.3 0.6 reduce.14
  248.0 6.1 %all-to-all-done.5 = bf16[16,32,256]{2,1,0:T(8,128)(2,1)S(1)} async-done(((bf16[16,32,256]{2,1,0:T(8,128)(2,1)}), bf16[16,32,256]{2,1,0:T(8,128)(2,1)S(1)}, u32[]{:S(2)}, u32[]{:S(2)}) %all-to-all-start.5) | async-done | bytes 262176 | tf_op jit(solution)/shard_map/all_to_all | solution.py:78
  254.1 0.5 fusion.17
  254.6 2.1 copy.37
  256.7 3.5 all-to-all-start.6
  260.2 63.7 %all-reduce.13.cloned.1.call-done = f32[1536,256]{1,0:T(8,128)} async-done(((f32[1536,256]{1,0:T(8,128)}), f32[1536,256]{1,0:T(8,128)}) %all-reduce.13.cloned.1.call-update) | async-done | bytes 1572880 | tf_op jit(solution)/shard_map/psum | solution.py:90
  323.8 2.9 fusion.49
  326.8 15.8 %all_gather.15 = bf16[1024,256]{1,0:T(8,128)(2,1)S(1)} all-gather(bf16[256,256]{1,0:T(8,128)(2,1)S(1)} %get-tuple-element.13), channel_id=1, replica_groups=mesh['lvl'=4,'prow'=4,'pcol'=2] {'prow'}, dimensions={0}, use_global_device_ids=true | all-gather | bytes 655360 | tf_op jit(solution)/shard_map/all_gather | solution.py:68
  342.6 0.3 convolution_convert_fusion
  342.9 0.6 gather_fusion.6
  343.5 0.8 broadcast_select_fusion
  344.3 3.4 all-to-all-start.7
  347.8 0.6 reduce.15
  348.5 6.1 %all-to-all-done.7 = bf16[16,32,256]{2,1,0:T(8,128)(2,1)S(1)} async-done(((bf16[16,32,256]{2,1,0:T(8,128)(2,1)}), bf16[16,32,256]{2,1,0:T(8,128)(2,1)S(1)}, u32[]{:S(2)}, u32[]{:S(2)}) %all-to-all-start.7) | async-done | bytes 262176 | tf_op jit(solution)/shard_map/all_to_all | solution.py:78
  354.6 0.5 fusion.15
  355.1 2.1 copy.40
  357.2 67.2 %all-reduce.15.cloned.1.call-done = f32[1536,256]{1,0:T(8,128)} async-done(((f32[1536,256]{1,0:T(8,128)}), f32[1536,256]{1,0:T(8,128)}) %all-reduce.15.cloned.1.call-update) | async-done | bytes 1572880 | tf_op jit(solution)/shard_map/psum | solution.py:90
  424.3 2.3 fusion.6
  (50 shorter events, 1.0 us)
Async XLA Ops:
  7.2 10.5 %copy-start = (s32[1,1,8]{2,1,0:T(1,128)S(1)}, s32[1,1,8]{2,1,0:T(1,128)}, u32[]{:S(2)}) copy-start(s32[1,1,8]{2,1,0:T(1,128)} %param.12) | copy-start | bytes 100
  7.2 13.4 %copy-start.3 = (bf16[1,1,256,1024]{3,2,1,0:T(8,128)(2,1)S(1)}, bf16[1,1,256,1024]{3,2,1,0:T(8,128)(2,1)}, u32[]{:S(2)}) copy-start(bf16[1,1,256,1024]{3,2,1,0:T(8,128)(2,1)} %param.10) | copy-start | bytes 1572868
  7.2 13.4 %copy-start.1 = (f32[1,1,1024,256]{3,2,1,0:T(8,128)S(1)}, f32[1,1,1024,256]{3,2,1,0:T(8,128)}, u32[]{:S(2)}) copy-start(f32[1,1,1024,256]{3,2,1,0:T(8,128)} %param.9) | copy-start | bytes 3145732
  11.8 28.2 %all-to-all-start = ((s32[8,2,1]{1,2,0:T(1,128)}), s32[8,2,1]{1,2,0:T(1,128)S(1)}, u32[]{:S(2)}, u32[]{:S(2)}) async-start(s32[8,2,1]{1,2,0:T(1,128)} %bitcast.9), calls=%async_computation | async-start | bytes 8192 | tf_op jit(solution)/shard_map/all_to_all | solution.py:79
  20.5 17.8 %copy-start.5 = (bf16[1,1,8,32,1024]{4,3,2,1,0:T(8,128)(2,1)S(1)}, bf16[1,1,8,32,1024]{4,3,2,1,0:T(8,128)(2,1)}, u32[]{:S(2)}) copy-start(bf16[1,1,8,32,1024]{4,3,2,1,0:T(8,128)(2,1)} %param.11) | copy-start | bytes 1572868
  40.0 10.7 %all-to-all-start.1 = ((bf16[16,32,256]{2,1,0:T(8,128)(2,1)}), bf16[16,32,256]{2,1,0:T(8,128)(2,1)S(1)}, u32[]{:S(2)}, u32[]{:S(2)}) async-start(bf16[16,32,256]{2,1,0:T(8,128)(2,1)} %broadcast_select_fusion.3), calls=%async_computation.1 | async-start | bytes 524288 | tf_op jit(solution)/shard_map/all_to_all | solution.py:78
  43.8 78.4 %all-reduce.9.cloned.1.call-start = ((), (), s32[]{:S(2)}) async-start(), calls=%async_computation.8 | async-start | bytes 3145728 | tf_op jit(solution)/shard_map/psum | solution.py:90
  53.3 88.7 %all-to-all-start.2 = ((s32[8,2,1]{1,2,0:T(1,128)}), s32[8,2,1]{1,2,0:T(1,128)S(1)}, u32[]{:S(2)}, u32[]{:S(2)}) async-start(s32[8,2,1]{1,2,0:T(1,128)} %bitcast.20), calls=%async_computation.2 | async-start | bytes 8192 | tf_op jit(solution)/shard_map/all_to_all | solution.py:79
  142.0 10.3 %all-to-all-start.3 = ((bf16[16,32,256]{2,1,0:T(8,128)(2,1)}), bf16[16,32,256]{2,1,0:T(8,128)(2,1)S(1)}, u32[]{:S(2)}, u32[]{:S(2)}) async-start(bf16[16,32,256]{2,1,0:T(8,128)(2,1)} %broadcast_select_fusion.2), calls=%async_computation.3 | async-start | bytes 524288 | tf_op jit(solution)/shard_map/all_to_all | solution.py:78
  145.4 76.6 %all-reduce.11.cloned.1.call-start = ((), (), s32[]{:S(2)}) async-start(), calls=%async_computation.9 | async-start | bytes 3145728 | tf_op jit(solution)/shard_map/psum | solution.py:90
  154.9 67.2 %copy-start.2 = (f32[1536,256]{1,0:T(8,128)S(1)}, f32[1536,256]{1,0:T(8,128)}, u32[]{:S(2)}) copy-start(f32[1536,256]{1,0:T(8,128)} %all-reduce.9.cloned.1.call-done) | copy-start | bytes 4718596
  154.9 88.9 %all-to-all-start.4 = ((s32[8,2,1]{1,2,0:T(1,128)}), s32[8,2,1]{1,2,0:T(1,128)S(1)}, u32[]{:S(2)}, u32[]{:S(2)}) async-start(s32[8,2,1]{1,2,0:T(1,128)} %bitcast.24), calls=%async_computation.4 | async-start | bytes 8192 | tf_op jit(solution)/shard_map/all_to_all | solution.py:79
  243.8 10.3 %all-to-all-start.5 = ((bf16[16,32,256]{2,1,0:T(8,128)(2,1)}), bf16[16,32,256]{2,1,0:T(8,128)(2,1)S(1)}, u32[]{:S(2)}, u32[]{:S(2)}) async-start(bf16[16,32,256]{2,1,0:T(8,128)(2,1)} %broadcast_select_fusion.1), calls=%async_computation.5 | async-start | bytes 524288 | tf_op jit(solution)/shard_map/all_to_all | solution.py:78
  247.2 76.6 %all-reduce.13.cloned.1.call-start = ((), (), s32[]{:S(2)}) async-start(), calls=%async_computation.10 | async-start | bytes 3145728 | tf_op jit(solution)/shard_map/psum | solution.py:90
  256.6 67.2 %copy-start.4 = (f32[256,256]{1,0:T(8,128)S(1)}, f32[256,256]{1,0:T(8,128)}, u32[]{:S(2)}) copy-start(f32[256,256]{1,0:T(8,128)} %get-tuple-element.25) | copy-start | bytes 786436
  256.7 87.6 %all-to-all-start.6 = ((s32[8,2,1]{1,2,0:T(1,128)}), s32[8,2,1]{1,2,0:T(1,128)S(1)}, u32[]{:S(2)}, u32[]{:S(2)}) async-start(s32[8,2,1]{1,2,0:T(1,128)} %bitcast.29), calls=%async_computation.6 | async-start | bytes 8192 | tf_op jit(solution)/shard_map/all_to_all | solution.py:79
  344.3 10.3 %all-to-all-start.7 = ((bf16[16,32,256]{2,1,0:T(8,128)(2,1)}), bf16[16,32,256]{2,1,0:T(8,128)(2,1)S(1)}, u32[]{:S(2)}, u32[]{:S(2)}) async-start(bf16[16,32,256]{2,1,0:T(8,128)(2,1)} %broadcast_select_fusion), calls=%async_computation.7 | async-start | bytes 524288 | tf_op jit(solution)/shard_map/all_to_all | solution.py:78
  347.7 76.6 %all-reduce.15.cloned.1.call-start = ((), (), s32[]{:S(2)}) async-start(), calls=%async_computation.11 | async-start | bytes 3145728 | tf_op jit(solution)/shard_map/psum | solution.py:90
Sparse Core Ops, SparseCore 0:
  53.4 68.6 all-reduce.8
  155.0 66.9 all-reduce.10
  256.8 66.9 all-reduce.12
  357.3 66.9 all-reduce.14
where the time goes:
time: 434 us; the launch traced here: 433 us
  waiting for transfers between devices  284 us (65%)
  blocking collectives  64.1 us (15%)
  starting transfers between devices  29.6 us (7%)
  local copies, waits for them, and re-layouts  15.8 us (4%)
  between operations  14.1 us (3%)
  other arithmetic  13.5 us (3%)
  matrix products  12 us (3%)
    psum x4, waiting for transfers between devices, per_device(): summed = lax.psum(summed, 'prow')  260 us
    all_gather x4, blocking collectives, per_device(): lax.all_gather(solved_rows.astype(jnp.bfloat16), 'prow', axis=0, tiled=True)  64.1 us
    all_to_all x4, waiting for transfers between devices, per_device(): lax.all_to_all(sending, ('lvl', 'pcol'), split_axis=0, concat_axis=0, til...  23.9 us
    all_to_all x4, starting transfers between devices, per_device(): lax.all_to_all(send_block, ('lvl', 'pcol'), split_axis=0, concat_axis=0,...  15.4 us
    all_to_all x4, starting transfers between devices, per_device(): lax.all_to_all(sending, ('lvl', 'pcol'), split_axis=0, concat_axis=0, til...  14 us
    dot_general x4, matrix products, per_device(): jnp.dot(inverse, right_part.astype(jnp.bfloat16), preferred_element_type=...  8.92 us
  transfers between devices with their start and end apart: 12, of which 8 were waited for; matrix products, arithmetic and copies ran while one was open for 6% of the time, Pallas kernels for 0%

commit v1 on v0

v1 whole, which is shorter than its diff:
```python
import jax
import jax.numpy as jnp
from jax import lax
from jax.sharding import PartitionSpec as P

CAP = 2
ABOVE = 512
NT = 48


def per_device(
    rhs, diag_inverse, off_tiles, panel_super, off_device, off_block, offdiag_block_panel
):
    n_lvl = lax.axis_size("lvl")
    n_pcol = lax.axis_size("pcol")
    n_prow = lax.axis_size("prow")
    groups = n_lvl * n_pcol
    level_index = lax.axis_index("lvl")
    row_index = lax.axis_index("prow")
    col_index = lax.axis_index("pcol")
    my_group = level_index * n_pcol + col_index
    width = rhs.shape[2]
    columns_all = rhs.shape[3]
    cols = columns_all // n_prow
    row_count = diag_inverse.shape[2]
    tile_count = off_tiles.shape[2]
    block_rows = off_tiles.shape[3]
    group_tiles = n_prow * tile_count
    slots = n_prow * CAP

    panels = panel_super[0, 0]
    panel_cols = width // panels.shape[0]
    col_super = jnp.repeat(panels, panel_cols)
    row_ids = row_index * row_count + jnp.arange(row_count, dtype=jnp.int32)
    row_super = jnp.take(col_super, row_ids)
    inverse = jnp.where(
        row_super[:, None] == col_super[None, :], diag_inverse[0, 0], jnp.zeros((), jnp.bfloat16)
    )
    tile_supernode = jnp.take(panels, offdiag_block_panel[0, 0])
    tiles_used = jnp.where(
        col_super[None, None, :] == tile_supernode[:, None, None],
        off_tiles[0, 0],
        jnp.zeros((), jnp.bfloat16),
    ).reshape(tile_count * block_rows, width)

    both = jnp.concatenate([inverse, tiles_used], axis=0)
    gathered = lax.all_gather(both, "prow", axis=0)
    inv_full = gathered[:, :row_count].reshape(n_prow * row_count, width)
    tiles_full = gathered[:, row_count:].reshape(group_tiles * block_rows, width)

    meta = jnp.stack([off_device[0, 0], off_block[0, 0]], axis=0)
    meta = lax.all_gather(meta, ("lvl", "pcol", "prow"), axis=0)
    meta = meta.reshape(groups, n_prow, 2, tile_count)
    target = jnp.transpose(meta[:, :, 0, :], (0, 1, 2)).reshape(groups, group_tiles)
    block = meta[:, :, 1, :].reshape(groups, group_tiles)
    tile_ids = jnp.arange(group_tiles, dtype=jnp.int32)
    source_row = tile_ids // tile_count
    earlier = (
        (target[:, :, None] == target[:, None, :])
        & (source_row[:, None] == source_row[None, :])[None]
        & (tile_ids[:, None] > tile_ids[None, :])[None]
    )
    position = jnp.sum(earlier.astype(jnp.int32), axis=2)
    local_slot = source_row[None, :] * CAP + position

    my_target = jnp.take(target, my_group, axis=0)
    my_slot = my_target * slots + jnp.take(local_slot, my_group, axis=0)
    send_pick = (
        my_slot[None, :] == jnp.arange(groups * slots, dtype=jnp.int32)[:, None]
    ).astype(jnp.bfloat16)

    to_me = target == my_group
    block_ids = jnp.arange(NT, dtype=jnp.int32)
    slot_ids = jnp.arange(slots, dtype=jnp.int32)
    pick = (
        to_me[:, None, None, :]
        & (local_slot[:, None, None, :] == slot_ids[None, None, :, None])
        & (block[:, None, None, :] == block_ids[None, :, None, None])
    )
    recv_pick = jnp.any(pick, axis=3).astype(jnp.bfloat16)
    recv_pick = recv_pick.reshape(n_lvl, n_pcol, NT, slots)
    recv_pick = jnp.transpose(recv_pick, (0, 2, 1, 3)).reshape(n_lvl, NT, n_pcol * slots)

    right = lax.dynamic_slice_in_dim(rhs[0, 0], row_index * cols, cols, axis=1)
    outer = jnp.zeros((ABOVE, cols), jnp.float32)
    solved = jnp.zeros((width, cols), jnp.float32)
    for section in range(n_lvl):
        solved_now = jnp.dot(
            inv_full, right.astype(jnp.bfloat16), preferred_element_type=jnp.float32
        )
        solved = jnp.where(level_index == section, solved_now, solved)
        updates = jnp.dot(
            tiles_full, solved_now.astype(jnp.bfloat16), preferred_element_type=jnp.float32
        ).astype(jnp.bfloat16)
        updates = updates.reshape(group_tiles, block_rows * cols)
        sending = jnp.dot(send_pick, updates, preferred_element_type=jnp.float32)
        sending = sending.astype(jnp.bfloat16).reshape(groups * slots, block_rows, cols)
        incoming = lax.all_to_all(
            sending, ("lvl", "pcol"), split_axis=0, concat_axis=0, tiled=True
        )
        incoming = incoming.reshape(n_lvl, n_pcol * slots, block_rows * cols)[section]
        summed = jnp.dot(recv_pick[section], incoming, preferred_element_type=jnp.float32)
        summed = summed.reshape(NT * block_rows, cols)
        right = right - summed[:width]
        outer = outer + summed[width:]

    rows_out = width // n_prow
    final = jnp.concatenate(
        [
            solved.reshape(n_prow, rows_out, cols),
            jnp.broadcast_to(outer[None], (n_prow, ABOVE, cols)),
        ],
        axis=1,
    )
    final = lax.all_to_all(final, "prow", split_axis=0, concat_axis=0, tiled=True)
    solution_rows = jnp.transpose(final[:, :rows_out], (1, 0, 2)).reshape(rows_out, columns_all)
    outer_all = jnp.transpose(final[:, rows_out:], (1, 0, 2)).reshape(ABOVE, columns_all)
    return (solution_rows[None, None], outer_all[None, None])


def solution(mesh):
    placed = (
        P("lvl", "pcol", None, None),
        P("lvl", "pcol", "prow", None),
        P("lvl", "pcol", "prow", None, None),
        P("lvl", "pcol", None),
        P("lvl", "pcol", "prow"),
        P("lvl", "pcol", "prow"),
        P("lvl", "pcol", "prow"),
    )
    return jax.shard_map(
        per_device,
        mesh=mesh,
        in_specs=placed,
        out_specs=(P("lvl", "pcol", "prow", None), P("lvl", "pcol", None, None)),
        check_vma=False,
    )
```

time: 434 us -> 247 us (0.57)
  waiting for transfers between devices: 284 us -> 35.7 us
  local copies, waits for them, and re-layouts: 15.8 us -> 57.9 us
  blocking collectives: 64.1 us -> 93 us
  starting transfers between devices: 29.6 us -> 15.5 us
  matrix products: 12 us -> 20.2 us
  other arithmetic: 13.5 us -> 8.9 us
    psum x4 -> x0, waiting for transfers between devices: 260 us -> none  [per_device(): summed = lax.psum(summed, 'prow')]
    all_to_all x0 -> x1, blocking collectives: none -> 22.1 us  [per_device(): lax.all_to_all(final, 'prow', split_axis=0, concat_axis=0, tiled=True)]
    unnamed x12 -> x40, local copies, waits for them, and re-layouts: 0.03 us -> 18.7 us
    all_to_all x4 -> x0, starting transfers between devices: 15.4 us -> none  [per_device(): lax.all_to_all(send_block, ('lvl', 'pcol'), split_axis=0, concat_axis=0,...]
    reshape x0 -> x9, local copies, waits for them, and re-layouts: none -> 10.7 us  [the longest x4 6.37 us: per_device(): sending.astype(jnp.bfloat16).reshape(groups * slots, block_rows, cols)]
    all_gather x0 -> x1, waiting for transfers between devices: none -> 10.6 us  [per_device(): gathered = lax.all_gather(both, 'prow', axis=0)]
    slice x0 -> x10, local copies, waits for them, and re-layouts: none -> 9.67 us  [the longest x4 4.05 us: per_device(): incoming.reshape(n_lvl, n_pcol * slots, block_rows * cols)[section]]
    dot_general x4 -> x0, local copies, waits for them, and re-layouts: 8.3 us -> none  [per_device(): jnp.einsum('at,apz->tpz', choosing_mask, incoming_block_rows, preferred_e...]
  transfers between devices with their start and end apart: 12 -> 5, of which waited for: 8 -> 5; matrix products, arithmetic and copies ran while one was open for 6% -> 2% of each run, Pallas kernels for 0% -> 0%
where the time goes in v1:
time: 247 us; the launch traced here: 246 us
  blocking collectives  93 us (38%)
  local copies, waits for them, and re-layouts  57.9 us (23%)
  waiting for transfers between devices  35.7 us (14%)
  matrix products  20.2 us (8%)
  starting transfers between devices  15.5 us (6%)
  between operations  14.4 us (6%)
  other arithmetic  8.9 us (4%)
    all_gather x1, blocking collectives, per_device(): meta = lax.all_gather(meta, ('lvl', 'pcol', 'prow'), axis=0)  70.9 us
    all_to_all x4, waiting for transfers between devices, per_device(): lax.all_to_all(sending, ('lvl', 'pcol'), split_axis=0, concat_axis=0, til...  25.1 us
    all_to_all x1, blocking collectives, per_device(): lax.all_to_all(final, 'prow', split_axis=0, concat_axis=0, tiled=True)  22.1 us
    unnamed x40, local copies, waits for them, and re-layouts  18.7 us
    all_to_all x4, starting transfers between devices, per_device(): lax.all_to_all(sending, ('lvl', 'pcol'), split_axis=0, concat_axis=0, til...  15.5 us
    all_gather x1, waiting for transfers between devices, per_device(): gathered = lax.all_gather(both, 'prow', axis=0)  10.6 us
    dot_general x4, matrix products, per_device(): jnp.dot(inv_full, right.astype(jnp.bfloat16), preferred_element_type=jnp....  7.38 us
    reshape x4, local copies, waits for them, and re-layouts, per_device(): sending.astype(jnp.bfloat16).reshape(groups * slots, block_rows, cols)  6.37 us
  transfers between devices with their start and end apart: 5, of which 5 were waited for; matrix products, arithmetic and copies ran while one was open for 2% of the time, Pallas kernels for 0%

profile of v1, /device:TPU:0, one launch (start us, length us, event | category | flops | bytes accessed | tf_op | source)
XLA Modules:
  0.0 245.7 jit_solution(3200089025834589920)
XLA Ops:
  7.2 0.8 broadcast_bitcast_fusion
  8.7 1.3 gather_fusion.1
  10.8 1.4 gather_fusion
  12.1 1.4 bitcast_select_fusion
  13.6 1.0 pad_maximum_fusion
  14.7 70.9 %all-gather.2 = s32[32,2,8]{2,1,0:T(2,128)S(1)} all-gather(s32[1,2,8]{2,1,0:T(2,128)S(1)} %add_bitcast_fusion), channel_id=3, replica_groups=mesh['lvl'=4,'prow'=4,'pcol'=2] {'lvl','pcol','prow'}, dimensions={0}, use_global_device_ids=true | all-gather | bytes 2112 | tf_op jit(solution)/shard_map/all_gather | solution.py:52
  86.3 1.0 constant_dynamic-slice_fusion.2
  87.3 0.7 iota_compare_fusion
  88.0 10.6 %all-gather.5.cloned.1.call-done = bf16[2048,1024]{1,0:T(8,128)(2,1)} async-done(((bf16[512,1024]{1,0:T(8,128)(2,1)}), bf16[2048,1024]{1,0:T(8,128)(2,1)}) %all-gather.5.cloned.1.call-update) | async-done | bytes 4194320 | tf_op jit(solution)/shard_map/all_gather | solution.py:47
  98.6 2.8 %fusion.26 = (bf16[4,256,1024]{2,1,0:T(8,128)(2,1)S(1)}, bf16[4,256,1024]{2,1,0:T(8,128)(2,1)S(1)}) fusion(bf16[4,512,1024]{2,1,0:T(8,128)(2,1)} %bitcast.95), kind=kLoop, calls=%fused_computation.83 | loop fusion | bytes 8388608 | tf_op jit(solution)/shard_map/slice | solution.py:48
  101.4 0.8 fusion.4
  102.9 0.8 convolution_convert_fusion.7
  104.3 1.3 reshape.343
  105.6 2.1 reshape.430
  107.8 3.8 %all-to-all-start = ((bf16[8,2,8192]{2,1,0:T(2,128)(2,1)}), bf16[8,2,8192]{2,1,0:T(2,128)(2,1)S(1)}, u32[]{:S(2)}, u32[]{:S(2)}) async-start(bf16[8,2,8192]{2,1,0:T(2,128)(2,1)} %reshape.430), calls=%async_computation | async-start | bytes 524288 | tf_op jit(solution)/shard_map/all_to_all | solution.py:98
  112.0 6.5 %all-to-all-done = bf16[8,2,8192]{2,1,0:T(2,128)(2,1)S(1)} async-done(((bf16[8,2,8192]{2,1,0:T(2,128)(2,1)}), bf16[8,2,8192]{2,1,0:T(2,128)(2,1)S(1)}, u32[]{:S(2)}, u32[]{:S(2)}) %all-to-all-start) | async-done | bytes 262176 | tf_op jit(solution)/shard_map/all_to_all | solution.py:98
  118.5 1.2 reshape.431
  119.7 0.9 slice.119
  120.6 0.8 squeeze.45
  121.4 1.1 fusion.19
  122.5 0.7 slice.120
  123.2 1.9 slice.88
  125.2 2.1 fusion.1
  128.0 1.4 convolution_convert_fusion.6
  129.4 1.7 copy.27
  131.1 1.9 reshape.344
  133.0 1.8 convolution_convert_fusion.2
  134.8 2.3 reshape.345
  137.1 2.1 reshape.432
  139.2 4.0 %all-to-all-start.1 = ((bf16[8,2,8192]{2,1,0:T(2,128)(2,1)}), bf16[8,2,8192]{2,1,0:T(2,128)(2,1)}, u32[]{:S(2)}, u32[]{:S(2)}) async-start(bf16[8,2,8192]{2,1,0:T(2,128)(2,1)} %reshape.432), calls=%async_computation.1 | async-start | bytes 524288 | tf_op jit(solution)/shard_map/all_to_all | solution.py:98
  143.3 1.9 dynamic_slice.6
  145.2 5.0 %all-to-all-done.1 = bf16[8,2,8192]{2,1,0:T(2,128)(2,1)} async-done(((bf16[8,2,8192]{2,1,0:T(2,128)(2,1)}), bf16[8,2,8192]{2,1,0:T(2,128)(2,1)}, u32[]{:S(2)}, u32[]{:S(2)}) %all-to-all-start.1) | async-done | bytes 262176 | tf_op jit(solution)/shard_map/all_to_all | solution.py:98
  150.2 2.1 reshape.433
  152.3 1.6 slice.122
  153.9 1.7 squeeze.47
  155.6 1.1 fusion.18
  156.7 0.7 copy-done.6
  157.4 1.7 fusion.25
  159.1 1.9 convert_element_type.77
  161.0 1.9 fusion.27
  163.6 1.4 convolution_convert_fusion.5
  165.0 1.7 copy.28
  166.7 1.9 reshape.346
  168.6 1.8 convolution_convert_fusion.1
  170.4 2.3 reshape.347
  172.7 2.1 reshape.434
  174.8 4.2 %all-to-all-start.2 = ((bf16[8,2,8192]{2,1,0:T(2,128)(2,1)}), bf16[8,2,8192]{2,1,0:T(2,128)(2,1)}, u32[]{:S(2)}, u32[]{:S(2)}) async-start(bf16[8,2,8192]{2,1,0:T(2,128)(2,1)} %reshape.434), calls=%async_computation.2 | async-start | bytes 524288 | tf_op jit(solution)/shard_map/all_to_all | solution.py:98
  179.0 6.8 %all-to-all-done.2 = bf16[8,2,8192]{2,1,0:T(2,128)(2,1)} async-done(((bf16[8,2,8192]{2,1,0:T(2,128)(2,1)}), bf16[8,2,8192]{2,1,0:T(2,128)(2,1)}, u32[]{:S(2)}, u32[]{:S(2)}) %all-to-all-start.2) | async-done | bytes 262176 | tf_op jit(solution)/shard_map/all_to_all | solution.py:98
  185.8 2.1 reshape.435
  187.9 1.6 slice.125
  189.5 1.7 squeeze.49
  191.2 1.1 fusion.17
  192.3 0.7 copy-done.10
  193.0 1.8 fusion.3
  194.8 1.9 convert_element_type.82
  196.7 2.7 %select_select_fusion = (f32[1024,64]{0,1:T(8,128)}, bf16[1024,64]{0,1:T(8,128)(2,1)S(1)}) fusion(f32[1024,64]{0,1:T(8,128)} %copy-done.7, f32[1024,64]{0,1:T(8,128)} %copy-done.9, f32[1024,64]{0,1:T(8,128)} %copy-done.8, pred[]{:T(512)S(6)} %eq.161, pred[]{:T(512)S(6)} %eq.160, pred[]{:T(512)S(6)} %eq.159, pred[]{:T(512)S(6)} %eq.134, ...), kind=kOutput, calls=%fused_computation.25 | convolution fusion | flops 134545408 | bytes 3407876 | tf_op jit(solution)/shard_map/dot_general | solution.py:88
  199.3 0.8 convolution_convert_fusion.4
  201.3 1.1 reshape.436
  202.4 3.4 %all-to-all-start.3 = ((bf16[8,2,8192]{2,1,0:T(2,128)(2,1)}), bf16[8,2,8192]{2,1,0:T(2,128)(2,1)S(1)}, u32[]{:S(2)}, u32[]{:S(2)}) async-start(bf16[8,2,8192]{2,1,0:T(2,128)(2,1)} %reshape.436), calls=%async_computation.3 | async-start | bytes 524288 | tf_op jit(solution)/shard_map/all_to_all | solution.py:98
  205.8 6.8 %all-to-all-done.3 = bf16[8,2,8192]{2,1,0:T(2,128)(2,1)S(1)} async-done(((bf16[8,2,8192]{2,1,0:T(2,128)(2,1)}), bf16[8,2,8192]{2,1,0:T(2,128)(2,1)S(1)}, u32[]{:S(2)}, u32[]{:S(2)}) %all-to-all-start.3) | async-done | bytes 262176 | tf_op jit(solution)/shard_map/all_to_all | solution.py:98
  213.2 1.2 convolution_add_fusion
  214.8 22.1 %all_to_all.25 = f32[4,768,64]{1,2,0:T(8,128)S(1)} all-to-all(f32[4,768,64]{1,2,0:T(8,128)S(1)} %pad_maximum_fusion.1), channel_id=1, replica_groups=mesh['lvl'=4,'prow'=4,'pcol'=2] {'prow'}, dimensions={0} | all-to-all | bytes 1572864 | tf_op jit(solution)/shard_map/all_to_all | solution.py:115
  237.0 0.8 copy.32
  237.9 1.0 copy.33
  (68 shorter events, 7.5 us)
Async XLA Ops:
  7.2 79.1 %copy-start = (f32[1,1,1024,256]{3,2,1,0:T(8,128)S(1)}, f32[1,1,1024,256]{3,2,1,0:T(8,128)}, u32[]{:S(2)}) copy-start(f32[1,1,1024,256]{3,2,1,0:T(8,128)} %param.9) | copy-start | bytes 3145732
  7.2 91.4 %all-gather.5.cloned.1.call-start = ((), (), s32[]{:S(2)}) async-start(), calls=%async_computation.5 | async-start | bytes 5242880 | tf_op jit(solution)/shard_map/all_gather | solution.py:47
  13.6 1.1 copy-start.13
  13.6 1.1 copy-start.14
  98.6 2.8 %copy-start.5 = (f32[1,1,1024,64]{3,2,1,0:T(8,128)S(1)}, f32[1,1,1024,64]{3,2,1,0:T(8,128)}, u32[]{:S(2)}) copy-start(f32[1,1,1024,64]{3,2,1,0:T(8,128)} %constant_dynamic-slice_fusion.2) | copy-start | bytes 786436
  101.4 1.3 copy-start.1
  102.1 0.7 copy-start.8
  104.3 7.3 %copy-start.12 = (pred[8,48,32]{1,2,0:T(8,128)(4,1)S(1)}, pred[8,48,32]{1,2,0:T(8,128)(4,1)}, u32[]{:S(2)}) copy-start(pred[8,48,32]{1,2,0:T(8,128)(4,1)} %iota_compare_fusion) | copy-start | bytes 36868
  107.8 10.7 %all-to-all-start = ((bf16[8,2,8192]{2,1,0:T(2,128)(2,1)}), bf16[8,2,8192]{2,1,0:T(2,128)(2,1)S(1)}, u32[]{:S(2)}, u32[]{:S(2)}) async-start(bf16[8,2,8192]{2,1,0:T(2,128)(2,1)} %reshape.430), calls=%async_computation | async-start | bytes 524288 | tf_op jit(solution)/shard_map/all_to_all | solution.py:98
  125.2 2.8 %copy-start.2 = (bf16[4,256,1024]{2,1,0:T(8,128)(2,1)S(1)}, bf16[4,256,1024]{2,1,0:T(8,128)(2,1)}, u32[]{:S(2)}) copy-start(bf16[4,256,1024]{2,1,0:T(8,128)(2,1)} %copy-done.1) | copy-start | bytes 6291460
  127.3 0.7 copy-start.9
  139.2 11.0 %all-to-all-start.1 = ((bf16[8,2,8192]{2,1,0:T(2,128)(2,1)}), bf16[8,2,8192]{2,1,0:T(2,128)(2,1)}, u32[]{:S(2)}, u32[]{:S(2)}) async-start(bf16[8,2,8192]{2,1,0:T(2,128)(2,1)} %reshape.432), calls=%async_computation.1 | async-start | bytes 524288 | tf_op jit(solution)/shard_map/all_to_all | solution.py:98
  156.7 0.7 copy-start.6
  161.0 2.6 %copy-start.3 = (bf16[4,256,1024]{2,1,0:T(8,128)(2,1)S(1)}, bf16[4,256,1024]{2,1,0:T(8,128)(2,1)}, u32[]{:S(2)}) copy-start(bf16[4,256,1024]{2,1,0:T(8,128)(2,1)} %copy-done.1) | copy-start | bytes 6291460
  162.8 0.7 copy-start.7
  174.8 11.0 %all-to-all-start.2 = ((bf16[8,2,8192]{2,1,0:T(2,128)(2,1)}), bf16[8,2,8192]{2,1,0:T(2,128)(2,1)}, u32[]{:S(2)}, u32[]{:S(2)}) async-start(bf16[8,2,8192]{2,1,0:T(2,128)(2,1)} %reshape.434), calls=%async_computation.2 | async-start | bytes 524288 | tf_op jit(solution)/shard_map/all_to_all | solution.py:98
  192.3 0.7 copy-start.10
  196.7 2.7 %copy-start.4 = (bf16[4,256,1024]{2,1,0:T(8,128)(2,1)S(1)}, bf16[4,256,1024]{2,1,0:T(8,128)(2,1)}, u32[]{:S(2)}) copy-start(bf16[4,256,1024]{2,1,0:T(8,128)(2,1)} %copy-done.1) | copy-start | bytes 6291460
  200.1 5.7 %copy-start.11 = (f32[1024,64]{0,1:T(8,128)S(1)}, f32[1024,64]{0,1:T(8,128)}, u32[]{:S(2)}) copy-start(f32[1024,64]{0,1:T(8,128)} %get-tuple-element.24) | copy-start | bytes 786436
  202.4 10.3 %all-to-all-start.3 = ((bf16[8,2,8192]{2,1,0:T(2,128)(2,1)}), bf16[8,2,8192]{2,1,0:T(2,128)(2,1)S(1)}, u32[]{:S(2)}, u32[]{:S(2)}) async-start(bf16[8,2,8192]{2,1,0:T(2,128)(2,1)} %reshape.436), calls=%async_computation.3 | async-start | bytes 524288 | tf_op jit(solution)/shard_map/all_to_all | solution.py:98
Sparse Core Ops, SparseCore 0:
  14.8 83.7 all-gather.4

commit v2 on v1

--- a/solution.py
+++ b/solution.py
@@ -47,11 +47,15 @@
     gathered = lax.all_gather(both, "prow", axis=0)
     inv_full = gathered[:, :row_count].reshape(n_prow * row_count, width)
     tiles_full = gathered[:, row_count:].reshape(group_tiles * block_rows, width)
+    tiles_full = jnp.concatenate(
+        [tiles_full, jnp.zeros((block_rows, width), jnp.bfloat16)], axis=0
+    )
 
     meta = jnp.stack([off_device[0, 0], off_block[0, 0]], axis=0)
-    meta = lax.all_gather(meta, ("lvl", "pcol", "prow"), axis=0)
-    meta = meta.reshape(groups, n_prow, 2, tile_count)
-    target = jnp.transpose(meta[:, :, 0, :], (0, 1, 2)).reshape(groups, group_tiles)
+    meta = lax.all_gather(meta, ("lvl", "prow", "pcol"), axis=0)
+    meta = meta.reshape(n_lvl, n_prow, n_pcol, 2, tile_count)
+    meta = jnp.transpose(meta, (0, 2, 1, 3, 4)).reshape(groups, n_prow, 2, tile_count)
+    target = meta[:, :, 0, :].reshape(groups, group_tiles)
     block = meta[:, :, 1, :].reshape(groups, group_tiles)
     tile_ids = jnp.arange(group_tiles, dtype=jnp.int32)
     source_row = tile_ids // tile_count
@@ -65,21 +69,20 @@
 
     my_target = jnp.take(target, my_group, axis=0)
     my_slot = my_target * slots + jnp.take(local_slot, my_group, axis=0)
-    send_pick = (
-        my_slot[None, :] == jnp.arange(groups * slots, dtype=jnp.int32)[:, None]
-    ).astype(jnp.bfloat16)
+    send_match = my_slot[None, :] == jnp.arange(groups * slots, dtype=jnp.int32)[:, None]
+    send_index = jnp.where(
+        jnp.any(send_match, axis=1),
+        jnp.sum(jnp.where(send_match, tile_ids[None, :], 0), axis=1),
+        group_tiles,
+    )
 
     to_me = target == my_group
-    block_ids = jnp.arange(NT, dtype=jnp.int32)
     slot_ids = jnp.arange(slots, dtype=jnp.int32)
-    pick = (
-        to_me[:, None, None, :]
-        & (local_slot[:, None, None, :] == slot_ids[None, None, :, None])
-        & (block[:, None, None, :] == block_ids[None, :, None, None])
+    pick = to_me[:, None, :] & (local_slot[:, None, :] == slot_ids[None, :, None])
+    recv_block = jnp.where(
+        jnp.any(pick, axis=2), jnp.sum(jnp.where(pick, block[:, None, :], 0), axis=2), NT
     )
-    recv_pick = jnp.any(pick, axis=3).astype(jnp.bfloat16)
-    recv_pick = recv_pick.reshape(n_lvl, n_pcol, NT, slots)
-    recv_pick = jnp.transpose(recv_pick, (0, 2, 1, 3)).reshape(n_lvl, NT, n_pcol * slots)
+    recv_block = recv_block.reshape(n_lvl, n_pcol * slots)
 
     right = lax.dynamic_slice_in_dim(rhs[0, 0], row_index * cols, cols, axis=1)
     outer = jnp.zeros((ABOVE, cols), jnp.float32)
@@ -92,15 +95,15 @@
         updates = jnp.dot(
             tiles_full, solved_now.astype(jnp.bfloat16), preferred_element_type=jnp.float32
         ).astype(jnp.bfloat16)
-        updates = updates.reshape(group_tiles, block_rows * cols)
-        sending = jnp.dot(send_pick, updates, preferred_element_type=jnp.float32)
-        sending = sending.astype(jnp.bfloat16).reshape(groups * slots, block_rows, cols)
+        updates = updates.reshape(group_tiles + 1, block_rows, cols)
+        sending = jnp.take(updates, send_index, axis=0)
         incoming = lax.all_to_all(
             sending, ("lvl", "pcol"), split_axis=0, concat_axis=0, tiled=True
         )
-        incoming = incoming.reshape(n_lvl, n_pcol * slots, block_rows * cols)[section]
-        summed = jnp.dot(recv_pick[section], incoming, preferred_element_type=jnp.float32)
-        summed = summed.reshape(NT * block_rows, cols)
+        incoming = incoming.reshape(n_lvl, n_pcol * slots, block_rows, cols)[section]
+        summed = jnp.zeros((NT + 1, block_rows, cols), jnp.float32)
+        summed = summed.at[recv_block[section]].add(incoming.astype(jnp.float32))
+        summed = summed[:NT].reshape(NT * block_rows, cols)
         right = right - summed[:width]
         outer = outer + summed[width:]
 

time: 247 us -> 236 us (0.955)
  waiting for transfers between devices: 35.7 us -> 64.1 us
  blocking collectives: 93 us -> 65.9 us
  local copies, waits for them, and re-layouts: 57.9 us -> 38 us
  other arithmetic: 8.9 us -> 28.3 us
  matrix products: 20.2 us -> 9.36 us
    all_gather x1, blocking collectives: 70.9 us -> 43.8 us  [per_device(): meta = lax.all_gather(meta, ('lvl', 'prow', 'pcol'), axis=0)]
    all_gather x1, waiting for transfers between devices: 10.6 us -> 37.6 us  [per_device(): gathered = lax.all_gather(both, 'prow', axis=0)]
    reshape x8 -> x1, local copies, waits for them, and re-layouts: 10.7 us -> 0.02 us  [per_device(): meta = meta.reshape(n_lvl, n_prow, n_pcol, 2, tile_count)]
    scatter-add x0 -> x4, other arithmetic: none -> 9.07 us  [per_device(): summed = summed.at[recv_block[section]].add(incoming.astype(jnp.float32))]
    dot_general x8 -> x0, matrix products: 8.53 us -> none  [the longest x4 4.5 us: per_device(): jnp.dot(recv_pick[section], incoming, preferred_element_type=jnp.float32)]
    gather x0 -> x4, local copies, waits for them, and re-layouts: none -> 6.14 us  [per_device(): sending = jnp.take(updates, send_index, axis=0)]
    select_n x0 -> x9, other arithmetic: none -> 6.12 us  [the longest x4 6.09 us: per_device(): sending = jnp.take(updates, send_index, axis=0)]
    squeeze x5 -> x4, local copies, waits for them, and re-layouts: 4.41 us -> 0.33 us  [per_device(): summed = summed.at[recv_block[section]].add(incoming.astype(jnp.float32))]
  transfers between devices with their start and end apart: 5 -> 5, of which waited for: 5 -> 5; matrix products, arithmetic and copies ran while one was open for 2% -> 1% of each run, Pallas kernels for 0% -> 0%
where the time goes in v2:
time: 236 us; the launch traced here: 235 us
  blocking collectives  65.9 us (28%)
  waiting for transfers between devices  64.1 us (27%)
  local copies, waits for them, and re-layouts  38 us (16%)
  other arithmetic  28.3 us (12%)
  starting transfers between devices  14.8 us (6%)
  between operations  14.5 us (6%)
  matrix products  9.36 us (4%)
    all_gather x1, blocking collectives, per_device(): meta = lax.all_gather(meta, ('lvl', 'prow', 'pcol'), axis=0)  43.8 us
    all_gather x1, waiting for transfers between devices, per_device(): gathered = lax.all_gather(both, 'prow', axis=0)  37.6 us
    all_to_all x4, waiting for transfers between devices, per_device(): lax.all_to_all(sending, ('lvl', 'pcol'), split_axis=0, concat_axis=0, til...  26.4 us
    all_to_all x1, blocking collectives, per_device(): lax.all_to_all(final, 'prow', split_axis=0, concat_axis=0, tiled=True)  22.1 us
    unnamed x46, local copies, waits for them, and re-layouts  15.7 us
    all_to_all x4, starting transfers between devices, per_device(): lax.all_to_all(sending, ('lvl', 'pcol'), split_axis=0, concat_axis=0, til...  14.7 us
    scatter-add x4, other arithmetic, per_device(): summed = summed.at[recv_block[section]].add(incoming.astype(jnp.float32))  9.07 us
    gather x4, local copies, waits for them, and re-layouts, per_device(): sending = jnp.take(updates, send_index, axis=0)  6.14 us
  transfers between devices with their start and end apart: 5, of which 5 were waited for; matrix products, arithmetic and copies ran while one was open for 1% of the time, Pallas kernels for 0%

profile of v2, /device:TPU:0, one launch (start us, length us, event | category | flops | bytes accessed | tf_op | source)
XLA Modules:
  0.0 234.9 jit_solution(14032246615957375715)
XLA Ops:
  7.3 0.8 broadcast_bitcast_fusion
  8.1 1.4 gather_fusion
  9.4 0.7 fusion.22
  10.1 1.3 gather_fusion.1
  11.4 0.7 and_select_fusion.1
  12.2 1.4 bitcast_select_fusion
  13.6 1.0 pad_maximum_fusion
  14.7 43.8 %all-gather.2 = s32[32,2,8]{2,1,0:T(2,128)S(1)} all-gather(s32[1,2,8]{2,1,0:T(2,128)S(1)} %add_bitcast_fusion), channel_id=3, replica_groups=mesh['lvl'=4,'prow'=4,'pcol'=2] {'lvl','prow','pcol'}, dimensions={0}, use_global_device_ids=true | all-gather | bytes 2112 | tf_op jit(solution)/shard_map/all_gather | solution.py:55
  59.8 1.0 constant_dynamic-slice_fusion.2
  60.8 37.6 %all-gather.5.cloned.1.call-done = bf16[2048,1024]{1,0:T(8,128)(2,1)} async-done(((bf16[512,1024]{1,0:T(8,128)(2,1)}), bf16[2048,1024]{1,0:T(8,128)(2,1)}) %all-gather.5.cloned.1.call-update) | async-done | bytes 4194320 | tf_op jit(solution)/shard_map/all_gather | solution.py:47
  98.4 2.8 %fusion.32 = (bf16[4,256,1024]{2,1,0:T(8,128)(2,1)S(1)}, bf16[4,256,1024]{2,1,0:T(8,128)(2,1)S(1)}) fusion(bf16[4,512,1024]{2,1,0:T(8,128)(2,1)} %bitcast.93), kind=kLoop, calls=%fused_computation.103 | loop fusion | bytes 8388608 | tf_op jit(solution)/shard_map/slice | solution.py:48
  101.2 0.8 fusion.8
  102.0 0.5 copy-done.1
  102.7 1.5 convolution_convert_fusion.3
  104.2 1.1 copy.44
  105.3 1.4 gather_fusion.2
  106.7 2.0 broadcast_select_fusion.3
  108.7 2.1 reshape.577
  110.8 3.7 %all-to-all-start = ((bf16[8,2,8192]{2,1,0:T(2,128)(2,1)}), bf16[8,2,8192]{2,1,0:T(2,128)(2,1)S(1)}, u32[]{:S(2)}, u32[]{:S(2)}) async-start(bf16[8,2,8192]{2,1,0:T(2,128)(2,1)} %reshape.577), calls=%async_computation | async-start | bytes 524288 | tf_op jit(solution)/shard_map/all_to_all | solution.py:100
  114.5 0.6 fusion.34
  115.2 6.3 %all-to-all-done = bf16[8,2,8192]{2,1,0:T(2,128)(2,1)S(1)} async-done(((bf16[8,2,8192]{2,1,0:T(2,128)(2,1)}), bf16[8,2,8192]{2,1,0:T(2,128)(2,1)S(1)}, u32[]{:S(2)}, u32[]{:S(2)}) %all-to-all-start) | async-done | bytes 262176 | tf_op jit(solution)/shard_map/all_to_all | solution.py:100
  121.5 1.2 reshape.578
  122.6 0.9 slice_convert_fusion.3
  123.6 1.0 broadcast.312.clone.1
  124.6 2.6 %scatter_fusion = f32[49,32,64]{2,1,0:T(8,128)} fusion(f32[49,32,64]{2,1,0:T(8,128)} %broadcast.312.clone.1, s32[16]{0:T(128)S(1)} %fusion.23, f32[16,32,64]{2,1,0:T(8,128)S(1)} %slice_convert_fusion.3), kind=kCustom, calls=%fused_computation.6 | custom fusion | flops 32768 | bytes 393280 | tf_op jit(solution)/shard_map/scatter-add | solution.py:105
  127.1 1.2 slice.137
  128.4 1.8 fusion.6
  130.2 0.7 copy-done.8
  130.9 1.5 convolution_convert_fusion.2
  132.4 1.1 copy.45
  133.5 1.4 gather_fusion.3
  134.9 2.0 broadcast_select_fusion.2
  136.9 2.1 reshape.579
  139.0 3.4 %all-to-all-start.1 = ((bf16[8,2,8192]{2,1,0:T(2,128)(2,1)}), bf16[8,2,8192]{2,1,0:T(2,128)(2,1)S(1)}, u32[]{:S(2)}, u32[]{:S(2)}) async-start(bf16[8,2,8192]{2,1,0:T(2,128)(2,1)} %reshape.579), calls=%async_computation.1 | async-start | bytes 524288 | tf_op jit(solution)/shard_map/all_to_all | solution.py:100
  142.5 6.8 %all-to-all-done.1 = bf16[8,2,8192]{2,1,0:T(2,128)(2,1)S(1)} async-done(((bf16[8,2,8192]{2,1,0:T(2,128)(2,1)}), bf16[8,2,8192]{2,1,0:T(2,128)(2,1)S(1)}, u32[]{:S(2)}, u32[]{:S(2)}) %all-to-all-start.1) | async-done | bytes 262176 | tf_op jit(solution)/shard_map/all_to_all | solution.py:100
  149.3 1.2 reshape.580
  150.5 0.9 slice_convert_fusion.2
  151.4 1.0 broadcast.312.clone
  152.4 2.6 %scatter_fusion.1 = f32[49,32,64]{2,1,0:T(8,128)} fusion(f32[49,32,64]{2,1,0:T(8,128)} %broadcast.312.clone, s32[16]{0:T(128)S(1)} %fusion.24, f32[16,32,64]{2,1,0:T(8,128)S(1)} %slice_convert_fusion.2), kind=kCustom, calls=%fused_computation.7 | custom fusion | flops 32768 | bytes 393280 | tf_op jit(solution)/shard_map/scatter-add | solution.py:105
  155.0 1.7 fusion.31
  156.7 0.8 fusion.35
  157.5 0.8 convolution_convert_fusion.1
  158.3 0.9 copy.46
  159.2 2.5 %gather_fusion.4 = bf16[64,32,64]{2,1,0:T(8,128)(2,1)} fusion(bf16[33,32,64]{2,1,0:T(8,128)(2,1)} %bitcast.97, s32[1024]{0:T(1024)} %copy-done.13), kind=kCustom, calls=%fused_computation.2.clone | custom fusion | bytes 524544 | tf_op jit(solution)/shard_map/jit(_take)/gather | solution.py:99
  161.7 2.0 broadcast_select_fusion.1
  163.6 2.1 reshape.581
  165.8 4.2 %all-to-all-start.2 = ((bf16[8,2,8192]{2,1,0:T(2,128)(2,1)}), bf16[8,2,8192]{2,1,0:T(2,128)(2,1)}, u32[]{:S(2)}, u32[]{:S(2)}) async-start(bf16[8,2,8192]{2,1,0:T(2,128)(2,1)} %reshape.581), calls=%async_computation.2 | async-start | bytes 524288 | tf_op jit(solution)/shard_map/all_to_all | solution.py:100
  170.1 6.7 %all-to-all-done.2 = bf16[8,2,8192]{2,1,0:T(2,128)(2,1)} async-done(((bf16[8,2,8192]{2,1,0:T(2,128)(2,1)}), bf16[8,2,8192]{2,1,0:T(2,128)(2,1)}, u32[]{:S(2)}, u32[]{:S(2)}) %all-to-all-start.2) | async-done | bytes 262176 | tf_op jit(solution)/shard_map/all_to_all | solution.py:100
  176.8 2.1 reshape.582
  178.9 1.6 slice_convert_fusion.1
  180.5 1.0 broadcast.312.clone.2
  181.5 2.7 %scatter_fusion.2 = f32[49,32,64]{2,1,0:T(8,128)} fusion(f32[49,32,64]{2,1,0:T(8,128)} %broadcast.312.clone.2, s32[16]{0:T(128)S(1)} %fusion.25, f32[16,32,64]{2,1,0:T(8,128)} %slice_convert_fusion.1), kind=kCustom, calls=%fused_computation.8 | custom fusion | flops 32768 | bytes 393280 | tf_op jit(solution)/shard_map/scatter-add | solution.py:105
  184.2 1.8 fusion.4
  186.0 1.5 select_select_fusion
  187.5 0.8 convolution_convert_fusion
  188.6 0.8 gather_fusion.5
  189.5 1.1 reshape.583
  190.6 3.4 %all-to-all-start.3 = ((bf16[8,2,8192]{2,1,0:T(2,128)(2,1)}), bf16[8,2,8192]{2,1,0:T(2,128)(2,1)S(1)}, u32[]{:S(2)}, u32[]{:S(2)}) async-start(bf16[8,2,8192]{2,1,0:T(2,128)(2,1)} %reshape.583), calls=%async_computation.3 | async-start | bytes 524288 | tf_op jit(solution)/shard_map/all_to_all | solution.py:100
  194.1 6.7 %all-to-all-done.3 = bf16[8,2,8192]{2,1,0:T(2,128)(2,1)S(1)} async-done(((bf16[8,2,8192]{2,1,0:T(2,128)(2,1)}), bf16[8,2,8192]{2,1,0:T(2,128)(2,1)S(1)}, u32[]{:S(2)}, u32[]{:S(2)}) %all-to-all-start.3) | async-done | bytes 262176 | tf_op jit(solution)/shard_map/all_to_all | solution.py:100
  201.4 1.2 scatter_fusion.3
  202.6 1.2 slice_add_fusion
  204.0 22.1 %all_to_all.25 = f32[4,768,64]{1,2,0:T(8,128)S(1)} all-to-all(f32[4,768,64]{1,2,0:T(8,128)S(1)} %pad_maximum_fusion.1), channel_id=1, replica_groups=mesh['lvl'=4,'prow'=4,'pcol'=2] {'prow'}, dimensions={0} | all-to-all | bytes 1572864 | tf_op jit(solution)/shard_map/all_to_all | solution.py:118
  226.2 1.0 copy.51
  227.2 0.8 copy.50
  (81 shorter events, 3.2 us)
Async XLA Ops:
  7.2 52.6 %copy-start = (f32[1,1,1024,256]{3,2,1,0:T(8,128)S(1)}, f32[1,1,1024,256]{3,2,1,0:T(8,128)}, u32[]{:S(2)}) copy-start(f32[1,1,1024,256]{3,2,1,0:T(8,128)} %param.11) | copy-start | bytes 3145732
  7.2 91.2 %all-gather.5.cloned.1.call-start = ((), (), s32[]{:S(2)}) async-start(), calls=%async_computation.5 | async-start | bytes 5242880 | tf_op jit(solution)/shard_map/all_gather | solution.py:47
  13.6 1.1 copy-start.16
  13.6 1.1 copy-start.17
  59.3 75.6 %copy-start.11 = (pred[64]{0:T(512)(128)(4,1)}, pred[64]{0:T(512)(128)(4,1)S(1)}, u32[]{:S(2)}) copy-start(pred[64]{0:T(512)(128)(4,1)S(1)} %get-tuple-element.23) | copy-start | bytes 196
  59.3 74.1 %copy-start.13 = (s32[1024]{0:T(1024)}, s32[1024]{0:T(1024)S(1)}, u32[]{:S(2)}) copy-start(s32[1024]{0:T(1024)S(1)} %pad_clamp_fusion) | copy-start | bytes 12292
  98.4 2.8 %copy-start.5 = (f32[1,1,1024,64]{3,2,1,0:T(8,128)S(1)}, f32[1,1,1024,64]{3,2,1,0:T(8,128)}, u32[]{:S(2)}) copy-start(f32[1,1,1024,64]{3,2,1,0:T(8,128)} %constant_dynamic-slice_fusion.2) | copy-start | bytes 786436
  101.2 1.3 copy-start.1
  102.0 0.7 copy-start.6
  110.8 10.6 %all-to-all-start = ((bf16[8,2,8192]{2,1,0:T(2,128)(2,1)}), bf16[8,2,8192]{2,1,0:T(2,128)(2,1)S(1)}, u32[]{:S(2)}, u32[]{:S(2)}) async-start(bf16[8,2,8192]{2,1,0:T(2,128)(2,1)} %reshape.577), calls=%async_computation | async-start | bytes 524288 | tf_op jit(solution)/shard_map/all_to_all | solution.py:100
  127.1 3.8 %copy-start.2 = (bf16[4,256,1024]{2,1,0:T(8,128)(2,1)S(1)}, bf16[4,256,1024]{2,1,0:T(8,128)(2,1)}, u32[]{:S(2)}) copy-start(bf16[4,256,1024]{2,1,0:T(8,128)(2,1)} %copy-done.1) | copy-start | bytes 6291460
  130.2 0.7 copy-start.8
  139.0 10.3 %all-to-all-start.1 = ((bf16[8,2,8192]{2,1,0:T(2,128)(2,1)}), bf16[8,2,8192]{2,1,0:T(2,128)(2,1)S(1)}, u32[]{:S(2)}, u32[]{:S(2)}) async-start(bf16[8,2,8192]{2,1,0:T(2,128)(2,1)} %reshape.579), calls=%async_computation.1 | async-start | bytes 524288 | tf_op jit(solution)/shard_map/all_to_all | solution.py:100
  155.0 2.4 %copy-start.3 = (bf16[4,256,1024]{2,1,0:T(8,128)(2,1)S(1)}, bf16[4,256,1024]{2,1,0:T(8,128)(2,1)}, u32[]{:S(2)}) copy-start(bf16[4,256,1024]{2,1,0:T(8,128)(2,1)} %copy-done.1) | copy-start | bytes 6291460
  159.2 10.9 %copy-start.15 = (s32[2,8]{1,0:T(2,128)S(1)}, s32[2,8]{1,0:T(2,128)}, u32[]{:S(2)}) copy-start(s32[2,8]{1,0:T(2,128)} %get-tuple-element.31) | copy-start | bytes 196
  165.8 11.0 %all-to-all-start.2 = ((bf16[8,2,8192]{2,1,0:T(2,128)(2,1)}), bf16[8,2,8192]{2,1,0:T(2,128)(2,1)}, u32[]{:S(2)}, u32[]{:S(2)}) async-start(bf16[8,2,8192]{2,1,0:T(2,128)(2,1)} %reshape.581), calls=%async_computation.2 | async-start | bytes 524288 | tf_op jit(solution)/shard_map/all_to_all | solution.py:100
  184.1 1.8 copy-start.7
  184.1 1.8 copy-start.9
  185.9 1.6 copy-start.4
  187.5 1.9 copy-start.12
  188.3 5.7 %copy-start.14 = (s32[2,8]{1,0:T(2,128)S(1)}, s32[2,8]{1,0:T(2,128)}, u32[]{:S(2)}) copy-start(s32[2,8]{1,0:T(2,128)} %get-tuple-element.30) | copy-start | bytes 196
  188.4 5.8 %copy-start.10 = (f32[1024,64]{0,1:T(8,128)S(1)}, f32[1024,64]{0,1:T(8,128)}, u32[]{:S(2)}) copy-start(f32[1024,64]{0,1:T(8,128)} %get-tuple-element.33) | copy-start | bytes 786436
  190.6 10.3 %all-to-all-start.3 = ((bf16[8,2,8192]{2,1,0:T(2,128)(2,1)}), bf16[8,2,8192]{2,1,0:T(2,128)(2,1)S(1)}, u32[]{:S(2)}, u32[]{:S(2)}) async-start(bf16[8,2,8192]{2,1,0:T(2,128)(2,1)} %reshape.583), calls=%async_computation.3 | async-start | bytes 524288 | tf_op jit(solution)/shard_map/all_to_all | solution.py:100
Sparse Core Ops, SparseCore 0:
  14.8 83.5 all-gather.4

commit v3 on v2

--- a/solution.py
+++ b/solution.py
@@ -43,10 +43,14 @@
         jnp.zeros((), jnp.bfloat16),
     ).reshape(tile_count * block_rows, width)
 
-    both = jnp.concatenate([inverse, tiles_used], axis=0)
-    gathered = lax.all_gather(both, "prow", axis=0)
-    inv_full = gathered[:, :row_count].reshape(n_prow * row_count, width)
-    tiles_full = gathered[:, row_count:].reshape(group_tiles * block_rows, width)
+    inv_full = lax.all_gather(inverse, "prow", axis=0, tiled=True)
+    tiles_full = lax.all_to_all(
+        jnp.broadcast_to(tiles_used[None], (n_prow,) + tiles_used.shape),
+        "prow",
+        split_axis=0,
+        concat_axis=0,
+        tiled=True,
+    ).reshape(group_tiles * block_rows, width)
     tiles_full = jnp.concatenate(
         [tiles_full, jnp.zeros((block_rows, width), jnp.bfloat16)], axis=0
     )

time: 236 us -> 255 us (1.081)
  blocking collectives: 65.9 us -> 133 us
  waiting for transfers between devices: 64.1 us -> 27 us
  other arithmetic: 28.3 us -> 18.8 us
  local copies, waits for them, and re-layouts: 38 us -> 30.4 us
  starting transfers between devices: 14.8 us -> 21 us
    all_gather x1, blocking collectives: 43.8 us -> 111 us  [per_device(): meta = lax.all_gather(meta, ('lvl', 'prow', 'pcol'), axis=0)]
    all_gather x1, waiting for transfers between devices: 37.6 us -> 0.02 us  [per_device(): inv_full = lax.all_gather(inverse, 'prow', axis=0, tiled=True)]
    all_to_all x0 -> x1, starting transfers between devices: none -> 6.45 us  [per_device(): lax.all_to_all(jnp.broadcast_to(tiles_used[None], (n_prow,) + tiles_used....]
    convert_element_type x2 -> x1, other arithmetic: 3.45 us -> 0.07 us  [per_device(): right.astype(jnp.bfloat16)]
    slice x1 -> x0, local copies, waits for them, and re-layouts: 2.77 us -> none  [per_device(): inv_full = gathered[:, :row_count].reshape(n_prow * row_count, width)]
    select_n x4, other arithmetic: 6.09 us -> 3.42 us  [per_device(): sending = jnp.take(updates, send_index, axis=0)]
    unnamed x46 -> x36, local copies, waits for them, and re-layouts: 15.7 us -> 13.9 us
  transfers between devices with their start and end apart: 5 -> 6, of which waited for: 5 -> 4; matrix products, arithmetic and copies ran while one was open for 1% -> 3% of each run, Pallas kernels for 0% -> 0%
where the time goes in v3:
time: 255 us; the launch traced here: 253 us
  blocking collectives  133 us (52%)
  local copies, waits for them, and re-layouts  30.4 us (12%)
  waiting for transfers between devices  27 us (11%)
  starting transfers between devices  21 us (8%)
  other arithmetic  18.8 us (7%)
  between operations  14.5 us (6%)
  matrix products  8.67 us (3%)
    all_gather x1, blocking collectives, per_device(): meta = lax.all_gather(meta, ('lvl', 'prow', 'pcol'), axis=0)  111 us
    all_to_all x4, waiting for transfers between devices, per_device(): lax.all_to_all(sending, ('lvl', 'pcol'), split_axis=0, concat_axis=0, til...  27 us
    all_to_all x1, blocking collectives, per_device(): lax.all_to_all(final, 'prow', split_axis=0, concat_axis=0, tiled=True)  22.1 us
    all_to_all x4, starting transfers between devices, per_device(): lax.all_to_all(sending, ('lvl', 'pcol'), split_axis=0, concat_axis=0, til...  14.5 us
    unnamed x36, local copies, waits for them, and re-layouts  13.9 us
    scatter-add x4, other arithmetic, per_device(): summed = summed.at[recv_block[section]].add(incoming.astype(jnp.float32))  7.51 us
    all_to_all x1, starting transfers between devices, per_device(): lax.all_to_all(jnp.broadcast_to(tiles_used[None], (n_prow,) + tiles_used....  6.45 us
    gather x4, local copies, waits for them, and re-layouts, per_device(): sending = jnp.take(updates, send_index, axis=0)  5.12 us
  transfers between devices with their start and end apart: 6, of which 4 were waited for; matrix products, arithmetic and copies ran while one was open for 3% of the time, Pallas kernels for 0%

profile of v3, /device:TPU:0, one launch (start us, length us, event | category | flops | bytes accessed | tf_op | source)
XLA Modules:
  0.0 253.5 jit_solution(12972729310027131417)
XLA Ops:
  7.3 0.5 copy-done
  7.9 1.4 gather_fusion
  9.3 2.0 compare_select_fusion
  11.4 0.6 gather_fusion.1
  12.2 1.6 broadcast_in_dim.122
  13.8 6.4 %all-to-all-start = ((bf16[4,256,1024]{2,1,0:T(8,128)(2,1)}), bf16[4,256,1024]{2,1,0:T(8,128)(2,1)S(1)}, u32[]{:S(2)}, u32[]{:S(2)}) async-start(bf16[4,256,1024]{2,1,0:T(8,128)(2,1)} %broadcast_in_dim.122), calls=%async_computation | async-start | bytes 4194304 | tf_op jit(solution)/shard_map/all_to_all | solution.py:47
  20.3 111.1 %all-gather.1 = s32[32,2,8]{2,1,0:T(2,128)S(1)} all-gather(s32[1,2,8]{2,1,0:T(2,128)S(1)} %add_bitcast_fusion), channel_id=2, replica_groups=mesh['lvl'=4,'prow'=4,'pcol'=2] {'lvl','prow','pcol'}, dimensions={0}, use_global_device_ids=true | all-gather | bytes 2112 | tf_op jit(solution)/shard_map/all_gather | solution.py:59
  131.6 0.3 convert_reduce_fusion
  132.2 0.2 fusion.15
  132.4 0.2 select_reduce_fusion
  132.7 2.5 fusion.5
  135.2 0.8 convolution_convert_fusion.3
  136.0 0.2 copy.44
  136.2 0.7 gather_fusion.2
  137.0 1.1 reshape.573
  138.1 3.4 %all-to-all-start.1 = ((bf16[8,2,8192]{2,1,0:T(2,128)(2,1)}), bf16[8,2,8192]{2,1,0:T(2,128)(2,1)S(1)}, u32[]{:S(2)}, u32[]{:S(2)}) async-start(bf16[8,2,8192]{2,1,0:T(2,128)(2,1)} %reshape.573), calls=%async_computation.1 | async-start | bytes 524288 | tf_op jit(solution)/shard_map/all_to_all | solution.py:104
  141.6 6.8 %all-to-all-done.1 = bf16[8,2,8192]{2,1,0:T(2,128)(2,1)S(1)} async-done(((bf16[8,2,8192]{2,1,0:T(2,128)(2,1)}), bf16[8,2,8192]{2,1,0:T(2,128)(2,1)S(1)}, u32[]{:S(2)}, u32[]{:S(2)}) %all-to-all-start.1) | async-done | bytes 262176 | tf_op jit(solution)/shard_map/all_to_all | solution.py:104
  148.4 0.3 reshape.574
  148.9 1.2 scatter_fusion
  150.1 0.9 copy-done.4
  151.0 1.4 bitcast_subtract_fusion.2
  152.4 0.3 copy-done.1
  152.7 0.8 fusion.8
  153.5 0.7 copy-done.7
  154.2 0.8 convolution_convert_fusion.2
  155.0 0.2 copy.45
  155.2 1.4 gather_fusion.3
  156.6 1.2 broadcast_select_fusion.2
  157.8 1.1 reshape.575
  158.9 3.4 %all-to-all-start.2 = ((bf16[8,2,8192]{2,1,0:T(2,128)(2,1)}), bf16[8,2,8192]{2,1,0:T(2,128)(2,1)S(1)}, u32[]{:S(2)}, u32[]{:S(2)}) async-start(bf16[8,2,8192]{2,1,0:T(2,128)(2,1)} %reshape.575), calls=%async_computation.2 | async-start | bytes 524288 | tf_op jit(solution)/shard_map/all_to_all | solution.py:104
  162.4 6.8 %all-to-all-done.2 = bf16[8,2,8192]{2,1,0:T(2,128)(2,1)S(1)} async-done(((bf16[8,2,8192]{2,1,0:T(2,128)(2,1)}), bf16[8,2,8192]{2,1,0:T(2,128)(2,1)S(1)}, u32[]{:S(2)}, u32[]{:S(2)}) %all-to-all-start.2) | async-done | bytes 262176 | tf_op jit(solution)/shard_map/all_to_all | solution.py:104
  169.2 0.3 reshape.576
  169.6 1.0 broadcast.316.clone.1
  170.6 2.4 scatter_fusion.1
  173.0 1.2 slice.135
  174.3 0.5 copy-done.2
  174.8 0.8 fusion.33
  175.5 1.5 convolution_convert_fusion.1
  177.0 1.8 copy.46
  178.8 2.4 gather_fusion.4
  181.1 2.0 broadcast_select_fusion.1
  183.1 2.1 reshape.577
  185.2 4.2 %all-to-all-start.3 = ((bf16[8,2,8192]{2,1,0:T(2,128)(2,1)}), bf16[8,2,8192]{2,1,0:T(2,128)(2,1)}, u32[]{:S(2)}, u32[]{:S(2)}) async-start(bf16[8,2,8192]{2,1,0:T(2,128)(2,1)} %reshape.577), calls=%async_computation.3 | async-start | bytes 524288 | tf_op jit(solution)/shard_map/all_to_all | solution.py:104
  189.6 6.7 %all-to-all-done.3 = bf16[8,2,8192]{2,1,0:T(2,128)(2,1)} async-done(((bf16[8,2,8192]{2,1,0:T(2,128)(2,1)}), bf16[8,2,8192]{2,1,0:T(2,128)(2,1)}, u32[]{:S(2)}, u32[]{:S(2)}) %all-to-all-start.3) | async-done | bytes 262176 | tf_op jit(solution)/shard_map/all_to_all | solution.py:104
  196.2 2.1 reshape.578
  198.4 1.6 slice_convert_fusion.1
  200.0 1.0 broadcast.316.clone.2
  201.0 2.7 %scatter_fusion.2 = f32[49,32,64]{2,1,0:T(8,128)} fusion(f32[49,32,64]{2,1,0:T(8,128)} %broadcast.316.clone.2, s32[16]{0:T(128)S(1)} %fusion.25, f32[16,32,64]{2,1,0:T(8,128)} %slice_convert_fusion.1), kind=kCustom, calls=%fused_computation.8 | custom fusion | flops 32768 | bytes 393280 | tf_op jit(solution)/shard_map/scatter-add | solution.py:109
  203.7 1.2 slice.137
  205.0 0.4 copy-done.3
  205.5 0.8 select_select_fusion
  206.2 0.8 convolution_convert_fusion
  207.1 0.2 copy.47
  207.2 0.7 gather_fusion.5
  207.9 0.1 broadcast_select_fusion
  208.1 1.1 reshape.579
  209.1 3.4 %all-to-all-start.4 = ((bf16[8,2,8192]{2,1,0:T(2,128)(2,1)}), bf16[8,2,8192]{2,1,0:T(2,128)(2,1)S(1)}, u32[]{:S(2)}, u32[]{:S(2)}) async-start(bf16[8,2,8192]{2,1,0:T(2,128)(2,1)} %reshape.579), calls=%async_computation.4 | async-start | bytes 524288 | tf_op jit(solution)/shard_map/all_to_all | solution.py:104
  212.7 6.8 %all-to-all-done.4 = bf16[8,2,8192]{2,1,0:T(2,128)(2,1)S(1)} async-done(((bf16[8,2,8192]{2,1,0:T(2,128)(2,1)}), bf16[8,2,8192]{2,1,0:T(2,128)(2,1)S(1)}, u32[]{:S(2)}, u32[]{:S(2)}) %all-to-all-start.4) | async-done | bytes 262176 | tf_op jit(solution)/shard_map/all_to_all | solution.py:104
  219.4 0.3 reshape.580
  219.9 1.2 scatter_fusion.3
  221.1 1.2 slice_add_fusion
  222.6 22.1 %all_to_all.30 = f32[4,768,64]{1,2,0:T(8,128)S(1)} all-to-all(f32[4,768,64]{1,2,0:T(8,128)S(1)} %pad_maximum_fusion), channel_id=1, replica_groups=mesh['lvl'=4,'prow'=4,'pcol'=2] {'prow'}, dimensions={0} | all-to-all | bytes 1572864 | tf_op jit(solution)/shard_map/all_to_all | solution.py:122
  244.8 1.0 copy.51
  245.8 0.8 copy.50
  (75 shorter events, 2.2 us)
Async XLA Ops:
  7.2 0.7 copy-start
  7.2 4.2 %copy-start.12 = (s32[1,1,8]{2,1,0:T(1,128)S(1)}, s32[1,1,8]{2,1,0:T(1,128)}, u32[]{:S(2)}) copy-start(s32[1,1,8]{2,1,0:T(1,128)} %param.17) | copy-start | bytes 100
  7.2 4.9 %copy-start.9 = (bf16[1,1,8,32,1024]{4,3,2,1,0:T(8,128)(2,1)S(1)}, bf16[1,1,8,32,1024]{4,3,2,1,0:T(8,128)(2,1)}, u32[]{:S(2)}) copy-start(bf16[1,1,8,32,1024]{4,3,2,1,0:T(8,128)(2,1)} %param.13) | copy-start | bytes 1572868
  7.2 125.5 %all-gather.4.cloned.1.call-start = ((), (), s32[]{:S(2)}) async-start(), calls=%async_computation.6 | async-start | bytes 2621440 | tf_op jit(solution)/shard_map/all_gather | solution.py:46
  13.8 6.5 %copy-start.10 = (s32[1,1,8]{2,1,0:T(1,128)S(1)}, s32[1,1,8]{2,1,0:T(1,128)}, u32[]{:S(2)}) copy-start(s32[1,1,8]{2,1,0:T(1,128)} %param.16) | copy-start | bytes 100
  13.8 6.5 %copy-start.11 = (s32[1,1,8]{2,1,0:T(1,128)S(1)}, s32[1,1,8]{2,1,0:T(1,128)}, u32[]{:S(2)}) copy-start(s32[1,1,8]{2,1,0:T(1,128)} %param.15) | copy-start | bytes 100
  13.8 121.4 %all-to-all-start = ((bf16[4,256,1024]{2,1,0:T(8,128)(2,1)}), bf16[4,256,1024]{2,1,0:T(8,128)(2,1)S(1)}, u32[]{:S(2)}, u32[]{:S(2)}) async-start(bf16[4,256,1024]{2,1,0:T(8,128)(2,1)} %broadcast_in_dim.122), calls=%async_computation | async-start | bytes 4194304 | tf_op jit(solution)/shard_map/all_to_all | solution.py:47
  135.2 1.8 copy-start.5
  138.1 10.3 %all-to-all-start.1 = ((bf16[8,2,8192]{2,1,0:T(2,128)(2,1)}), bf16[8,2,8192]{2,1,0:T(2,128)(2,1)S(1)}, u32[]{:S(2)}, u32[]{:S(2)}) async-start(bf16[8,2,8192]{2,1,0:T(2,128)(2,1)} %reshape.573), calls=%async_computation.1 | async-start | bytes 524288 | tf_op jit(solution)/shard_map/all_to_all | solution.py:104
  150.1 0.9 copy-start.4
  151.0 1.7 copy-start.1
  153.5 0.7 copy-start.7
  158.9 10.3 %all-to-all-start.2 = ((bf16[8,2,8192]{2,1,0:T(2,128)(2,1)}), bf16[8,2,8192]{2,1,0:T(2,128)(2,1)S(1)}, u32[]{:S(2)}, u32[]{:S(2)}) async-start(bf16[8,2,8192]{2,1,0:T(2,128)(2,1)} %reshape.575), calls=%async_computation.2 | async-start | bytes 524288 | tf_op jit(solution)/shard_map/all_to_all | solution.py:104
  173.0 1.7 copy-start.2
  185.2 11.0 %all-to-all-start.3 = ((bf16[8,2,8192]{2,1,0:T(2,128)(2,1)}), bf16[8,2,8192]{2,1,0:T(2,128)(2,1)}, u32[]{:S(2)}, u32[]{:S(2)}) async-start(bf16[8,2,8192]{2,1,0:T(2,128)(2,1)} %reshape.577), calls=%async_computation.3 | async-start | bytes 524288 | tf_op jit(solution)/shard_map/all_to_all | solution.py:104
  203.7 1.7 copy-start.3
  203.7 1.7 copy-start.6
  203.7 1.8 copy-start.8
  209.1 10.3 %all-to-all-start.4 = ((bf16[8,2,8192]{2,1,0:T(2,128)(2,1)}), bf16[8,2,8192]{2,1,0:T(2,128)(2,1)S(1)}, u32[]{:S(2)}, u32[]{:S(2)}) async-start(bf16[8,2,8192]{2,1,0:T(2,128)(2,1)} %reshape.579), calls=%async_computation.4 | async-start | bytes 524288 | tf_op jit(solution)/shard_map/all_to_all | solution.py:104
Sparse Core Ops, SparseCore 0:
  11.5 86.4 all-gather.3

commit v4 on v2

--- a/solution.py
+++ b/solution.py
@@ -43,44 +43,39 @@
         jnp.zeros((), jnp.bfloat16),
     ).reshape(tile_count * block_rows, width)
 
-    both = jnp.concatenate([inverse, tiles_used], axis=0)
+    meta_rows = jnp.zeros((16, width), jnp.bfloat16)
+    meta_rows = meta_rows.at[0, :tile_count].set(off_device[0, 0].astype(jnp.bfloat16))
+    meta_rows = meta_rows.at[1, :tile_count].set(off_block[0, 0].astype(jnp.bfloat16))
+    both = jnp.concatenate([inverse, tiles_used, meta_rows], axis=0)
     gathered = lax.all_gather(both, "prow", axis=0)
     inv_full = gathered[:, :row_count].reshape(n_prow * row_count, width)
-    tiles_full = gathered[:, row_count:].reshape(group_tiles * block_rows, width)
+    tile_end = row_count + tile_count * block_rows
+    tiles_full = gathered[:, row_count:tile_end].reshape(group_tiles * block_rows, width)
     tiles_full = jnp.concatenate(
         [tiles_full, jnp.zeros((block_rows, width), jnp.bfloat16)], axis=0
     )
+    meta = gathered[:, tile_end : tile_end + 2, :tile_count].astype(jnp.int32)
+    target = meta[:, 0, :].reshape(group_tiles)
+    block = meta[:, 1, :].reshape(group_tiles)
 
-    meta = jnp.stack([off_device[0, 0], off_block[0, 0]], axis=0)
-    meta = lax.all_gather(meta, ("lvl", "prow", "pcol"), axis=0)
-    meta = meta.reshape(n_lvl, n_prow, n_pcol, 2, tile_count)
-    meta = jnp.transpose(meta, (0, 2, 1, 3, 4)).reshape(groups, n_prow, 2, tile_count)
-    target = meta[:, :, 0, :].reshape(groups, group_tiles)
-    block = meta[:, :, 1, :].reshape(groups, group_tiles)
     tile_ids = jnp.arange(group_tiles, dtype=jnp.int32)
     source_row = tile_ids // tile_count
     earlier = (
-        (target[:, :, None] == target[:, None, :])
-        & (source_row[:, None] == source_row[None, :])[None]
-        & (tile_ids[:, None] > tile_ids[None, :])[None]
+        (target[:, None] == target[None, :])
+        & (source_row[:, None] == source_row[None, :])
+        & (tile_ids[:, None] > tile_ids[None, :])
     )
-    position = jnp.sum(earlier.astype(jnp.int32), axis=2)
-    local_slot = source_row[None, :] * CAP + position
+    position = jnp.sum(earlier.astype(jnp.int32), axis=1)
+    my_slot = target * slots + source_row * CAP + position
 
-    my_target = jnp.take(target, my_group, axis=0)
-    my_slot = my_target * slots + jnp.take(local_slot, my_group, axis=0)
     send_match = my_slot[None, :] == jnp.arange(groups * slots, dtype=jnp.int32)[:, None]
+    filled = jnp.any(send_match, axis=1)
     send_index = jnp.where(
-        jnp.any(send_match, axis=1),
-        jnp.sum(jnp.where(send_match, tile_ids[None, :], 0), axis=1),
-        group_tiles,
+        filled, jnp.sum(jnp.where(send_match, tile_ids[None, :], 0), axis=1), group_tiles
     )
-
-    to_me = target == my_group
-    slot_ids = jnp.arange(slots, dtype=jnp.int32)
-    pick = to_me[:, None, :] & (local_slot[:, None, :] == slot_ids[None, :, None])
-    recv_block = jnp.where(
-        jnp.any(pick, axis=2), jnp.sum(jnp.where(pick, block[:, None, :], 0), axis=2), NT
+    slot_block = jnp.where(filled, jnp.take(block, jnp.minimum(send_index, group_tiles - 1)), NT)
+    recv_block = lax.all_to_all(
+        slot_block.reshape(groups, slots), ("lvl", "pcol"), split_axis=0, concat_axis=0, tiled=True
     )
     recv_block = recv_block.reshape(n_lvl, n_pcol * slots)
 

time: 236 us -> 250 us (1.059)
  waiting for transfers between devices: 64.1 us -> 111 us
  blocking collectives: 65.9 us -> 22.1 us
  starting transfers between devices: 14.8 us -> 19 us
  local copies, waits for them, and re-layouts: 38 us -> 41.1 us
    all_gather x1, waiting for transfers between devices: 37.6 us -> 84.8 us  [per_device(): gathered = lax.all_gather(both, 'prow', axis=0)]
    all_gather x1 -> x0, blocking collectives: 43.8 us -> none  [per_device(): meta = lax.all_gather(meta, ('lvl', 'prow', 'pcol'), axis=0)]
    all_to_all x0 -> x1, starting transfers between devices: none -> 3.69 us  [per_device(): lax.all_to_all(slot_block.reshape(groups, slots), ('lvl', 'pcol'), split_...]
    unnamed x46 -> x40, local copies, waits for them, and re-layouts: 15.7 us -> 15.6 us
  transfers between devices with their start and end apart: 5 -> 6, of which waited for: 5 -> 5; matrix products, arithmetic and copies ran while one was open for 1% -> 3% of each run, Pallas kernels for 0% -> 0%
where the time goes in v4:
time: 250 us; the launch traced here: 248 us
  waiting for transfers between devices  111 us (44%)
  local copies, waits for them, and re-layouts  41.1 us (16%)
  other arithmetic  29.5 us (12%)
  blocking collectives  22.1 us (9%)
  starting transfers between devices  19 us (8%)
  between operations  14.4 us (6%)
  matrix products  10.5 us (4%)
    all_gather x1, waiting for transfers between devices, per_device(): gathered = lax.all_gather(both, 'prow', axis=0)  84.8 us
    all_to_all x4, waiting for transfers between devices, per_device(): lax.all_to_all(sending, ('lvl', 'pcol'), split_axis=0, concat_axis=0, til...  26.5 us
    all_to_all x1, blocking collectives, per_device(): lax.all_to_all(final, 'prow', split_axis=0, concat_axis=0, tiled=True)  22.1 us
    unnamed x40, local copies, waits for them, and re-layouts  15.6 us
    all_to_all x4, starting transfers between devices, per_device(): lax.all_to_all(sending, ('lvl', 'pcol'), split_axis=0, concat_axis=0, til...  15.2 us
    scatter-add x4, other arithmetic, per_device(): summed = summed.at[recv_block[section]].add(incoming.astype(jnp.float32))  9.04 us
    gather x4, local copies, waits for them, and re-layouts, per_device(): sending = jnp.take(updates, send_index, axis=0)  6.07 us
    select_n x4, other arithmetic, per_device(): sending = jnp.take(updates, send_index, axis=0)  6.02 us
  transfers between devices with their start and end apart: 6, of which 5 were waited for; matrix products, arithmetic and copies ran while one was open for 3% of the time, Pallas kernels for 0%

profile of v4, /device:TPU:0, one launch (start us, length us, event | category | flops | bytes accessed | tf_op | source)
XLA Modules:
  0.0 248.0 jit_solution(16064908975091900314)
XLA Ops:
  7.3 0.8 broadcast_bitcast_fusion
  8.1 1.4 gather_fusion
  10.1 1.3 gather_fusion.1
  11.4 0.7 and_select_fusion.1
  13.5 1.4 bitcast_select_fusion
  15.1 1.1 pad_maximum_fusion
  16.2 1.0 constant_dynamic-slice_fusion
  17.2 84.8 %all-gather.3.cloned.1.call-done = bf16[2112,1024]{1,0:T(8,128)(2,1)} async-done(((bf16[528,1024]{1,0:T(8,128)(2,1)}), bf16[2112,1024]{1,0:T(8,128)(2,1)}) %all-gather.3.cloned.1.call-update) | async-done | bytes 4325392 | tf_op jit(solution)/shard_map/all_gather | solution.py:50
  102.0 0.7 slice.171
  103.1 4.2 %fusion.28 = (bf16[4,256,1024]{2,1,0:T(8,128)(2,1)S(1)}, bf16[4,256,1024]{2,1,0:T(8,128)(2,1)}) fusion(bf16[4,528,1024]{2,1,0:T(8,128)(2,1)} %bitcast.85), kind=kLoop, calls=%fused_computation.101 | loop fusion | bytes 8388608 | tf_op jit(solution)/shard_map/slice | solution.py:51
  107.6 1.9 fusion.8
  109.5 0.7 copy-done.5
  110.2 1.5 convolution_convert_fusion.3
  111.7 1.1 copy.32
  112.9 0.8 gather_fusion.2
  114.4 3.7 %all-to-all-start = ((s32[8,1,8]{2,1,0:T(1,128)}), s32[8,1,8]{2,1,0:T(1,128)S(1)}, u32[]{:S(2)}, u32[]{:S(2)}) async-start(s32[8,1,8]{2,1,0:T(1,128)} %bitcast.16), calls=%async_computation | async-start | bytes 8192 | tf_op jit(solution)/shard_map/all_to_all | solution.py:77
  118.1 1.4 gather_fusion.3
  119.5 2.0 broadcast_select_fusion.3
  121.4 2.1 reshape.671
  123.6 4.2 %all-to-all-start.1 = ((bf16[8,2,8192]{2,1,0:T(2,128)(2,1)}), bf16[8,2,8192]{2,1,0:T(2,128)(2,1)S(1)}, u32[]{:S(2)}, u32[]{:S(2)}) async-start(bf16[8,2,8192]{2,1,0:T(2,128)(2,1)} %reshape.671), calls=%async_computation.1 | async-start | bytes 524288 | tf_op jit(solution)/shard_map/all_to_all | solution.py:95
  128.4 6.3 %all-to-all-done.1 = bf16[8,2,8192]{2,1,0:T(2,128)(2,1)S(1)} async-done(((bf16[8,2,8192]{2,1,0:T(2,128)(2,1)}), bf16[8,2,8192]{2,1,0:T(2,128)(2,1)S(1)}, u32[]{:S(2)}, u32[]{:S(2)}) %all-to-all-start.1) | async-done | bytes 262176 | tf_op jit(solution)/shard_map/all_to_all | solution.py:95
  134.7 1.1 reshape.672
  135.8 0.9 slice_convert_fusion.3
  136.8 1.0 broadcast.427.clone.1
  137.8 2.5 %scatter_fusion = f32[49,32,64]{2,1,0:T(8,128)} fusion(f32[49,32,64]{2,1,0:T(8,128)} %broadcast.427.clone.1, s32[16]{0:T(128)S(1)} %fusion.19, f32[16,32,64]{2,1,0:T(8,128)S(1)} %slice_convert_fusion.3), kind=kCustom, calls=%fused_computation.7 | custom fusion | flops 32768 | bytes 393280 | tf_op jit(solution)/shard_map/scatter-add | solution.py:100
  140.3 1.2 slice.177
  141.5 1.8 fusion.6
  143.3 0.7 copy-done.7
  144.0 1.5 convolution_convert_fusion.2
  145.5 1.1 copy.33
  146.6 1.4 gather_fusion.4
  148.0 2.0 broadcast_select_fusion.2
  150.0 2.1 reshape.673
  152.1 3.4 %all-to-all-start.2 = ((bf16[8,2,8192]{2,1,0:T(2,128)(2,1)}), bf16[8,2,8192]{2,1,0:T(2,128)(2,1)S(1)}, u32[]{:S(2)}, u32[]{:S(2)}) async-start(bf16[8,2,8192]{2,1,0:T(2,128)(2,1)} %reshape.673), calls=%async_computation.2 | async-start | bytes 524288 | tf_op jit(solution)/shard_map/all_to_all | solution.py:95
  155.6 6.8 %all-to-all-done.2 = bf16[8,2,8192]{2,1,0:T(2,128)(2,1)S(1)} async-done(((bf16[8,2,8192]{2,1,0:T(2,128)(2,1)}), bf16[8,2,8192]{2,1,0:T(2,128)(2,1)S(1)}, u32[]{:S(2)}, u32[]{:S(2)}) %all-to-all-start.2) | async-done | bytes 262176 | tf_op jit(solution)/shard_map/all_to_all | solution.py:95
  162.4 1.1 reshape.674
  163.5 0.9 slice_convert_fusion.2
  164.5 1.0 broadcast.427.clone
  165.5 2.6 %scatter_fusion.1 = f32[49,32,64]{2,1,0:T(8,128)} fusion(f32[49,32,64]{2,1,0:T(8,128)} %broadcast.427.clone, s32[16]{0:T(128)S(1)} %fusion.20, f32[16,32,64]{2,1,0:T(8,128)S(1)} %slice_convert_fusion.2), kind=kCustom, calls=%fused_computation.8 | custom fusion | flops 32768 | bytes 393280 | tf_op jit(solution)/shard_map/scatter-add | solution.py:100
  168.1 1.7 fusion.27
  169.7 0.8 fusion.30
  170.5 0.8 convolution_convert_fusion.1
  171.3 0.9 copy.34
  172.2 2.5 %gather_fusion.5 = bf16[64,32,64]{2,1,0:T(8,128)(2,1)} fusion(bf16[33,32,64]{2,1,0:T(8,128)(2,1)} %bitcast.89, s32[1024]{0:T(1024)} %copy-done.12), kind=kCustom, calls=%fused_computation.2.clone | custom fusion | bytes 524544 | tf_op jit(solution)/shard_map/jit(_take)/gather | solution.py:94
  174.7 2.0 broadcast_select_fusion.1
  176.6 2.1 reshape.675
  178.8 4.2 %all-to-all-start.3 = ((bf16[8,2,8192]{2,1,0:T(2,128)(2,1)}), bf16[8,2,8192]{2,1,0:T(2,128)(2,1)}, u32[]{:S(2)}, u32[]{:S(2)}) async-start(bf16[8,2,8192]{2,1,0:T(2,128)(2,1)} %reshape.675), calls=%async_computation.3 | async-start | bytes 524288 | tf_op jit(solution)/shard_map/all_to_all | solution.py:95
  183.1 6.7 %all-to-all-done.3 = bf16[8,2,8192]{2,1,0:T(2,128)(2,1)} async-done(((bf16[8,2,8192]{2,1,0:T(2,128)(2,1)}), bf16[8,2,8192]{2,1,0:T(2,128)(2,1)}, u32[]{:S(2)}, u32[]{:S(2)}) %all-to-all-start.3) | async-done | bytes 262176 | tf_op jit(solution)/shard_map/all_to_all | solution.py:95
  189.8 2.1 reshape.676
  191.9 1.6 slice_convert_fusion.1
  193.5 1.0 broadcast.427.clone.2
  194.5 2.7 %scatter_fusion.2 = f32[49,32,64]{2,1,0:T(8,128)} fusion(f32[49,32,64]{2,1,0:T(8,128)} %broadcast.427.clone.2, s32[16]{0:T(128)S(1)} %fusion.21, f32[16,32,64]{2,1,0:T(8,128)} %slice_convert_fusion.1), kind=kCustom, calls=%fused_computation.9 | custom fusion | flops 32768 | bytes 393280 | tf_op jit(solution)/shard_map/scatter-add | solution.py:100
  197.2 1.8 fusion.4
  199.1 1.5 select_select_fusion
  200.6 0.8 convolution_convert_fusion
  201.7 0.8 gather_fusion.6
  202.6 1.1 reshape.677
  203.7 3.4 %all-to-all-start.4 = ((bf16[8,2,8192]{2,1,0:T(2,128)(2,1)}), bf16[8,2,8192]{2,1,0:T(2,128)(2,1)S(1)}, u32[]{:S(2)}, u32[]{:S(2)}) async-start(bf16[8,2,8192]{2,1,0:T(2,128)(2,1)} %reshape.677), calls=%async_computation.4 | async-start | bytes 524288 | tf_op jit(solution)/shard_map/all_to_all | solution.py:95
  207.2 6.7 %all-to-all-done.4 = bf16[8,2,8192]{2,1,0:T(2,128)(2,1)S(1)} async-done(((bf16[8,2,8192]{2,1,0:T(2,128)(2,1)}), bf16[8,2,8192]{2,1,0:T(2,128)(2,1)S(1)}, u32[]{:S(2)}, u32[]{:S(2)}) %all-to-all-start.4) | async-done | bytes 262176 | tf_op jit(solution)/shard_map/all_to_all | solution.py:95
  214.4 1.2 scatter_fusion.3
  215.7 1.2 slice_add_fusion
  217.1 22.1 %all_to_all.31 = f32[4,768,64]{1,2,0:T(8,128)S(1)} all-to-all(f32[4,768,64]{1,2,0:T(8,128)S(1)} %pad_maximum_fusion.1), channel_id=1, replica_groups=mesh['lvl'=4,'prow'=4,'pcol'=2] {'prow'}, dimensions={0} | all-to-all | bytes 1572864 | tf_op jit(solution)/shard_map/all_to_all | solution.py:113
  239.3 1.0 copy.39
  240.3 0.8 copy.38
  (78 shorter events, 5.9 us)
Async XLA Ops:
  7.2 9.0 %copy-start = (f32[1,1,1024,256]{3,2,1,0:T(8,128)S(1)}, f32[1,1,1024,256]{3,2,1,0:T(8,128)}, u32[]{:S(2)}) copy-start(f32[1,1,1024,256]{3,2,1,0:T(8,128)} %param.13) | copy-start | bytes 3145732
  7.2 94.8 %all-gather.3.cloned.1.call-start = ((), (), s32[]{:S(2)}) async-start(), calls=%async_computation.6 | async-start | bytes 5406720 | tf_op jit(solution)/shard_map/all_gather | solution.py:50
  107.3 40.7 %copy-start.10 = (pred[64]{0:T(512)(128)(4,1)}, pred[64]{0:T(512)(128)(4,1)S(1)}, u32[]{:S(2)}) copy-start(pred[64]{0:T(512)(128)(4,1)S(1)} %get-tuple-element.37) | copy-start | bytes 196
  107.5 2.7 %copy-start.1 = (bf16[4,256,1024]{2,1,0:T(8,128)(2,1)S(1)}, bf16[4,256,1024]{2,1,0:T(8,128)(2,1)}, u32[]{:S(2)}) copy-start(bf16[4,256,1024]{2,1,0:T(8,128)(2,1)} %get-tuple-element.40) | copy-start | bytes 6291460
  107.6 39.0 %copy-start.12 = (s32[1024]{0:T(1024)}, s32[1024]{0:T(1024)S(1)}, u32[]{:S(2)}) copy-start(s32[1024]{0:T(1024)S(1)} %pad_clamp_fusion) | copy-start | bytes 12292
  109.5 0.7 copy-start.5
  114.4 9.2 %all-to-all-start = ((s32[8,1,8]{2,1,0:T(1,128)}), s32[8,1,8]{2,1,0:T(1,128)S(1)}, u32[]{:S(2)}, u32[]{:S(2)}) async-start(s32[8,1,8]{2,1,0:T(1,128)} %bitcast.16), calls=%async_computation | async-start | bytes 8192 | tf_op jit(solution)/shard_map/all_to_all | solution.py:77
  123.6 11.1 %all-to-all-start.1 = ((bf16[8,2,8192]{2,1,0:T(2,128)(2,1)}), bf16[8,2,8192]{2,1,0:T(2,128)(2,1)S(1)}, u32[]{:S(2)}, u32[]{:S(2)}) async-start(bf16[8,2,8192]{2,1,0:T(2,128)(2,1)} %reshape.671), calls=%async_computation.1 | async-start | bytes 524288 | tf_op jit(solution)/shard_map/all_to_all | solution.py:95
  140.3 3.8 %copy-start.2 = (bf16[4,256,1024]{2,1,0:T(8,128)(2,1)S(1)}, bf16[4,256,1024]{2,1,0:T(8,128)(2,1)}, u32[]{:S(2)}) copy-start(bf16[4,256,1024]{2,1,0:T(8,128)(2,1)} %get-tuple-element.40) | copy-start | bytes 6291460
  143.3 0.7 copy-start.7
  152.1 10.3 %all-to-all-start.2 = ((bf16[8,2,8192]{2,1,0:T(2,128)(2,1)}), bf16[8,2,8192]{2,1,0:T(2,128)(2,1)S(1)}, u32[]{:S(2)}, u32[]{:S(2)}) async-start(bf16[8,2,8192]{2,1,0:T(2,128)(2,1)} %reshape.673), calls=%async_computation.2 | async-start | bytes 524288 | tf_op jit(solution)/shard_map/all_to_all | solution.py:95
  168.1 2.4 copy-start.3
  172.2 10.8 %copy-start.14 = (s32[2,8]{1,0:T(2,128)S(1)}, s32[2,8]{1,0:T(2,128)}, u32[]{:S(2)}) copy-start(s32[2,8]{1,0:T(2,128)} %get-tuple-element.35) | copy-start | bytes 196
  178.8 11.0 %all-to-all-start.3 = ((bf16[8,2,8192]{2,1,0:T(2,128)(2,1)}), bf16[8,2,8192]{2,1,0:T(2,128)(2,1)}, u32[]{:S(2)}, u32[]{:S(2)}) async-start(bf16[8,2,8192]{2,1,0:T(2,128)(2,1)} %reshape.675), calls=%async_computation.3 | async-start | bytes 524288 | tf_op jit(solution)/shard_map/all_to_all | solution.py:95
  197.2 1.8 copy-start.6
  197.2 1.8 copy-start.8
  199.0 1.6 copy-start.4
  200.5 1.9 copy-start.11
  201.4 5.7 %copy-start.13 = (s32[2,8]{1,0:T(2,128)S(1)}, s32[2,8]{1,0:T(2,128)}, u32[]{:S(2)}) copy-start(s32[2,8]{1,0:T(2,128)} %get-tuple-element.34) | copy-start | bytes 196
  201.4 5.8 %copy-start.9 = (f32[1024,64]{0,1:T(8,128)S(1)}, f32[1024,64]{0,1:T(8,128)}, u32[]{:S(2)}) copy-start(f32[1024,64]{0,1:T(8,128)} %get-tuple-element.43) | copy-start | bytes 786436
  203.7 10.3 %all-to-all-start.4 = ((bf16[8,2,8192]{2,1,0:T(2,128)(2,1)}), bf16[8,2,8192]{2,1,0:T(2,128)(2,1)S(1)}, u32[]{:S(2)}, u32[]{:S(2)}) async-start(bf16[8,2,8192]{2,1,0:T(2,128)(2,1)} %reshape.677), calls=%async_computation.4 | async-start | bytes 524288 | tf_op jit(solution)/shard_map/all_to_all | solution.py:95
Sparse Core Ops, SparseCore 0:
  16.3 85.6 all-gather.2

commit v5 on v2

--- a/solution.py
+++ b/solution.py
@@ -29,14 +29,21 @@
     slots = n_prow * CAP
 
     panels = panel_super[0, 0]
-    panel_cols = width // panels.shape[0]
-    col_super = jnp.repeat(panels, panel_cols)
+    panel_count = panels.shape[0]
+    panel_cols = width // panel_count
+    panel_ids = jnp.arange(panel_count, dtype=jnp.int32)
+
+    def super_of(panel):
+        hit = panel[..., None] == panel_ids
+        return jnp.sum(jnp.where(hit, panels, 0), axis=-1)
+
+    col_super = super_of(jnp.arange(width, dtype=jnp.int32) // panel_cols)
     row_ids = row_index * row_count + jnp.arange(row_count, dtype=jnp.int32)
-    row_super = jnp.take(col_super, row_ids)
+    row_super = super_of(row_ids // panel_cols)
     inverse = jnp.where(
         row_super[:, None] == col_super[None, :], diag_inverse[0, 0], jnp.zeros((), jnp.bfloat16)
     )
-    tile_supernode = jnp.take(panels, offdiag_block_panel[0, 0])
+    tile_supernode = super_of(offdiag_block_panel[0, 0])
     tiles_used = jnp.where(
         col_super[None, None, :] == tile_supernode[:, None, None],
         off_tiles[0, 0],
@@ -84,10 +91,12 @@
     )
     recv_block = recv_block.reshape(n_lvl, n_pcol * slots)
 
-    right = lax.dynamic_slice_in_dim(rhs[0, 0], row_index * cols, cols, axis=1)
-    outer = jnp.zeros((ABOVE, cols), jnp.float32)
+    rhs_cols = lax.dynamic_slice_in_dim(rhs[0, 0], row_index * cols, cols, axis=1)
+    window_blocks = width // block_rows
+    acc = jnp.zeros((NT + 1, block_rows, cols), jnp.float32)
     solved = jnp.zeros((width, cols), jnp.float32)
     for section in range(n_lvl):
+        right = rhs_cols - acc[:window_blocks].reshape(width, cols)
         solved_now = jnp.dot(
             inv_full, right.astype(jnp.bfloat16), preferred_element_type=jnp.float32
         )
@@ -96,16 +105,13 @@
             tiles_full, solved_now.astype(jnp.bfloat16), preferred_element_type=jnp.float32
         ).astype(jnp.bfloat16)
         updates = updates.reshape(group_tiles + 1, block_rows, cols)
-        sending = jnp.take(updates, send_index, axis=0)
+        sending = jnp.take(updates, send_index, axis=0, mode="clip")
         incoming = lax.all_to_all(
             sending, ("lvl", "pcol"), split_axis=0, concat_axis=0, tiled=True
         )
         incoming = incoming.reshape(n_lvl, n_pcol * slots, block_rows, cols)[section]
-        summed = jnp.zeros((NT + 1, block_rows, cols), jnp.float32)
-        summed = summed.at[recv_block[section]].add(incoming.astype(jnp.float32))
-        summed = summed[:NT].reshape(NT * block_rows, cols)
-        right = right - summed[:width]
-        outer = outer + summed[width:]
+        acc = acc.at[recv_block[section]].add(incoming.astype(jnp.float32), mode="clip")
+    outer = acc[window_blocks:NT].reshape(ABOVE, cols)
 
     rows_out = width // n_prow
     final = jnp.concatenate(

time: 236 us -> 217 us (0.919)
  other arithmetic: 28.3 us -> 14.2 us
  local copies, waits for them, and re-layouts: 38 us -> 26.4 us
  matrix products: 9.36 us -> 14.7 us
    select_n x12 -> x3, other arithmetic: 7.46 us -> 0.02 us  [the longest x1 0.01 us: per_device(): row_super = super_of(row_ids // panel_cols)]
    dot_general x4, matrix products: 4.83 us -> 10.2 us  [per_device(): jnp.dot(inv_full, right.astype(jnp.bfloat16), preferred_element_type=jnp....]
    convert_element_type x6 -> x4, other arithmetic: 6.95 us -> 2.59 us  [per_device(): incoming.astype(jnp.float32)]
    gather x6 -> x4, local copies, waits for them, and re-layouts: 8.8 us -> 5.11 us  [per_device(): sending = jnp.take(updates, send_index, axis=0, mode='clip')]
    scatter-add x4, other arithmetic: 9.07 us -> 5.58 us  [per_device(): acc.at[recv_block[section]].add(incoming.astype(jnp.float32), mode='clip')]
    another operation x4 -> x0, local copies, waits for them, and re-layouts: 3.04 us -> none
    unnamed x46 -> x20, local copies, waits for them, and re-layouts: 15.7 us -> 14.4 us
where the time goes in v5:
time: 217 us; the launch traced here: 216 us
  blocking collectives  65.9 us (30%)
  waiting for transfers between devices  65.7 us (30%)
  local copies, waits for them, and re-layouts  26.4 us (12%)
  starting transfers between devices  14.8 us (7%)
  matrix products  14.7 us (7%)
  between operations  14.4 us (7%)
  other arithmetic  14.2 us (7%)
    all_gather x1, blocking collectives, per_device(): meta = lax.all_gather(meta, ('lvl', 'prow', 'pcol'), axis=0)  43.8 us
    all_gather x1, waiting for transfers between devices, per_device(): gathered = lax.all_gather(both, 'prow', axis=0)  38.6 us
    all_to_all x4, waiting for transfers between devices, per_device(): lax.all_to_all(sending, ('lvl', 'pcol'), split_axis=0, concat_axis=0, til...  27 us
    all_to_all x1, blocking collectives, per_device(): lax.all_to_all(final, 'prow', split_axis=0, concat_axis=0, tiled=True)  22.1 us
    all_to_all x4, starting transfers between devices, per_device(): lax.all_to_all(sending, ('lvl', 'pcol'), split_axis=0, concat_axis=0, til...  14.7 us
    unnamed x20, local copies, waits for them, and re-layouts  14.4 us
    dot_general x4, matrix products, per_device(): jnp.dot(inv_full, right.astype(jnp.bfloat16), preferred_element_type=jnp....  10.2 us
    scatter-add x4, other arithmetic, per_device(): acc.at[recv_block[section]].add(incoming.astype(jnp.float32), mode='clip')  5.58 us
  transfers between devices with their start and end apart: 5, of which 5 were waited for; matrix products, arithmetic and copies ran while one was open for 1% of the time, Pallas kernels for 0%

profile of v5, /device:TPU:0, one launch (start us, length us, event | category | flops | bytes accessed | tf_op | source)
XLA Modules:
  0.0 216.2 jit_solution(15778400779898245158)
XLA Ops:
  7.2 0.7 select_reduce_fusion.1
  8.0 0.9 select_reduce_fusion.4
  8.8 0.7 select_reduce_fusion.3
  9.6 1.4 bitcast_select_fusion
  11.1 1.0 pad_maximum_fusion
  12.2 43.8 %all-gather.2 = s32[32,2,8]{2,1,0:T(2,128)S(1)} all-gather(s32[1,2,8]{2,1,0:T(2,128)S(1)} %add_bitcast_fusion), channel_id=3, replica_groups=mesh['lvl'=4,'prow'=4,'pcol'=2] {'lvl','prow','pcol'}, dimensions={0}, use_global_device_ids=true | all-gather | bytes 2112 | tf_op jit(solution)/shard_map/all_gather | solution.py:62
  56.0 0.1 reshape_squeeze.3
  56.1 0.1 broadcast_in_dim.138
  56.3 0.3 convert_reduce_fusion
  56.6 0.1 fusion.22
  56.7 0.1 select_reduce_fusion.2
  56.8 0.2 fusion.21
  57.1 0.2 select_reduce_fusion
  57.3 38.6 %all-gather.5.cloned.1.call-done = bf16[2048,1024]{1,0:T(8,128)(2,1)} async-done(((bf16[512,1024]{1,0:T(8,128)(2,1)}), bf16[2048,1024]{1,0:T(8,128)(2,1)}) %all-gather.5.cloned.1.call-update) | async-done | bytes 4194320 | tf_op jit(solution)/shard_map/all_gather | solution.py:54
  95.9 2.7 %fusion.46 = (bf16[4,256,1024]{2,1,0:T(8,128)(2,1)S(1)}, bf16[4,256,1024]{2,1,0:T(8,128)(2,1)S(1)}) fusion(bf16[4,512,1024]{2,1,0:T(8,128)(2,1)} %bitcast.86), kind=kLoop, calls=%fused_computation.109 | loop fusion | bytes 8388608 | tf_op jit(solution)/shard_map/slice | solution.py:55
  98.7 1.3 copy-done
  100.0 1.9 fusion.5
  101.9 0.7 copy-done.1
  102.6 0.8 convolution_convert_fusion.3
  103.4 0.2 copy.44
  103.6 0.7 gather_fusion
  104.3 1.1 reshape.501
  105.4 3.7 %all-to-all-start = ((bf16[8,2,8192]{2,1,0:T(2,128)(2,1)}), bf16[8,2,8192]{2,1,0:T(2,128)(2,1)S(1)}, u32[]{:S(2)}, u32[]{:S(2)}) async-start(bf16[8,2,8192]{2,1,0:T(2,128)(2,1)} %reshape.501), calls=%async_computation | async-start | bytes 524288 | tf_op jit(solution)/shard_map/all_to_all | solution.py:109
  109.1 0.1 squeeze.29
  109.2 6.8 %all-to-all-done = bf16[8,2,8192]{2,1,0:T(2,128)(2,1)S(1)} async-done(((bf16[8,2,8192]{2,1,0:T(2,128)(2,1)}), bf16[8,2,8192]{2,1,0:T(2,128)(2,1)S(1)}, u32[]{:S(2)}, u32[]{:S(2)}) %all-to-all-start) | async-done | bytes 262176 | tf_op jit(solution)/shard_map/all_to_all | solution.py:109
  116.0 0.3 reshape.502
  116.4 0.1 broadcast_in_dim.137
  116.5 1.2 scatter_fusion
  117.7 2.5 %fusion.8 = f32[1024,64]{0,1:T(8,128)S(1)} fusion(bf16[1024,1024]{1,0:T(8,128)(2,1)} %bitcast.83, f32[1,1,1024,64]{3,2,1,0:T(8,128)S(1)} %bitcast.92, f32[1,1,1024,256]{3,2,1,0:T(8,128)} %param.9, s32[]{:T(128)S(6)} %select_n.167), kind=kOutput, calls=%fused_computation.27 | convolution fusion | flops 134348800 | bytes 3145732 | tf_op jit(solution)/shard_map/dot_general | solution.py:100
  120.2 1.5 convolution_convert_fusion.2
  121.7 1.1 copy.45
  122.8 1.4 gather_fusion.1
  124.2 2.1 reshape.503
  126.4 3.4 %all-to-all-start.1 = ((bf16[8,2,8192]{2,1,0:T(2,128)(2,1)}), bf16[8,2,8192]{2,1,0:T(2,128)(2,1)S(1)}, u32[]{:S(2)}, u32[]{:S(2)}) async-start(bf16[8,2,8192]{2,1,0:T(2,128)(2,1)} %reshape.503), calls=%async_computation.1 | async-start | bytes 524288 | tf_op jit(solution)/shard_map/all_to_all | solution.py:109
  129.8 0.1 squeeze.30
  129.9 6.8 %all-to-all-done.1 = bf16[8,2,8192]{2,1,0:T(2,128)(2,1)S(1)} async-done(((bf16[8,2,8192]{2,1,0:T(2,128)(2,1)}), bf16[8,2,8192]{2,1,0:T(2,128)(2,1)S(1)}, u32[]{:S(2)}, u32[]{:S(2)}) %all-to-all-start.1) | async-done | bytes 262176 | tf_op jit(solution)/shard_map/all_to_all | solution.py:109
  136.7 1.2 reshape.504
  137.8 0.9 slice_convert_fusion.2
  138.7 1.2 scatter_fusion.1
  140.0 2.5 %fusion.11 = f32[1024,64]{0,1:T(8,128)S(1)} fusion(bf16[1024,1024]{1,0:T(8,128)(2,1)} %bitcast.84, f32[1,1,1024,64]{3,2,1,0:T(8,128)S(1)} %bitcast.93, f32[1,1,1024,256]{3,2,1,0:T(8,128)} %param.9, s32[]{:T(128)S(6)} %select_n.167), kind=kOutput, calls=%fused_computation.29 | convolution fusion | flops 134348800 | bytes 3145732 | tf_op jit(solution)/shard_map/dot_general | solution.py:100
  142.5 1.5 convolution_convert_fusion.1
  144.0 1.8 copy.46
  145.8 2.4 %gather_fusion.2 = bf16[64,32,64]{2,1,0:T(8,128)(2,1)} fusion(bf16[33,32,64]{2,1,0:T(8,128)(2,1)} %bitcast.90, s32[1024]{0:T(1024)S(1)} %pad_clamp_fusion), kind=kCustom, calls=%fused_computation.2 | custom fusion | bytes 524544 | tf_op jit(solution)/shard_map/jit(_take)/gather | solution.py:108
  148.2 2.1 reshape.505
  150.3 4.2 %all-to-all-start.2 = ((bf16[8,2,8192]{2,1,0:T(2,128)(2,1)}), bf16[8,2,8192]{2,1,0:T(2,128)(2,1)}, u32[]{:S(2)}, u32[]{:S(2)}) async-start(bf16[8,2,8192]{2,1,0:T(2,128)(2,1)} %reshape.505), calls=%async_computation.2 | async-start | bytes 524288 | tf_op jit(solution)/shard_map/all_to_all | solution.py:109
  154.5 0.1 squeeze.31
  154.6 6.7 %all-to-all-done.2 = bf16[8,2,8192]{2,1,0:T(2,128)(2,1)} async-done(((bf16[8,2,8192]{2,1,0:T(2,128)(2,1)}), bf16[8,2,8192]{2,1,0:T(2,128)(2,1)}, u32[]{:S(2)}, u32[]{:S(2)}) %all-to-all-start.2) | async-done | bytes 262176 | tf_op jit(solution)/shard_map/all_to_all | solution.py:109
  161.3 2.1 reshape.506
  163.4 1.6 slice_convert_fusion.1
  165.1 1.9 scatter_fusion.2
  167.1 3.3 %select_select_fusion = (f32[1024,64]{0,1:T(8,128)}, bf16[1024,64]{0,1:T(8,128)(2,1)S(1)}) fusion(f32[1024,64]{0,1:T(8,128)S(1)} %fusion.11, f32[1024,64]{0,1:T(8,128)S(1)} %fusion.8, f32[1024,64]{0,1:T(8,128)} %copy-done.1, pred[]{:T(512)S(6)} %eq.183, pred[]{:T(512)S(6)} %eq.182, pred[]{:T(512)S(6)} %eq.181, pred[]{:T(512)S(6)} %eq.150, ...), kind=kOutput, calls=%fused_computation.33 | convolution fusion | flops 134676480 | bytes 4063240 | tf_op jit(solution)/shard_map/dot_general | solution.py:100
  170.3 0.8 convolution_convert_fusion
  171.2 0.2 copy.47
  171.3 0.7 gather_fusion.3
  172.0 1.1 reshape.507
  173.1 3.4 %all-to-all-start.3 = ((bf16[8,2,8192]{2,1,0:T(2,128)(2,1)}), bf16[8,2,8192]{2,1,0:T(2,128)(2,1)S(1)}, u32[]{:S(2)}, u32[]{:S(2)}) async-start(bf16[8,2,8192]{2,1,0:T(2,128)(2,1)} %reshape.507), calls=%async_computation.3 | async-start | bytes 524288 | tf_op jit(solution)/shard_map/all_to_all | solution.py:109
  176.5 0.1 squeeze.32
  176.7 6.7 %all-to-all-done.3 = bf16[8,2,8192]{2,1,0:T(2,128)(2,1)S(1)} async-done(((bf16[8,2,8192]{2,1,0:T(2,128)(2,1)}), bf16[8,2,8192]{2,1,0:T(2,128)(2,1)S(1)}, u32[]{:S(2)}, u32[]{:S(2)}) %all-to-all-start.3) | async-done | bytes 262176 | tf_op jit(solution)/shard_map/all_to_all | solution.py:109
  183.4 0.3 reshape.508
  183.8 1.2 scatter_fusion.3
  185.0 0.1 copy.48
  185.3 22.1 %all_to_all.25 = f32[4,768,64]{1,2,0:T(8,128)S(1)} all-to-all(f32[4,768,64]{1,2,0:T(8,128)S(1)} %pad_maximum_fusion.1), channel_id=1, replica_groups=mesh['lvl'=4,'prow'=4,'pcol'=2] {'prow'}, dimensions={0} | all-to-all | bytes 1572864 | tf_op jit(solution)/shard_map/all_to_all | solution.py:124
  207.5 1.0 copy.51
  208.5 0.8 copy.50
  (43 shorter events, 0.7 us)
Async XLA Ops:
  7.2 88.8 %all-gather.5.cloned.1.call-start = ((), (), s32[]{:S(2)}) async-start(), calls=%async_computation.5 | async-start | bytes 5242880 | tf_op jit(solution)/shard_map/all_gather | solution.py:54
  11.1 1.1 copy-start.3
  11.1 1.1 copy-start.4
  98.6 1.4 copy-start
  101.9 0.7 copy-start.1
  105.4 10.6 %all-to-all-start = ((bf16[8,2,8192]{2,1,0:T(2,128)(2,1)}), bf16[8,2,8192]{2,1,0:T(2,128)(2,1)S(1)}, u32[]{:S(2)}, u32[]{:S(2)}) async-start(bf16[8,2,8192]{2,1,0:T(2,128)(2,1)} %reshape.501), calls=%async_computation | async-start | bytes 524288 | tf_op jit(solution)/shard_map/all_to_all | solution.py:109
  126.4 10.3 %all-to-all-start.1 = ((bf16[8,2,8192]{2,1,0:T(2,128)(2,1)}), bf16[8,2,8192]{2,1,0:T(2,128)(2,1)S(1)}, u32[]{:S(2)}, u32[]{:S(2)}) async-start(bf16[8,2,8192]{2,1,0:T(2,128)(2,1)} %reshape.503), calls=%async_computation.1 | async-start | bytes 524288 | tf_op jit(solution)/shard_map/all_to_all | solution.py:109
  150.3 11.0 %all-to-all-start.2 = ((bf16[8,2,8192]{2,1,0:T(2,128)(2,1)}), bf16[8,2,8192]{2,1,0:T(2,128)(2,1)}, u32[]{:S(2)}, u32[]{:S(2)}) async-start(bf16[8,2,8192]{2,1,0:T(2,128)(2,1)} %reshape.505), calls=%async_computation.2 | async-start | bytes 524288 | tf_op jit(solution)/shard_map/all_to_all | solution.py:109
  170.3 6.3 %copy-start.2 = (f32[1024,64]{0,1:T(8,128)S(1)}, f32[1024,64]{0,1:T(8,128)}, u32[]{:S(2)}) copy-start(f32[1024,64]{0,1:T(8,128)} %get-tuple-element.30) | copy-start | bytes 786436
  173.1 10.3 %all-to-all-start.3 = ((bf16[8,2,8192]{2,1,0:T(2,128)(2,1)}), bf16[8,2,8192]{2,1,0:T(2,128)(2,1)S(1)}, u32[]{:S(2)}, u32[]{:S(2)}) async-start(bf16[8,2,8192]{2,1,0:T(2,128)(2,1)} %reshape.507), calls=%async_computation.3 | async-start | bytes 524288 | tf_op jit(solution)/shard_map/all_to_all | solution.py:109
Sparse Core Ops, SparseCore 0:
  12.3 83.5 all-gather.4

commit v6 on v5

--- a/solution.py
+++ b/solution.py
@@ -50,10 +50,9 @@
         jnp.zeros((), jnp.bfloat16),
     ).reshape(tile_count * block_rows, width)
 
-    both = jnp.concatenate([inverse, tiles_used], axis=0)
-    gathered = lax.all_gather(both, "prow", axis=0)
-    inv_full = gathered[:, :row_count].reshape(n_prow * row_count, width)
-    tiles_full = gathered[:, row_count:].reshape(group_tiles * block_rows, width)
+    tiles_full = lax.all_gather(tiles_used, "prow", axis=0, tiled=True)
+    inverse, tiles_full = lax.optimization_barrier((inverse, tiles_full))
+    inv_full = lax.all_gather(inverse, "prow", axis=0, tiled=True)
     tiles_full = jnp.concatenate(
         [tiles_full, jnp.zeros((block_rows, width), jnp.bfloat16)], axis=0
     )
@@ -95,14 +94,26 @@
     window_blocks = width // block_rows
     acc = jnp.zeros((NT + 1, block_rows, cols), jnp.float32)
     solved = jnp.zeros((width, cols), jnp.float32)
+    rows_out = width // n_prow
+    first_rows = jnp.dot(
+        inverse, rhs[0, 0].astype(jnp.bfloat16), preferred_element_type=jnp.float32
+    )
+    first_half = first_rows.astype(jnp.bfloat16).reshape(rows_out, n_prow, cols)
+    first_cols = lax.all_to_all(
+        jnp.transpose(first_half, (1, 0, 2)), "prow", split_axis=0, concat_axis=0, tiled=True
+    ).reshape(width, cols)
     for section in range(n_lvl):
-        right = rhs_cols - acc[:window_blocks].reshape(width, cols)
-        solved_now = jnp.dot(
-            inv_full, right.astype(jnp.bfloat16), preferred_element_type=jnp.float32
-        )
-        solved = jnp.where(level_index == section, solved_now, solved)
+        if section == 0:
+            solved_half = first_cols
+        else:
+            right = rhs_cols - acc[:window_blocks].reshape(width, cols)
+            solved_now = jnp.dot(
+                inv_full, right.astype(jnp.bfloat16), preferred_element_type=jnp.float32
+            )
+            solved = jnp.where(level_index == section, solved_now, solved)
+            solved_half = solved_now.astype(jnp.bfloat16)
         updates = jnp.dot(
-            tiles_full, solved_now.astype(jnp.bfloat16), preferred_element_type=jnp.float32
+            tiles_full, solved_half, preferred_element_type=jnp.float32
         ).astype(jnp.bfloat16)
         updates = updates.reshape(group_tiles + 1, block_rows, cols)
         sending = jnp.take(updates, send_index, axis=0, mode="clip")
@@ -113,7 +124,6 @@
         acc = acc.at[recv_block[section]].add(incoming.astype(jnp.float32), mode="clip")
     outer = acc[window_blocks:NT].reshape(ABOVE, cols)
 
-    rows_out = width // n_prow
     final = jnp.concatenate(
         [
             solved.reshape(n_prow, rows_out, cols),
@@ -123,6 +133,7 @@
     )
     final = lax.all_to_all(final, "prow", split_axis=0, concat_axis=0, tiled=True)
     solution_rows = jnp.transpose(final[:, :rows_out], (1, 0, 2)).reshape(rows_out, columns_all)
+    solution_rows = jnp.where(level_index == 0, first_rows, solution_rows)
     outer_all = jnp.transpose(final[:, rows_out:], (1, 0, 2)).reshape(ABOVE, columns_all)
     return (solution_rows[None, None], outer_all[None, None])
 

time: 217 us -> 209 us (0.963)
  blocking collectives: 65.9 us -> 43.7 us
  starting transfers between devices: 14.8 us -> 22.6 us
  waiting for transfers between devices: 65.7 us -> 73.4 us
  other arithmetic: 14.2 us -> 20.4 us
  local copies, waits for them, and re-layouts: 26.4 us -> 22.3 us
  matrix products: 14.7 us -> 11.2 us
    all_to_all x0 -> x2, waiting for transfers between devices: none -> 27.7 us  [the longest x1 19.7 us: per_device(): lax.all_to_all(final, 'prow', split_axis=0, concat_axis=0, tiled=True)]
    all_to_all x1 -> x0, blocking collectives: 22.1 us -> none  [per_device(): lax.all_to_all(final, 'prow', split_axis=0, concat_axis=0, tiled=True)]
    all_gather x1 -> x2, waiting for transfers between devices: 38.6 us -> 18.5 us  [the longest x1 15.9 us: per_device(): inv_full = lax.all_gather(inverse, 'prow', axis=0, tiled=True)]
    all_to_all x0 -> x2, starting transfers between devices: none -> 6.82 us  [the longest x1 3.49 us: per_device(): lax.all_to_all(final, 'prow', split_axis=0, concat_axis=0, tiled=True)]
    dot_general x4 -> x3, matrix products: 10.2 us -> 4.58 us  [per_device(): jnp.dot(inv_full, right.astype(jnp.bfloat16), preferred_element_type=jnp....]
    convert_element_type x0 -> x3, other arithmetic: none -> 4.14 us  [per_device(): right.astype(jnp.bfloat16)]
    slice x1 -> x0, local copies, waits for them, and re-layouts: 2.7 us -> none  [per_device(): inv_full = gathered[:, :row_count].reshape(n_prow * row_count, width)]
    dot_general x4 -> x5, matrix products: 4.54 us -> 6.66 us  [the longest x4 4.54 us: per_device(): jnp.dot(tiles_full, solved_half, preferred_element_type=jnp.float32)]
  transfers between devices with their start and end apart: 5 -> 8, of which waited for: 5 -> 8; matrix products, arithmetic and copies ran while one was open for 1% -> 6% of each run, Pallas kernels for 0% -> 0%
where the time goes in v6:
time: 209 us; the launch traced here: 208 us
  waiting for transfers between devices  73.4 us (35%)
  blocking collectives  43.7 us (21%)
  starting transfers between devices  22.6 us (11%)
  local copies, waits for them, and re-layouts  22.3 us (11%)
  other arithmetic  20.4 us (10%)
  between operations  14.5 us (7%)
  matrix products  11.2 us (5%)
    all_gather x1, blocking collectives, per_device(): meta = lax.all_gather(meta, ('lvl', 'prow', 'pcol'), axis=0)  43.7 us
    all_to_all x4, waiting for transfers between devices, per_device(): lax.all_to_all(sending, ('lvl', 'pcol'), split_axis=0, concat_axis=0, til...  27.1 us
    all_to_all x1, waiting for transfers between devices, per_device(): lax.all_to_all(final, 'prow', split_axis=0, concat_axis=0, tiled=True)  19.7 us
    all_gather x1, waiting for transfers between devices, per_device(): inv_full = lax.all_gather(inverse, 'prow', axis=0, tiled=True)  15.9 us
    all_to_all x4, starting transfers between devices, per_device(): lax.all_to_all(sending, ('lvl', 'pcol'), split_axis=0, concat_axis=0, til...  15.7 us
    unnamed x24, local copies, waits for them, and re-layouts  12.9 us
    all_to_all x1, waiting for transfers between devices, per_device(): lax.all_to_all(jnp.transpose(first_half, (1, 0, 2)), 'prow', split_axis=0...  8 us
    scatter-add x4, other arithmetic, per_device(): acc.at[recv_block[section]].add(incoming.astype(jnp.float32), mode='clip')  5.55 us
  transfers between devices with their start and end apart: 8, of which 8 were waited for; matrix products, arithmetic and copies ran while one was open for 6% of the time, Pallas kernels for 0%

profile of v6, /device:TPU:0, one launch (start us, length us, event | category | flops | bytes accessed | tf_op | source)
XLA Modules:
  0.0 208.1 jit_solution(12212814192737465938)
XLA Ops:
  7.2 0.8 select_reduce_fusion.1
  8.1 0.9 select_reduce_fusion.4
  9.0 1.9 bitcast_select_fusion
  11.0 0.7 add_bitcast_fusion
  11.7 43.7 %all-gather.1 = s32[32,2,8]{2,1,0:T(2,128)S(1)} all-gather(s32[1,2,8]{2,1,0:T(2,128)S(1)} %add_bitcast_fusion), channel_id=2, replica_groups=mesh['lvl'=4,'prow'=4,'pcol'=2] {'lvl','prow','pcol'}, dimensions={0}, use_global_device_ids=true | all-gather | bytes 2112 | tf_op jit(solution)/shard_map/all_gather | solution.py:61
  55.4 0.7 select_reduce_fusion.3
  56.2 1.0 compare_select_fusion
  57.2 2.7 %all-gather.5.cloned.1.call-done = bf16[1024,1024]{1,0:T(8,128)(2,1)} async-done(((bf16[256,1024]{1,0:T(8,128)(2,1)}), bf16[1024,1024]{1,0:T(8,128)(2,1)}) %all-gather.5.cloned.1.call-update) | async-done | bytes 2097168 | tf_op jit(solution)/shard_map/all_gather | solution.py:53
  60.1 0.3 convert_reduce_fusion
  60.4 0.1 fusion.15
  60.6 0.2 fusion.14
  60.8 0.2 select_reduce_fusion
  61.1 2.1 %fusion.37 = (bf16[256,256]{0,1:T(8,128)(2,1)}, f32[256,256]{0,1:T(8,128)}) fusion(bf16[256,1024]{1,0:T(8,128)(2,1)} %compare_select_fusion, f32[1,1,1024,256]{3,2,1,0:T(8,128)S(1)} %copy-done.3), kind=kOutput, calls=%fused_computation.103 | convolution fusion | flops 134545408 | bytes 1966080 | tf_op jit(solution)/shard_map/dot_general | solution.py:98
  63.2 3.3 %all-to-all-start = ((bf16[4,256,64]{1,2,0:T(8,128)(2,1)}), bf16[4,256,64]{1,2,0:T(8,128)(2,1)S(1)}, u32[]{:S(2)}, u32[]{:S(2)}) async-start(bf16[4,256,64]{1,2,0:T(8,128)(2,1)} %bitcast.16), calls=%async_computation | async-start | bytes 262144 | tf_op jit(solution)/shard_map/all_to_all | solution.py:102
  66.5 8.0 %all-to-all-done = bf16[4,256,64]{1,2,0:T(8,128)(2,1)S(1)} async-done(((bf16[4,256,64]{1,2,0:T(8,128)(2,1)}), bf16[4,256,64]{1,2,0:T(8,128)(2,1)S(1)}, u32[]{:S(2)}, u32[]{:S(2)}) %all-to-all-start) | async-done | bytes 131104 | tf_op jit(solution)/shard_map/all_to_all | solution.py:102
  74.6 0.8 convolution_convert_fusion.3
  75.4 0.2 copy.51
  75.6 0.7 gather_fusion
  76.2 1.1 reshape.498
  77.4 4.1 %all-to-all-start.1 = ((bf16[8,2,8192]{2,1,0:T(2,128)(2,1)}), bf16[8,2,8192]{2,1,0:T(2,128)(2,1)S(1)}, u32[]{:S(2)}, u32[]{:S(2)}) async-start(bf16[8,2,8192]{2,1,0:T(2,128)(2,1)} %reshape.498), calls=%async_computation.1 | async-start | bytes 524288 | tf_op jit(solution)/shard_map/all_to_all | solution.py:120
  81.6 6.8 %all-to-all-done.1 = bf16[8,2,8192]{2,1,0:T(2,128)(2,1)S(1)} async-done(((bf16[8,2,8192]{2,1,0:T(2,128)(2,1)}), bf16[8,2,8192]{2,1,0:T(2,128)(2,1)S(1)}, u32[]{:S(2)}, u32[]{:S(2)}) %all-to-all-start.1) | async-done | bytes 262176 | tf_op jit(solution)/shard_map/all_to_all | solution.py:120
  88.4 0.3 reshape.499
  88.9 1.2 scatter_fusion
  90.2 1.3 fusion.6
  91.5 15.9 %all-gather.7.cloned.1.call-done = bf16[1024,1024]{1,0:T(8,128)(2,1)} async-done(((bf16[256,1024]{1,0:T(8,128)(2,1)}), bf16[1024,1024]{1,0:T(8,128)(2,1)}) %all-gather.7.cloned.1.call-update) | async-done | bytes 2097168 | tf_op jit(solution)/shard_map/all_gather | solution.py:55
  107.3 2.3 %fusion.38 = f32[1024,64]{0,1:T(8,128)S(1)} fusion(bf16[1024,1024]{1,0:T(8,128)(2,1)} %all-gather.7.cloned.1.call-done, bf16[1024,64]{1,0:T(8,128)(2,1)S(1)} %fusion.6), kind=kOutput, calls=%fused_computation.104 | convolution fusion | flops 134217728 | bytes 2490368 | tf_op jit(solution)/shard_map/dot_general | solution.py:110
  109.7 1.5 convolution_convert_fusion.2
  111.2 1.1 copy.52
  112.3 1.4 gather_fusion.1
  113.7 2.2 %reshape.500 = bf16[8,2,8192]{2,1,0:T(2,128)(2,1)} reshape(bf16[64,32,64]{2,1,0:T(8,128)(2,1)} %gather_fusion.1) | data formatting | bytes 524288
  115.8 4.0 %all-to-all-start.2 = ((bf16[8,2,8192]{2,1,0:T(2,128)(2,1)}), bf16[8,2,8192]{2,1,0:T(2,128)(2,1)S(1)}, u32[]{:S(2)}, u32[]{:S(2)}) async-start(bf16[8,2,8192]{2,1,0:T(2,128)(2,1)} %reshape.500), calls=%async_computation.2 | async-start | bytes 524288 | tf_op jit(solution)/shard_map/all_to_all | solution.py:120
  119.9 6.8 %all-to-all-done.2 = bf16[8,2,8192]{2,1,0:T(2,128)(2,1)S(1)} async-done(((bf16[8,2,8192]{2,1,0:T(2,128)(2,1)}), bf16[8,2,8192]{2,1,0:T(2,128)(2,1)S(1)}, u32[]{:S(2)}, u32[]{:S(2)}) %all-to-all-start.2) | async-done | bytes 262176 | tf_op jit(solution)/shard_map/all_to_all | solution.py:120
  126.7 1.2 reshape.501
  127.9 0.9 slice_convert_fusion.2
  128.8 1.2 scatter_fusion.1
  130.1 1.4 fusion.5
  131.5 0.3 copy-done.1
  131.8 0.8 fusion.39
  132.5 1.5 convolution_convert_fusion.1
  134.0 1.8 copy.53
  135.8 2.4 %gather_fusion.2 = bf16[64,32,64]{2,1,0:T(8,128)(2,1)} fusion(bf16[33,32,64]{2,1,0:T(8,128)(2,1)} %bitcast.93, s32[1024]{0:T(1024)S(1)} %pad_clamp_fusion), kind=kCustom, calls=%fused_computation.2 | custom fusion | bytes 524544 | tf_op jit(solution)/shard_map/jit(_take)/gather | solution.py:119
  138.2 2.1 %reshape.502 = bf16[8,2,8192]{2,1,0:T(2,128)(2,1)} reshape(bf16[64,32,64]{2,1,0:T(8,128)(2,1)} %gather_fusion.2) | data formatting | bytes 524288
  140.3 4.2 %all-to-all-start.3 = ((bf16[8,2,8192]{2,1,0:T(2,128)(2,1)}), bf16[8,2,8192]{2,1,0:T(2,128)(2,1)}, u32[]{:S(2)}, u32[]{:S(2)}) async-start(bf16[8,2,8192]{2,1,0:T(2,128)(2,1)} %reshape.502), calls=%async_computation.3 | async-start | bytes 524288 | tf_op jit(solution)/shard_map/all_to_all | solution.py:120
  144.6 6.7 %all-to-all-done.3 = bf16[8,2,8192]{2,1,0:T(2,128)(2,1)} async-done(((bf16[8,2,8192]{2,1,0:T(2,128)(2,1)}), bf16[8,2,8192]{2,1,0:T(2,128)(2,1)}, u32[]{:S(2)}, u32[]{:S(2)}) %all-to-all-start.3) | async-done | bytes 262176 | tf_op jit(solution)/shard_map/all_to_all | solution.py:120
  151.3 2.1 %reshape.503 = bf16[64,32,64]{2,1,0:T(8,128)(2,1)} reshape(bf16[8,2,8192]{2,1,0:T(2,128)(2,1)} %all-to-all-done.3) | data formatting | bytes 524288
  153.4 1.7 slice_convert_fusion.1
  155.1 1.9 scatter_fusion.2
  157.1 1.4 fusion.4
  158.5 0.3 copy-done.2
  158.8 1.5 select_select_fusion
  160.3 0.8 convolution_convert_fusion
  161.1 0.2 copy.54
  161.3 0.7 gather_fusion.3
  161.9 1.1 reshape.504
  163.0 3.4 %all-to-all-start.4 = ((bf16[8,2,8192]{2,1,0:T(2,128)(2,1)}), bf16[8,2,8192]{2,1,0:T(2,128)(2,1)S(1)}, u32[]{:S(2)}, u32[]{:S(2)}) async-start(bf16[8,2,8192]{2,1,0:T(2,128)(2,1)} %reshape.504), calls=%async_computation.4 | async-start | bytes 524288 | tf_op jit(solution)/shard_map/all_to_all | solution.py:120
  166.6 6.7 %all-to-all-done.4 = bf16[8,2,8192]{2,1,0:T(2,128)(2,1)S(1)} async-done(((bf16[8,2,8192]{2,1,0:T(2,128)(2,1)}), bf16[8,2,8192]{2,1,0:T(2,128)(2,1)S(1)}, u32[]{:S(2)}, u32[]{:S(2)}) %all-to-all-start.4) | async-done | bytes 262176 | tf_op jit(solution)/shard_map/all_to_all | solution.py:120
  173.3 0.3 reshape.505
  173.7 1.2 scatter_fusion.3
  174.9 0.1 copy.55
  175.1 0.9 pad_maximum_fusion
  176.1 3.5 %all-to-all-start.5 = ((f32[4,768,64]{1,2,0:T(8,128)}), f32[4,768,64]{1,2,0:T(8,128)S(1)}, u32[]{:S(2)}, u32[]{:S(2)}) async-start(f32[4,768,64]{1,2,0:T(8,128)} %pad_maximum_fusion), calls=%async_computation.5 | async-start | bytes 1572864 | tf_op jit(solution)/shard_map/all_to_all | solution.py:134
  179.6 19.7 %all-to-all-done.5 = f32[4,768,64]{1,2,0:T(8,128)S(1)} async-done(((f32[4,768,64]{1,2,0:T(8,128)}), f32[4,768,64]{1,2,0:T(8,128)S(1)}, u32[]{:S(2)}, u32[]{:S(2)}) %all-to-all-start.5) | async-done | bytes 786464 | tf_op jit(solution)/shard_map/all_to_all | solution.py:134
  199.3 0.8 copy.57
  200.2 1.0 copy.58
  (57 shorter events, 1.5 us)
Async XLA Ops:
  7.2 49.0 %copy-start.6 = (bf16[1,1,256,1024]{3,2,1,0:T(8,128)(2,1)S(1)}, bf16[1,1,256,1024]{3,2,1,0:T(8,128)(2,1)}, u32[]{:S(2)}) copy-start(bf16[1,1,256,1024]{3,2,1,0:T(8,128)(2,1)} %param.10) | copy-start | bytes 1572868
  7.2 53.9 %copy-start.3 = (f32[1,1,1024,256]{3,2,1,0:T(8,128)S(1)}, f32[1,1,1024,256]{3,2,1,0:T(8,128)}, u32[]{:S(2)}) copy-start(f32[1,1,1024,256]{3,2,1,0:T(8,128)} %param.9) | copy-start | bytes 3145732
  7.2 52.7 %all-gather.5.cloned.1.call-start = ((), (), s32[]{:S(2)}) async-start(), calls=%async_computation.6 | async-start | bytes 2621440 | tf_op jit(solution)/shard_map/all_gather | solution.py:53
  10.9 96.4 %all-gather.7.cloned.1.call-start = ((), (), s32[]{:S(2)}) async-start(), calls=%async_computation.7 | async-start | bytes 2621440 | tf_op jit(solution)/shard_map/all_gather | solution.py:55
  59.9 14.7 %copy-start = (bf16[1024,1024]{1,0:T(8,128)(2,1)S(1)}, bf16[1024,1024]{1,0:T(8,128)(2,1)}, u32[]{:S(2)}) copy-start(bf16[1024,1024]{1,0:T(8,128)(2,1)} %all-gather.5.cloned.1.call-done) | copy-start | bytes 6291460
  63.2 11.3 %all-to-all-start = ((bf16[4,256,64]{1,2,0:T(8,128)(2,1)}), bf16[4,256,64]{1,2,0:T(8,128)(2,1)S(1)}, u32[]{:S(2)}, u32[]{:S(2)}) async-start(bf16[4,256,64]{1,2,0:T(8,128)(2,1)} %bitcast.16), calls=%async_computation | async-start | bytes 262144 | tf_op jit(solution)/shard_map/all_to_all | solution.py:102
  77.4 11.1 %all-to-all-start.1 = ((bf16[8,2,8192]{2,1,0:T(2,128)(2,1)}), bf16[8,2,8192]{2,1,0:T(2,128)(2,1)S(1)}, u32[]{:S(2)}, u32[]{:S(2)}) async-start(bf16[8,2,8192]{2,1,0:T(2,128)(2,1)} %reshape.498), calls=%async_computation.1 | async-start | bytes 524288 | tf_op jit(solution)/shard_map/all_to_all | solution.py:120
  115.8 10.9 %all-to-all-start.2 = ((bf16[8,2,8192]{2,1,0:T(2,128)(2,1)}), bf16[8,2,8192]{2,1,0:T(2,128)(2,1)S(1)}, u32[]{:S(2)}, u32[]{:S(2)}) async-start(bf16[8,2,8192]{2,1,0:T(2,128)(2,1)} %reshape.500), calls=%async_computation.2 | async-start | bytes 524288 | tf_op jit(solution)/shard_map/all_to_all | solution.py:120
  130.0 1.7 copy-start.1
  140.3 11.0 %all-to-all-start.3 = ((bf16[8,2,8192]{2,1,0:T(2,128)(2,1)}), bf16[8,2,8192]{2,1,0:T(2,128)(2,1)}, u32[]{:S(2)}, u32[]{:S(2)}) async-start(bf16[8,2,8192]{2,1,0:T(2,128)(2,1)} %reshape.502), calls=%async_computation.3 | async-start | bytes 524288 | tf_op jit(solution)/shard_map/all_to_all | solution.py:120
  157.0 1.7 copy-start.2
  160.3 6.3 %copy-start.4 = (f32[1024,64]{0,1:T(8,128)S(1)}, f32[1024,64]{0,1:T(8,128)}, u32[]{:S(2)}) copy-start(f32[1024,64]{0,1:T(8,128)} %get-tuple-element.36) | copy-start | bytes 786436
  163.0 10.3 %all-to-all-start.4 = ((bf16[8,2,8192]{2,1,0:T(2,128)(2,1)}), bf16[8,2,8192]{2,1,0:T(2,128)(2,1)S(1)}, u32[]{:S(2)}, u32[]{:S(2)}) async-start(bf16[8,2,8192]{2,1,0:T(2,128)(2,1)} %reshape.504), calls=%async_computation.4 | async-start | bytes 524288 | tf_op jit(solution)/shard_map/all_to_all | solution.py:120
  175.0 24.2 %copy-start.5 = (f32[256,256]{0,1:T(8,128)S(1)}, f32[256,256]{0,1:T(8,128)}, u32[]{:S(2)}) copy-start(f32[256,256]{0,1:T(8,128)} %get-tuple-element.35) | copy-start | bytes 786436
  176.1 23.2 %all-to-all-start.5 = ((f32[4,768,64]{1,2,0:T(8,128)}), f32[4,768,64]{1,2,0:T(8,128)S(1)}, u32[]{:S(2)}, u32[]{:S(2)}) async-start(f32[4,768,64]{1,2,0:T(8,128)} %pad_maximum_fusion), calls=%async_computation.5 | async-start | bytes 1572864 | tf_op jit(solution)/shard_map/all_to_all | solution.py:134
Sparse Core Ops, SparseCore 0:
  11.0 48.7 all-gather.4
  62.0 45.3 all-gather.6

commit v7 on v6

--- a/solution.py
+++ b/solution.py
@@ -51,14 +51,29 @@
     ).reshape(tile_count * block_rows, width)
 
     tiles_full = lax.all_gather(tiles_used, "prow", axis=0, tiled=True)
-    inverse, tiles_full = lax.optimization_barrier((inverse, tiles_full))
+    rows_out = width // n_prow
+    first_rows = jnp.dot(
+        inverse, rhs[0, 0].astype(jnp.bfloat16), preferred_element_type=jnp.float32
+    )
+    first_half = first_rows.astype(jnp.bfloat16).reshape(rows_out, n_prow, cols)
+    first_cols = lax.all_to_all(
+        jnp.transpose(first_half, (1, 0, 2)), "prow", split_axis=0, concat_axis=0, tiled=True
+    ).reshape(width, cols)
+    inverse, tiles_full, first_cols = lax.optimization_barrier((inverse, tiles_full, first_cols))
     inv_full = lax.all_gather(inverse, "prow", axis=0, tiled=True)
     tiles_full = jnp.concatenate(
         [tiles_full, jnp.zeros((block_rows, width), jnp.bfloat16)], axis=0
     )
 
     meta = jnp.stack([off_device[0, 0], off_block[0, 0]], axis=0)
-    meta = lax.all_gather(meta, ("lvl", "prow", "pcol"), axis=0)
+    devices = n_lvl * n_prow * n_pcol
+    meta = lax.all_to_all(
+        jnp.broadcast_to(meta[None], (devices,) + meta.shape),
+        ("lvl", "prow", "pcol"),
+        split_axis=0,
+        concat_axis=0,
+        tiled=True,
+    )
     meta = meta.reshape(n_lvl, n_prow, n_pcol, 2, tile_count)
     meta = jnp.transpose(meta, (0, 2, 1, 3, 4)).reshape(groups, n_prow, 2, tile_count)
     target = meta[:, :, 0, :].reshape(groups, group_tiles)
@@ -94,14 +109,6 @@
     window_blocks = width // block_rows
     acc = jnp.zeros((NT + 1, block_rows, cols), jnp.float32)
     solved = jnp.zeros((width, cols), jnp.float32)
-    rows_out = width // n_prow
-    first_rows = jnp.dot(
-        inverse, rhs[0, 0].astype(jnp.bfloat16), preferred_element_type=jnp.float32
-    )
-    first_half = first_rows.astype(jnp.bfloat16).reshape(rows_out, n_prow, cols)
-    first_cols = lax.all_to_all(
-        jnp.transpose(first_half, (1, 0, 2)), "prow", split_axis=0, concat_axis=0, tiled=True
-    ).reshape(width, cols)
     for section in range(n_lvl):
         if section == 0:
             solved_half = first_cols

time: 209 us -> 210 us (level)
  blocking collectives: 43.7 us -> 0 us
  waiting for transfers between devices: 73.4 us -> 108 us
  starting transfers between devices: 22.6 us -> 30.2 us
    all_gather x1 -> x0, blocking collectives: 43.7 us -> none  [per_device(): meta = lax.all_gather(meta, ('lvl', 'prow', 'pcol'), axis=0)]
    all_gather x1, waiting for transfers between devices: 2.66 us -> 26.8 us  [per_device(): tiles_full = lax.all_gather(tiles_used, 'prow', axis=0, tiled=True)]
    all_gather x1, waiting for transfers between devices: 15.9 us -> 26.8 us  [per_device(): inv_full = lax.all_gather(inverse, 'prow', axis=0, tiled=True)]
    all_to_all x0 -> x1, starting transfers between devices: none -> 5.36 us  [per_device(): lax.all_to_all(jnp.broadcast_to(meta[None], (devices,) + meta.shape), ('l...]
    all_to_all x1, starting transfers between devices: 3.32 us -> 6.32 us  [per_device(): lax.all_to_all(jnp.transpose(first_half, (1, 0, 2)), 'prow', split_axis=0...]
    unnamed x24 -> x28, local copies, waits for them, and re-layouts: 12.9 us -> 12.9 us
  transfers between devices with their start and end apart: 8 -> 9, of which waited for: 8 -> 8; matrix products, arithmetic and copies ran while one was open for 6% -> 7% of each run, Pallas kernels for 0% -> 0%
where the time goes in v7:
time: 210 us; the launch traced here: 209 us
  waiting for transfers between devices  108 us (51%)
  starting transfers between devices  30.2 us (14%)
  local copies, waits for them, and re-layouts  22.9 us (11%)
  other arithmetic  19.9 us (9%)
  between operations  14.5 us (7%)
  matrix products  12.9 us (6%)
    all_to_all x4, waiting for transfers between devices, per_device(): lax.all_to_all(sending, ('lvl', 'pcol'), split_axis=0, concat_axis=0, til...  27.1 us
    all_gather x1, waiting for transfers between devices, per_device(): inv_full = lax.all_gather(inverse, 'prow', axis=0, tiled=True)  26.8 us
    all_gather x1, waiting for transfers between devices, per_device(): tiles_full = lax.all_gather(tiles_used, 'prow', axis=0, tiled=True)  26.8 us
    all_to_all x1, waiting for transfers between devices, per_device(): lax.all_to_all(final, 'prow', split_axis=0, concat_axis=0, tiled=True)  19.7 us
    all_to_all x4, starting transfers between devices, per_device(): lax.all_to_all(sending, ('lvl', 'pcol'), split_axis=0, concat_axis=0, til...  15 us
    unnamed x28, local copies, waits for them, and re-layouts  12.9 us
    all_to_all x1, waiting for transfers between devices, per_device(): lax.all_to_all(jnp.transpose(first_half, (1, 0, 2)), 'prow', split_axis=0...  7.61 us
    all_to_all x1, starting transfers between devices, per_device(): lax.all_to_all(jnp.transpose(first_half, (1, 0, 2)), 'prow', split_axis=0...  6.32 us
  transfers between devices with their start and end apart: 9, of which 8 were waited for; matrix products, arithmetic and copies ran while one was open for 7% of the time, Pallas kernels for 0%

profile of v7, /device:TPU:0, one launch (start us, length us, event | category | flops | bytes accessed | tf_op | source)
XLA Modules:
  0.0 208.5 jit_solution(4118324994653424887)
XLA Ops:
  7.3 0.8 select_reduce_fusion.1
  8.1 0.9 select_reduce_fusion.4
  9.0 1.9 bitcast_select_fusion
  11.0 0.7 select_reduce_fusion.3
  11.7 2.2 %fusion.43 = (bf16[256,256]{0,1:T(8,128)(2,1)}, f32[256,256]{0,1:T(8,128)}) fusion(f32[1,1,1024,256]{3,2,1,0:T(8,128)S(1)} %copy-done.3, bf16[1,1,256,1024]{3,2,1,0:T(8,128)(2,1)} %param.10, s32[1024]{0:T(1024)S(1)} %select_reduce_fusion.1, s32[256]{0:T(256)S(1)} %select_reduce_fusion.3), kind=kOutput, calls=%fused_computation.109 | convolution fusion | flops 135069696 | bytes 1971200 | tf_op jit(solution)/shard_map/dot_general | solution.py:55
  13.9 6.3 %all-to-all-start = ((bf16[4,256,64]{1,2,0:T(8,128)(2,1)}), bf16[4,256,64]{1,2,0:T(8,128)(2,1)S(1)}, u32[]{:S(2)}, u32[]{:S(2)}) async-start(bf16[4,256,64]{1,2,0:T(8,128)(2,1)} %bitcast.8), calls=%async_computation | async-start | bytes 262144 | tf_op jit(solution)/shard_map/all_to_all | solution.py:59
  20.3 1.0 compare_select_fusion
  21.3 7.6 %all-to-all-done = bf16[4,256,64]{1,2,0:T(8,128)(2,1)S(1)} async-done(((bf16[4,256,64]{1,2,0:T(8,128)(2,1)}), bf16[4,256,64]{1,2,0:T(8,128)(2,1)S(1)}, u32[]{:S(2)}, u32[]{:S(2)}) %all-to-all-start) | async-done | bytes 131104 | tf_op jit(solution)/shard_map/all_to_all | solution.py:59
  28.9 0.6 broadcast_in_dim.150
  29.6 5.4 %all-to-all-start.1 = ((s32[32,2,8]{2,1,0:T(2,128)}), s32[32,2,8]{2,1,0:T(2,128)S(1)}, u32[]{:S(2)}, u32[]{:S(2)}) async-start(s32[32,2,8]{2,1,0:T(2,128)} %broadcast_in_dim.150), calls=%async_computation.1 | async-start | bytes 65536 | tf_op jit(solution)/shard_map/all_to_all | solution.py:70
  35.0 26.8 %all-gather.3.cloned.1.call-done = bf16[1024,1024]{1,0:T(8,128)(2,1)} async-done(((bf16[256,1024]{1,0:T(8,128)(2,1)}), bf16[1024,1024]{1,0:T(8,128)(2,1)}) %all-gather.3.cloned.1.call-update) | async-done | bytes 2097168 | tf_op jit(solution)/shard_map/all_gather | solution.py:53
  62.1 0.3 convert_reduce_fusion
  62.4 0.1 fusion.20
  62.6 0.2 fusion.19
  62.9 0.2 select_reduce_fusion
  63.1 2.4 %convolution_convert_fusion.3 = bf16[1056,64]{0,1:T(8,128)(2,1)S(1)} fusion(bf16[1024,64]{0,1:T(8,128)(2,1)S(1)} %bitcast.101, bf16[1024,1024]{1,0:T(8,128)(2,1)} %all-gather.3.cloned.1.call-done), kind=kOutput, calls=%fused_computation.11 | convolution fusion | flops 138479616 | bytes 2363392 | tf_op jit(solution)/shard_map/dot_general | solution.py:122
  65.5 0.2 copy.62
  65.7 0.7 gather_fusion
  66.4 1.1 reshape.536
  67.5 3.7 %all-to-all-start.2 = ((bf16[8,2,8192]{2,1,0:T(2,128)(2,1)}), bf16[8,2,8192]{2,1,0:T(2,128)(2,1)S(1)}, u32[]{:S(2)}, u32[]{:S(2)}) async-start(bf16[8,2,8192]{2,1,0:T(2,128)(2,1)} %reshape.536), calls=%async_computation.2 | async-start | bytes 524288 | tf_op jit(solution)/shard_map/all_to_all | solution.py:127
  71.3 6.8 %all-to-all-done.2 = bf16[8,2,8192]{2,1,0:T(2,128)(2,1)S(1)} async-done(((bf16[8,2,8192]{2,1,0:T(2,128)(2,1)}), bf16[8,2,8192]{2,1,0:T(2,128)(2,1)S(1)}, u32[]{:S(2)}, u32[]{:S(2)}) %all-to-all-start.2) | async-done | bytes 262176 | tf_op jit(solution)/shard_map/all_to_all | solution.py:127
  78.1 0.3 reshape.537
  78.6 1.2 scatter_fusion
  79.9 1.4 fusion.9
  81.3 26.8 %all-gather.5.cloned.1.call-done = bf16[1024,1024]{1,0:T(8,128)(2,1)} async-done(((bf16[256,1024]{1,0:T(8,128)(2,1)}), bf16[1024,1024]{1,0:T(8,128)(2,1)}) %all-gather.5.cloned.1.call-update) | async-done | bytes 2097168 | tf_op jit(solution)/shard_map/all_gather | solution.py:63
  108.1 2.3 %fusion.44 = f32[1024,64]{0,1:T(8,128)S(1)} fusion(bf16[1024,1024]{1,0:T(8,128)(2,1)} %all-gather.5.cloned.1.call-done, bf16[1024,64]{1,0:T(8,128)(2,1)S(1)} %fusion.9), kind=kOutput, calls=%fused_computation.110 | convolution fusion | flops 134217728 | bytes 2490368 | tf_op jit(solution)/shard_map/dot_general | solution.py:117
  110.5 1.5 convolution_convert_fusion.2
  112.0 1.1 copy.63
  113.0 1.4 gather_fusion.1
  114.5 2.2 %reshape.538 = bf16[8,2,8192]{2,1,0:T(2,128)(2,1)} reshape(bf16[64,32,64]{2,1,0:T(8,128)(2,1)} %gather_fusion.1) | data formatting | bytes 524288
  116.6 3.6 %all-to-all-start.3 = ((bf16[8,2,8192]{2,1,0:T(2,128)(2,1)}), bf16[8,2,8192]{2,1,0:T(2,128)(2,1)S(1)}, u32[]{:S(2)}, u32[]{:S(2)}) async-start(bf16[8,2,8192]{2,1,0:T(2,128)(2,1)} %reshape.538), calls=%async_computation.3 | async-start | bytes 524288 | tf_op jit(solution)/shard_map/all_to_all | solution.py:127
  120.4 6.8 %all-to-all-done.3 = bf16[8,2,8192]{2,1,0:T(2,128)(2,1)S(1)} async-done(((bf16[8,2,8192]{2,1,0:T(2,128)(2,1)}), bf16[8,2,8192]{2,1,0:T(2,128)(2,1)S(1)}, u32[]{:S(2)}, u32[]{:S(2)}) %all-to-all-start.3) | async-done | bytes 262176 | tf_op jit(solution)/shard_map/all_to_all | solution.py:127
  127.2 1.2 reshape.539
  128.4 0.9 slice_convert_fusion.2
  129.3 1.2 scatter_fusion.1
  130.6 1.4 fusion.8
  132.0 0.3 copy-done.1
  132.2 0.8 fusion.45
  133.0 1.5 convolution_convert_fusion.1
  134.5 1.8 copy.64
  136.3 2.4 %gather_fusion.2 = bf16[64,32,64]{2,1,0:T(8,128)(2,1)} fusion(bf16[33,32,64]{2,1,0:T(8,128)(2,1)} %bitcast.95, s32[1024]{0:T(1024)S(1)} %pad_clamp_fusion), kind=kCustom, calls=%fused_computation.2 | custom fusion | bytes 524544 | tf_op jit(solution)/shard_map/jit(_take)/gather | solution.py:126
  138.6 2.1 %reshape.540 = bf16[8,2,8192]{2,1,0:T(2,128)(2,1)} reshape(bf16[64,32,64]{2,1,0:T(8,128)(2,1)} %gather_fusion.2) | data formatting | bytes 524288
  140.8 4.2 %all-to-all-start.4 = ((bf16[8,2,8192]{2,1,0:T(2,128)(2,1)}), bf16[8,2,8192]{2,1,0:T(2,128)(2,1)}, u32[]{:S(2)}, u32[]{:S(2)}) async-start(bf16[8,2,8192]{2,1,0:T(2,128)(2,1)} %reshape.540), calls=%async_computation.4 | async-start | bytes 524288 | tf_op jit(solution)/shard_map/all_to_all | solution.py:127
  145.1 6.7 %all-to-all-done.4 = bf16[8,2,8192]{2,1,0:T(2,128)(2,1)} async-done(((bf16[8,2,8192]{2,1,0:T(2,128)(2,1)}), bf16[8,2,8192]{2,1,0:T(2,128)(2,1)}, u32[]{:S(2)}, u32[]{:S(2)}) %all-to-all-start.4) | async-done | bytes 262176 | tf_op jit(solution)/shard_map/all_to_all | solution.py:127
  151.8 2.1 %reshape.541 = bf16[64,32,64]{2,1,0:T(8,128)(2,1)} reshape(bf16[8,2,8192]{2,1,0:T(2,128)(2,1)} %all-to-all-done.4) | data formatting | bytes 524288
  153.9 1.7 slice_convert_fusion.1
  155.6 1.9 scatter_fusion.2
  157.6 1.4 fusion.7
  159.0 0.3 copy-done.2
  159.3 1.5 select_select_fusion
  160.7 0.8 convolution_convert_fusion
  161.5 0.2 copy.65
  161.7 0.7 gather_fusion.3
  162.4 1.1 reshape.542
  163.5 3.4 %all-to-all-start.5 = ((bf16[8,2,8192]{2,1,0:T(2,128)(2,1)}), bf16[8,2,8192]{2,1,0:T(2,128)(2,1)S(1)}, u32[]{:S(2)}, u32[]{:S(2)}) async-start(bf16[8,2,8192]{2,1,0:T(2,128)(2,1)} %reshape.542), calls=%async_computation.5 | async-start | bytes 524288 | tf_op jit(solution)/shard_map/all_to_all | solution.py:127
  167.0 6.7 %all-to-all-done.5 = bf16[8,2,8192]{2,1,0:T(2,128)(2,1)S(1)} async-done(((bf16[8,2,8192]{2,1,0:T(2,128)(2,1)}), bf16[8,2,8192]{2,1,0:T(2,128)(2,1)S(1)}, u32[]{:S(2)}, u32[]{:S(2)}) %all-to-all-start.5) | async-done | bytes 262176 | tf_op jit(solution)/shard_map/all_to_all | solution.py:127
  173.8 0.3 reshape.543
  174.2 1.2 scatter_fusion.3
  175.4 0.1 copy.66
  175.6 0.9 pad_maximum_fusion
  176.5 3.5 %all-to-all-start.6 = ((f32[4,768,64]{1,2,0:T(8,128)}), f32[4,768,64]{1,2,0:T(8,128)S(1)}, u32[]{:S(2)}, u32[]{:S(2)}) async-start(f32[4,768,64]{1,2,0:T(8,128)} %pad_maximum_fusion), calls=%async_computation.6 | async-start | bytes 1572864 | tf_op jit(solution)/shard_map/all_to_all | solution.py:141
  180.0 19.7 %all-to-all-done.6 = f32[4,768,64]{1,2,0:T(8,128)S(1)} async-done(((f32[4,768,64]{1,2,0:T(8,128)}), f32[4,768,64]{1,2,0:T(8,128)S(1)}, u32[]{:S(2)}, u32[]{:S(2)}) %all-to-all-start.6) | async-done | bytes 786464 | tf_op jit(solution)/shard_map/all_to_all | solution.py:141
  199.8 0.8 copy.68
  200.7 1.0 copy.69
  (64 shorter events, 1.5 us)
Async XLA Ops:
  7.2 4.6 %copy-start.3 = (f32[1,1,1024,256]{3,2,1,0:T(8,128)S(1)}, f32[1,1,1024,256]{3,2,1,0:T(8,128)}, u32[]{:S(2)}) copy-start(f32[1,1,1024,256]{3,2,1,0:T(8,128)} %param.9) | copy-start | bytes 3145732
  7.2 13.1 %copy-start.4 = (bf16[1,1,256,1024]{3,2,1,0:T(8,128)(2,1)S(1)}, bf16[1,1,256,1024]{3,2,1,0:T(8,128)(2,1)}, u32[]{:S(2)}) copy-start(bf16[1,1,256,1024]{3,2,1,0:T(8,128)(2,1)} %param.10) | copy-start | bytes 1572868
  7.2 13.1 %copy-start.7 = (s32[1,1,8]{2,1,0:T(1,128)S(1)}, s32[1,1,8]{2,1,0:T(1,128)}, u32[]{:S(2)}) copy-start(s32[1,1,8]{2,1,0:T(1,128)} %param.14) | copy-start | bytes 100
  7.2 13.0 %copy-start.8 = (s32[1,1,8]{2,1,0:T(1,128)S(1)}, s32[1,1,8]{2,1,0:T(1,128)}, u32[]{:S(2)}) copy-start(s32[1,1,8]{2,1,0:T(1,128)} %param.13) | copy-start | bytes 100
  7.2 54.6 %all-gather.3.cloned.1.call-start = ((), (), s32[]{:S(2)}) async-start(), calls=%async_computation.7 | async-start | bytes 2621440 | tf_op jit(solution)/shard_map/all_gather | solution.py:53
  13.9 15.0 %all-to-all-start = ((bf16[4,256,64]{1,2,0:T(8,128)(2,1)}), bf16[4,256,64]{1,2,0:T(8,128)(2,1)S(1)}, u32[]{:S(2)}, u32[]{:S(2)}) async-start(bf16[4,256,64]{1,2,0:T(8,128)(2,1)} %bitcast.8), calls=%async_computation | async-start | bytes 262144 | tf_op jit(solution)/shard_map/all_to_all | solution.py:59
  29.6 32.3 %all-to-all-start.1 = ((s32[32,2,8]{2,1,0:T(2,128)}), s32[32,2,8]{2,1,0:T(2,128)S(1)}, u32[]{:S(2)}, u32[]{:S(2)}) async-start(s32[32,2,8]{2,1,0:T(2,128)} %broadcast_in_dim.150), calls=%async_computation.1 | async-start | bytes 65536 | tf_op jit(solution)/shard_map/all_to_all | solution.py:70
  34.9 73.2 %all-gather.5.cloned.1.call-start = ((), (), s32[]{:S(2)}) async-start(), calls=%async_computation.8 | async-start | bytes 2621440 | tf_op jit(solution)/shard_map/all_gather | solution.py:63
  67.5 10.7 %all-to-all-start.2 = ((bf16[8,2,8192]{2,1,0:T(2,128)(2,1)}), bf16[8,2,8192]{2,1,0:T(2,128)(2,1)S(1)}, u32[]{:S(2)}, u32[]{:S(2)}) async-start(bf16[8,2,8192]{2,1,0:T(2,128)(2,1)} %reshape.536), calls=%async_computation.2 | async-start | bytes 524288 | tf_op jit(solution)/shard_map/all_to_all | solution.py:127
  79.8 30.6 %copy-start = (bf16[1024,1024]{1,0:T(8,128)(2,1)S(1)}, bf16[1024,1024]{1,0:T(8,128)(2,1)}, u32[]{:S(2)}) copy-start(bf16[1024,1024]{1,0:T(8,128)(2,1)} %all-gather.3.cloned.1.call-done) | copy-start | bytes 6291460
  116.6 10.6 %all-to-all-start.3 = ((bf16[8,2,8192]{2,1,0:T(2,128)(2,1)}), bf16[8,2,8192]{2,1,0:T(2,128)(2,1)S(1)}, u32[]{:S(2)}, u32[]{:S(2)}) async-start(bf16[8,2,8192]{2,1,0:T(2,128)(2,1)} %reshape.538), calls=%async_computation.3 | async-start | bytes 524288 | tf_op jit(solution)/shard_map/all_to_all | solution.py:127
  130.5 1.7 copy-start.1
  140.8 11.0 %all-to-all-start.4 = ((bf16[8,2,8192]{2,1,0:T(2,128)(2,1)}), bf16[8,2,8192]{2,1,0:T(2,128)(2,1)}, u32[]{:S(2)}, u32[]{:S(2)}) async-start(bf16[8,2,8192]{2,1,0:T(2,128)(2,1)} %reshape.540), calls=%async_computation.4 | async-start | bytes 524288 | tf_op jit(solution)/shard_map/all_to_all | solution.py:127
  157.5 1.7 copy-start.2
  160.7 6.3 %copy-start.5 = (f32[1024,64]{0,1:T(8,128)S(1)}, f32[1024,64]{0,1:T(8,128)}, u32[]{:S(2)}) copy-start(f32[1024,64]{0,1:T(8,128)} %get-tuple-element.40) | copy-start | bytes 786436
  163.5 10.3 %all-to-all-start.5 = ((bf16[8,2,8192]{2,1,0:T(2,128)(2,1)}), bf16[8,2,8192]{2,1,0:T(2,128)(2,1)S(1)}, u32[]{:S(2)}, u32[]{:S(2)}) async-start(bf16[8,2,8192]{2,1,0:T(2,128)(2,1)} %reshape.542), calls=%async_computation.5 | async-start | bytes 524288 | tf_op jit(solution)/shard_map/all_to_all | solution.py:127
  175.5 24.2 %copy-start.6 = (f32[256,256]{0,1:T(8,128)S(1)}, f32[256,256]{0,1:T(8,128)}, u32[]{:S(2)}) copy-start(f32[256,256]{0,1:T(8,128)} %get-tuple-element.39) | copy-start | bytes 786436
  176.5 23.2 %all-to-all-start.6 = ((f32[4,768,64]{1,2,0:T(8,128)}), f32[4,768,64]{1,2,0:T(8,128)S(1)}, u32[]{:S(2)}, u32[]{:S(2)}) async-start(f32[4,768,64]{1,2,0:T(8,128)} %pad_maximum_fusion), calls=%async_computation.6 | async-start | bytes 1572864 | tf_op jit(solution)/shard_map/all_to_all | solution.py:141
Sparse Core Ops, SparseCore 0:
  11.1 50.6 all-gather.2
  63.4 44.7 all-gather.4

commit v8 on v7

--- a/solution.py
+++ b/solution.py
@@ -50,19 +50,50 @@
         jnp.zeros((), jnp.bfloat16),
     ).reshape(tile_count * block_rows, width)
 
-    tiles_full = lax.all_gather(tiles_used, "prow", axis=0, tiled=True)
+    both = jnp.concatenate([inverse, tiles_used], axis=0)
+    gathered = lax.all_gather(both, "prow", axis=0)
+    inv_full = gathered[:, :row_count].reshape(n_prow * row_count, width)
+    tiles_full = gathered[:, row_count:].reshape(group_tiles * block_rows, width)
+    tiles_full = jnp.concatenate(
+        [tiles_full, jnp.zeros((block_rows, width), jnp.bfloat16)], axis=0
+    )
+
+    all_axes = ("lvl", "prow", "pcol")
+
+    def level0_shift(x, shift):
+        pairs = [
+            (p * n_pcol + c, ((p + shift) % n_prow) * n_pcol + c)
+            for p in range(n_prow)
+            for c in range(n_pcol)
+        ]
+        return lax.ppermute(x, all_axes, pairs)
+
+    def by_source(chunks):
+        stacked = jnp.stack(chunks)
+        order = (row_index - jnp.arange(n_prow, dtype=jnp.int32)) % n_prow
+        return jnp.take(stacked, order, axis=0, mode="clip")
+
     rows_out = width // n_prow
     first_rows = jnp.dot(
         inverse, rhs[0, 0].astype(jnp.bfloat16), preferred_element_type=jnp.float32
     )
-    first_half = first_rows.astype(jnp.bfloat16).reshape(rows_out, n_prow, cols)
-    first_cols = lax.all_to_all(
-        jnp.transpose(first_half, (1, 0, 2)), "prow", split_axis=0, concat_axis=0, tiled=True
-    ).reshape(width, cols)
-    inverse, tiles_full, first_cols = lax.optimization_barrier((inverse, tiles_full, first_cols))
-    inv_full = lax.all_gather(inverse, "prow", axis=0, tiled=True)
-    tiles_full = jnp.concatenate(
-        [tiles_full, jnp.zeros((block_rows, width), jnp.bfloat16)], axis=0
+    first_half = first_rows.astype(jnp.bfloat16)
+    first_all = by_source(
+        [first_half] + [level0_shift(first_half, k) for k in range(1, n_prow)]
+    ).reshape(width, columns_all)
+    first_updates = jnp.dot(
+        tiles_used, first_all, preferred_element_type=jnp.float32
+    ).astype(jnp.bfloat16)
+
+    def column_block(k):
+        start = ((row_index + k) % n_prow) * cols
+        return lax.dynamic_slice_in_dim(first_updates, start, cols, axis=1)
+
+    first_cols = by_source(
+        [column_block(0)] + [level0_shift(column_block(k), k) for k in range(1, n_prow)]
+    ).reshape(group_tiles * block_rows, cols)
+    first_cols = jnp.concatenate(
+        [first_cols, jnp.zeros((block_rows, cols), jnp.bfloat16)], axis=0
     )
 
     meta = jnp.stack([off_device[0, 0], off_block[0, 0]], axis=0)
@@ -111,17 +142,16 @@
     solved = jnp.zeros((width, cols), jnp.float32)
     for section in range(n_lvl):
         if section == 0:
-            solved_half = first_cols
+            updates = first_cols
         else:
             right = rhs_cols - acc[:window_blocks].reshape(width, cols)
             solved_now = jnp.dot(
                 inv_full, right.astype(jnp.bfloat16), preferred_element_type=jnp.float32
             )
             solved = jnp.where(level_index == section, solved_now, solved)
-            solved_half = solved_now.astype(jnp.bfloat16)
-        updates = jnp.dot(
-            tiles_full, solved_half, preferred_element_type=jnp.float32
-        ).astype(jnp.bfloat16)
+            updates = jnp.dot(
+                tiles_full, solved_now.astype(jnp.bfloat16), preferred_element_type=jnp.float32
+            ).astype(jnp.bfloat16)
         updates = updates.reshape(group_tiles + 1, block_rows, cols)
         sending = jnp.take(updates, send_index, axis=0, mode="clip")
         incoming = lax.all_to_all(

time: 210 us -> 210 us (level)
  waiting for transfers between devices: 108 us -> 84.8 us
  starting transfers between devices: 30.2 us -> 52.7 us
  local copies, waits for them, and re-layouts: 22.9 us -> 28.3 us
  other arithmetic: 19.9 us -> 16 us
    all_gather x2 -> x1, waiting for transfers between devices: 53.6 us -> 20.8 us  [per_device(): gathered = lax.all_gather(both, 'prow', axis=0)]
    ppermute x0 -> x6, starting transfers between devices: none -> 30.5 us  [level0_shift(): return lax.ppermute(x, all_axes, pairs)]
    all_to_all x1, waiting for transfers between devices: 0.01 us -> 12.3 us  [per_device(): lax.all_to_all(jnp.broadcast_to(meta[None], (devices,) + meta.shape), ('l...]
    all_to_all x1 -> x0, waiting for transfers between devices: 7.61 us -> none  [per_device(): lax.all_to_all(jnp.transpose(first_half, (1, 0, 2)), 'prow', split_axis=0...]
    all_to_all x1 -> x0, starting transfers between devices: 6.32 us -> none  [per_device(): lax.all_to_all(jnp.transpose(first_half, (1, 0, 2)), 'prow', split_axis=0...]
    ppermute x0 -> x6, waiting for transfers between devices: none -> 5.32 us  [level0_shift(): return lax.ppermute(x, all_axes, pairs)]
    convert_element_type x3 -> x0, other arithmetic: 4.28 us -> none  [per_device(): right.astype(jnp.bfloat16)]
    slice x0 -> x1, local copies, waits for them, and re-layouts: none -> 2.81 us  [per_device(): inv_full = gathered[:, :row_count].reshape(n_prow * row_count, width)]
  transfers between devices with their start and end apart: 9 -> 13, of which waited for: 8 -> 9; matrix products, arithmetic and copies ran while one was open for 7% -> 5% of each run, Pallas kernels for 0% -> 0%
where the time goes in v8:
time: 210 us; the launch traced here: 208 us
  waiting for transfers between devices  84.8 us (40%)
  starting transfers between devices  52.7 us (25%)
  local copies, waits for them, and re-layouts  28.3 us (13%)
  other arithmetic  16 us (8%)
  between operations  14.7 us (7%)
  matrix products  11.7 us (6%)
    ppermute x6, starting transfers between devices, level0_shift(): return lax.ppermute(x, all_axes, pairs)  30.5 us
    all_to_all x4, waiting for transfers between devices, per_device(): lax.all_to_all(sending, ('lvl', 'pcol'), split_axis=0, concat_axis=0, til...  26.9 us
    all_gather x1, waiting for transfers between devices, per_device(): gathered = lax.all_gather(both, 'prow', axis=0)  20.8 us
    all_to_all x1, waiting for transfers between devices, per_device(): lax.all_to_all(final, 'prow', split_axis=0, concat_axis=0, tiled=True)  19.4 us
    all_to_all x4, starting transfers between devices, per_device(): lax.all_to_all(sending, ('lvl', 'pcol'), split_axis=0, concat_axis=0, til...  14.5 us
    unnamed x30, local copies, waits for them, and re-layouts  13.6 us
    all_to_all x1, waiting for transfers between devices, per_device(): lax.all_to_all(jnp.broadcast_to(meta[None], (devices,) + meta.shape), ('l...  12.3 us
    dot_general x3, matrix products, per_device(): jnp.dot(inv_full, right.astype(jnp.bfloat16), preferred_element_type=jnp....  6.58 us
  transfers between devices with their start and end apart: 13, of which 9 were waited for; matrix products, arithmetic and copies ran while one was open for 5% of the time, Pallas kernels for 0%

profile of v8, /device:TPU:0, one launch (start us, length us, event | category | flops | bytes accessed | tf_op | source)
XLA Modules:
  0.0 208.3 jit_solution(1897455829864467735)
XLA Ops:
  7.2 0.7 select_reduce_fusion.1
  8.0 0.7 select_reduce_fusion.3
  8.7 0.9 select_reduce_fusion.4
  9.7 1.4 bitcast_select_fusion
  11.1 1.0 pad_maximum_fusion
  12.2 0.5 copy-done.1
  12.8 1.1 fusion.53
  13.9 6.9 %collective-permute-start.2 = (bf16[256,256]{1,0:T(8,128)(2,1)S(1)}, bf16[256,256]{1,0:T(8,128)(2,1)S(1)}, u32[]{:S(2)}, u32[]{:S(2)}) collective-permute-start(bf16[256,256]{1,0:T(8,128)(2,1)S(1)} %get-tuple-element.36), channel_id=1, source_target_pairs={{0,6},{1,7},{2,0},{3,1},{4,2},{5,3},{6,4},{7,5}} | collective-permute-start | bytes 393224 | tf_op jit(solution)/shard_map/ppermute | solution.py:69
  20.9 1.9 collective-permute-start.1
  22.8 2.9 %collective-permute-start = (bf16[256,256]{1,0:T(8,128)(2,1)S(1)}, bf16[256,256]{1,0:T(8,128)(2,1)S(1)}, u32[]{:S(2)}, u32[]{:S(2)}) collective-permute-start(bf16[256,256]{1,0:T(8,128)(2,1)S(1)} %get-tuple-element.36), channel_id=1, source_target_pairs={{0,2},{1,3},{2,4},{3,5},{4,6},{5,7},{6,0},{7,1}} | collective-permute-start | bytes 393224 | tf_op jit(solution)/shard_map/ppermute | solution.py:69
  25.7 0.6 broadcast_in_dim.157
  26.4 3.2 %all-to-all-start = ((s32[32,2,8]{2,1,0:T(2,128)}), s32[32,2,8]{2,1,0:T(2,128)S(1)}, u32[]{:S(2)}, u32[]{:S(2)}) async-start(s32[32,2,8]{2,1,0:T(2,128)} %broadcast_in_dim.157), calls=%async_computation | async-start | bytes 65536 | tf_op jit(solution)/shard_map/all_to_all | solution.py:101
  29.8 12.3 %all-to-all-done = s32[32,2,8]{2,1,0:T(2,128)S(1)} async-done(((s32[32,2,8]{2,1,0:T(2,128)}), s32[32,2,8]{2,1,0:T(2,128)S(1)}, u32[]{:S(2)}, u32[]{:S(2)}) %all-to-all-start) | async-done | bytes 2080 | tf_op jit(solution)/shard_map/all_to_all | solution.py:101
  43.4 0.6 gather_fusion
  44.0 0.4 convolution_convert_fusion.3
  44.4 13.8 %collective-permute-start.5 = (bf16[256,64]{0,1:T(8,128)(2,1)S(1)}, bf16[256,64]{0,1:T(8,128)(2,1)S(1)}, u32[]{:S(2)}, u32[]{:S(2)}) collective-permute-start(bf16[256,64]{0,1:T(8,128)(2,1)S(1)} %get-tuple-element.27), channel_id=1, source_target_pairs={{0,6},{1,7},{2,0},{3,1},{4,2},{5,3},{6,4},{7,5}} | collective-permute-start | bytes 98312 | tf_op jit(solution)/shard_map/ppermute | solution.py:69
  58.2 1.9 collective-permute-start.4
  60.1 2.9 %collective-permute-start.3 = (bf16[256,64]{0,1:T(8,128)(2,1)S(1)}, bf16[256,64]{0,1:T(8,128)(2,1)S(1)}, u32[]{:S(2)}, u32[]{:S(2)}) collective-permute-start(bf16[256,64]{0,1:T(8,128)(2,1)S(1)} %get-tuple-element.29), channel_id=1, source_target_pairs={{0,2},{1,3},{2,4},{3,5},{4,6},{5,7},{6,0},{7,1}} | collective-permute-start | bytes 98312 | tf_op jit(solution)/shard_map/ppermute | solution.py:69
  63.1 2.6 %collective-permute-done.4 = bf16[256,64]{0,1:T(8,128)(2,1)S(1)} collective-permute-done((bf16[256,64]{0,1:T(8,128)(2,1)S(1)}, bf16[256,64]{0,1:T(8,128)(2,1)S(1)}, u32[]{:S(2)}, u32[]{:S(2)}) %collective-permute-start.4) | collective-permute-done | bytes 32800 | tf_op jit(solution)/shard_map/ppermute | solution.py:69
  65.8 2.7 %collective-permute-done.3 = bf16[256,64]{0,1:T(8,128)(2,1)S(1)} collective-permute-done((bf16[256,64]{0,1:T(8,128)(2,1)S(1)}, bf16[256,64]{0,1:T(8,128)(2,1)S(1)}, u32[]{:S(2)}, u32[]{:S(2)}) %collective-permute-start.3) | collective-permute-done | bytes 32800 | tf_op jit(solution)/shard_map/ppermute | solution.py:69
  68.4 0.6 gather_fusion.1
  69.2 0.7 gather_fusion.2
  69.9 1.1 reshape.621
  71.0 3.4 %all-to-all-start.1 = ((bf16[8,2,8192]{2,1,0:T(2,128)(2,1)}), bf16[8,2,8192]{2,1,0:T(2,128)(2,1)S(1)}, u32[]{:S(2)}, u32[]{:S(2)}) async-start(bf16[8,2,8192]{2,1,0:T(2,128)(2,1)} %reshape.621), calls=%async_computation.1 | async-start | bytes 524288 | tf_op jit(solution)/shard_map/all_to_all | solution.py:157
  74.5 6.8 %all-to-all-done.1 = bf16[8,2,8192]{2,1,0:T(2,128)(2,1)S(1)} async-done(((bf16[8,2,8192]{2,1,0:T(2,128)(2,1)}), bf16[8,2,8192]{2,1,0:T(2,128)(2,1)S(1)}, u32[]{:S(2)}, u32[]{:S(2)}) %all-to-all-start.1) | async-done | bytes 262176 | tf_op jit(solution)/shard_map/all_to_all | solution.py:157
  81.3 0.3 reshape.622
  81.8 1.2 scatter_fusion
  83.0 0.8 slice.104
  83.8 20.8 %all-gather.3.cloned.1.call-done = bf16[2048,1024]{1,0:T(8,128)(2,1)} async-done(((bf16[512,1024]{1,0:T(8,128)(2,1)}), bf16[2048,1024]{1,0:T(8,128)(2,1)}) %all-gather.3.cloned.1.call-update) | async-done | bytes 4194320 | tf_op jit(solution)/shard_map/all_gather | solution.py:54
  104.7 2.8 %fusion.50 = (bf16[4,256,1024]{2,1,0:T(8,128)(2,1)S(1)}, bf16[4,256,1024]{2,1,0:T(8,128)(2,1)S(1)}) fusion(bf16[4,512,1024]{2,1,0:T(8,128)(2,1)} %bitcast.108), kind=kLoop, calls=%fused_computation.127 | loop fusion | bytes 8388608 | tf_op jit(solution)/shard_map/slice | solution.py:55
  107.5 1.3 copy-done
  108.8 0.8 fusion.11
  109.7 1.5 convolution_convert_fusion.2
  111.1 1.1 copy.59
  112.2 1.4 gather_fusion.3
  113.6 2.2 %reshape.623 = bf16[8,2,8192]{2,1,0:T(2,128)(2,1)} reshape(bf16[64,32,64]{2,1,0:T(8,128)(2,1)} %gather_fusion.3) | data formatting | bytes 524288
  115.8 3.4 %all-to-all-start.2 = ((bf16[8,2,8192]{2,1,0:T(2,128)(2,1)}), bf16[8,2,8192]{2,1,0:T(2,128)(2,1)S(1)}, u32[]{:S(2)}, u32[]{:S(2)}) async-start(bf16[8,2,8192]{2,1,0:T(2,128)(2,1)} %reshape.623), calls=%async_computation.2 | async-start | bytes 524288 | tf_op jit(solution)/shard_map/all_to_all | solution.py:157
  119.3 6.8 %all-to-all-done.2 = bf16[8,2,8192]{2,1,0:T(2,128)(2,1)S(1)} async-done(((bf16[8,2,8192]{2,1,0:T(2,128)(2,1)}), bf16[8,2,8192]{2,1,0:T(2,128)(2,1)S(1)}, u32[]{:S(2)}, u32[]{:S(2)}) %all-to-all-start.2) | async-done | bytes 262176 | tf_op jit(solution)/shard_map/all_to_all | solution.py:157
  126.1 1.2 reshape.624
  127.2 0.9 slice_convert_fusion.2
  128.2 1.2 scatter_fusion.1
  129.4 2.5 %fusion.14 = f32[1024,64]{0,1:T(8,128)S(1)} fusion(bf16[1024,1024]{1,0:T(8,128)(2,1)} %bitcast.106, f32[1,1,1024,64]{3,2,1,0:T(8,128)S(1)} %bitcast.118, f32[1,1,1024,256]{3,2,1,0:T(8,128)} %param.9, s32[]{:T(128)S(6)} %select_n.233), kind=kOutput, calls=%fused_computation.36 | convolution fusion | flops 134348800 | bytes 3145732 | tf_op jit(solution)/shard_map/dot_general | solution.py:148
  131.9 1.5 convolution_convert_fusion.1
  133.4 1.8 copy.60
  135.2 2.4 %gather_fusion.4 = bf16[64,32,64]{2,1,0:T(8,128)(2,1)} fusion(bf16[33,32,64]{2,1,0:T(8,128)(2,1)} %bitcast.112, s32[1024]{0:T(1024)S(1)} %pad_clamp_fusion), kind=kCustom, calls=%fused_computation.4 | custom fusion | bytes 524544 | tf_op jit(solution)/shard_map/jit(_take)/gather | solution.py:156
  137.6 2.1 %reshape.625 = bf16[8,2,8192]{2,1,0:T(2,128)(2,1)} reshape(bf16[64,32,64]{2,1,0:T(8,128)(2,1)} %gather_fusion.4) | data formatting | bytes 524288
  139.7 4.2 %all-to-all-start.3 = ((bf16[8,2,8192]{2,1,0:T(2,128)(2,1)}), bf16[8,2,8192]{2,1,0:T(2,128)(2,1)}, u32[]{:S(2)}, u32[]{:S(2)}) async-start(bf16[8,2,8192]{2,1,0:T(2,128)(2,1)} %reshape.625), calls=%async_computation.3 | async-start | bytes 524288 | tf_op jit(solution)/shard_map/all_to_all | solution.py:157
  144.0 6.7 %all-to-all-done.3 = bf16[8,2,8192]{2,1,0:T(2,128)(2,1)} async-done(((bf16[8,2,8192]{2,1,0:T(2,128)(2,1)}), bf16[8,2,8192]{2,1,0:T(2,128)(2,1)}, u32[]{:S(2)}, u32[]{:S(2)}) %all-to-all-start.3) | async-done | bytes 262176 | tf_op jit(solution)/shard_map/all_to_all | solution.py:157
  150.7 2.1 %reshape.626 = bf16[64,32,64]{2,1,0:T(8,128)(2,1)} reshape(bf16[8,2,8192]{2,1,0:T(2,128)(2,1)} %all-to-all-done.3) | data formatting | bytes 524288
  152.8 1.6 slice_convert_fusion.1
  154.5 2.0 scatter_fusion.2
  156.5 3.2 %select_select_fusion = (f32[1024,64]{0,1:T(8,128)}, bf16[1024,64]{0,1:T(8,128)(2,1)S(1)}) fusion(f32[1024,64]{0,1:T(8,128)S(1)} %fusion.14, f32[1024,64]{0,1:T(8,128)S(1)} %fusion.11, pred[]{:T(512)S(6)} %eq.207, pred[]{:T(512)S(6)} %eq.206, pred[]{:T(512)S(6)} %eq.181, bf16[1024,1024]{1,0:T(8,128)(2,1)} %bitcast.107, ...), kind=kOutput, calls=%fused_computation.41 | convolution fusion | flops 134610944 | bytes 3801095 | tf_op jit(solution)/shard_map/dot_general | solution.py:148
  159.7 0.8 convolution_convert_fusion
  160.7 0.7 gather_fusion.5
  161.4 1.1 reshape.627
  162.5 3.4 %all-to-all-start.4 = ((bf16[8,2,8192]{2,1,0:T(2,128)(2,1)}), bf16[8,2,8192]{2,1,0:T(2,128)(2,1)S(1)}, u32[]{:S(2)}, u32[]{:S(2)}) async-start(bf16[8,2,8192]{2,1,0:T(2,128)(2,1)} %reshape.627), calls=%async_computation.4 | async-start | bytes 524288 | tf_op jit(solution)/shard_map/all_to_all | solution.py:157
  166.0 6.7 %all-to-all-done.4 = bf16[8,2,8192]{2,1,0:T(2,128)(2,1)S(1)} async-done(((bf16[8,2,8192]{2,1,0:T(2,128)(2,1)}), bf16[8,2,8192]{2,1,0:T(2,128)(2,1)S(1)}, u32[]{:S(2)}, u32[]{:S(2)}) %all-to-all-start.4) | async-done | bytes 262176 | tf_op jit(solution)/shard_map/all_to_all | solution.py:157
  172.7 0.3 reshape.628
  173.1 1.2 scatter_fusion.3
  174.5 0.9 pad_maximum_fusion.1
  175.5 4.6 %all-to-all-start.5 = ((f32[4,768,64]{1,2,0:T(8,128)}), f32[4,768,64]{1,2,0:T(8,128)S(1)}, u32[]{:S(2)}, u32[]{:S(2)}) async-start(f32[4,768,64]{1,2,0:T(8,128)} %pad_maximum_fusion.1), calls=%async_computation.5 | async-start | bytes 1572864 | tf_op jit(solution)/shard_map/all_to_all | solution.py:171
  180.1 19.4 %all-to-all-done.5 = f32[4,768,64]{1,2,0:T(8,128)S(1)} async-done(((f32[4,768,64]{1,2,0:T(8,128)}), f32[4,768,64]{1,2,0:T(8,128)S(1)}, u32[]{:S(2)}, u32[]{:S(2)}) %all-to-all-start.5) | async-done | bytes 786464 | tf_op jit(solution)/shard_map/all_to_all | solution.py:171
  199.7 1.0 copy.65
  200.7 0.7 select_bitcast_fusion
  (79 shorter events, 3.1 us)
Async XLA Ops:
  7.2 97.5 %all-gather.3.cloned.1.call-start = ((), (), s32[]{:S(2)}) async-start(), calls=%async_computation.6 | async-start | bytes 5242880 | tf_op jit(solution)/shard_map/all_gather | solution.py:54
  11.1 1.6 copy-start.1
  11.1 1.7 copy-start.3
  11.1 14.6 %copy-start.8 = (s32[1,1,8]{2,1,0:T(1,128)S(1)}, s32[1,1,8]{2,1,0:T(1,128)}, u32[]{:S(2)}) copy-start(s32[1,1,8]{2,1,0:T(1,128)} %param.14) | copy-start | bytes 100
  11.1 14.6 %copy-start.9 = (s32[1,1,8]{2,1,0:T(1,128)S(1)}, s32[1,1,8]{2,1,0:T(1,128)}, u32[]{:S(2)}) copy-start(s32[1,1,8]{2,1,0:T(1,128)} %param.13) | copy-start | bytes 100
  12.2 17.5 %copy-start.4 = (bf16[1,1,8,32,1024]{4,3,2,1,0:T(8,128)(2,1)S(1)}, bf16[1,1,8,32,1024]{4,3,2,1,0:T(8,128)(2,1)}, u32[]{:S(2)}) copy-start(bf16[1,1,8,32,1024]{4,3,2,1,0:T(8,128)(2,1)} %param.11) | copy-start | bytes 1572868
  13.9 29.4 %collective-permute-start.2 = (bf16[256,256]{1,0:T(8,128)(2,1)S(1)}, bf16[256,256]{1,0:T(8,128)(2,1)S(1)}, u32[]{:S(2)}, u32[]{:S(2)}) collective-permute-start(bf16[256,256]{1,0:T(8,128)(2,1)S(1)} %get-tuple-element.36), channel_id=1, source_target_pairs={{0,6},{1,7},{2,0},{3,1},{4,2},{5,3},{6,4},{7,5}} | collective-permute-start | bytes 393224 | tf_op jit(solution)/shard_map/ppermute | solution.py:69
  20.9 22.4 %collective-permute-start.1 = (bf16[256,256]{1,0:T(8,128)(2,1)S(1)}, bf16[256,256]{1,0:T(8,128)(2,1)S(1)}, u32[]{:S(2)}, u32[]{:S(2)}) collective-permute-start(bf16[256,256]{1,0:T(8,128)(2,1)S(1)} %get-tuple-element.36), channel_id=1, source_target_pairs={{0,4},{1,5},{2,6},{3,7},{4,0},{5,1},{6,2},{7,3}} | collective-permute-start | bytes 393224 | tf_op jit(solution)/shard_map/ppermute | solution.py:69
  22.8 20.5 %collective-permute-start = (bf16[256,256]{1,0:T(8,128)(2,1)S(1)}, bf16[256,256]{1,0:T(8,128)(2,1)S(1)}, u32[]{:S(2)}, u32[]{:S(2)}) collective-permute-start(bf16[256,256]{1,0:T(8,128)(2,1)S(1)} %get-tuple-element.36), channel_id=1, source_target_pairs={{0,2},{1,3},{2,4},{3,5},{4,6},{5,7},{6,0},{7,1}} | collective-permute-start | bytes 393224 | tf_op jit(solution)/shard_map/ppermute | solution.py:69
  26.4 15.7 %all-to-all-start = ((s32[32,2,8]{2,1,0:T(2,128)}), s32[32,2,8]{2,1,0:T(2,128)S(1)}, u32[]{:S(2)}, u32[]{:S(2)}) async-start(s32[32,2,8]{2,1,0:T(2,128)} %broadcast_in_dim.157), calls=%async_computation | async-start | bytes 65536 | tf_op jit(solution)/shard_map/all_to_all | solution.py:101
  44.4 18.7 %collective-permute-start.5 = (bf16[256,64]{0,1:T(8,128)(2,1)S(1)}, bf16[256,64]{0,1:T(8,128)(2,1)S(1)}, u32[]{:S(2)}, u32[]{:S(2)}) collective-permute-start(bf16[256,64]{0,1:T(8,128)(2,1)S(1)} %get-tuple-element.27), channel_id=1, source_target_pairs={{0,6},{1,7},{2,0},{3,1},{4,2},{5,3},{6,4},{7,5}} | collective-permute-start | bytes 98312 | tf_op jit(solution)/shard_map/ppermute | solution.py:69
  58.2 7.5 %collective-permute-start.4 = (bf16[256,64]{0,1:T(8,128)(2,1)S(1)}, bf16[256,64]{0,1:T(8,128)(2,1)S(1)}, u32[]{:S(2)}, u32[]{:S(2)}) collective-permute-start(bf16[256,64]{0,1:T(8,128)(2,1)S(1)} %get-tuple-element.28), channel_id=1, source_target_pairs={{0,4},{1,5},{2,6},{3,7},{4,0},{5,1},{6,2},{7,3}} | collective-permute-start | bytes 98312 | tf_op jit(solution)/shard_map/ppermute | solution.py:69
  60.1 8.3 %collective-permute-start.3 = (bf16[256,64]{0,1:T(8,128)(2,1)S(1)}, bf16[256,64]{0,1:T(8,128)(2,1)S(1)}, u32[]{:S(2)}, u32[]{:S(2)}) collective-permute-start(bf16[256,64]{0,1:T(8,128)(2,1)S(1)} %get-tuple-element.29), channel_id=1, source_target_pairs={{0,2},{1,3},{2,4},{3,5},{4,6},{5,7},{6,0},{7,1}} | collective-permute-start | bytes 98312 | tf_op jit(solution)/shard_map/ppermute | solution.py:69
  71.0 10.3 %all-to-all-start.1 = ((bf16[8,2,8192]{2,1,0:T(2,128)(2,1)}), bf16[8,2,8192]{2,1,0:T(2,128)(2,1)S(1)}, u32[]{:S(2)}, u32[]{:S(2)}) async-start(bf16[8,2,8192]{2,1,0:T(2,128)(2,1)} %reshape.621), calls=%async_computation.1 | async-start | bytes 524288 | tf_op jit(solution)/shard_map/all_to_all | solution.py:157
  104.7 4.2 %copy-start.2 = (f32[1,1,1024,256]{3,2,1,0:T(8,128)S(1)}, f32[1,1,1024,256]{3,2,1,0:T(8,128)}, u32[]{:S(2)}) copy-start(f32[1,1,1024,256]{3,2,1,0:T(8,128)} %param.9) | copy-start | bytes 3145732
  104.7 4.2 %copy-start.5 = (f32[32,32,64]{2,1,0:T(8,128)S(1)}, f32[32,32,64]{2,1,0:T(8,128)}, u32[]{:S(2)}) copy-start(f32[32,32,64]{2,1,0:T(8,128)} %slice.104) | copy-start | bytes 786436
  107.5 1.3 copy-start
  115.8 10.3 %all-to-all-start.2 = ((bf16[8,2,8192]{2,1,0:T(2,128)(2,1)}), bf16[8,2,8192]{2,1,0:T(2,128)(2,1)S(1)}, u32[]{:S(2)}, u32[]{:S(2)}) async-start(bf16[8,2,8192]{2,1,0:T(2,128)(2,1)} %reshape.623), calls=%async_computation.2 | async-start | bytes 524288 | tf_op jit(solution)/shard_map/all_to_all | solution.py:157
  139.7 11.0 %all-to-all-start.3 = ((bf16[8,2,8192]{2,1,0:T(2,128)(2,1)}), bf16[8,2,8192]{2,1,0:T(2,128)(2,1)}, u32[]{:S(2)}, u32[]{:S(2)}) async-start(bf16[8,2,8192]{2,1,0:T(2,128)(2,1)} %reshape.625), calls=%async_computation.3 | async-start | bytes 524288 | tf_op jit(solution)/shard_map/all_to_all | solution.py:157
  159.7 6.3 %copy-start.6 = (f32[1024,64]{0,1:T(8,128)S(1)}, f32[1024,64]{0,1:T(8,128)}, u32[]{:S(2)}) copy-start(f32[1024,64]{0,1:T(8,128)} %get-tuple-element.38) | copy-start | bytes 786436
  162.5 10.3 %all-to-all-start.4 = ((bf16[8,2,8192]{2,1,0:T(2,128)(2,1)}), bf16[8,2,8192]{2,1,0:T(2,128)(2,1)S(1)}, u32[]{:S(2)}, u32[]{:S(2)}) async-start(bf16[8,2,8192]{2,1,0:T(2,128)(2,1)} %reshape.627), calls=%async_computation.4 | async-start | bytes 524288 | tf_op jit(solution)/shard_map/all_to_all | solution.py:157
  175.5 25.2 %copy-start.7 = (f32[256,256]{1,0:T(8,128)S(1)}, f32[256,256]{1,0:T(8,128)}, u32[]{:S(2)}) copy-start(f32[256,256]{1,0:T(8,128)} %get-tuple-element.37) | copy-start | bytes 786436
  175.5 24.0 %all-to-all-start.5 = ((f32[4,768,64]{1,2,0:T(8,128)}), f32[4,768,64]{1,2,0:T(8,128)S(1)}, u32[]{:S(2)}, u32[]{:S(2)}) async-start(f32[4,768,64]{1,2,0:T(8,128)} %pad_maximum_fusion.1), calls=%async_computation.5 | async-start | bytes 1572864 | tf_op jit(solution)/shard_map/all_to_all | solution.py:171
Sparse Core Ops, SparseCore 0:
  12.3 92.2 all-gather.2

commit v9 on v8

--- a/solution.py
+++ b/solution.py
@@ -140,20 +140,35 @@
     window_blocks = width // block_rows
     acc = jnp.zeros((NT + 1, block_rows, cols), jnp.float32)
     solved = jnp.zeros((width, cols), jnp.float32)
+    slot_rows = groups * slots * block_rows
+    direct = slot_rows * width * 2 <= (8 << 20)
+    if direct:
+        tiles_slots = jnp.take(
+            tiles_full.reshape(group_tiles + 1, block_rows, width), send_index, axis=0, mode="clip"
+        ).reshape(slot_rows, width)
     for section in range(n_lvl):
         if section == 0:
             updates = first_cols
-        else:
+        if section > 0:
             right = rhs_cols - acc[:window_blocks].reshape(width, cols)
             solved_now = jnp.dot(
                 inv_full, right.astype(jnp.bfloat16), preferred_element_type=jnp.float32
             )
             solved = jnp.where(level_index == section, solved_now, solved)
-            updates = jnp.dot(
-                tiles_full, solved_now.astype(jnp.bfloat16), preferred_element_type=jnp.float32
+        if section > 0 and direct:
+            sending = jnp.dot(
+                tiles_slots, solved_now.astype(jnp.bfloat16), preferred_element_type=jnp.float32
             ).astype(jnp.bfloat16)
-        updates = updates.reshape(group_tiles + 1, block_rows, cols)
-        sending = jnp.take(updates, send_index, axis=0, mode="clip")
+            sending = sending.reshape(groups * slots, block_rows, cols)
+        else:
+            if section > 0:
+                updates = jnp.dot(
+                    tiles_full,
+                    solved_now.astype(jnp.bfloat16),
+                    preferred_element_type=jnp.float32,
+                ).astype(jnp.bfloat16)
+            updates = updates.reshape(group_tiles + 1, block_rows, cols)
+            sending = jnp.take(updates, send_index, axis=0, mode="clip")
         incoming = lax.all_to_all(
             sending, ("lvl", "pcol"), split_axis=0, concat_axis=0, tiled=True
         )

time: 210 us -> 213 us (1.014)
  matrix products: 11.7 us -> 15.3 us
    gather x4 -> x1, local copies, waits for them, and re-layouts: 5.1 us -> 0.65 us  [per_device(): sending = jnp.take(updates, send_index, axis=0, mode='clip')]
    gather x0 -> x1, local copies, waits for them, and re-layouts: none -> 4.36 us  [per_device(): jnp.take(tiles_full.reshape(group_tiles + 1, block_rows, width), send_ind...]
    dot_general x3, matrix products: 3.74 us -> 7.06 us  [per_device(): jnp.dot(tiles_slots, solved_now.astype(jnp.bfloat16), preferred_element_t...]
    unnamed x30 -> x28, local copies, waits for them, and re-layouts: 13.6 us -> 11.9 us
  transfers between devices with their start and end apart: 13 -> 13, of which waited for: 9 -> 9; matrix products, arithmetic and copies ran while one was open for 5% -> 4% of each run, Pallas kernels for 0% -> 0%
where the time goes in v9:
time: 213 us; the launch traced here: 212 us
  waiting for transfers between devices  84.2 us (40%)
  starting transfers between devices  53.3 us (25%)
  local copies, waits for them, and re-layouts  28.1 us (13%)
  other arithmetic  16.1 us (8%)
  matrix products  15.3 us (7%)
  between operations  14.7 us (7%)
    ppermute x6, starting transfers between devices, level0_shift(): return lax.ppermute(x, all_axes, pairs)  31.1 us
    all_to_all x4, waiting for transfers between devices, per_device(): lax.all_to_all(sending, ('lvl', 'pcol'), split_axis=0, concat_axis=0, til...  26.9 us
    all_gather x1, waiting for transfers between devices, per_device(): gathered = lax.all_gather(both, 'prow', axis=0)  20.8 us
    all_to_all x1, waiting for transfers between devices, per_device(): lax.all_to_all(final, 'prow', split_axis=0, concat_axis=0, tiled=True)  19.5 us
    all_to_all x4, starting transfers between devices, per_device(): lax.all_to_all(sending, ('lvl', 'pcol'), split_axis=0, concat_axis=0, til...  14.5 us
    unnamed x28, local copies, waits for them, and re-layouts  11.9 us
    all_to_all x1, waiting for transfers between devices, per_device(): lax.all_to_all(jnp.broadcast_to(meta[None], (devices,) + meta.shape), ('l...  11.7 us
    dot_general x3, matrix products, per_device(): jnp.dot(tiles_slots, solved_now.astype(jnp.bfloat16), preferred_element_t...  7.06 us
  transfers between devices with their start and end apart: 13, of which 9 were waited for; matrix products, arithmetic and copies ran while one was open for 4% of the time, Pallas kernels for 0%

profile of v9, /device:TPU:0, one launch (start us, length us, event | category | flops | bytes accessed | tf_op | source)
XLA Modules:
  0.0 211.7 jit_solution(5048139028083167537)
XLA Ops:
  7.2 0.7 select_reduce_fusion.1
  8.0 0.7 select_reduce_fusion.3
  8.7 0.9 select_reduce_fusion.4
  9.7 1.6 bitcast_select_fusion
  11.3 1.0 pad_maximum_fusion
  12.4 1.1 fusion.47
  13.4 6.9 %collective-permute-start.2 = (bf16[256,256]{1,0:T(8,128)(2,1)S(1)}, bf16[256,256]{1,0:T(8,128)(2,1)S(1)}, u32[]{:S(2)}, u32[]{:S(2)}) collective-permute-start(bf16[256,256]{1,0:T(8,128)(2,1)S(1)} %get-tuple-element.36), channel_id=1, source_target_pairs={{0,6},{1,7},{2,0},{3,1},{4,2},{5,3},{6,4},{7,5}} | collective-permute-start | bytes 393224 | tf_op jit(solution)/shard_map/ppermute | solution.py:69
  20.4 1.9 collective-permute-start.1
  22.3 2.9 %collective-permute-start = (bf16[256,256]{1,0:T(8,128)(2,1)S(1)}, bf16[256,256]{1,0:T(8,128)(2,1)S(1)}, u32[]{:S(2)}, u32[]{:S(2)}) collective-permute-start(bf16[256,256]{1,0:T(8,128)(2,1)S(1)} %get-tuple-element.36), channel_id=1, source_target_pairs={{0,2},{1,3},{2,4},{3,5},{4,6},{5,7},{6,0},{7,1}} | collective-permute-start | bytes 393224 | tf_op jit(solution)/shard_map/ppermute | solution.py:69
  25.3 0.6 broadcast_in_dim.156
  25.9 3.2 %all-to-all-start = ((s32[32,2,8]{2,1,0:T(2,128)}), s32[32,2,8]{2,1,0:T(2,128)S(1)}, u32[]{:S(2)}, u32[]{:S(2)}) async-start(s32[32,2,8]{2,1,0:T(2,128)} %broadcast_in_dim.156), calls=%async_computation | async-start | bytes 65536 | tf_op jit(solution)/shard_map/all_to_all | solution.py:101
  29.3 11.7 %all-to-all-done = s32[32,2,8]{2,1,0:T(2,128)S(1)} async-done(((s32[32,2,8]{2,1,0:T(2,128)}), s32[32,2,8]{2,1,0:T(2,128)S(1)}, u32[]{:S(2)}, u32[]{:S(2)}) %all-to-all-start) | async-done | bytes 2080 | tf_op jit(solution)/shard_map/all_to_all | solution.py:101
  41.2 0.3 convert_reduce_fusion
  42.3 0.6 gather_fusion
  42.9 0.4 convolution_convert_fusion.3
  43.3 14.4 %collective-permute-start.5 = (bf16[256,64]{0,1:T(8,128)(2,1)S(1)}, bf16[256,64]{0,1:T(8,128)(2,1)S(1)}, u32[]{:S(2)}, u32[]{:S(2)}) collective-permute-start(bf16[256,64]{0,1:T(8,128)(2,1)S(1)} %get-tuple-element.27), channel_id=1, source_target_pairs={{0,6},{1,7},{2,0},{3,1},{4,2},{5,3},{6,4},{7,5}} | collective-permute-start | bytes 98312 | tf_op jit(solution)/shard_map/ppermute | solution.py:69
  57.7 1.9 collective-permute-start.4
  59.7 2.9 %collective-permute-start.3 = (bf16[256,64]{0,1:T(8,128)(2,1)S(1)}, bf16[256,64]{0,1:T(8,128)(2,1)S(1)}, u32[]{:S(2)}, u32[]{:S(2)}) collective-permute-start(bf16[256,64]{0,1:T(8,128)(2,1)S(1)} %get-tuple-element.29), channel_id=1, source_target_pairs={{0,2},{1,3},{2,4},{3,5},{4,6},{5,7},{6,0},{7,1}} | collective-permute-start | bytes 98312 | tf_op jit(solution)/shard_map/ppermute | solution.py:69
  62.6 2.8 %collective-permute-done.4 = bf16[256,64]{0,1:T(8,128)(2,1)S(1)} collective-permute-done((bf16[256,64]{0,1:T(8,128)(2,1)S(1)}, bf16[256,64]{0,1:T(8,128)(2,1)S(1)}, u32[]{:S(2)}, u32[]{:S(2)}) %collective-permute-start.4) | collective-permute-done | bytes 32800 | tf_op jit(solution)/shard_map/ppermute | solution.py:69
  65.5 2.5 %collective-permute-done.3 = bf16[256,64]{0,1:T(8,128)(2,1)S(1)} collective-permute-done((bf16[256,64]{0,1:T(8,128)(2,1)S(1)}, bf16[256,64]{0,1:T(8,128)(2,1)S(1)}, u32[]{:S(2)}, u32[]{:S(2)}) %collective-permute-start.3) | collective-permute-done | bytes 32800 | tf_op jit(solution)/shard_map/ppermute | solution.py:69
  68.0 0.6 gather_fusion.1
  68.8 0.7 gather_fusion.2
  69.4 1.1 reshape.611
  70.5 3.4 %all-to-all-start.1 = ((bf16[8,2,8192]{2,1,0:T(2,128)(2,1)}), bf16[8,2,8192]{2,1,0:T(2,128)(2,1)S(1)}, u32[]{:S(2)}, u32[]{:S(2)}) async-start(bf16[8,2,8192]{2,1,0:T(2,128)(2,1)} %reshape.611), calls=%async_computation.1 | async-start | bytes 524288 | tf_op jit(solution)/shard_map/all_to_all | solution.py:172
  74.1 6.8 %all-to-all-done.1 = bf16[8,2,8192]{2,1,0:T(2,128)(2,1)S(1)} async-done(((bf16[8,2,8192]{2,1,0:T(2,128)(2,1)}), bf16[8,2,8192]{2,1,0:T(2,128)(2,1)S(1)}, u32[]{:S(2)}, u32[]{:S(2)}) %all-to-all-start.1) | async-done | bytes 262176 | tf_op jit(solution)/shard_map/all_to_all | solution.py:172
  80.8 0.3 reshape.612
  81.3 1.2 scatter_fusion
  82.5 0.8 slice.100
  83.3 20.8 %all-gather.3.cloned.1.call-done = bf16[2048,1024]{1,0:T(8,128)(2,1)} async-done(((bf16[512,1024]{1,0:T(8,128)(2,1)}), bf16[2048,1024]{1,0:T(8,128)(2,1)}) %all-gather.3.cloned.1.call-update) | async-done | bytes 4194320 | tf_op jit(solution)/shard_map/all_gather | solution.py:54
  104.2 2.7 %fusion.44 = (bf16[4,256,1024]{2,1,0:T(8,128)(2,1)S(1)}, bf16[4,256,1024]{2,1,0:T(8,128)(2,1)S(1)}) fusion(bf16[4,512,1024]{2,1,0:T(8,128)(2,1)} %bitcast.115), kind=kLoop, calls=%fused_computation.119 | loop fusion | bytes 8388608 | tf_op jit(solution)/shard_map/slice | solution.py:55
  106.9 1.5 concatenate.14
  108.4 4.4 %gather_fusion.3 = bf16[64,32,1024]{2,1,0:T(8,128)(2,1)} fusion(bf16[33,32,1024]{2,1,0:T(8,128)(2,1)} %bitcast.113, s32[1024]{0:T(1024)S(1)} %pad_clamp_fusion), kind=kCustom, calls=%fused_computation.3 | custom fusion | bytes 8388864 | tf_op jit(solution)/shard_map/jit(_take)/gather | solution.py:146
  112.7 2.0 fusion.8
  114.8 3.6 %convolution_convert_fusion.2 = bf16[2048,64]{0,1:T(8,128)(2,1)S(1)} fusion(bf16[2048,1024]{1,0:T(8,128)(2,1)} %bitcast.107, f32[1024,64]{0,1:T(8,128)S(1)} %fusion.8), kind=kOutput, calls=%fused_computation.10 | convolution fusion | flops 268632064 | bytes 4718592 | tf_op jit(solution)/shard_map/dot_general | solution.py:159
  118.4 1.0 copy.59
  119.4 2.1 %reshape.613 = bf16[8,2,8192]{2,1,0:T(2,128)(2,1)} reshape(bf16[64,32,64]{2,1,0:T(8,128)(2,1)} %bitcast.118) | data formatting | bytes 524288
  121.5 3.4 %all-to-all-start.2 = ((bf16[8,2,8192]{2,1,0:T(2,128)(2,1)}), bf16[8,2,8192]{2,1,0:T(2,128)(2,1)S(1)}, u32[]{:S(2)}, u32[]{:S(2)}) async-start(bf16[8,2,8192]{2,1,0:T(2,128)(2,1)} %reshape.613), calls=%async_computation.2 | async-start | bytes 524288 | tf_op jit(solution)/shard_map/all_to_all | solution.py:172
  125.0 6.8 %all-to-all-done.2 = bf16[8,2,8192]{2,1,0:T(2,128)(2,1)S(1)} async-done(((bf16[8,2,8192]{2,1,0:T(2,128)(2,1)}), bf16[8,2,8192]{2,1,0:T(2,128)(2,1)S(1)}, u32[]{:S(2)}, u32[]{:S(2)}) %all-to-all-start.2) | async-done | bytes 262176 | tf_op jit(solution)/shard_map/all_to_all | solution.py:172
  131.8 1.2 reshape.614
  132.9 0.9 slice_convert_fusion.2
  133.9 1.2 scatter_fusion.1
  135.1 2.0 fusion.11
  137.2 0.3 copy-done
  137.4 2.1 convolution_convert_fusion.1
  139.5 2.0 copy.60
  141.5 2.1 %reshape.615 = bf16[8,2,8192]{2,1,0:T(2,128)(2,1)} reshape(bf16[64,32,64]{2,1,0:T(8,128)(2,1)} %bitcast.119) | data formatting | bytes 524288
  143.6 4.2 %all-to-all-start.3 = ((bf16[8,2,8192]{2,1,0:T(2,128)(2,1)}), bf16[8,2,8192]{2,1,0:T(2,128)(2,1)}, u32[]{:S(2)}, u32[]{:S(2)}) async-start(bf16[8,2,8192]{2,1,0:T(2,128)(2,1)} %reshape.615), calls=%async_computation.3 | async-start | bytes 524288 | tf_op jit(solution)/shard_map/all_to_all | solution.py:172
  147.9 6.7 %all-to-all-done.3 = bf16[8,2,8192]{2,1,0:T(2,128)(2,1)} async-done(((bf16[8,2,8192]{2,1,0:T(2,128)(2,1)}), bf16[8,2,8192]{2,1,0:T(2,128)(2,1)}, u32[]{:S(2)}, u32[]{:S(2)}) %all-to-all-start.3) | async-done | bytes 262176 | tf_op jit(solution)/shard_map/all_to_all | solution.py:172
  154.6 2.1 %reshape.616 = bf16[64,32,64]{2,1,0:T(8,128)(2,1)} reshape(bf16[8,2,8192]{2,1,0:T(2,128)(2,1)} %all-to-all-done.3) | data formatting | bytes 524288
  156.7 1.6 slice_convert_fusion.1
  158.4 1.9 scatter_fusion.2
  160.4 2.8 %select_select_fusion = (f32[1024,64]{0,1:T(8,128)}, bf16[1024,64]{0,1:T(8,128)(2,1)S(1)}) fusion(f32[1024,64]{0,1:T(8,128)S(1)} %fusion.11, f32[1024,64]{0,1:T(8,128)S(1)} %fusion.8, pred[]{:T(512)S(6)} %eq.207, pred[]{:T(512)S(6)} %eq.206, pred[]{:T(512)S(6)} %eq.181, bf16[1024,1024]{1,0:T(8,128)(2,1)S(1)} %bitcast.112, ...), kind=kOutput, calls=%fused_computation.36 | convolution fusion | flops 134610944 | bytes 3801095 | tf_op jit(solution)/shard_map/dot_general | solution.py:154
  163.1 1.4 convolution_convert_fusion
  164.5 0.3 copy.61
  164.8 1.1 reshape.617
  165.9 3.4 %all-to-all-start.4 = ((bf16[8,2,8192]{2,1,0:T(2,128)(2,1)}), bf16[8,2,8192]{2,1,0:T(2,128)(2,1)S(1)}, u32[]{:S(2)}, u32[]{:S(2)}) async-start(bf16[8,2,8192]{2,1,0:T(2,128)(2,1)} %reshape.617), calls=%async_computation.4 | async-start | bytes 524288 | tf_op jit(solution)/shard_map/all_to_all | solution.py:172
  169.4 6.7 %all-to-all-done.4 = bf16[8,2,8192]{2,1,0:T(2,128)(2,1)S(1)} async-done(((bf16[8,2,8192]{2,1,0:T(2,128)(2,1)}), bf16[8,2,8192]{2,1,0:T(2,128)(2,1)S(1)}, u32[]{:S(2)}, u32[]{:S(2)}) %all-to-all-start.4) | async-done | bytes 262176 | tf_op jit(solution)/shard_map/all_to_all | solution.py:172
  176.2 0.3 reshape.618
  176.5 1.2 scatter_fusion.3
  178.0 0.9 pad_maximum_fusion.1
  178.9 4.5 %all-to-all-start.5 = ((f32[4,768,64]{1,2,0:T(8,128)}), f32[4,768,64]{1,2,0:T(8,128)S(1)}, u32[]{:S(2)}, u32[]{:S(2)}) async-start(f32[4,768,64]{1,2,0:T(8,128)} %pad_maximum_fusion.1), calls=%async_computation.5 | async-start | bytes 1572864 | tf_op jit(solution)/shard_map/all_to_all | solution.py:186
  183.5 19.5 %all-to-all-done.5 = f32[4,768,64]{1,2,0:T(8,128)S(1)} async-done(((f32[4,768,64]{1,2,0:T(8,128)}), f32[4,768,64]{1,2,0:T(8,128)S(1)}, u32[]{:S(2)}, u32[]{:S(2)}) %all-to-all-start.5) | async-done | bytes 786464 | tf_op jit(solution)/shard_map/all_to_all | solution.py:186
  203.1 1.0 copy.65
  204.1 0.7 select_bitcast_fusion
  (76 shorter events, 2.5 us)
Async XLA Ops:
  7.2 97.0 %all-gather.3.cloned.1.call-start = ((), (), s32[]{:S(2)}) async-start(), calls=%async_computation.6 | async-start | bytes 5242880 | tf_op jit(solution)/shard_map/all_gather | solution.py:54
  9.7 2.7 %copy-start.2 = (f32[1,1,1024,256]{3,2,1,0:T(8,128)S(1)}, f32[1,1,1024,256]{3,2,1,0:T(8,128)}, u32[]{:S(2)}) copy-start(f32[1,1,1024,256]{3,2,1,0:T(8,128)} %param.9) | copy-start | bytes 3145732
  9.7 2.7 %copy-start.3 = (bf16[1,1,256,1024]{3,2,1,0:T(8,128)(2,1)S(1)}, bf16[1,1,256,1024]{3,2,1,0:T(8,128)(2,1)}, u32[]{:S(2)}) copy-start(bf16[1,1,256,1024]{3,2,1,0:T(8,128)(2,1)} %param.10) | copy-start | bytes 1572868
  11.2 14.0 %copy-start.7 = (s32[1,1,8]{2,1,0:T(1,128)S(1)}, s32[1,1,8]{2,1,0:T(1,128)}, u32[]{:S(2)}) copy-start(s32[1,1,8]{2,1,0:T(1,128)} %param.14) | copy-start | bytes 100
  11.2 14.0 %copy-start.8 = (s32[1,1,8]{2,1,0:T(1,128)S(1)}, s32[1,1,8]{2,1,0:T(1,128)}, u32[]{:S(2)}) copy-start(s32[1,1,8]{2,1,0:T(1,128)} %param.13) | copy-start | bytes 100
  11.2 18.0 %copy-start.4 = (bf16[1,1,8,32,1024]{4,3,2,1,0:T(8,128)(2,1)S(1)}, bf16[1,1,8,32,1024]{4,3,2,1,0:T(8,128)(2,1)}, u32[]{:S(2)}) copy-start(bf16[1,1,8,32,1024]{4,3,2,1,0:T(8,128)(2,1)} %param.11) | copy-start | bytes 1572868
  13.4 28.8 %collective-permute-start.2 = (bf16[256,256]{1,0:T(8,128)(2,1)S(1)}, bf16[256,256]{1,0:T(8,128)(2,1)S(1)}, u32[]{:S(2)}, u32[]{:S(2)}) collective-permute-start(bf16[256,256]{1,0:T(8,128)(2,1)S(1)} %get-tuple-element.36), channel_id=1, source_target_pairs={{0,6},{1,7},{2,0},{3,1},{4,2},{5,3},{6,4},{7,5}} | collective-permute-start | bytes 393224 | tf_op jit(solution)/shard_map/ppermute | solution.py:69
  20.4 21.9 %collective-permute-start.1 = (bf16[256,256]{1,0:T(8,128)(2,1)S(1)}, bf16[256,256]{1,0:T(8,128)(2,1)S(1)}, u32[]{:S(2)}, u32[]{:S(2)}) collective-permute-start(bf16[256,256]{1,0:T(8,128)(2,1)S(1)} %get-tuple-element.36), channel_id=1, source_target_pairs={{0,4},{1,5},{2,6},{3,7},{4,0},{5,1},{6,2},{7,3}} | collective-permute-start | bytes 393224 | tf_op jit(solution)/shard_map/ppermute | solution.py:69
  22.3 19.9 %collective-permute-start = (bf16[256,256]{1,0:T(8,128)(2,1)S(1)}, bf16[256,256]{1,0:T(8,128)(2,1)S(1)}, u32[]{:S(2)}, u32[]{:S(2)}) collective-permute-start(bf16[256,256]{1,0:T(8,128)(2,1)S(1)} %get-tuple-element.36), channel_id=1, source_target_pairs={{0,2},{1,3},{2,4},{3,5},{4,6},{5,7},{6,0},{7,1}} | collective-permute-start | bytes 393224 | tf_op jit(solution)/shard_map/ppermute | solution.py:69
  25.9 15.1 %all-to-all-start = ((s32[32,2,8]{2,1,0:T(2,128)}), s32[32,2,8]{2,1,0:T(2,128)S(1)}, u32[]{:S(2)}, u32[]{:S(2)}) async-start(s32[32,2,8]{2,1,0:T(2,128)} %broadcast_in_dim.156), calls=%async_computation | async-start | bytes 65536 | tf_op jit(solution)/shard_map/all_to_all | solution.py:101
  43.3 19.3 %collective-permute-start.5 = (bf16[256,64]{0,1:T(8,128)(2,1)S(1)}, bf16[256,64]{0,1:T(8,128)(2,1)S(1)}, u32[]{:S(2)}, u32[]{:S(2)}) collective-permute-start(bf16[256,64]{0,1:T(8,128)(2,1)S(1)} %get-tuple-element.27), channel_id=1, source_target_pairs={{0,6},{1,7},{2,0},{3,1},{4,2},{5,3},{6,4},{7,5}} | collective-permute-start | bytes 98312 | tf_op jit(solution)/shard_map/ppermute | solution.py:69
  57.7 7.7 %collective-permute-start.4 = (bf16[256,64]{0,1:T(8,128)(2,1)S(1)}, bf16[256,64]{0,1:T(8,128)(2,1)S(1)}, u32[]{:S(2)}, u32[]{:S(2)}) collective-permute-start(bf16[256,64]{0,1:T(8,128)(2,1)S(1)} %get-tuple-element.28), channel_id=1, source_target_pairs={{0,4},{1,5},{2,6},{3,7},{4,0},{5,1},{6,2},{7,3}} | collective-permute-start | bytes 98312 | tf_op jit(solution)/shard_map/ppermute | solution.py:69
  59.7 8.3 %collective-permute-start.3 = (bf16[256,64]{0,1:T(8,128)(2,1)S(1)}, bf16[256,64]{0,1:T(8,128)(2,1)S(1)}, u32[]{:S(2)}, u32[]{:S(2)}) collective-permute-start(bf16[256,64]{0,1:T(8,128)(2,1)S(1)} %get-tuple-element.29), channel_id=1, source_target_pairs={{0,2},{1,3},{2,4},{3,5},{4,6},{5,7},{6,0},{7,1}} | collective-permute-start | bytes 98312 | tf_op jit(solution)/shard_map/ppermute | solution.py:69
  70.5 10.3 %all-to-all-start.1 = ((bf16[8,2,8192]{2,1,0:T(2,128)(2,1)}), bf16[8,2,8192]{2,1,0:T(2,128)(2,1)S(1)}, u32[]{:S(2)}, u32[]{:S(2)}) async-start(bf16[8,2,8192]{2,1,0:T(2,128)(2,1)} %reshape.611), calls=%async_computation.1 | async-start | bytes 524288 | tf_op jit(solution)/shard_map/all_to_all | solution.py:172
  121.5 10.3 %all-to-all-start.2 = ((bf16[8,2,8192]{2,1,0:T(2,128)(2,1)}), bf16[8,2,8192]{2,1,0:T(2,128)(2,1)S(1)}, u32[]{:S(2)}, u32[]{:S(2)}) async-start(bf16[8,2,8192]{2,1,0:T(2,128)(2,1)} %reshape.613), calls=%async_computation.2 | async-start | bytes 524288 | tf_op jit(solution)/shard_map/all_to_all | solution.py:172
  135.1 2.3 %copy-start = (bf16[64,32,1024]{2,1,0:T(8,128)(2,1)S(1)}, bf16[64,32,1024]{2,1,0:T(8,128)(2,1)}, u32[]{:S(2)}) copy-start(bf16[64,32,1024]{2,1,0:T(8,128)(2,1)} %gather_fusion.3) | copy-start | bytes 12582916
  143.6 11.0 %all-to-all-start.3 = ((bf16[8,2,8192]{2,1,0:T(2,128)(2,1)}), bf16[8,2,8192]{2,1,0:T(2,128)(2,1)}, u32[]{:S(2)}, u32[]{:S(2)}) async-start(bf16[8,2,8192]{2,1,0:T(2,128)(2,1)} %reshape.615), calls=%async_computation.3 | async-start | bytes 524288 | tf_op jit(solution)/shard_map/all_to_all | solution.py:172
  160.3 2.8 %copy-start.1 = (bf16[64,32,1024]{2,1,0:T(8,128)(2,1)S(1)}, bf16[64,32,1024]{2,1,0:T(8,128)(2,1)}, u32[]{:S(2)}) copy-start(bf16[64,32,1024]{2,1,0:T(8,128)(2,1)} %gather_fusion.3) | copy-start | bytes 12582916
  164.5 4.9 %copy-start.5 = (f32[1024,64]{0,1:T(8,128)S(1)}, f32[1024,64]{0,1:T(8,128)}, u32[]{:S(2)}) copy-start(f32[1024,64]{0,1:T(8,128)} %get-tuple-element.38) | copy-start | bytes 786436
  165.9 10.3 %all-to-all-start.4 = ((bf16[8,2,8192]{2,1,0:T(2,128)(2,1)}), bf16[8,2,8192]{2,1,0:T(2,128)(2,1)S(1)}, u32[]{:S(2)}, u32[]{:S(2)}) async-start(bf16[8,2,8192]{2,1,0:T(2,128)(2,1)} %reshape.617), calls=%async_computation.4 | async-start | bytes 524288 | tf_op jit(solution)/shard_map/all_to_all | solution.py:172
  178.9 25.2 %copy-start.6 = (f32[256,256]{1,0:T(8,128)S(1)}, f32[256,256]{1,0:T(8,128)}, u32[]{:S(2)}) copy-start(f32[256,256]{1,0:T(8,128)} %get-tuple-element.37) | copy-start | bytes 786436
  178.9 24.0 %all-to-all-start.5 = ((f32[4,768,64]{1,2,0:T(8,128)}), f32[4,768,64]{1,2,0:T(8,128)S(1)}, u32[]{:S(2)}, u32[]{:S(2)}) async-start(f32[4,768,64]{1,2,0:T(8,128)} %pad_maximum_fusion.1), calls=%async_computation.5 | async-start | bytes 1572864 | tf_op jit(solution)/shard_map/all_to_all | solution.py:186
Sparse Core Ops, SparseCore 0:
  12.5 91.6 all-gather.2

commit v10 on v8

--- a/solution.py
+++ b/solution.py
@@ -68,6 +68,9 @@
         ]
         return lax.ppermute(x, all_axes, pairs)
 
+    def prow_shift(x, shift):
+        return lax.ppermute(x, "prow", [(p, (p + shift) % n_prow) for p in range(n_prow)])
+
     def by_source(chunks):
         stacked = jnp.stack(chunks)
         order = (row_index - jnp.arange(n_prow, dtype=jnp.int32)) % n_prow
@@ -140,7 +143,11 @@
     window_blocks = width // block_rows
     acc = jnp.zeros((NT + 1, block_rows, cols), jnp.float32)
     solved = jnp.zeros((width, cols), jnp.float32)
+    last = n_lvl - 1
     for section in range(n_lvl):
+        if section == last:
+            partial = acc[window_blocks:NT].reshape(ABOVE, cols)
+            partial = by_source([partial] + [prow_shift(partial, k) for k in range(1, n_prow)])
         if section == 0:
             updates = first_cols
         else:
@@ -158,20 +165,22 @@
             sending, ("lvl", "pcol"), split_axis=0, concat_axis=0, tiled=True
         )
         incoming = incoming.reshape(n_lvl, n_pcol * slots, block_rows, cols)[section]
-        acc = acc.at[recv_block[section]].add(incoming.astype(jnp.float32), mode="clip")
-    outer = acc[window_blocks:NT].reshape(ABOVE, cols)
-
-    final = jnp.concatenate(
-        [
-            solved.reshape(n_prow, rows_out, cols),
-            jnp.broadcast_to(outer[None], (n_prow, ABOVE, cols)),
-        ],
-        axis=1,
-    )
-    final = lax.all_to_all(final, "prow", split_axis=0, concat_axis=0, tiled=True)
-    solution_rows = jnp.transpose(final[:, :rows_out], (1, 0, 2)).reshape(rows_out, columns_all)
+        if section < last:
+            acc = acc.at[recv_block[section]].add(incoming.astype(jnp.float32), mode="clip")
+
+    final = lax.all_to_all(
+        solved.reshape(n_prow, rows_out, cols), "prow", split_axis=0, concat_axis=0, tiled=True
+    )
+    solution_rows = jnp.transpose(final, (1, 0, 2)).reshape(rows_out, columns_all)
     solution_rows = jnp.where(level_index == 0, first_rows, solution_rows)
-    outer_all = jnp.transpose(final[:, rows_out:], (1, 0, 2)).reshape(ABOVE, columns_all)
+    last_slots = by_source([incoming] + [prow_shift(incoming, k) for k in range(1, n_prow)])
+    last_slots = jnp.transpose(last_slots, (1, 2, 0, 3)).reshape(
+        n_pcol * slots, block_rows, columns_all
+    )
+    outer_last = jnp.zeros((NT + 1, block_rows, columns_all), jnp.float32)
+    outer_last = outer_last.at[recv_block[last]].add(last_slots.astype(jnp.float32), mode="clip")
+    outer_all = jnp.transpose(partial, (1, 0, 2)).reshape(ABOVE, columns_all)
+    outer_all = outer_all + outer_last[window_blocks:NT].reshape(ABOVE, columns_all)
     return (solution_rows[None, None], outer_all[None, None])
 
 

time: 210 us -> 212 us (level)
  waiting for transfers between devices: 84.8 us -> 75.7 us
  starting transfers between devices: 52.7 us -> 61.4 us
  local copies, waits for them, and re-layouts: 28.3 us -> 32 us
    all_to_all x1, waiting for transfers between devices: 19.4 us -> 0.01 us  [per_device(): lax.all_to_all(solved.reshape(n_prow, rows_out, cols), 'prow', split_axis...]
    ppermute x0 -> x6, waiting for transfers between devices: none -> 15.1 us  [prow_shift(): lax.ppermute(x, 'prow', [(p, (p + shift) % n_prow) for p in range(n_prow)])]
    ppermute x0 -> x6, starting transfers between devices: none -> 8.84 us  [prow_shift(): lax.ppermute(x, 'prow', [(p, (p + shift) % n_prow) for p in range(n_prow)])]
    all_to_all x4, waiting for transfers between devices: 26.9 us -> 22.1 us  [per_device(): lax.all_to_all(sending, ('lvl', 'pcol'), split_axis=0, concat_axis=0, til...]
    scatter-add x4 -> x3, other arithmetic: 5.59 us -> 4.37 us  [per_device(): acc.at[recv_block[section]].add(incoming.astype(jnp.float32), mode='clip')]
  transfers between devices with their start and end apart: 13 -> 19, of which waited for: 9 -> 11; matrix products, arithmetic and copies ran while one was open for 5% -> 8% of each run, Pallas kernels for 0% -> 0%
where the time goes in v10:
time: 212 us; the launch traced here: 211 us
  waiting for transfers between devices  75.7 us (36%)
  starting transfers between devices  61.4 us (29%)
  local copies, waits for them, and re-layouts  32 us (15%)
  other arithmetic  15.5 us (7%)
  between operations  14.8 us (7%)
  matrix products  11.7 us (6%)
    ppermute x6, starting transfers between devices, level0_shift(): return lax.ppermute(x, all_axes, pairs)  30.5 us
    all_to_all x4, waiting for transfers between devices, per_device(): lax.all_to_all(sending, ('lvl', 'pcol'), split_axis=0, concat_axis=0, til...  22.1 us
    all_gather x1, waiting for transfers between devices, per_device(): gathered = lax.all_gather(both, 'prow', axis=0)  20.8 us
    ppermute x6, waiting for transfers between devices, prow_shift(): lax.ppermute(x, 'prow', [(p, (p + shift) % n_prow) for p in range(n_prow)])  15.1 us
    all_to_all x4, starting transfers between devices, per_device(): lax.all_to_all(sending, ('lvl', 'pcol'), split_axis=0, concat_axis=0, til...  14.5 us
    unnamed x30, local copies, waits for them, and re-layouts  13.6 us
    all_to_all x1, waiting for transfers between devices, per_device(): lax.all_to_all(jnp.broadcast_to(meta[None], (devices,) + meta.shape), ('l...  12.3 us
    ppermute x6, starting transfers between devices, prow_shift(): lax.ppermute(x, 'prow', [(p, (p + shift) % n_prow) for p in range(n_prow)])  8.84 us
  transfers between devices with their start and end apart: 19, of which 11 were waited for; matrix products, arithmetic and copies ran while one was open for 8% of the time, Pallas kernels for 0%

profile of v10, /device:TPU:0, one launch (start us, length us, event | category | flops | bytes accessed | tf_op | source)
XLA Modules:
  0.0 211.2 jit_solution(8079031896620858170)
XLA Ops:
  7.2 0.7 select_reduce_fusion.1
  8.0 0.7 select_reduce_fusion.3
  8.7 0.9 select_reduce_fusion.4
  9.7 1.4 bitcast_select_fusion
  11.1 1.0 pad_maximum_fusion
  12.8 1.1 fusion.53
  13.9 6.9 %collective-permute-start.2 = (bf16[256,256]{1,0:T(8,128)(2,1)S(1)}, bf16[256,256]{1,0:T(8,128)(2,1)S(1)}, u32[]{:S(2)}, u32[]{:S(2)}) collective-permute-start(bf16[256,256]{1,0:T(8,128)(2,1)S(1)} %get-tuple-element.38), channel_id=1, source_target_pairs={{0,6},{1,7},{2,0},{3,1},{4,2},{5,3},{6,4},{7,5}} | collective-permute-start | bytes 393224 | tf_op jit(solution)/shard_map/ppermute | solution.py:69
  20.9 1.9 collective-permute-start.1
  22.8 2.9 %collective-permute-start = (bf16[256,256]{1,0:T(8,128)(2,1)S(1)}, bf16[256,256]{1,0:T(8,128)(2,1)S(1)}, u32[]{:S(2)}, u32[]{:S(2)}) collective-permute-start(bf16[256,256]{1,0:T(8,128)(2,1)S(1)} %get-tuple-element.38), channel_id=1, source_target_pairs={{0,2},{1,3},{2,4},{3,5},{4,6},{5,7},{6,0},{7,1}} | collective-permute-start | bytes 393224 | tf_op jit(solution)/shard_map/ppermute | solution.py:69
  26.4 3.2 %all-to-all-start = ((s32[32,2,8]{2,1,0:T(2,128)}), s32[32,2,8]{2,1,0:T(2,128)S(1)}, u32[]{:S(2)}, u32[]{:S(2)}) async-start(s32[32,2,8]{2,1,0:T(2,128)} %broadcast_in_dim.158), calls=%async_computation | async-start | bytes 65536 | tf_op jit(solution)/shard_map/all_to_all | solution.py:104
  29.8 12.3 %all-to-all-done = s32[32,2,8]{2,1,0:T(2,128)S(1)} async-done(((s32[32,2,8]{2,1,0:T(2,128)}), s32[32,2,8]{2,1,0:T(2,128)S(1)}, u32[]{:S(2)}, u32[]{:S(2)}) %all-to-all-start) | async-done | bytes 2080 | tf_op jit(solution)/shard_map/all_to_all | solution.py:104
  44.4 13.8 %collective-permute-start.5 = (bf16[256,64]{0,1:T(8,128)(2,1)S(1)}, bf16[256,64]{0,1:T(8,128)(2,1)S(1)}, u32[]{:S(2)}, u32[]{:S(2)}) collective-permute-start(bf16[256,64]{0,1:T(8,128)(2,1)S(1)} %get-tuple-element.29), channel_id=1, source_target_pairs={{0,6},{1,7},{2,0},{3,1},{4,2},{5,3},{6,4},{7,5}} | collective-permute-start | bytes 98312 | tf_op jit(solution)/shard_map/ppermute | solution.py:69
  58.2 1.9 collective-permute-start.4
  60.1 2.9 %collective-permute-start.3 = (bf16[256,64]{0,1:T(8,128)(2,1)S(1)}, bf16[256,64]{0,1:T(8,128)(2,1)S(1)}, u32[]{:S(2)}, u32[]{:S(2)}) collective-permute-start(bf16[256,64]{0,1:T(8,128)(2,1)S(1)} %get-tuple-element.31), channel_id=1, source_target_pairs={{0,2},{1,3},{2,4},{3,5},{4,6},{5,7},{6,0},{7,1}} | collective-permute-start | bytes 98312 | tf_op jit(solution)/shard_map/ppermute | solution.py:69
  63.1 2.6 %collective-permute-done.4 = bf16[256,64]{0,1:T(8,128)(2,1)S(1)} collective-permute-done((bf16[256,64]{0,1:T(8,128)(2,1)S(1)}, bf16[256,64]{0,1:T(8,128)(2,1)S(1)}, u32[]{:S(2)}, u32[]{:S(2)}) %collective-permute-start.4) | collective-permute-done | bytes 32800 | tf_op jit(solution)/shard_map/ppermute | solution.py:69
  65.8 2.7 %collective-permute-done.3 = bf16[256,64]{0,1:T(8,128)(2,1)S(1)} collective-permute-done((bf16[256,64]{0,1:T(8,128)(2,1)S(1)}, bf16[256,64]{0,1:T(8,128)(2,1)S(1)}, u32[]{:S(2)}, u32[]{:S(2)}) %collective-permute-start.3) | collective-permute-done | bytes 32800 | tf_op jit(solution)/shard_map/ppermute | solution.py:69
  69.2 0.7 gather_fusion.2
  69.9 1.1 reshape.669
  71.0 3.4 %all-to-all-start.1 = ((bf16[8,2,8192]{2,1,0:T(2,128)(2,1)}), bf16[8,2,8192]{2,1,0:T(2,128)(2,1)S(1)}, u32[]{:S(2)}, u32[]{:S(2)}) async-start(bf16[8,2,8192]{2,1,0:T(2,128)(2,1)} %reshape.669), calls=%async_computation.1 | async-start | bytes 524288 | tf_op jit(solution)/shard_map/all_to_all | solution.py:164
  74.5 6.8 %all-to-all-done.1 = bf16[8,2,8192]{2,1,0:T(2,128)(2,1)S(1)} async-done(((bf16[8,2,8192]{2,1,0:T(2,128)(2,1)}), bf16[8,2,8192]{2,1,0:T(2,128)(2,1)S(1)}, u32[]{:S(2)}, u32[]{:S(2)}) %all-to-all-start.1) | async-done | bytes 262176 | tf_op jit(solution)/shard_map/all_to_all | solution.py:164
  81.8 1.2 scatter_fusion
  83.0 0.8 slice.107
  83.8 20.8 %all-gather.3.cloned.1.call-done = bf16[2048,1024]{1,0:T(8,128)(2,1)} async-done(((bf16[512,1024]{1,0:T(8,128)(2,1)}), bf16[2048,1024]{1,0:T(8,128)(2,1)}) %all-gather.3.cloned.1.call-update) | async-done | bytes 4194320 | tf_op jit(solution)/shard_map/all_gather | solution.py:54
  104.7 2.8 %fusion.50 = (bf16[4,256,1024]{2,1,0:T(8,128)(2,1)S(1)}, bf16[4,256,1024]{2,1,0:T(8,128)(2,1)S(1)}) fusion(bf16[4,512,1024]{2,1,0:T(8,128)(2,1)} %bitcast.121), kind=kLoop, calls=%fused_computation.131 | loop fusion | bytes 8388608 | tf_op jit(solution)/shard_map/slice | solution.py:56
  107.5 1.3 copy-done
  108.8 0.8 fusion.11
  109.7 1.5 convolution_convert_fusion.2
  111.1 1.1 copy.79
  112.2 1.4 gather_fusion.3
  113.6 2.1 %reshape.671 = bf16[8,2,8192]{2,1,0:T(2,128)(2,1)} reshape(bf16[64,32,64]{2,1,0:T(8,128)(2,1)} %gather_fusion.3) | data formatting | bytes 524288
  115.8 3.4 %all-to-all-start.2 = ((bf16[8,2,8192]{2,1,0:T(2,128)(2,1)}), bf16[8,2,8192]{2,1,0:T(2,128)(2,1)S(1)}, u32[]{:S(2)}, u32[]{:S(2)}) async-start(bf16[8,2,8192]{2,1,0:T(2,128)(2,1)} %reshape.671), calls=%async_computation.2 | async-start | bytes 524288 | tf_op jit(solution)/shard_map/all_to_all | solution.py:164
  119.3 6.8 %all-to-all-done.2 = bf16[8,2,8192]{2,1,0:T(2,128)(2,1)S(1)} async-done(((bf16[8,2,8192]{2,1,0:T(2,128)(2,1)}), bf16[8,2,8192]{2,1,0:T(2,128)(2,1)S(1)}, u32[]{:S(2)}, u32[]{:S(2)}) %all-to-all-start.2) | async-done | bytes 262176 | tf_op jit(solution)/shard_map/all_to_all | solution.py:164
  126.1 1.2 reshape.672
  127.2 0.9 slice_convert_fusion.1
  128.1 1.2 scatter_fusion.1
  129.4 2.5 %fusion.14 = f32[1024,64]{0,1:T(8,128)S(1)} fusion(bf16[1024,1024]{1,0:T(8,128)(2,1)} %bitcast.118, f32[1,1,1024,64]{3,2,1,0:T(8,128)S(1)} %bitcast.133, f32[1,1,1024,256]{3,2,1,0:T(8,128)} %param.9, s32[]{:T(128)S(6)} %select_n.237), kind=kOutput, calls=%fused_computation.40 | convolution fusion | flops 134348800 | bytes 3145732 | tf_op jit(solution)/shard_map/dot_general | solution.py:155
  131.9 1.5 convolution_convert_fusion.1
  133.4 1.8 copy.80
  135.2 2.4 %gather_fusion.4 = bf16[64,32,64]{2,1,0:T(8,128)(2,1)} fusion(bf16[33,32,64]{2,1,0:T(8,128)(2,1)} %bitcast.127, s32[1024]{0:T(1024)S(1)} %pad_clamp_fusion), kind=kCustom, calls=%fused_computation.4 | custom fusion | bytes 524544 | tf_op jit(solution)/shard_map/jit(_take)/gather | solution.py:163
  137.5 2.1 %reshape.673 = bf16[8,2,8192]{2,1,0:T(2,128)(2,1)} reshape(bf16[64,32,64]{2,1,0:T(8,128)(2,1)} %gather_fusion.4) | data formatting | bytes 524288
  139.7 4.2 %all-to-all-start.3 = ((bf16[8,2,8192]{2,1,0:T(2,128)(2,1)}), bf16[8,2,8192]{2,1,0:T(2,128)(2,1)}, u32[]{:S(2)}, u32[]{:S(2)}) async-start(bf16[8,2,8192]{2,1,0:T(2,128)(2,1)} %reshape.673), calls=%async_computation.3 | async-start | bytes 524288 | tf_op jit(solution)/shard_map/all_to_all | solution.py:164
  144.0 6.7 %all-to-all-done.3 = bf16[8,2,8192]{2,1,0:T(2,128)(2,1)} async-done(((bf16[8,2,8192]{2,1,0:T(2,128)(2,1)}), bf16[8,2,8192]{2,1,0:T(2,128)(2,1)}, u32[]{:S(2)}, u32[]{:S(2)}) %all-to-all-start.3) | async-done | bytes 262176 | tf_op jit(solution)/shard_map/all_to_all | solution.py:164
  150.7 2.1 %reshape.674 = bf16[64,32,64]{2,1,0:T(8,128)(2,1)} reshape(bf16[8,2,8192]{2,1,0:T(2,128)(2,1)} %all-to-all-done.3) | data formatting | bytes 524288
  152.8 1.6 slice_convert_fusion
  154.4 1.9 scatter_fusion.2
  156.4 3.2 %select_select_fusion = (f32[1024,64]{0,1:T(8,128)}, bf16[1024,64]{0,1:T(8,128)(2,1)S(1)}) fusion(f32[1024,64]{0,1:T(8,128)S(1)} %fusion.14, f32[1024,64]{0,1:T(8,128)S(1)} %fusion.11, pred[]{:T(512)S(6)} %eq.209, pred[]{:T(512)S(6)} %eq.208, pred[]{:T(512)S(6)} %eq.183, bf16[1024,1024]{1,0:T(8,128)(2,1)} %bitcast.119, ...), kind=kOutput, calls=%fused_computation.45 | convolution fusion | flops 134610944 | bytes 3801095 | tf_op jit(solution)/shard_map/dot_general | solution.py:155
  159.7 0.8 convolution_convert_fusion
  160.7 0.7 gather_fusion.6
  161.3 1.1 reshape.675
  162.4 3.4 %all-to-all-start.5 = ((bf16[8,2,8192]{2,1,0:T(2,128)(2,1)}), bf16[8,2,8192]{2,1,0:T(2,128)(2,1)S(1)}, u32[]{:S(2)}, u32[]{:S(2)}) async-start(bf16[8,2,8192]{2,1,0:T(2,128)(2,1)} %reshape.675), calls=%async_computation.5 | async-start | bytes 524288 | tf_op jit(solution)/shard_map/all_to_all | solution.py:164
  166.1 3.2 %collective-permute-start.8 = (f32[512,64]{0,1:T(8,128)S(1)}, f32[512,64]{0,1:T(8,128)S(1)}, u32[]{:S(2)}, u32[]{:S(2)}) collective-permute-start(f32[512,64]{0,1:T(8,128)S(1)} %copy.83), channel_id=1, source_target_pairs={{0,6},{2,0},{4,2},{6,4},{1,7},{3,1},{5,3},{7,5},{8,14},{10,8},{12,... | collective-permute-start | bytes 393224 | tf_op jit(solution)/shard_map/ppermute | solution.py:72
  169.9 0.7 copy.96
  170.8 1.9 all-to-all-done.5
  172.7 4.4 %all-to-all-start.4 = ((f32[4,256,64]{1,2,0:T(8,128)}), f32[4,256,64]{1,2,0:T(8,128)S(1)}, u32[]{:S(2)}, u32[]{:S(2)}) async-start(f32[4,256,64]{1,2,0:T(8,128)} %bitcast.113), calls=%async_computation.4 | async-start | bytes 524288 | tf_op jit(solution)/shard_map/all_to_all | solution.py:171
  177.5 3.9 %collective-permute-start.11 = (bf16[16,32,64]{2,1,0:T(8,128)(2,1)S(1)}, bf16[16,32,64]{2,1,0:T(8,128)(2,1)S(1)}, u32[]{:S(2)}, u32[]{:S(2)}) collective-permute-start(bf16[16,32,64]{2,1,0:T(8,128)(2,1)S(1)} %get-tuple-element.27), channel_id=1, source_target_pairs={{0,6},{2,0},{4,2},{6,4},{1,7},{3,1},{5,3},{7,5},{8,14},{10,8},{12,... | collective-permute-start | bytes 196616 | tf_op jit(solution)/shard_map/ppermute | solution.py:72
  181.4 1.1 collective-permute-start.9
  182.5 1.3 collective-permute-done.7
  184.5 3.6 %collective-permute-done.11 = bf16[16,32,64]{2,1,0:T(8,128)(2,1)S(1)} collective-permute-done((bf16[16,32,64]{2,1,0:T(8,128)(2,1)S(1)}, bf16[16,32,64]{2,1,0:T(8,128)(2,1)S(1)}, u32[]{:S(2)}, u32[]{:S(2)}) %collective-permute-start.11) | collective-permute-done | bytes 65568 | tf_op jit(solution)/shard_map/ppermute | solution.py:72
  188.0 10.2 %collective-permute-done.10 = bf16[16,32,64]{2,1,0:T(8,128)(2,1)S(1)} collective-permute-done((bf16[16,32,64]{2,1,0:T(8,128)(2,1)S(1)}, bf16[16,32,64]{2,1,0:T(8,128)(2,1)S(1)}, u32[]{:S(2)}, u32[]{:S(2)}) %collective-permute-start.10) | collective-permute-done | bytes 65568 | tf_op jit(solution)/shard_map/ppermute | solution.py:72
  198.4 0.6 gather_fusion.7
  199.2 0.7 copy.88
  200.7 1.3 scatter_fusion.3
  202.4 1.0 copy.90
  203.6 0.7 select_bitcast_fusion
  (99 shorter events, 9.1 us)
Async XLA Ops:
  7.2 97.5 %all-gather.3.cloned.1.call-start = ((), (), s32[]{:S(2)}) async-start(), calls=%async_computation.6 | async-start | bytes 5242880 | tf_op jit(solution)/shard_map/all_gather | solution.py:54
  11.1 1.6 copy-start.1
  11.1 1.7 copy-start.3
  11.1 14.6 %copy-start.8 = (s32[1,1,8]{2,1,0:T(1,128)S(1)}, s32[1,1,8]{2,1,0:T(1,128)}, u32[]{:S(2)}) copy-start(s32[1,1,8]{2,1,0:T(1,128)} %param.14) | copy-start | bytes 100
  11.1 14.6 %copy-start.9 = (s32[1,1,8]{2,1,0:T(1,128)S(1)}, s32[1,1,8]{2,1,0:T(1,128)}, u32[]{:S(2)}) copy-start(s32[1,1,8]{2,1,0:T(1,128)} %param.13) | copy-start | bytes 100
  12.2 17.5 %copy-start.4 = (bf16[1,1,8,32,1024]{4,3,2,1,0:T(8,128)(2,1)S(1)}, bf16[1,1,8,32,1024]{4,3,2,1,0:T(8,128)(2,1)}, u32[]{:S(2)}) copy-start(bf16[1,1,8,32,1024]{4,3,2,1,0:T(8,128)(2,1)} %param.11) | copy-start | bytes 1572868
  13.9 29.4 %collective-permute-start.2 = (bf16[256,256]{1,0:T(8,128)(2,1)S(1)}, bf16[256,256]{1,0:T(8,128)(2,1)S(1)}, u32[]{:S(2)}, u32[]{:S(2)}) collective-permute-start(bf16[256,256]{1,0:T(8,128)(2,1)S(1)} %get-tuple-element.38), channel_id=1, source_target_pairs={{0,6},{1,7},{2,0},{3,1},{4,2},{5,3},{6,4},{7,5}} | collective-permute-start | bytes 393224 | tf_op jit(solution)/shard_map/ppermute | solution.py:69
  20.9 22.5 %collective-permute-start.1 = (bf16[256,256]{1,0:T(8,128)(2,1)S(1)}, bf16[256,256]{1,0:T(8,128)(2,1)S(1)}, u32[]{:S(2)}, u32[]{:S(2)}) collective-permute-start(bf16[256,256]{1,0:T(8,128)(2,1)S(1)} %get-tuple-element.38), channel_id=1, source_target_pairs={{0,4},{1,5},{2,6},{3,7},{4,0},{5,1},{6,2},{7,3}} | collective-permute-start | bytes 393224 | tf_op jit(solution)/shard_map/ppermute | solution.py:69
  22.8 20.5 %collective-permute-start = (bf16[256,256]{1,0:T(8,128)(2,1)S(1)}, bf16[256,256]{1,0:T(8,128)(2,1)S(1)}, u32[]{:S(2)}, u32[]{:S(2)}) collective-permute-start(bf16[256,256]{1,0:T(8,128)(2,1)S(1)} %get-tuple-element.38), channel_id=1, source_target_pairs={{0,2},{1,3},{2,4},{3,5},{4,6},{5,7},{6,0},{7,1}} | collective-permute-start | bytes 393224 | tf_op jit(solution)/shard_map/ppermute | solution.py:69
  26.4 15.7 %all-to-all-start = ((s32[32,2,8]{2,1,0:T(2,128)}), s32[32,2,8]{2,1,0:T(2,128)S(1)}, u32[]{:S(2)}, u32[]{:S(2)}) async-start(s32[32,2,8]{2,1,0:T(2,128)} %broadcast_in_dim.158), calls=%async_computation | async-start | bytes 65536 | tf_op jit(solution)/shard_map/all_to_all | solution.py:104
  44.4 18.7 %collective-permute-start.5 = (bf16[256,64]{0,1:T(8,128)(2,1)S(1)}, bf16[256,64]{0,1:T(8,128)(2,1)S(1)}, u32[]{:S(2)}, u32[]{:S(2)}) collective-permute-start(bf16[256,64]{0,1:T(8,128)(2,1)S(1)} %get-tuple-element.29), channel_id=1, source_target_pairs={{0,6},{1,7},{2,0},{3,1},{4,2},{5,3},{6,4},{7,5}} | collective-permute-start | bytes 98312 | tf_op jit(solution)/shard_map/ppermute | solution.py:69
  58.2 7.6 %collective-permute-start.4 = (bf16[256,64]{0,1:T(8,128)(2,1)S(1)}, bf16[256,64]{0,1:T(8,128)(2,1)S(1)}, u32[]{:S(2)}, u32[]{:S(2)}) collective-permute-start(bf16[256,64]{0,1:T(8,128)(2,1)S(1)} %get-tuple-element.30), channel_id=1, source_target_pairs={{0,4},{1,5},{2,6},{3,7},{4,0},{5,1},{6,2},{7,3}} | collective-permute-start | bytes 98312 | tf_op jit(solution)/shard_map/ppermute | solution.py:69
  60.1 8.3 %collective-permute-start.3 = (bf16[256,64]{0,1:T(8,128)(2,1)S(1)}, bf16[256,64]{0,1:T(8,128)(2,1)S(1)}, u32[]{:S(2)}, u32[]{:S(2)}) collective-permute-start(bf16[256,64]{0,1:T(8,128)(2,1)S(1)} %get-tuple-element.31), channel_id=1, source_target_pairs={{0,2},{1,3},{2,4},{3,5},{4,6},{5,7},{6,0},{7,1}} | collective-permute-start | bytes 98312 | tf_op jit(solution)/shard_map/ppermute | solution.py:69
  71.0 10.3 %all-to-all-start.1 = ((bf16[8,2,8192]{2,1,0:T(2,128)(2,1)}), bf16[8,2,8192]{2,1,0:T(2,128)(2,1)S(1)}, u32[]{:S(2)}, u32[]{:S(2)}) async-start(bf16[8,2,8192]{2,1,0:T(2,128)(2,1)} %reshape.669), calls=%async_computation.1 | async-start | bytes 524288 | tf_op jit(solution)/shard_map/all_to_all | solution.py:164
  104.7 4.2 %copy-start.2 = (f32[1,1,1024,256]{3,2,1,0:T(8,128)S(1)}, f32[1,1,1024,256]{3,2,1,0:T(8,128)}, u32[]{:S(2)}) copy-start(f32[1,1,1024,256]{3,2,1,0:T(8,128)} %param.9) | copy-start | bytes 3145732
  104.7 4.2 %copy-start.5 = (f32[32,32,64]{2,1,0:T(8,128)S(1)}, f32[32,32,64]{2,1,0:T(8,128)}, u32[]{:S(2)}) copy-start(f32[32,32,64]{2,1,0:T(8,128)} %slice.107) | copy-start | bytes 786436
  107.5 1.3 copy-start
  115.8 10.3 %all-to-all-start.2 = ((bf16[8,2,8192]{2,1,0:T(2,128)(2,1)}), bf16[8,2,8192]{2,1,0:T(2,128)(2,1)S(1)}, u32[]{:S(2)}, u32[]{:S(2)}) async-start(bf16[8,2,8192]{2,1,0:T(2,128)(2,1)} %reshape.671), calls=%async_computation.2 | async-start | bytes 524288 | tf_op jit(solution)/shard_map/all_to_all | solution.py:164
  139.7 11.0 %all-to-all-start.3 = ((bf16[8,2,8192]{2,1,0:T(2,128)(2,1)}), bf16[8,2,8192]{2,1,0:T(2,128)(2,1)}, u32[]{:S(2)}, u32[]{:S(2)}) async-start(bf16[8,2,8192]{2,1,0:T(2,128)(2,1)} %reshape.673), calls=%async_computation.3 | async-start | bytes 524288 | tf_op jit(solution)/shard_map/all_to_all | solution.py:164
  160.5 9.5 %copy-start.6 = (f32[1024,64]{0,1:T(8,128)S(1)}, f32[1024,64]{0,1:T(8,128)}, u32[]{:S(2)}) copy-start(f32[1024,64]{0,1:T(8,128)} %get-tuple-element.40) | copy-start | bytes 786436
  162.4 10.3 %all-to-all-start.5 = ((bf16[8,2,8192]{2,1,0:T(2,128)(2,1)}), bf16[8,2,8192]{2,1,0:T(2,128)(2,1)S(1)}, u32[]{:S(2)}, u32[]{:S(2)}) async-start(bf16[8,2,8192]{2,1,0:T(2,128)(2,1)} %reshape.675), calls=%async_computation.5 | async-start | bytes 524288 | tf_op jit(solution)/shard_map/all_to_all | solution.py:164
  166.1 15.3 %collective-permute-start.8 = (f32[512,64]{0,1:T(8,128)S(1)}, f32[512,64]{0,1:T(8,128)S(1)}, u32[]{:S(2)}, u32[]{:S(2)}) collective-permute-start(f32[512,64]{0,1:T(8,128)S(1)} %copy.83), channel_id=1, source_target_pairs={{0,6},{2,0},{4,2},{6,4},{1,7},{3,1},{5,3},{7,5},{8,14},{10,8},{12,... | collective-permute-start | bytes 393224 | tf_op jit(solution)/shard_map/ppermute | solution.py:72
  169.3 14.5 %collective-permute-start.7 = (f32[512,64]{0,1:T(8,128)S(1)}, f32[512,64]{0,1:T(8,128)S(1)}, u32[]{:S(2)}, u32[]{:S(2)}) collective-permute-start(f32[512,64]{0,1:T(8,128)S(1)} %copy.83), channel_id=1, source_target_pairs={{0,4},{2,6},{4,0},{6,2},{1,5},{3,7},{5,1},{7,3},{8,12},{10,14},{12... | collective-permute-start | bytes 393224 | tf_op jit(solution)/shard_map/ppermute | solution.py:72
  169.3 14.5 %collective-permute-start.6 = (f32[512,64]{0,1:T(8,128)S(1)}, f32[512,64]{0,1:T(8,128)S(1)}, u32[]{:S(2)}, u32[]{:S(2)}) collective-permute-start(f32[512,64]{0,1:T(8,128)S(1)} %copy.83), channel_id=1, source_target_pairs={{0,2},{2,4},{4,6},{6,0},{1,3},{3,5},{5,7},{7,1},{8,10},{10,12},{12... | collective-permute-start | bytes 393224 | tf_op jit(solution)/shard_map/ppermute | solution.py:72
  172.7 30.7 %all-to-all-start.4 = ((f32[4,256,64]{1,2,0:T(8,128)}), f32[4,256,64]{1,2,0:T(8,128)S(1)}, u32[]{:S(2)}, u32[]{:S(2)}) async-start(f32[4,256,64]{1,2,0:T(8,128)} %bitcast.113), calls=%async_computation.4 | async-start | bytes 524288 | tf_op jit(solution)/shard_map/all_to_all | solution.py:171
  177.5 10.5 %collective-permute-start.11 = (bf16[16,32,64]{2,1,0:T(8,128)(2,1)S(1)}, bf16[16,32,64]{2,1,0:T(8,128)(2,1)S(1)}, u32[]{:S(2)}, u32[]{:S(2)}) collective-permute-start(bf16[16,32,64]{2,1,0:T(8,128)(2,1)S(1)} %get-tuple-element.27), channel_id=1, source_target_pairs={{0,6},{2,0},{4,2},{6,4},{1,7},{3,1},{5,3},{7,5},{8,14},{10,8},{12,... | collective-permute-start | bytes 196616 | tf_op jit(solution)/shard_map/ppermute | solution.py:72
  181.4 16.8 %collective-permute-start.10 = (bf16[16,32,64]{2,1,0:T(8,128)(2,1)S(1)}, bf16[16,32,64]{2,1,0:T(8,128)(2,1)S(1)}, u32[]{:S(2)}, u32[]{:S(2)}) collective-permute-start(bf16[16,32,64]{2,1,0:T(8,128)(2,1)S(1)} %get-tuple-element.27), channel_id=1, source_target_pairs={{0,4},{2,6},{4,0},{6,2},{1,5},{3,7},{5,1},{7,3},{8,12},{10,14},{12... | collective-permute-start | bytes 196616 | tf_op jit(solution)/shard_map/ppermute | solution.py:72
  181.4 16.8 %collective-permute-start.9 = (bf16[16,32,64]{2,1,0:T(8,128)(2,1)S(1)}, bf16[16,32,64]{2,1,0:T(8,128)(2,1)S(1)}, u32[]{:S(2)}, u32[]{:S(2)}) collective-permute-start(bf16[16,32,64]{2,1,0:T(8,128)(2,1)S(1)} %get-tuple-element.27), channel_id=1, source_target_pairs={{0,2},{2,4},{4,6},{6,0},{1,3},{3,5},{5,7},{7,1},{8,10},{10,12},{12... | collective-permute-start | bytes 196616 | tf_op jit(solution)/shard_map/ppermute | solution.py:72
  202.1 1.4 copy-start.7
Sparse Core Ops, SparseCore 0:
  12.3 92.2 all-gather.2

commit v11 on v8

--- a/solution.py
+++ b/solution.py
@@ -51,7 +51,20 @@
     ).reshape(tile_count * block_rows, width)
 
     both = jnp.concatenate([inverse, tiles_used], axis=0)
-    gathered = lax.all_gather(both, "prow", axis=0)
+    if both.size * 2 <= (2 << 20):
+        to_right = [(p, p + 1) for p in range(n_prow - 1)]
+        to_left = [(p + 1, p) for p in range(n_prow - 1)]
+        chunks = [both]
+        from_left = from_right = both
+        for _ in range(n_prow - 1):
+            from_left = lax.ppermute(from_left, "prow", to_right)
+            from_right = lax.ppermute(from_right, "prow", to_left)
+            chunks += [from_left, from_right]
+        offsets = jnp.arange(n_prow, dtype=jnp.int32) - row_index
+        chunk_of = jnp.where(offsets < 0, -2 * offsets - 1, 2 * offsets)
+        gathered = jnp.take(jnp.stack(chunks), chunk_of, axis=0, mode="clip")
+    else:
+        gathered = lax.all_gather(both, "prow", axis=0)
     inv_full = gathered[:, :row_count].reshape(n_prow * row_count, width)
     tiles_full = gathered[:, row_count:].reshape(group_tiles * block_rows, width)
     tiles_full = jnp.concatenate(

time: 210 us -> 232 us (1.10)
  waiting for transfers between devices: 84.8 us -> 99.5 us
  local copies, waits for them, and re-layouts: 28.3 us -> 42.6 us
  between operations: 14.7 us -> 1.32 us
  starting transfers between devices: 52.7 us -> 58.4 us
    all_gather x1 -> x0, waiting for transfers between devices: 20.8 us -> none  [per_device(): gathered = lax.all_gather(both, 'prow', axis=0)]
    ppermute x0 -> x6, waiting for transfers between devices: none -> 19.1 us  [the longest x3 13.7 us: per_device(): from_left = lax.ppermute(from_left, 'prow', to_right)]
    ppermute x0 -> x6, starting transfers between devices: none -> 16.2 us  [the longest x3 12.3 us: per_device(): from_left = lax.ppermute(from_left, 'prow', to_right)]
    ppermute x6, starting transfers between devices: 30.5 us -> 20.8 us  [level0_shift(): return lax.ppermute(x, all_axes, pairs)]
    ppermute x6, waiting for transfers between devices: 5.32 us -> 13.6 us  [level0_shift(): return lax.ppermute(x, all_axes, pairs)]
    all_to_all x1, waiting for transfers between devices: 12.3 us -> 20.4 us  [per_device(): lax.all_to_all(jnp.broadcast_to(meta[None], (devices,) + meta.shape), ('l...]
    unnamed x30 -> x35, local copies, waits for them, and re-layouts: 13.6 us -> 20.8 us
    gather x0 -> x1, local copies, waits for them, and re-layouts: none -> 5.98 us  [per_device(): gathered = jnp.take(jnp.stack(chunks), chunk_of, axis=0, mode='clip')]
  transfers between devices with their start and end apart: 13 -> 18, of which waited for: 9 -> 11; matrix products, arithmetic and copies ran while one was open for 5% -> 8% of each run, Pallas kernels for 0% -> 0%
where the time goes in v11:
time: 232 us; the launch traced here: 231 us
  waiting for transfers between devices  99.5 us (43%)
  starting transfers between devices  58.4 us (25%)
  local copies, waits for them, and re-layouts  42.6 us (18%)
  other arithmetic  17.1 us (7%)
  matrix products  11.7 us (5%)
    all_to_all x4, waiting for transfers between devices, per_device(): lax.all_to_all(sending, ('lvl', 'pcol'), split_axis=0, concat_axis=0, til...  26.9 us
    ppermute x6, starting transfers between devices, level0_shift(): return lax.ppermute(x, all_axes, pairs)  20.8 us
    unnamed x35, local copies, waits for them, and re-layouts  20.8 us
    all_to_all x1, waiting for transfers between devices, per_device(): lax.all_to_all(jnp.broadcast_to(meta[None], (devices,) + meta.shape), ('l...  20.4 us
    all_to_all x1, waiting for transfers between devices, per_device(): lax.all_to_all(final, 'prow', split_axis=0, concat_axis=0, tiled=True)  19.4 us
    all_to_all x4, starting transfers between devices, per_device(): lax.all_to_all(sending, ('lvl', 'pcol'), split_axis=0, concat_axis=0, til...  14.5 us
    ppermute x3, waiting for transfers between devices, per_device(): from_left = lax.ppermute(from_left, 'prow', to_right)  13.7 us
    ppermute x6, waiting for transfers between devices, level0_shift(): return lax.ppermute(x, all_axes, pairs)  13.6 us
  transfers between devices with their start and end apart: 18, of which 11 were waited for; matrix products, arithmetic and copies ran while one was open for 8% of the time, Pallas kernels for 0%

profile of v11, /device:TPU:0, one launch (start us, length us, event | category | flops | bytes accessed | tf_op | source)
XLA Modules:
  0.0 230.7 jit_solution(734358128078524764)
XLA Ops:
  0.7 0.8 select_reduce_fusion.3
  2.3 0.9 select_reduce_fusion.4
  3.2 1.4 bitcast_select_fusion
  4.7 1.0 pad_maximum_fusion
  5.7 6.1 %collective-permute-start = (bf16[512,1024]{1,0:T(8,128)(2,1)}, bf16[512,1024]{1,0:T(8,128)(2,1)}, u32[]{:S(2)}, u32[]{:S(2)}) collective-permute-start(bf16[512,1024]{1,0:T(8,128)(2,1)} %pad_maximum_fusion), channel_id=1, source_target_pairs={{0,2},{2,4},{4,6},{1,3},{3,5},{5,7},{8,10},{10,12},{12,14},{9,11},... | collective-permute-start | bytes 3145736 | tf_op jit(solution)/shard_map/ppermute | solution.py:60
  11.8 1.3 collective-permute-start.1
  13.1 1.1 fusion.54
  14.2 4.5 %collective-permute-start.6 = (bf16[256,256]{1,0:T(8,128)(2,1)S(1)}, bf16[256,256]{1,0:T(8,128)(2,1)S(1)}, u32[]{:S(2)}, u32[]{:S(2)}) collective-permute-start(bf16[256,256]{1,0:T(8,128)(2,1)S(1)} %get-tuple-element.36), channel_id=1, source_target_pairs={{0,2},{1,3},{2,4},{3,5},{4,6},{5,7},{6,0},{7,1}} | collective-permute-start | bytes 393224 | tf_op jit(solution)/shard_map/ppermute | solution.py:82
  18.7 4.5 %collective-permute-start.7 = (bf16[256,256]{1,0:T(8,128)(2,1)S(1)}, bf16[256,256]{1,0:T(8,128)(2,1)S(1)}, u32[]{:S(2)}, u32[]{:S(2)}) collective-permute-start(bf16[256,256]{1,0:T(8,128)(2,1)S(1)} %get-tuple-element.36), channel_id=1, source_target_pairs={{0,4},{1,5},{2,6},{3,7},{4,0},{5,1},{6,2},{7,3}} | collective-permute-start | bytes 393224 | tf_op jit(solution)/shard_map/ppermute | solution.py:82
  23.2 2.3 collective-permute-start.8
  26.1 2.6 %all-to-all-start = ((s32[32,2,8]{2,1,0:T(2,128)}), s32[32,2,8]{2,1,0:T(2,128)S(1)}, u32[]{:S(2)}, u32[]{:S(2)}) async-start(s32[32,2,8]{2,1,0:T(2,128)} %broadcast_in_dim.159), calls=%async_computation | async-start | bytes 65536 | tf_op jit(solution)/shard_map/all_to_all | solution.py:114
  28.7 1.0 bitcast_dynamic-update-slice_fusion.6
  30.0 20.4 %all-to-all-done = s32[32,2,8]{2,1,0:T(2,128)S(1)} async-done(((s32[32,2,8]{2,1,0:T(2,128)}), s32[32,2,8]{2,1,0:T(2,128)S(1)}, u32[]{:S(2)}, u32[]{:S(2)}) %all-to-all-start) | async-done | bytes 2080 | tf_op jit(solution)/shard_map/all_to_all | solution.py:114
  52.3 2.5 %collective-permute-start.2 = (bf16[512,1024]{1,0:T(8,128)(2,1)}, bf16[512,1024]{1,0:T(8,128)(2,1)S(1)}, u32[]{:S(2)}, u32[]{:S(2)}) collective-permute-start(bf16[512,1024]{1,0:T(8,128)(2,1)} %collective-permute-done), channel_id=1, source_target_pairs={{0,2},{2,4},{4,6},{1,3},{3,5},{5,7},{8,10},{10,12},{12,14},{9,11},... | collective-permute-start | bytes 3145736 | tf_op jit(solution)/shard_map/ppermute | solution.py:60
  55.2 1.9 collective-permute-start.9
  57.1 1.9 collective-permute-start.10
  59.0 5.7 %collective-permute-start.11 = (bf16[256,64]{0,1:T(8,128)(2,1)S(1)}, bf16[256,64]{0,1:T(8,128)(2,1)S(1)}, u32[]{:S(2)}, u32[]{:S(2)}) collective-permute-start(bf16[256,64]{0,1:T(8,128)(2,1)S(1)} %get-tuple-element.27), channel_id=1, source_target_pairs={{0,6},{1,7},{2,0},{3,1},{4,2},{5,3},{6,4},{7,5}} | collective-permute-start | bytes 98312 | tf_op jit(solution)/shard_map/ppermute | solution.py:82
  64.8 1.3 collective-permute-start.3
  66.1 12.9 %collective-permute-done.9 = bf16[256,64]{0,1:T(8,128)(2,1)S(1)} collective-permute-done((bf16[256,64]{0,1:T(8,128)(2,1)S(1)}, bf16[256,64]{0,1:T(8,128)(2,1)S(1)}, u32[]{:S(2)}, u32[]{:S(2)}) %collective-permute-start.9) | collective-permute-done | bytes 32800 | tf_op jit(solution)/shard_map/ppermute | solution.py:82
  81.2 1.1 reshape.650
  82.3 3.4 %all-to-all-start.1 = ((bf16[8,2,8192]{2,1,0:T(2,128)(2,1)}), bf16[8,2,8192]{2,1,0:T(2,128)(2,1)S(1)}, u32[]{:S(2)}, u32[]{:S(2)}) async-start(bf16[8,2,8192]{2,1,0:T(2,128)(2,1)} %reshape.650), calls=%async_computation.1 | async-start | bytes 524288 | tf_op jit(solution)/shard_map/all_to_all | solution.py:170
  85.8 6.8 %all-to-all-done.1 = bf16[8,2,8192]{2,1,0:T(2,128)(2,1)S(1)} async-done(((bf16[8,2,8192]{2,1,0:T(2,128)(2,1)}), bf16[8,2,8192]{2,1,0:T(2,128)(2,1)S(1)}, u32[]{:S(2)}, u32[]{:S(2)}) %all-to-all-start.1) | async-done | bytes 262176 | tf_op jit(solution)/shard_map/all_to_all | solution.py:170
  93.1 1.2 scatter_fusion
  95.1 3.7 %collective-permute-start.4 = (bf16[512,1024]{1,0:T(8,128)(2,1)S(1)}, bf16[512,1024]{1,0:T(8,128)(2,1)S(1)}, u32[]{:S(2)}, u32[]{:S(2)}) collective-permute-start(bf16[512,1024]{1,0:T(8,128)(2,1)S(1)} %collective-permute-done.2), channel_id=1, source_target_pairs={{0,2},{2,4},{4,6},{1,3},{3,5},{5,7},{8,10},{10,12},{12,14},{9,11},... | collective-permute-start | bytes 3145736 | tf_op jit(solution)/shard_map/ppermute | solution.py:60
  98.9 2.3 %bitcast_dynamic-update-slice_fusion.5 = bf16[7,512,1024]{2,1,0:T(8,128)(2,1)} fusion(bf16[7,512,1024]{2,1,0:T(8,128)(2,1)} %bitcast_dynamic-update-slice_fusion.6, bf16[512,1024]{1,0:T(8,128)(2,1)} %collective-permute-done), kind=kLoop, calls=%fused_computation.24 | loop fusion | bytes 2097152
  101.2 1.3 collective-permute-start.5
  102.5 2.3 bitcast_dynamic-update-slice_fusion.4
  104.8 1.1 bitcast_dynamic-update-slice_fusion.3
  105.9 1.0 bitcast_dynamic-update-slice_fusion.2
  106.9 13.6 %collective-permute-done.4 = bf16[512,1024]{1,0:T(8,128)(2,1)S(1)} collective-permute-done((bf16[512,1024]{1,0:T(8,128)(2,1)S(1)}, bf16[512,1024]{1,0:T(8,128)(2,1)S(1)}, u32[]{:S(2)}, u32[]{:S(2)}) %collective-permute-start.4) | collective-permute-done | bytes 1048608 | tf_op jit(solution)/shard_map/ppermute | solution.py:60
  120.6 1.1 bitcast_dynamic-update-slice_fusion.1
  121.6 5.4 %collective-permute-done.5 = bf16[512,1024]{1,0:T(8,128)(2,1)S(1)} collective-permute-done((bf16[512,1024]{1,0:T(8,128)(2,1)S(1)}, bf16[512,1024]{1,0:T(8,128)(2,1)S(1)}, u32[]{:S(2)}, u32[]{:S(2)}) %collective-permute-start.5) | collective-permute-done | bytes 1048608 | tf_op jit(solution)/shard_map/ppermute | solution.py:61
  127.1 1.1 bitcast_dynamic-update-slice_fusion
  128.1 6.0 %gather_fusion = bf16[4,512,1024]{2,1,0:T(8,128)(2,1)} fusion(bf16[7,512,1024]{2,1,0:T(8,128)(2,1)} %bitcast_dynamic-update-slice_fusion, s32[1024]{0:T(1024)S(1)} %pad_clamp_fusion.2), kind=kCustom, calls=%fused_computation | custom fusion | bytes 8388624 | tf_op jit(solution)/shard_map/jit(_take)/gather | solution.py:65
  134.1 2.8 %fusion.51 = (bf16[4,256,1024]{2,1,0:T(8,128)(2,1)S(1)}, bf16[4,256,1024]{2,1,0:T(8,128)(2,1)S(1)}) fusion(bf16[4,512,1024]{2,1,0:T(8,128)(2,1)} %gather_fusion), kind=kLoop, calls=%fused_computation.138 | loop fusion | bytes 8388608 | tf_op jit(solution)/shard_map/slice | solution.py:68
  137.0 1.3 copy-done
  139.1 1.5 convolution_convert_fusion.2
  140.6 1.1 copy.59
  141.7 1.4 gather_fusion.4
  143.1 2.1 reshape.652
  145.3 3.4 %all-to-all-start.2 = ((bf16[8,2,8192]{2,1,0:T(2,128)(2,1)}), bf16[8,2,8192]{2,1,0:T(2,128)(2,1)S(1)}, u32[]{:S(2)}, u32[]{:S(2)}) async-start(bf16[8,2,8192]{2,1,0:T(2,128)(2,1)} %reshape.652), calls=%async_computation.2 | async-start | bytes 524288 | tf_op jit(solution)/shard_map/all_to_all | solution.py:170
  148.8 6.8 %all-to-all-done.2 = bf16[8,2,8192]{2,1,0:T(2,128)(2,1)S(1)} async-done(((bf16[8,2,8192]{2,1,0:T(2,128)(2,1)}), bf16[8,2,8192]{2,1,0:T(2,128)(2,1)S(1)}, u32[]{:S(2)}, u32[]{:S(2)}) %all-to-all-start.2) | async-done | bytes 262176 | tf_op jit(solution)/shard_map/all_to_all | solution.py:170
  155.5 1.2 reshape.653
  156.7 0.9 slice_convert_fusion.2
  157.6 1.2 scatter_fusion.1
  158.9 2.5 %fusion.14 = f32[1024,64]{0,1:T(8,128)S(1)} fusion(bf16[1024,1024]{1,0:T(8,128)(2,1)} %bitcast.121, f32[1,1,1024,64]{3,2,1,0:T(8,128)S(1)} %bitcast.132, f32[1,1,1024,256]{3,2,1,0:T(8,128)} %param.9, s32[]{:T(128)S(6)} %select_n.245), kind=kOutput, calls=%fused_computation.44 | convolution fusion | flops 134348800 | bytes 3145732 | tf_op jit(solution)/shard_map/dot_general | solution.py:161
  161.4 1.5 convolution_convert_fusion.1
  162.9 1.8 copy.60
  164.6 2.4 %gather_fusion.5 = bf16[64,32,64]{2,1,0:T(8,128)(2,1)} fusion(bf16[33,32,64]{2,1,0:T(8,128)(2,1)} %bitcast.126, s32[1024]{0:T(1024)S(1)} %pad_clamp_fusion), kind=kCustom, calls=%fused_computation.5 | custom fusion | bytes 524544 | tf_op jit(solution)/shard_map/jit(_take)/gather | solution.py:169
  167.0 2.1 reshape.654
  169.1 4.2 %all-to-all-start.3 = ((bf16[8,2,8192]{2,1,0:T(2,128)(2,1)}), bf16[8,2,8192]{2,1,0:T(2,128)(2,1)}, u32[]{:S(2)}, u32[]{:S(2)}) async-start(bf16[8,2,8192]{2,1,0:T(2,128)(2,1)} %reshape.654), calls=%async_computation.3 | async-start | bytes 524288 | tf_op jit(solution)/shard_map/all_to_all | solution.py:170
  173.5 6.7 %all-to-all-done.3 = bf16[8,2,8192]{2,1,0:T(2,128)(2,1)} async-done(((bf16[8,2,8192]{2,1,0:T(2,128)(2,1)}), bf16[8,2,8192]{2,1,0:T(2,128)(2,1)}, u32[]{:S(2)}, u32[]{:S(2)}) %all-to-all-start.3) | async-done | bytes 262176 | tf_op jit(solution)/shard_map/all_to_all | solution.py:170
  180.1 2.1 reshape.655
  182.3 1.6 slice_convert_fusion.1
  183.9 1.9 scatter_fusion.2
  185.9 3.2 %select_select_fusion = (f32[1024,64]{0,1:T(8,128)}, bf16[1024,64]{0,1:T(8,128)(2,1)S(1)}) fusion(f32[1024,64]{0,1:T(8,128)S(1)} %fusion.14, f32[1024,64]{0,1:T(8,128)S(1)} %fusion.11, pred[]{:T(512)S(6)} %eq.207, pred[]{:T(512)S(6)} %eq.206, pred[]{:T(512)S(6)} %eq.181, bf16[1024,1024]{1,0:T(8,128)(2,1)} %bitcast.122, ...), kind=kOutput, calls=%fused_computation.49 | convolution fusion | flops 134610944 | bytes 3801095 | tf_op jit(solution)/shard_map/dot_general | solution.py:161
  190.8 1.1 reshape.656
  191.9 3.4 %all-to-all-start.4 = ((bf16[8,2,8192]{2,1,0:T(2,128)(2,1)}), bf16[8,2,8192]{2,1,0:T(2,128)(2,1)S(1)}, u32[]{:S(2)}, u32[]{:S(2)}) async-start(bf16[8,2,8192]{2,1,0:T(2,128)(2,1)} %reshape.656), calls=%async_computation.4 | async-start | bytes 524288 | tf_op jit(solution)/shard_map/all_to_all | solution.py:170
  195.4 6.7 %all-to-all-done.4 = bf16[8,2,8192]{2,1,0:T(2,128)(2,1)S(1)} async-done(((bf16[8,2,8192]{2,1,0:T(2,128)(2,1)}), bf16[8,2,8192]{2,1,0:T(2,128)(2,1)S(1)}, u32[]{:S(2)}, u32[]{:S(2)}) %all-to-all-start.4) | async-done | bytes 262176 | tf_op jit(solution)/shard_map/all_to_all | solution.py:170
  202.6 1.2 scatter_fusion.3
  204.0 0.9 pad_maximum_fusion.1
  204.9 4.4 %all-to-all-start.5 = ((f32[4,768,64]{1,2,0:T(8,128)}), f32[4,768,64]{1,2,0:T(8,128)S(1)}, u32[]{:S(2)}, u32[]{:S(2)}) async-start(f32[4,768,64]{1,2,0:T(8,128)} %pad_maximum_fusion.1), calls=%async_computation.5 | async-start | bytes 1572864 | tf_op jit(solution)/shard_map/all_to_all | solution.py:184
  209.3 19.4 %all-to-all-done.5 = f32[4,768,64]{1,2,0:T(8,128)S(1)} async-done(((f32[4,768,64]{1,2,0:T(8,128)}), f32[4,768,64]{1,2,0:T(8,128)S(1)}, u32[]{:S(2)}, u32[]{:S(2)}) %all-to-all-start.5) | async-done | bytes 786464 | tf_op jit(solution)/shard_map/all_to_all | solution.py:184
  228.8 1.0 copy.65
  (98 shorter events, 11.7 us)
Async XLA Ops:
  0.6 12.5 %copy-start.3 = (bf16[1,1,256,1024]{3,2,1,0:T(8,128)(2,1)S(1)}, bf16[1,1,256,1024]{3,2,1,0:T(8,128)(2,1)}, u32[]{:S(2)}) copy-start(bf16[1,1,256,1024]{3,2,1,0:T(8,128)(2,1)} %param.10) | copy-start | bytes 1572868
  0.6 12.5 %copy-start.1 = (f32[1,1,1024,256]{3,2,1,0:T(8,128)S(1)}, f32[1,1,1024,256]{3,2,1,0:T(8,128)}, u32[]{:S(2)}) copy-start(f32[1,1,1024,256]{3,2,1,0:T(8,128)} %param.9) | copy-start | bytes 3145732
  4.7 20.8 %copy-start.8 = (s32[1,1,8]{2,1,0:T(1,128)S(1)}, s32[1,1,8]{2,1,0:T(1,128)}, u32[]{:S(2)}) copy-start(s32[1,1,8]{2,1,0:T(1,128)} %param.14) | copy-start | bytes 100
  4.7 20.8 %copy-start.9 = (s32[1,1,8]{2,1,0:T(1,128)S(1)}, s32[1,1,8]{2,1,0:T(1,128)}, u32[]{:S(2)}) copy-start(s32[1,1,8]{2,1,0:T(1,128)} %param.13) | copy-start | bytes 100
  5.7 24.1 %copy-start.4 = (bf16[1,1,8,32,1024]{4,3,2,1,0:T(8,128)(2,1)S(1)}, bf16[1,1,8,32,1024]{4,3,2,1,0:T(8,128)(2,1)}, u32[]{:S(2)}) copy-start(bf16[1,1,8,32,1024]{4,3,2,1,0:T(8,128)(2,1)} %param.11) | copy-start | bytes 1572868
  5.7 46.6 %collective-permute-start = (bf16[512,1024]{1,0:T(8,128)(2,1)}, bf16[512,1024]{1,0:T(8,128)(2,1)}, u32[]{:S(2)}, u32[]{:S(2)}) collective-permute-start(bf16[512,1024]{1,0:T(8,128)(2,1)} %pad_maximum_fusion), channel_id=1, source_target_pairs={{0,2},{2,4},{4,6},{1,3},{3,5},{5,7},{8,10},{10,12},{12,14},{9,11},... | collective-permute-start | bytes 3145736 | tf_op jit(solution)/shard_map/ppermute | solution.py:60
  11.8 53.0 %collective-permute-start.1 = (bf16[512,1024]{1,0:T(8,128)(2,1)}, bf16[512,1024]{1,0:T(8,128)(2,1)}, u32[]{:S(2)}, u32[]{:S(2)}) collective-permute-start(bf16[512,1024]{1,0:T(8,128)(2,1)} %pad_maximum_fusion), channel_id=1, source_target_pairs={{2,0},{4,2},{6,4},{3,1},{5,3},{7,5},{10,8},{12,10},{14,12},{11,9},... | collective-permute-start | bytes 3145736 | tf_op jit(solution)/shard_map/ppermute | solution.py:61
  14.2 37.4 %collective-permute-start.6 = (bf16[256,256]{1,0:T(8,128)(2,1)S(1)}, bf16[256,256]{1,0:T(8,128)(2,1)S(1)}, u32[]{:S(2)}, u32[]{:S(2)}) collective-permute-start(bf16[256,256]{1,0:T(8,128)(2,1)S(1)} %get-tuple-element.36), channel_id=1, source_target_pairs={{0,2},{1,3},{2,4},{3,5},{4,6},{5,7},{6,0},{7,1}} | collective-permute-start | bytes 393224 | tf_op jit(solution)/shard_map/ppermute | solution.py:82
  18.7 32.9 %collective-permute-start.7 = (bf16[256,256]{1,0:T(8,128)(2,1)S(1)}, bf16[256,256]{1,0:T(8,128)(2,1)S(1)}, u32[]{:S(2)}, u32[]{:S(2)}) collective-permute-start(bf16[256,256]{1,0:T(8,128)(2,1)S(1)} %get-tuple-element.36), channel_id=1, source_target_pairs={{0,4},{1,5},{2,6},{3,7},{4,0},{5,1},{6,2},{7,3}} | collective-permute-start | bytes 393224 | tf_op jit(solution)/shard_map/ppermute | solution.py:82
  23.2 28.4 %collective-permute-start.8 = (bf16[256,256]{1,0:T(8,128)(2,1)S(1)}, bf16[256,256]{1,0:T(8,128)(2,1)S(1)}, u32[]{:S(2)}, u32[]{:S(2)}) collective-permute-start(bf16[256,256]{1,0:T(8,128)(2,1)S(1)} %get-tuple-element.36), channel_id=1, source_target_pairs={{0,6},{1,7},{2,0},{3,1},{4,2},{5,3},{6,4},{7,5}} | collective-permute-start | bytes 393224 | tf_op jit(solution)/shard_map/ppermute | solution.py:82
  26.1 24.2 %all-to-all-start = ((s32[32,2,8]{2,1,0:T(2,128)}), s32[32,2,8]{2,1,0:T(2,128)S(1)}, u32[]{:S(2)}, u32[]{:S(2)}) async-start(s32[32,2,8]{2,1,0:T(2,128)} %broadcast_in_dim.159), calls=%async_computation | async-start | bytes 65536 | tf_op jit(solution)/shard_map/all_to_all | solution.py:114
  52.3 42.8 %collective-permute-start.2 = (bf16[512,1024]{1,0:T(8,128)(2,1)}, bf16[512,1024]{1,0:T(8,128)(2,1)S(1)}, u32[]{:S(2)}, u32[]{:S(2)}) collective-permute-start(bf16[512,1024]{1,0:T(8,128)(2,1)} %collective-permute-done), channel_id=1, source_target_pairs={{0,2},{2,4},{4,6},{1,3},{3,5},{5,7},{8,10},{10,12},{12,14},{9,11},... | collective-permute-start | bytes 3145736 | tf_op jit(solution)/shard_map/ppermute | solution.py:60
  55.2 23.8 %collective-permute-start.9 = (bf16[256,64]{0,1:T(8,128)(2,1)S(1)}, bf16[256,64]{0,1:T(8,128)(2,1)S(1)}, u32[]{:S(2)}, u32[]{:S(2)}) collective-permute-start(bf16[256,64]{0,1:T(8,128)(2,1)S(1)} %get-tuple-element.29), channel_id=1, source_target_pairs={{0,2},{1,3},{2,4},{3,5},{4,6},{5,7},{6,0},{7,1}} | collective-permute-start | bytes 98312 | tf_op jit(solution)/shard_map/ppermute | solution.py:82
  57.1 22.3 %collective-permute-start.10 = (bf16[256,64]{0,1:T(8,128)(2,1)S(1)}, bf16[256,64]{0,1:T(8,128)(2,1)S(1)}, u32[]{:S(2)}, u32[]{:S(2)}) collective-permute-start(bf16[256,64]{0,1:T(8,128)(2,1)S(1)} %get-tuple-element.28), channel_id=1, source_target_pairs={{0,4},{1,5},{2,6},{3,7},{4,0},{5,1},{6,2},{7,3}} | collective-permute-start | bytes 98312 | tf_op jit(solution)/shard_map/ppermute | solution.py:82
  59.0 20.7 %collective-permute-start.11 = (bf16[256,64]{0,1:T(8,128)(2,1)S(1)}, bf16[256,64]{0,1:T(8,128)(2,1)S(1)}, u32[]{:S(2)}, u32[]{:S(2)}) collective-permute-start(bf16[256,64]{0,1:T(8,128)(2,1)S(1)} %get-tuple-element.27), channel_id=1, source_target_pairs={{0,6},{1,7},{2,0},{3,1},{4,2},{5,3},{6,4},{7,5}} | collective-permute-start | bytes 98312 | tf_op jit(solution)/shard_map/ppermute | solution.py:82
  64.8 36.4 %collective-permute-start.3 = (bf16[512,1024]{1,0:T(8,128)(2,1)}, bf16[512,1024]{1,0:T(8,128)(2,1)S(1)}, u32[]{:S(2)}, u32[]{:S(2)}) collective-permute-start(bf16[512,1024]{1,0:T(8,128)(2,1)} %collective-permute-done.1), channel_id=1, source_target_pairs={{2,0},{4,2},{6,4},{3,1},{5,3},{7,5},{10,8},{12,10},{14,12},{11,9},... | collective-permute-start | bytes 3145736 | tf_op jit(solution)/shard_map/ppermute | solution.py:61
  82.3 10.3 %all-to-all-start.1 = ((bf16[8,2,8192]{2,1,0:T(2,128)(2,1)}), bf16[8,2,8192]{2,1,0:T(2,128)(2,1)S(1)}, u32[]{:S(2)}, u32[]{:S(2)}) async-start(bf16[8,2,8192]{2,1,0:T(2,128)(2,1)} %reshape.650), calls=%async_computation.1 | async-start | bytes 524288 | tf_op jit(solution)/shard_map/all_to_all | solution.py:170
  95.1 25.4 %collective-permute-start.4 = (bf16[512,1024]{1,0:T(8,128)(2,1)S(1)}, bf16[512,1024]{1,0:T(8,128)(2,1)S(1)}, u32[]{:S(2)}, u32[]{:S(2)}) collective-permute-start(bf16[512,1024]{1,0:T(8,128)(2,1)S(1)} %collective-permute-done.2), channel_id=1, source_target_pairs={{0,2},{2,4},{4,6},{1,3},{3,5},{5,7},{8,10},{10,12},{12,14},{9,11},... | collective-permute-start | bytes 3145736 | tf_op jit(solution)/shard_map/ppermute | solution.py:60
  101.2 25.9 %collective-permute-start.5 = (bf16[512,1024]{1,0:T(8,128)(2,1)S(1)}, bf16[512,1024]{1,0:T(8,128)(2,1)S(1)}, u32[]{:S(2)}, u32[]{:S(2)}) collective-permute-start(bf16[512,1024]{1,0:T(8,128)(2,1)S(1)} %collective-permute-done.3), channel_id=1, source_target_pairs={{2,0},{4,2},{6,4},{3,1},{5,3},{7,5},{10,8},{12,10},{14,12},{11,9},... | collective-permute-start | bytes 3145736 | tf_op jit(solution)/shard_map/ppermute | solution.py:61
  134.1 4.2 %copy-start.2 = (f32[1,1,1024,256]{3,2,1,0:T(8,128)S(1)}, f32[1,1,1024,256]{3,2,1,0:T(8,128)}, u32[]{:S(2)}) copy-start(f32[1,1,1024,256]{3,2,1,0:T(8,128)} %param.9) | copy-start | bytes 3145732
  134.1 4.2 %copy-start.5 = (f32[32,32,64]{2,1,0:T(8,128)S(1)}, f32[32,32,64]{2,1,0:T(8,128)}, u32[]{:S(2)}) copy-start(f32[32,32,64]{2,1,0:T(8,128)} %slice.106) | copy-start | bytes 786436
  136.9 1.4 copy-start
  145.3 10.3 %all-to-all-start.2 = ((bf16[8,2,8192]{2,1,0:T(2,128)(2,1)}), bf16[8,2,8192]{2,1,0:T(2,128)(2,1)S(1)}, u32[]{:S(2)}, u32[]{:S(2)}) async-start(bf16[8,2,8192]{2,1,0:T(2,128)(2,1)} %reshape.652), calls=%async_computation.2 | async-start | bytes 524288 | tf_op jit(solution)/shard_map/all_to_all | solution.py:170
  169.1 11.0 %all-to-all-start.3 = ((bf16[8,2,8192]{2,1,0:T(2,128)(2,1)}), bf16[8,2,8192]{2,1,0:T(2,128)(2,1)}, u32[]{:S(2)}, u32[]{:S(2)}) async-start(bf16[8,2,8192]{2,1,0:T(2,128)(2,1)} %reshape.654), calls=%async_computation.3 | async-start | bytes 524288 | tf_op jit(solution)/shard_map/all_to_all | solution.py:170
  189.1 6.3 %copy-start.6 = (f32[1024,64]{0,1:T(8,128)S(1)}, f32[1024,64]{0,1:T(8,128)}, u32[]{:S(2)}) copy-start(f32[1024,64]{0,1:T(8,128)} %get-tuple-element.38) | copy-start | bytes 786436
  191.9 10.3 %all-to-all-start.4 = ((bf16[8,2,8192]{2,1,0:T(2,128)(2,1)}), bf16[8,2,8192]{2,1,0:T(2,128)(2,1)S(1)}, u32[]{:S(2)}, u32[]{:S(2)}) async-start(bf16[8,2,8192]{2,1,0:T(2,128)(2,1)} %reshape.656), calls=%async_computation.4 | async-start | bytes 524288 | tf_op jit(solution)/shard_map/all_to_all | solution.py:170
  204.9 25.1 %copy-start.7 = (f32[256,256]{1,0:T(8,128)S(1)}, f32[256,256]{1,0:T(8,128)}, u32[]{:S(2)}) copy-start(f32[256,256]{1,0:T(8,128)} %get-tuple-element.37) | copy-start | bytes 786436
  204.9 23.8 %all-to-all-start.5 = ((f32[4,768,64]{1,2,0:T(8,128)}), f32[4,768,64]{1,2,0:T(8,128)S(1)}, u32[]{:S(2)}, u32[]{:S(2)}) async-start(f32[4,768,64]{1,2,0:T(8,128)} %pad_maximum_fusion.1), calls=%async_computation.5 | async-start | bytes 1572864 | tf_op jit(solution)/shard_map/all_to_all | solution.py:184

commit v12 on v5

--- a/solution.py
+++ b/solution.py
@@ -51,7 +51,20 @@
     ).reshape(tile_count * block_rows, width)
 
     both = jnp.concatenate([inverse, tiles_used], axis=0)
-    gathered = lax.all_gather(both, "prow", axis=0)
+    if both.size * 2 <= (2 << 20):
+        to_right = [(p, p + 1) for p in range(n_prow - 1)]
+        to_left = [(p + 1, p) for p in range(n_prow - 1)]
+        chunks = [both]
+        from_left = from_right = both
+        for _ in range(n_prow - 1):
+            from_left = lax.ppermute(from_left, "prow", to_right)
+            from_right = lax.ppermute(from_right, "prow", to_left)
+            chunks += [from_left, from_right]
+        offsets = jnp.arange(n_prow, dtype=jnp.int32) - row_index
+        chunk_of = jnp.where(offsets < 0, -2 * offsets - 1, 2 * offsets)
+        gathered = jnp.take(jnp.stack(chunks), chunk_of, axis=0, mode="clip")
+    else:
+        gathered = lax.all_gather(both, "prow", axis=0)
     inv_full = gathered[:, :row_count].reshape(n_prow * row_count, width)
     tiles_full = gathered[:, row_count:].reshape(group_tiles * block_rows, width)
     tiles_full = jnp.concatenate(
@@ -59,7 +72,14 @@
     )
 
     meta = jnp.stack([off_device[0, 0], off_block[0, 0]], axis=0)
-    meta = lax.all_gather(meta, ("lvl", "prow", "pcol"), axis=0)
+    devices = n_lvl * n_prow * n_pcol
+    meta = lax.all_to_all(
+        jnp.broadcast_to(meta[None], (devices,) + meta.shape),
+        ("lvl", "prow", "pcol"),
+        split_axis=0,
+        concat_axis=0,
+        tiled=True,
+    )
     meta = meta.reshape(n_lvl, n_prow, n_pcol, 2, tile_count)
     meta = jnp.transpose(meta, (0, 2, 1, 3, 4)).reshape(groups, n_prow, 2, tile_count)
     target = meta[:, :, 0, :].reshape(groups, group_tiles)

time: 217 us -> 220 us (1.014)
  blocking collectives: 65.9 us -> 22.1 us
  waiting for transfers between devices: 65.7 us -> 88.9 us
  starting transfers between devices: 14.8 us -> 37.1 us
  between operations: 14.4 us -> 1.13 us
  local copies, waits for them, and re-layouts: 26.4 us -> 39.5 us
    all_gather x1 -> x0, blocking collectives: 43.8 us -> none  [per_device(): meta = lax.all_gather(meta, ('lvl', 'prow', 'pcol'), axis=0)]
    ppermute x0 -> x6, waiting for transfers between devices: none -> 41.1 us  [the longest x3 36.9 us: per_device(): from_left = lax.ppermute(from_left, 'prow', to_right)]
    all_gather x1 -> x0, waiting for transfers between devices: 38.6 us -> none  [per_device(): gathered = lax.all_gather(both, 'prow', axis=0)]
    all_to_all x0 -> x1, waiting for transfers between devices: none -> 20.9 us  [per_device(): lax.all_to_all(jnp.broadcast_to(meta[None], (devices,) + meta.shape), ('l...]
    ppermute x0 -> x6, starting transfers between devices: none -> 15.8 us  [the longest x3 11.9 us: per_device(): from_left = lax.ppermute(from_left, 'prow', to_right)]
    all_to_all x0 -> x1, starting transfers between devices: none -> 6.91 us  [per_device(): lax.all_to_all(jnp.broadcast_to(meta[None], (devices,) + meta.shape), ('l...]
    gather x0 -> x1, local copies, waits for them, and re-layouts: none -> 5.98 us  [per_device(): gathered = jnp.take(jnp.stack(chunks), chunk_of, axis=0, mode='clip')]
    unnamed x20 -> x25, local copies, waits for them, and re-layouts: 14.4 us -> 19.7 us
  transfers between devices with their start and end apart: 5 -> 11, of which waited for: 5 -> 8; matrix products, arithmetic and copies ran while one was open for 1% -> 4% of each run, Pallas kernels for 0% -> 0%
where the time goes in v12:
time: 220 us; the launch traced here: 219 us
  waiting for transfers between devices  88.9 us (40%)
  local copies, waits for them, and re-layouts  39.5 us (18%)
  starting transfers between devices  37.1 us (17%)
  blocking collectives  22.1 us (10%)
  other arithmetic  15.3 us (7%)
  matrix products  14.7 us (7%)
    ppermute x3, waiting for transfers between devices, per_device(): from_left = lax.ppermute(from_left, 'prow', to_right)  36.9 us
    all_to_all x4, waiting for transfers between devices, per_device(): lax.all_to_all(sending, ('lvl', 'pcol'), split_axis=0, concat_axis=0, til...  26.9 us
    all_to_all x1, blocking collectives, per_device(): lax.all_to_all(final, 'prow', split_axis=0, concat_axis=0, tiled=True)  22.1 us
    all_to_all x1, waiting for transfers between devices, per_device(): lax.all_to_all(jnp.broadcast_to(meta[None], (devices,) + meta.shape), ('l...  20.9 us
    unnamed x25, local copies, waits for them, and re-layouts  19.7 us
    all_to_all x4, starting transfers between devices, per_device(): lax.all_to_all(sending, ('lvl', 'pcol'), split_axis=0, concat_axis=0, til...  14.5 us
    ppermute x3, starting transfers between devices, per_device(): from_left = lax.ppermute(from_left, 'prow', to_right)  11.9 us
    dot_general x4, matrix products, per_device(): jnp.dot(inv_full, right.astype(jnp.bfloat16), preferred_element_type=jnp....  10.2 us
  transfers between devices with their start and end apart: 11, of which 8 were waited for; matrix products, arithmetic and copies ran while one was open for 4% of the time, Pallas kernels for 0%

profile of v12, /device:TPU:0, one launch (start us, length us, event | category | flops | bytes accessed | tf_op | source)
XLA Modules:
  0.0 218.8 jit_solution(1977129082839994534)
XLA Ops:
  0.7 0.7 select_reduce_fusion.3
  1.4 0.7 select_reduce_fusion.1
  2.2 0.9 select_reduce_fusion.4
  3.1 1.4 bitcast_select_fusion
  4.5 1.0 pad_maximum_fusion
  5.6 5.0 %collective-permute-start = (bf16[512,1024]{1,0:T(8,128)(2,1)}, bf16[512,1024]{1,0:T(8,128)(2,1)S(1)}, u32[]{:S(2)}, u32[]{:S(2)}) collective-permute-start(bf16[512,1024]{1,0:T(8,128)(2,1)} %pad_maximum_fusion), channel_id=1, source_target_pairs={{0,2},{2,4},{4,6},{1,3},{3,5},{5,7},{8,10},{10,12},{12,14},{9,11},... | collective-permute-start | bytes 3145736 | tf_op jit(solution)/shard_map/ppermute | solution.py:60
  10.6 1.3 collective-permute-start.1
  12.5 6.9 %all-to-all-start = ((s32[32,2,8]{2,1,0:T(2,128)}), s32[32,2,8]{2,1,0:T(2,128)S(1)}, u32[]{:S(2)}, u32[]{:S(2)}) async-start(s32[32,2,8]{2,1,0:T(2,128)} %broadcast_in_dim.146), calls=%async_computation | async-start | bytes 65536 | tf_op jit(solution)/shard_map/all_to_all | solution.py:76
  19.6 1.1 bitcast_dynamic-update-slice_fusion.6
  20.6 20.9 %all-to-all-done = s32[32,2,8]{2,1,0:T(2,128)S(1)} async-done(((s32[32,2,8]{2,1,0:T(2,128)}), s32[32,2,8]{2,1,0:T(2,128)S(1)}, u32[]{:S(2)}, u32[]{:S(2)}) %all-to-all-start) | async-done | bytes 2080 | tf_op jit(solution)/shard_map/all_to_all | solution.py:76
  42.1 2.5 %collective-permute-start.2 = (bf16[512,1024]{1,0:T(8,128)(2,1)S(1)}, bf16[512,1024]{1,0:T(8,128)(2,1)S(1)}, u32[]{:S(2)}, u32[]{:S(2)}) collective-permute-start(bf16[512,1024]{1,0:T(8,128)(2,1)S(1)} %collective-permute-done), channel_id=1, source_target_pairs={{0,2},{2,4},{4,6},{1,3},{3,5},{5,7},{8,10},{10,12},{12,14},{9,11},... | collective-permute-start | bytes 3145736 | tf_op jit(solution)/shard_map/ppermute | solution.py:60
  44.8 1.3 collective-permute-start.3
  46.6 20.7 %collective-permute-done.2 = bf16[512,1024]{1,0:T(8,128)(2,1)S(1)} collective-permute-done((bf16[512,1024]{1,0:T(8,128)(2,1)S(1)}, bf16[512,1024]{1,0:T(8,128)(2,1)S(1)}, u32[]{:S(2)}, u32[]{:S(2)}) %collective-permute-start.2) | collective-permute-done | bytes 1048608 | tf_op jit(solution)/shard_map/ppermute | solution.py:60
  67.2 4.4 %collective-permute-start.4 = (bf16[512,1024]{1,0:T(8,128)(2,1)S(1)}, bf16[512,1024]{1,0:T(8,128)(2,1)S(1)}, u32[]{:S(2)}, u32[]{:S(2)}) collective-permute-start(bf16[512,1024]{1,0:T(8,128)(2,1)S(1)} %collective-permute-done.2), channel_id=1, source_target_pairs={{0,2},{2,4},{4,6},{1,3},{3,5},{5,7},{8,10},{10,12},{12,14},{9,11},... | collective-permute-start | bytes 3145736 | tf_op jit(solution)/shard_map/ppermute | solution.py:60
  71.7 1.1 bitcast_dynamic-update-slice_fusion.5
  72.8 1.3 collective-permute-start.5
  74.0 1.1 bitcast_dynamic-update-slice_fusion.4
  75.1 1.0 bitcast_dynamic-update-slice_fusion.3
  76.2 1.0 bitcast_dynamic-update-slice_fusion.2
  77.2 16.2 %collective-permute-done.4 = bf16[512,1024]{1,0:T(8,128)(2,1)S(1)} collective-permute-done((bf16[512,1024]{1,0:T(8,128)(2,1)S(1)}, bf16[512,1024]{1,0:T(8,128)(2,1)S(1)}, u32[]{:S(2)}, u32[]{:S(2)}) %collective-permute-start.4) | collective-permute-done | bytes 1048608 | tf_op jit(solution)/shard_map/ppermute | solution.py:60
  93.4 1.1 bitcast_dynamic-update-slice_fusion.1
  94.5 4.2 %collective-permute-done.5 = bf16[512,1024]{1,0:T(8,128)(2,1)S(1)} collective-permute-done((bf16[512,1024]{1,0:T(8,128)(2,1)S(1)}, bf16[512,1024]{1,0:T(8,128)(2,1)S(1)}, u32[]{:S(2)}, u32[]{:S(2)}) %collective-permute-start.5) | collective-permute-done | bytes 1048608 | tf_op jit(solution)/shard_map/ppermute | solution.py:61
  98.7 1.1 bitcast_dynamic-update-slice_fusion
  99.8 6.0 %gather_fusion = bf16[4,512,1024]{2,1,0:T(8,128)(2,1)} fusion(bf16[7,512,1024]{2,1,0:T(8,128)(2,1)} %bitcast_dynamic-update-slice_fusion, s32[1024]{0:T(1024)S(1)} %pad_clamp_fusion.1), kind=kCustom, calls=%fused_computation | custom fusion | bytes 8388624 | tf_op jit(solution)/shard_map/jit(_take)/gather | solution.py:65
  105.8 2.7 %fusion.47 = (bf16[4,256,1024]{2,1,0:T(8,128)(2,1)S(1)}, bf16[4,256,1024]{2,1,0:T(8,128)(2,1)S(1)}) fusion(bf16[4,512,1024]{2,1,0:T(8,128)(2,1)} %gather_fusion), kind=kLoop, calls=%fused_computation.120 | loop fusion | bytes 8388608 | tf_op jit(solution)/shard_map/slice | solution.py:68
  108.5 1.3 copy-done
  109.8 1.9 fusion.5
  111.7 0.7 copy-done.1
  112.4 0.8 convolution_convert_fusion.3
  113.4 0.7 gather_fusion.1
  114.1 1.1 reshape.526
  115.2 3.4 %all-to-all-start.1 = ((bf16[8,2,8192]{2,1,0:T(2,128)(2,1)}), bf16[8,2,8192]{2,1,0:T(2,128)(2,1)S(1)}, u32[]{:S(2)}, u32[]{:S(2)}) async-start(bf16[8,2,8192]{2,1,0:T(2,128)(2,1)} %reshape.526), calls=%async_computation.1 | async-start | bytes 524288 | tf_op jit(solution)/shard_map/all_to_all | solution.py:129
  118.7 6.8 %all-to-all-done.1 = bf16[8,2,8192]{2,1,0:T(2,128)(2,1)S(1)} async-done(((bf16[8,2,8192]{2,1,0:T(2,128)(2,1)}), bf16[8,2,8192]{2,1,0:T(2,128)(2,1)S(1)}, u32[]{:S(2)}, u32[]{:S(2)}) %all-to-all-start.1) | async-done | bytes 262176 | tf_op jit(solution)/shard_map/all_to_all | solution.py:129
  126.0 1.2 scatter_fusion
  127.2 2.5 %fusion.8 = f32[1024,64]{0,1:T(8,128)S(1)} fusion(bf16[1024,1024]{1,0:T(8,128)(2,1)} %bitcast.96, f32[1,1,1024,64]{3,2,1,0:T(8,128)S(1)} %bitcast.104, f32[1,1,1024,256]{3,2,1,0:T(8,128)} %param.9, s32[]{:T(128)S(6)} %select_n.179), kind=kOutput, calls=%fused_computation.35 | convolution fusion | flops 134348800 | bytes 3145732 | tf_op jit(solution)/shard_map/dot_general | solution.py:120
  129.7 1.5 convolution_convert_fusion.2
  131.2 1.1 copy.55
  132.3 1.4 gather_fusion.2
  133.7 2.1 reshape.528
  135.9 3.4 %all-to-all-start.2 = ((bf16[8,2,8192]{2,1,0:T(2,128)(2,1)}), bf16[8,2,8192]{2,1,0:T(2,128)(2,1)S(1)}, u32[]{:S(2)}, u32[]{:S(2)}) async-start(bf16[8,2,8192]{2,1,0:T(2,128)(2,1)} %reshape.528), calls=%async_computation.2 | async-start | bytes 524288 | tf_op jit(solution)/shard_map/all_to_all | solution.py:129
  139.4 6.8 %all-to-all-done.2 = bf16[8,2,8192]{2,1,0:T(2,128)(2,1)S(1)} async-done(((bf16[8,2,8192]{2,1,0:T(2,128)(2,1)}), bf16[8,2,8192]{2,1,0:T(2,128)(2,1)S(1)}, u32[]{:S(2)}, u32[]{:S(2)}) %all-to-all-start.2) | async-done | bytes 262176 | tf_op jit(solution)/shard_map/all_to_all | solution.py:129
  146.2 1.2 reshape.529
  147.3 0.9 slice_convert_fusion.2
  148.2 1.2 scatter_fusion.1
  149.5 2.5 %fusion.11 = f32[1024,64]{0,1:T(8,128)S(1)} fusion(bf16[1024,1024]{1,0:T(8,128)(2,1)} %bitcast.97, f32[1,1,1024,64]{3,2,1,0:T(8,128)S(1)} %bitcast.105, f32[1,1,1024,256]{3,2,1,0:T(8,128)} %param.9, s32[]{:T(128)S(6)} %select_n.179), kind=kOutput, calls=%fused_computation.37 | convolution fusion | flops 134348800 | bytes 3145732 | tf_op jit(solution)/shard_map/dot_general | solution.py:120
  152.0 1.5 convolution_convert_fusion.1
  153.5 1.8 copy.56
  155.3 2.4 %gather_fusion.3 = bf16[64,32,64]{2,1,0:T(8,128)(2,1)} fusion(bf16[33,32,64]{2,1,0:T(8,128)(2,1)} %bitcast.102, s32[1024]{0:T(1024)S(1)} %pad_clamp_fusion), kind=kCustom, calls=%fused_computation.3 | custom fusion | bytes 524544 | tf_op jit(solution)/shard_map/jit(_take)/gather | solution.py:128
  157.7 2.1 reshape.530
  159.8 4.2 %all-to-all-start.3 = ((bf16[8,2,8192]{2,1,0:T(2,128)(2,1)}), bf16[8,2,8192]{2,1,0:T(2,128)(2,1)}, u32[]{:S(2)}, u32[]{:S(2)}) async-start(bf16[8,2,8192]{2,1,0:T(2,128)(2,1)} %reshape.530), calls=%async_computation.3 | async-start | bytes 524288 | tf_op jit(solution)/shard_map/all_to_all | solution.py:129
  164.1 6.7 %all-to-all-done.3 = bf16[8,2,8192]{2,1,0:T(2,128)(2,1)} async-done(((bf16[8,2,8192]{2,1,0:T(2,128)(2,1)}), bf16[8,2,8192]{2,1,0:T(2,128)(2,1)}, u32[]{:S(2)}, u32[]{:S(2)}) %all-to-all-start.3) | async-done | bytes 262176 | tf_op jit(solution)/shard_map/all_to_all | solution.py:129
  170.8 2.1 reshape.531
  172.9 1.6 slice_convert_fusion.1
  174.6 2.0 scatter_fusion.2
  176.6 3.3 %select_select_fusion = (f32[1024,64]{0,1:T(8,128)}, bf16[1024,64]{0,1:T(8,128)(2,1)S(1)}) fusion(f32[1024,64]{0,1:T(8,128)S(1)} %fusion.11, f32[1024,64]{0,1:T(8,128)S(1)} %fusion.8, f32[1024,64]{0,1:T(8,128)} %copy-done.1, pred[]{:T(512)S(6)} %eq.183, pred[]{:T(512)S(6)} %eq.182, pred[]{:T(512)S(6)} %eq.181, pred[]{:T(512)S(6)} %eq.150, ...), kind=kOutput, calls=%fused_computation.41 | convolution fusion | flops 134676480 | bytes 4063240 | tf_op jit(solution)/shard_map/dot_general | solution.py:120
  179.9 0.8 convolution_convert_fusion
  180.8 0.7 gather_fusion.4
  181.5 1.1 reshape.532
  182.6 3.4 %all-to-all-start.4 = ((bf16[8,2,8192]{2,1,0:T(2,128)(2,1)}), bf16[8,2,8192]{2,1,0:T(2,128)(2,1)S(1)}, u32[]{:S(2)}, u32[]{:S(2)}) async-start(bf16[8,2,8192]{2,1,0:T(2,128)(2,1)} %reshape.532), calls=%async_computation.4 | async-start | bytes 524288 | tf_op jit(solution)/shard_map/all_to_all | solution.py:129
  186.2 6.7 %all-to-all-done.4 = bf16[8,2,8192]{2,1,0:T(2,128)(2,1)S(1)} async-done(((bf16[8,2,8192]{2,1,0:T(2,128)(2,1)}), bf16[8,2,8192]{2,1,0:T(2,128)(2,1)S(1)}, u32[]{:S(2)}, u32[]{:S(2)}) %all-to-all-start.4) | async-done | bytes 262176 | tf_op jit(solution)/shard_map/all_to_all | solution.py:129
  193.3 1.2 scatter_fusion.3
  194.8 22.1 %all_to_all.30 = f32[4,768,64]{1,2,0:T(8,128)S(1)} all-to-all(f32[4,768,64]{1,2,0:T(8,128)S(1)} %pad_maximum_fusion.1), channel_id=1, replica_groups=mesh['lvl'=4,'prow'=4,'pcol'=2] {'prow'}, dimensions={0} | all-to-all | bytes 1572864 | tf_op jit(solution)/shard_map/all_to_all | solution.py:144
  217.0 1.0 copy.61
  218.0 0.8 copy.60
  (65 shorter events, 4.0 us)
Async XLA Ops:
  0.6 11.2 %copy-start.4 = (s32[1,1,8]{2,1,0:T(1,128)S(1)}, s32[1,1,8]{2,1,0:T(1,128)}, u32[]{:S(2)}) copy-start(s32[1,1,8]{2,1,0:T(1,128)} %param.13) | copy-start | bytes 100
  0.6 11.2 %copy-start.3 = (s32[1,1,8]{2,1,0:T(1,128)S(1)}, s32[1,1,8]{2,1,0:T(1,128)}, u32[]{:S(2)}) copy-start(s32[1,1,8]{2,1,0:T(1,128)} %param.14) | copy-start | bytes 100
  5.6 36.5 %collective-permute-start = (bf16[512,1024]{1,0:T(8,128)(2,1)}, bf16[512,1024]{1,0:T(8,128)(2,1)S(1)}, u32[]{:S(2)}, u32[]{:S(2)}) collective-permute-start(bf16[512,1024]{1,0:T(8,128)(2,1)} %pad_maximum_fusion), channel_id=1, source_target_pairs={{0,2},{2,4},{4,6},{1,3},{3,5},{5,7},{8,10},{10,12},{12,14},{9,11},... | collective-permute-start | bytes 3145736 | tf_op jit(solution)/shard_map/ppermute | solution.py:60
  10.6 34.2 %collective-permute-start.1 = (bf16[512,1024]{1,0:T(8,128)(2,1)}, bf16[512,1024]{1,0:T(8,128)(2,1)S(1)}, u32[]{:S(2)}, u32[]{:S(2)}) collective-permute-start(bf16[512,1024]{1,0:T(8,128)(2,1)} %pad_maximum_fusion), channel_id=1, source_target_pairs={{2,0},{4,2},{6,4},{3,1},{5,3},{7,5},{10,8},{12,10},{14,12},{11,9},... | collective-permute-start | bytes 3145736 | tf_op jit(solution)/shard_map/ppermute | solution.py:61
  12.5 29.0 %all-to-all-start = ((s32[32,2,8]{2,1,0:T(2,128)}), s32[32,2,8]{2,1,0:T(2,128)S(1)}, u32[]{:S(2)}, u32[]{:S(2)}) async-start(s32[32,2,8]{2,1,0:T(2,128)} %broadcast_in_dim.146), calls=%async_computation | async-start | bytes 65536 | tf_op jit(solution)/shard_map/all_to_all | solution.py:76
  42.1 25.1 %collective-permute-start.2 = (bf16[512,1024]{1,0:T(8,128)(2,1)S(1)}, bf16[512,1024]{1,0:T(8,128)(2,1)S(1)}, u32[]{:S(2)}, u32[]{:S(2)}) collective-permute-start(bf16[512,1024]{1,0:T(8,128)(2,1)S(1)} %collective-permute-done), channel_id=1, source_target_pairs={{0,2},{2,4},{4,6},{1,3},{3,5},{5,7},{8,10},{10,12},{12,14},{9,11},... | collective-permute-start | bytes 3145736 | tf_op jit(solution)/shard_map/ppermute | solution.py:60
  44.8 28.0 %collective-permute-start.3 = (bf16[512,1024]{1,0:T(8,128)(2,1)S(1)}, bf16[512,1024]{1,0:T(8,128)(2,1)S(1)}, u32[]{:S(2)}, u32[]{:S(2)}) collective-permute-start(bf16[512,1024]{1,0:T(8,128)(2,1)S(1)} %collective-permute-done.1), channel_id=1, source_target_pairs={{2,0},{4,2},{6,4},{3,1},{5,3},{7,5},{10,8},{12,10},{14,12},{11,9},... | collective-permute-start | bytes 3145736 | tf_op jit(solution)/shard_map/ppermute | solution.py:61
  67.2 26.2 %collective-permute-start.4 = (bf16[512,1024]{1,0:T(8,128)(2,1)S(1)}, bf16[512,1024]{1,0:T(8,128)(2,1)S(1)}, u32[]{:S(2)}, u32[]{:S(2)}) collective-permute-start(bf16[512,1024]{1,0:T(8,128)(2,1)S(1)} %collective-permute-done.2), channel_id=1, source_target_pairs={{0,2},{2,4},{4,6},{1,3},{3,5},{5,7},{8,10},{10,12},{12,14},{9,11},... | collective-permute-start | bytes 3145736 | tf_op jit(solution)/shard_map/ppermute | solution.py:60
  72.8 25.9 %collective-permute-start.5 = (bf16[512,1024]{1,0:T(8,128)(2,1)S(1)}, bf16[512,1024]{1,0:T(8,128)(2,1)S(1)}, u32[]{:S(2)}, u32[]{:S(2)}) collective-permute-start(bf16[512,1024]{1,0:T(8,128)(2,1)S(1)} %collective-permute-done.3), channel_id=1, source_target_pairs={{2,0},{4,2},{6,4},{3,1},{5,3},{7,5},{10,8},{12,10},{14,12},{11,9},... | collective-permute-start | bytes 3145736 | tf_op jit(solution)/shard_map/ppermute | solution.py:61
  108.5 1.4 copy-start
  111.7 0.7 copy-start.1
  115.2 10.3 %all-to-all-start.1 = ((bf16[8,2,8192]{2,1,0:T(2,128)(2,1)}), bf16[8,2,8192]{2,1,0:T(2,128)(2,1)S(1)}, u32[]{:S(2)}, u32[]{:S(2)}) async-start(bf16[8,2,8192]{2,1,0:T(2,128)(2,1)} %reshape.526), calls=%async_computation.1 | async-start | bytes 524288 | tf_op jit(solution)/shard_map/all_to_all | solution.py:129
  135.9 10.3 %all-to-all-start.2 = ((bf16[8,2,8192]{2,1,0:T(2,128)(2,1)}), bf16[8,2,8192]{2,1,0:T(2,128)(2,1)S(1)}, u32[]{:S(2)}, u32[]{:S(2)}) async-start(bf16[8,2,8192]{2,1,0:T(2,128)(2,1)} %reshape.528), calls=%async_computation.2 | async-start | bytes 524288 | tf_op jit(solution)/shard_map/all_to_all | solution.py:129
  159.8 11.0 %all-to-all-start.3 = ((bf16[8,2,8192]{2,1,0:T(2,128)(2,1)}), bf16[8,2,8192]{2,1,0:T(2,128)(2,1)}, u32[]{:S(2)}, u32[]{:S(2)}) async-start(bf16[8,2,8192]{2,1,0:T(2,128)(2,1)} %reshape.530), calls=%async_computation.3 | async-start | bytes 524288 | tf_op jit(solution)/shard_map/all_to_all | solution.py:129
  179.8 6.3 %copy-start.2 = (f32[1024,64]{0,1:T(8,128)S(1)}, f32[1024,64]{0,1:T(8,128)}, u32[]{:S(2)}) copy-start(f32[1024,64]{0,1:T(8,128)} %get-tuple-element.32) | copy-start | bytes 786436
  182.6 10.3 %all-to-all-start.4 = ((bf16[8,2,8192]{2,1,0:T(2,128)(2,1)}), bf16[8,2,8192]{2,1,0:T(2,128)(2,1)S(1)}, u32[]{:S(2)}, u32[]{:S(2)}) async-start(bf16[8,2,8192]{2,1,0:T(2,128)(2,1)} %reshape.532), calls=%async_computation.4 | async-start | bytes 524288 | tf_op jit(solution)/shard_map/all_to_all | solution.py:129

commit v13 on v8

--- a/solution.py
+++ b/solution.py
@@ -161,17 +161,23 @@
         acc = acc.at[recv_block[section]].add(incoming.astype(jnp.float32), mode="clip")
     outer = acc[window_blocks:NT].reshape(ABOVE, cols)
 
+    solved_blocks = solved.reshape(n_prow, rows_out, cols)
+    solved_high = lax.reduce_precision(solved_blocks, exponent_bits=8, mantissa_bits=7)
+    solved_low = solved_blocks - solved_high
     final = jnp.concatenate(
         [
-            solved.reshape(n_prow, rows_out, cols),
-            jnp.broadcast_to(outer[None], (n_prow, ABOVE, cols)),
+            solved_high.astype(jnp.bfloat16),
+            solved_low.astype(jnp.bfloat16),
+            jnp.broadcast_to(outer.astype(jnp.bfloat16)[None], (n_prow, ABOVE, cols)),
         ],
         axis=1,
     )
     final = lax.all_to_all(final, "prow", split_axis=0, concat_axis=0, tiled=True)
-    solution_rows = jnp.transpose(final[:, :rows_out], (1, 0, 2)).reshape(rows_out, columns_all)
+    final = final.astype(jnp.float32)
+    solution_cols = final[:, :rows_out] + final[:, rows_out : 2 * rows_out]
+    solution_rows = jnp.transpose(solution_cols, (1, 0, 2)).reshape(rows_out, columns_all)
     solution_rows = jnp.where(level_index == 0, first_rows, solution_rows)
-    outer_all = jnp.transpose(final[:, rows_out:], (1, 0, 2)).reshape(ABOVE, columns_all)
+    outer_all = jnp.transpose(final[:, 2 * rows_out :], (1, 0, 2)).reshape(ABOVE, columns_all)
     return (solution_rows[None, None], outer_all[None, None])
 
 

time: 210 us -> 204 us (0.971)
  waiting for transfers between devices: 84.8 us -> 79.2 us
    all_to_all x1, waiting for transfers between devices: 19.4 us -> 13.8 us  [per_device(): lax.all_to_all(final, 'prow', split_axis=0, concat_axis=0, tiled=True)]
where the time goes in v13:
time: 204 us; the launch traced here: 202 us
  waiting for transfers between devices  79.2 us (39%)
  starting transfers between devices  52.6 us (26%)
  local copies, waits for them, and re-layouts  28.2 us (14%)
  other arithmetic  16.1 us (8%)
  between operations  14.7 us (7%)
  matrix products  11.7 us (6%)
    ppermute x6, starting transfers between devices, level0_shift(): return lax.ppermute(x, all_axes, pairs)  30.5 us
    all_to_all x4, waiting for transfers between devices, per_device(): lax.all_to_all(sending, ('lvl', 'pcol'), split_axis=0, concat_axis=0, til...  26.9 us
    all_gather x1, waiting for transfers between devices, per_device(): gathered = lax.all_gather(both, 'prow', axis=0)  20.8 us
    all_to_all x4, starting transfers between devices, per_device(): lax.all_to_all(sending, ('lvl', 'pcol'), split_axis=0, concat_axis=0, til...  14.5 us
    all_to_all x1, waiting for transfers between devices, per_device(): lax.all_to_all(final, 'prow', split_axis=0, concat_axis=0, tiled=True)  13.8 us
    unnamed x30, local copies, waits for them, and re-layouts  13.6 us
    all_to_all x1, waiting for transfers between devices, per_device(): lax.all_to_all(jnp.broadcast_to(meta[None], (devices,) + meta.shape), ('l...  12.2 us
    dot_general x3, matrix products, per_device(): jnp.dot(inv_full, right.astype(jnp.bfloat16), preferred_element_type=jnp....  6.58 us
  transfers between devices with their start and end apart: 13, of which 9 were waited for; matrix products, arithmetic and copies ran while one was open for 5% of the time, Pallas kernels for 0%

profile of v13, /device:TPU:0, one launch (start us, length us, event | category | flops | bytes accessed | tf_op | source)
XLA Modules:
  0.0 202.5 jit_solution(6604815266863924807)
XLA Ops:
  7.2 0.7 select_reduce_fusion.1
  8.0 0.7 select_reduce_fusion.3
  8.7 0.9 select_reduce_fusion.4
  9.7 1.4 bitcast_select_fusion
  11.1 1.1 pad_maximum_fusion
  12.2 0.5 copy-done.1
  12.8 1.1 fusion.54
  13.9 6.9 %collective-permute-start.2 = (bf16[256,256]{1,0:T(8,128)(2,1)S(1)}, bf16[256,256]{1,0:T(8,128)(2,1)S(1)}, u32[]{:S(2)}, u32[]{:S(2)}) collective-permute-start(bf16[256,256]{1,0:T(8,128)(2,1)S(1)} %get-tuple-element.38), channel_id=1, source_target_pairs={{0,6},{1,7},{2,0},{3,1},{4,2},{5,3},{6,4},{7,5}} | collective-permute-start | bytes 393224 | tf_op jit(solution)/shard_map/ppermute | solution.py:69
  20.9 1.9 collective-permute-start.1
  22.8 2.9 %collective-permute-start = (bf16[256,256]{1,0:T(8,128)(2,1)S(1)}, bf16[256,256]{1,0:T(8,128)(2,1)S(1)}, u32[]{:S(2)}, u32[]{:S(2)}) collective-permute-start(bf16[256,256]{1,0:T(8,128)(2,1)S(1)} %get-tuple-element.38), channel_id=1, source_target_pairs={{0,2},{1,3},{2,4},{3,5},{4,6},{5,7},{6,0},{7,1}} | collective-permute-start | bytes 393224 | tf_op jit(solution)/shard_map/ppermute | solution.py:69
  25.7 0.6 broadcast_in_dim.156
  26.4 3.2 %all-to-all-start = ((s32[32,2,8]{2,1,0:T(2,128)}), s32[32,2,8]{2,1,0:T(2,128)S(1)}, u32[]{:S(2)}, u32[]{:S(2)}) async-start(s32[32,2,8]{2,1,0:T(2,128)} %broadcast_in_dim.156), calls=%async_computation | async-start | bytes 65536 | tf_op jit(solution)/shard_map/all_to_all | solution.py:101
  29.8 12.2 %all-to-all-done = s32[32,2,8]{2,1,0:T(2,128)S(1)} async-done(((s32[32,2,8]{2,1,0:T(2,128)}), s32[32,2,8]{2,1,0:T(2,128)S(1)}, u32[]{:S(2)}, u32[]{:S(2)}) %all-to-all-start) | async-done | bytes 2080 | tf_op jit(solution)/shard_map/all_to_all | solution.py:101
  43.4 0.6 gather_fusion
  44.0 0.4 convolution_convert_fusion.3
  44.4 13.8 %collective-permute-start.5 = (bf16[256,64]{0,1:T(8,128)(2,1)S(1)}, bf16[256,64]{0,1:T(8,128)(2,1)S(1)}, u32[]{:S(2)}, u32[]{:S(2)}) collective-permute-start(bf16[256,64]{0,1:T(8,128)(2,1)S(1)} %get-tuple-element.29), channel_id=1, source_target_pairs={{0,6},{1,7},{2,0},{3,1},{4,2},{5,3},{6,4},{7,5}} | collective-permute-start | bytes 98312 | tf_op jit(solution)/shard_map/ppermute | solution.py:69
  58.2 1.9 collective-permute-start.4
  60.1 2.9 %collective-permute-start.3 = (bf16[256,64]{0,1:T(8,128)(2,1)S(1)}, bf16[256,64]{0,1:T(8,128)(2,1)S(1)}, u32[]{:S(2)}, u32[]{:S(2)}) collective-permute-start(bf16[256,64]{0,1:T(8,128)(2,1)S(1)} %get-tuple-element.31), channel_id=1, source_target_pairs={{0,2},{1,3},{2,4},{3,5},{4,6},{5,7},{6,0},{7,1}} | collective-permute-start | bytes 98312 | tf_op jit(solution)/shard_map/ppermute | solution.py:69
  63.1 2.6 %collective-permute-done.4 = bf16[256,64]{0,1:T(8,128)(2,1)S(1)} collective-permute-done((bf16[256,64]{0,1:T(8,128)(2,1)S(1)}, bf16[256,64]{0,1:T(8,128)(2,1)S(1)}, u32[]{:S(2)}, u32[]{:S(2)}) %collective-permute-start.4) | collective-permute-done | bytes 32800 | tf_op jit(solution)/shard_map/ppermute | solution.py:69
  65.8 2.7 %collective-permute-done.3 = bf16[256,64]{0,1:T(8,128)(2,1)S(1)} collective-permute-done((bf16[256,64]{0,1:T(8,128)(2,1)S(1)}, bf16[256,64]{0,1:T(8,128)(2,1)S(1)}, u32[]{:S(2)}, u32[]{:S(2)}) %collective-permute-start.3) | collective-permute-done | bytes 32800 | tf_op jit(solution)/shard_map/ppermute | solution.py:69
  68.4 0.6 gather_fusion.1
  69.2 0.7 gather_fusion.2
  69.9 1.1 reshape.627
  71.0 3.4 %all-to-all-start.1 = ((bf16[8,2,8192]{2,1,0:T(2,128)(2,1)}), bf16[8,2,8192]{2,1,0:T(2,128)(2,1)S(1)}, u32[]{:S(2)}, u32[]{:S(2)}) async-start(bf16[8,2,8192]{2,1,0:T(2,128)(2,1)} %reshape.627), calls=%async_computation.1 | async-start | bytes 524288 | tf_op jit(solution)/shard_map/all_to_all | solution.py:157
  74.5 6.8 %all-to-all-done.1 = bf16[8,2,8192]{2,1,0:T(2,128)(2,1)S(1)} async-done(((bf16[8,2,8192]{2,1,0:T(2,128)(2,1)}), bf16[8,2,8192]{2,1,0:T(2,128)(2,1)S(1)}, u32[]{:S(2)}, u32[]{:S(2)}) %all-to-all-start.1) | async-done | bytes 262176 | tf_op jit(solution)/shard_map/all_to_all | solution.py:157
  81.3 0.3 reshape.628
  81.8 1.2 scatter_fusion
  83.0 0.8 slice.109
  83.8 20.8 %all-gather.3.cloned.1.call-done = bf16[2048,1024]{1,0:T(8,128)(2,1)} async-done(((bf16[512,1024]{1,0:T(8,128)(2,1)}), bf16[2048,1024]{1,0:T(8,128)(2,1)}) %all-gather.3.cloned.1.call-update) | async-done | bytes 4194320 | tf_op jit(solution)/shard_map/all_gather | solution.py:54
  104.7 2.8 %fusion.51 = (bf16[4,256,1024]{2,1,0:T(8,128)(2,1)S(1)}, bf16[4,256,1024]{2,1,0:T(8,128)(2,1)S(1)}) fusion(bf16[4,512,1024]{2,1,0:T(8,128)(2,1)} %bitcast.108), kind=kLoop, calls=%fused_computation.131 | loop fusion | bytes 8388608 | tf_op jit(solution)/shard_map/slice | solution.py:55
  107.5 1.3 copy-done
  108.8 0.8 fusion.12
  109.6 1.5 convolution_convert_fusion.2
  111.1 1.1 copy.64
  112.2 1.4 gather_fusion.3
  113.6 2.1 %reshape.629 = bf16[8,2,8192]{2,1,0:T(2,128)(2,1)} reshape(bf16[64,32,64]{2,1,0:T(8,128)(2,1)} %gather_fusion.3) | data formatting | bytes 524288
  115.8 3.4 %all-to-all-start.2 = ((bf16[8,2,8192]{2,1,0:T(2,128)(2,1)}), bf16[8,2,8192]{2,1,0:T(2,128)(2,1)S(1)}, u32[]{:S(2)}, u32[]{:S(2)}) async-start(bf16[8,2,8192]{2,1,0:T(2,128)(2,1)} %reshape.629), calls=%async_computation.2 | async-start | bytes 524288 | tf_op jit(solution)/shard_map/all_to_all | solution.py:157
  119.4 6.7 %all-to-all-done.2 = bf16[8,2,8192]{2,1,0:T(2,128)(2,1)S(1)} async-done(((bf16[8,2,8192]{2,1,0:T(2,128)(2,1)}), bf16[8,2,8192]{2,1,0:T(2,128)(2,1)S(1)}, u32[]{:S(2)}, u32[]{:S(2)}) %all-to-all-start.2) | async-done | bytes 262176 | tf_op jit(solution)/shard_map/all_to_all | solution.py:157
  126.1 1.2 reshape.630
  127.2 0.9 slice_convert_fusion.3
  128.1 1.2 scatter_fusion.1
  129.4 2.5 %fusion.15 = f32[1024,64]{0,1:T(8,128)S(1)} fusion(bf16[1024,1024]{1,0:T(8,128)(2,1)} %bitcast.106, f32[1,1,1024,64]{3,2,1,0:T(8,128)S(1)} %bitcast.118, f32[1,1,1024,256]{3,2,1,0:T(8,128)} %param.9, s32[]{:T(128)S(6)} %select_n.233), kind=kOutput, calls=%fused_computation.39 | convolution fusion | flops 134348800 | bytes 3145732 | tf_op jit(solution)/shard_map/dot_general | solution.py:148
  131.9 1.5 convolution_convert_fusion.1
  133.4 1.8 copy.65
  135.2 2.4 %gather_fusion.4 = bf16[64,32,64]{2,1,0:T(8,128)(2,1)} fusion(bf16[33,32,64]{2,1,0:T(8,128)(2,1)} %bitcast.112, s32[1024]{0:T(1024)S(1)} %pad_clamp_fusion), kind=kCustom, calls=%fused_computation.4 | custom fusion | bytes 524544 | tf_op jit(solution)/shard_map/jit(_take)/gather | solution.py:156
  137.5 2.1 %reshape.631 = bf16[8,2,8192]{2,1,0:T(2,128)(2,1)} reshape(bf16[64,32,64]{2,1,0:T(8,128)(2,1)} %gather_fusion.4) | data formatting | bytes 524288
  139.7 4.2 %all-to-all-start.3 = ((bf16[8,2,8192]{2,1,0:T(2,128)(2,1)}), bf16[8,2,8192]{2,1,0:T(2,128)(2,1)}, u32[]{:S(2)}, u32[]{:S(2)}) async-start(bf16[8,2,8192]{2,1,0:T(2,128)(2,1)} %reshape.631), calls=%async_computation.3 | async-start | bytes 524288 | tf_op jit(solution)/shard_map/all_to_all | solution.py:157
  144.0 6.7 %all-to-all-done.3 = bf16[8,2,8192]{2,1,0:T(2,128)(2,1)} async-done(((bf16[8,2,8192]{2,1,0:T(2,128)(2,1)}), bf16[8,2,8192]{2,1,0:T(2,128)(2,1)}, u32[]{:S(2)}, u32[]{:S(2)}) %all-to-all-start.3) | async-done | bytes 262176 | tf_op jit(solution)/shard_map/all_to_all | solution.py:157
  150.7 2.1 %reshape.632 = bf16[64,32,64]{2,1,0:T(8,128)(2,1)} reshape(bf16[8,2,8192]{2,1,0:T(2,128)(2,1)} %all-to-all-done.3) | data formatting | bytes 524288
  152.8 1.6 slice_convert_fusion.2
  154.4 1.9 scatter_fusion.2
  156.4 3.2 %select_select_fusion = (f32[1024,64]{0,1:T(8,128)}, bf16[1024,64]{0,1:T(8,128)(2,1)S(1)}) fusion(f32[1024,64]{0,1:T(8,128)S(1)} %fusion.15, f32[1024,64]{0,1:T(8,128)S(1)} %fusion.12, pred[]{:T(512)S(6)} %eq.207, pred[]{:T(512)S(6)} %eq.206, pred[]{:T(512)S(6)} %eq.181, bf16[1024,1024]{1,0:T(8,128)(2,1)} %bitcast.107, ...), kind=kOutput, calls=%fused_computation.45 | convolution fusion | flops 134610944 | bytes 3801095 | tf_op jit(solution)/shard_map/dot_general | solution.py:148
  159.7 0.8 convolution_convert_fusion
  160.7 0.7 gather_fusion.5
  161.3 1.1 reshape.633
  162.4 3.4 %all-to-all-start.4 = ((bf16[8,2,8192]{2,1,0:T(2,128)(2,1)}), bf16[8,2,8192]{2,1,0:T(2,128)(2,1)S(1)}, u32[]{:S(2)}, u32[]{:S(2)}) async-start(bf16[8,2,8192]{2,1,0:T(2,128)(2,1)} %reshape.633), calls=%async_computation.4 | async-start | bytes 524288 | tf_op jit(solution)/shard_map/all_to_all | solution.py:157
  165.9 6.8 %all-to-all-done.4 = bf16[8,2,8192]{2,1,0:T(2,128)(2,1)S(1)} async-done(((bf16[8,2,8192]{2,1,0:T(2,128)(2,1)}), bf16[8,2,8192]{2,1,0:T(2,128)(2,1)S(1)}, u32[]{:S(2)}, u32[]{:S(2)}) %all-to-all-start.4) | async-done | bytes 262176 | tf_op jit(solution)/shard_map/all_to_all | solution.py:157
  172.7 0.3 reshape.634
  173.1 1.2 scatter_fusion.3
  174.5 0.9 pad_maximum_fusion.2
  175.3 4.4 %all-to-all-start.5 = ((bf16[4,1024,64]{1,2,0:T(8,128)(2,1)}), bf16[4,1024,64]{1,2,0:T(8,128)(2,1)S(1)}, u32[]{:S(2)}, u32[]{:S(2)}) async-start(bf16[4,1024,64]{1,2,0:T(8,128)(2,1)} %pad_maximum_fusion.2), calls=%async_computation.5 | async-start | bytes 1048576 | tf_op jit(solution)/shard_map/all_to_all | solution.py:175
  179.7 13.8 %all-to-all-done.5 = bf16[4,1024,64]{1,2,0:T(8,128)(2,1)S(1)} async-done(((bf16[4,1024,64]{1,2,0:T(8,128)(2,1)}), bf16[4,1024,64]{1,2,0:T(8,128)(2,1)S(1)}, u32[]{:S(2)}, u32[]{:S(2)}) %all-to-all-start.5) | async-done | bytes 524320 | tf_op jit(solution)/shard_map/all_to_all | solution.py:175
  193.9 1.0 copy.71
  194.9 0.7 select_bitcast_fusion
  (80 shorter events, 3.2 us)
Async XLA Ops:
  7.2 97.5 %all-gather.3.cloned.1.call-start = ((), (), s32[]{:S(2)}) async-start(), calls=%async_computation.6 | async-start | bytes 5242880 | tf_op jit(solution)/shard_map/all_gather | solution.py:54
  11.1 1.6 copy-start.1
  11.1 1.7 copy-start.3
  11.1 14.6 %copy-start.8 = (s32[1,1,8]{2,1,0:T(1,128)S(1)}, s32[1,1,8]{2,1,0:T(1,128)}, u32[]{:S(2)}) copy-start(s32[1,1,8]{2,1,0:T(1,128)} %param.14) | copy-start | bytes 100
  11.1 14.6 %copy-start.9 = (s32[1,1,8]{2,1,0:T(1,128)S(1)}, s32[1,1,8]{2,1,0:T(1,128)}, u32[]{:S(2)}) copy-start(s32[1,1,8]{2,1,0:T(1,128)} %param.13) | copy-start | bytes 100
  12.2 17.5 %copy-start.4 = (bf16[1,1,8,32,1024]{4,3,2,1,0:T(8,128)(2,1)S(1)}, bf16[1,1,8,32,1024]{4,3,2,1,0:T(8,128)(2,1)}, u32[]{:S(2)}) copy-start(bf16[1,1,8,32,1024]{4,3,2,1,0:T(8,128)(2,1)} %param.11) | copy-start | bytes 1572868
  13.9 29.4 %collective-permute-start.2 = (bf16[256,256]{1,0:T(8,128)(2,1)S(1)}, bf16[256,256]{1,0:T(8,128)(2,1)S(1)}, u32[]{:S(2)}, u32[]{:S(2)}) collective-permute-start(bf16[256,256]{1,0:T(8,128)(2,1)S(1)} %get-tuple-element.38), channel_id=1, source_target_pairs={{0,6},{1,7},{2,0},{3,1},{4,2},{5,3},{6,4},{7,5}} | collective-permute-start | bytes 393224 | tf_op jit(solution)/shard_map/ppermute | solution.py:69
  20.9 22.4 %collective-permute-start.1 = (bf16[256,256]{1,0:T(8,128)(2,1)S(1)}, bf16[256,256]{1,0:T(8,128)(2,1)S(1)}, u32[]{:S(2)}, u32[]{:S(2)}) collective-permute-start(bf16[256,256]{1,0:T(8,128)(2,1)S(1)} %get-tuple-element.38), channel_id=1, source_target_pairs={{0,4},{1,5},{2,6},{3,7},{4,0},{5,1},{6,2},{7,3}} | collective-permute-start | bytes 393224 | tf_op jit(solution)/shard_map/ppermute | solution.py:69
  22.8 20.5 %collective-permute-start = (bf16[256,256]{1,0:T(8,128)(2,1)S(1)}, bf16[256,256]{1,0:T(8,128)(2,1)S(1)}, u32[]{:S(2)}, u32[]{:S(2)}) collective-permute-start(bf16[256,256]{1,0:T(8,128)(2,1)S(1)} %get-tuple-element.38), channel_id=1, source_target_pairs={{0,2},{1,3},{2,4},{3,5},{4,6},{5,7},{6,0},{7,1}} | collective-permute-start | bytes 393224 | tf_op jit(solution)/shard_map/ppermute | solution.py:69
  26.4 15.7 %all-to-all-start = ((s32[32,2,8]{2,1,0:T(2,128)}), s32[32,2,8]{2,1,0:T(2,128)S(1)}, u32[]{:S(2)}, u32[]{:S(2)}) async-start(s32[32,2,8]{2,1,0:T(2,128)} %broadcast_in_dim.156), calls=%async_computation | async-start | bytes 65536 | tf_op jit(solution)/shard_map/all_to_all | solution.py:101
  44.4 18.8 %collective-permute-start.5 = (bf16[256,64]{0,1:T(8,128)(2,1)S(1)}, bf16[256,64]{0,1:T(8,128)(2,1)S(1)}, u32[]{:S(2)}, u32[]{:S(2)}) collective-permute-start(bf16[256,64]{0,1:T(8,128)(2,1)S(1)} %get-tuple-element.29), channel_id=1, source_target_pairs={{0,6},{1,7},{2,0},{3,1},{4,2},{5,3},{6,4},{7,5}} | collective-permute-start | bytes 98312 | tf_op jit(solution)/shard_map/ppermute | solution.py:69
  58.2 7.6 %collective-permute-start.4 = (bf16[256,64]{0,1:T(8,128)(2,1)S(1)}, bf16[256,64]{0,1:T(8,128)(2,1)S(1)}, u32[]{:S(2)}, u32[]{:S(2)}) collective-permute-start(bf16[256,64]{0,1:T(8,128)(2,1)S(1)} %get-tuple-element.30), channel_id=1, source_target_pairs={{0,4},{1,5},{2,6},{3,7},{4,0},{5,1},{6,2},{7,3}} | collective-permute-start | bytes 98312 | tf_op jit(solution)/shard_map/ppermute | solution.py:69
  60.1 8.3 %collective-permute-start.3 = (bf16[256,64]{0,1:T(8,128)(2,1)S(1)}, bf16[256,64]{0,1:T(8,128)(2,1)S(1)}, u32[]{:S(2)}, u32[]{:S(2)}) collective-permute-start(bf16[256,64]{0,1:T(8,128)(2,1)S(1)} %get-tuple-element.31), channel_id=1, source_target_pairs={{0,2},{1,3},{2,4},{3,5},{4,6},{5,7},{6,0},{7,1}} | collective-permute-start | bytes 98312 | tf_op jit(solution)/shard_map/ppermute | solution.py:69
  71.0 10.3 %all-to-all-start.1 = ((bf16[8,2,8192]{2,1,0:T(2,128)(2,1)}), bf16[8,2,8192]{2,1,0:T(2,128)(2,1)S(1)}, u32[]{:S(2)}, u32[]{:S(2)}) async-start(bf16[8,2,8192]{2,1,0:T(2,128)(2,1)} %reshape.627), calls=%async_computation.1 | async-start | bytes 524288 | tf_op jit(solution)/shard_map/all_to_all | solution.py:157
  104.7 4.1 %copy-start.2 = (f32[1,1,1024,256]{3,2,1,0:T(8,128)S(1)}, f32[1,1,1024,256]{3,2,1,0:T(8,128)}, u32[]{:S(2)}) copy-start(f32[1,1,1024,256]{3,2,1,0:T(8,128)} %param.9) | copy-start | bytes 3145732
  104.7 4.1 %copy-start.5 = (f32[32,32,64]{2,1,0:T(8,128)S(1)}, f32[32,32,64]{2,1,0:T(8,128)}, u32[]{:S(2)}) copy-start(f32[32,32,64]{2,1,0:T(8,128)} %slice.109) | copy-start | bytes 786436
  107.5 1.3 copy-start
  115.8 10.3 %all-to-all-start.2 = ((bf16[8,2,8192]{2,1,0:T(2,128)(2,1)}), bf16[8,2,8192]{2,1,0:T(2,128)(2,1)S(1)}, u32[]{:S(2)}, u32[]{:S(2)}) async-start(bf16[8,2,8192]{2,1,0:T(2,128)(2,1)} %reshape.629), calls=%async_computation.2 | async-start | bytes 524288 | tf_op jit(solution)/shard_map/all_to_all | solution.py:157
  139.7 11.0 %all-to-all-start.3 = ((bf16[8,2,8192]{2,1,0:T(2,128)(2,1)}), bf16[8,2,8192]{2,1,0:T(2,128)(2,1)}, u32[]{:S(2)}, u32[]{:S(2)}) async-start(bf16[8,2,8192]{2,1,0:T(2,128)(2,1)} %reshape.631), calls=%async_computation.3 | async-start | bytes 524288 | tf_op jit(solution)/shard_map/all_to_all | solution.py:157
  159.7 6.2 %copy-start.6 = (f32[1024,64]{0,1:T(8,128)S(1)}, f32[1024,64]{0,1:T(8,128)}, u32[]{:S(2)}) copy-start(f32[1024,64]{0,1:T(8,128)} %get-tuple-element.40) | copy-start | bytes 786436
  162.4 10.3 %all-to-all-start.4 = ((bf16[8,2,8192]{2,1,0:T(2,128)(2,1)}), bf16[8,2,8192]{2,1,0:T(2,128)(2,1)S(1)}, u32[]{:S(2)}, u32[]{:S(2)}) async-start(bf16[8,2,8192]{2,1,0:T(2,128)(2,1)} %reshape.633), calls=%async_computation.4 | async-start | bytes 524288 | tf_op jit(solution)/shard_map/all_to_all | solution.py:157
  175.3 18.2 %all-to-all-start.5 = ((bf16[4,1024,64]{1,2,0:T(8,128)(2,1)}), bf16[4,1024,64]{1,2,0:T(8,128)(2,1)S(1)}, u32[]{:S(2)}, u32[]{:S(2)}) async-start(bf16[4,1024,64]{1,2,0:T(8,128)(2,1)} %pad_maximum_fusion.2), calls=%async_computation.5 | async-start | bytes 1048576 | tf_op jit(solution)/shard_map/all_to_all | solution.py:175
  193.7 1.2 copy-start.7
Sparse Core Ops, SparseCore 0:
  12.3 92.2 all-gather.2

commit v14 on v13

--- a/solution.py
+++ b/solution.py
@@ -50,10 +50,15 @@
         jnp.zeros((), jnp.bfloat16),
     ).reshape(tile_count * block_rows, width)
 
-    both = jnp.concatenate([inverse, tiles_used], axis=0)
-    gathered = lax.all_gather(both, "prow", axis=0)
-    inv_full = gathered[:, :row_count].reshape(n_prow * row_count, width)
-    tiles_full = gathered[:, row_count:].reshape(group_tiles * block_rows, width)
+    if inverse.shape == tiles_used.shape:
+        gathered = lax.all_gather(jnp.stack([inverse, tiles_used]), "prow", axis=1)
+        inv_full = gathered[0].reshape(n_prow * row_count, width)
+        tiles_full = gathered[1].reshape(group_tiles * block_rows, width)
+    else:
+        both = jnp.concatenate([inverse, tiles_used], axis=0)
+        gathered = lax.all_gather(both, "prow", axis=0)
+        inv_full = gathered[:, :row_count].reshape(n_prow * row_count, width)
+        tiles_full = gathered[:, row_count:].reshape(group_tiles * block_rows, width)
     tiles_full = jnp.concatenate(
         [tiles_full, jnp.zeros((block_rows, width), jnp.bfloat16)], axis=0
     )

time: 204 us -> 204 us (level)
    slice x1 -> x0, local copies, waits for them, and re-layouts: 2.81 us -> none  [per_device(): inv_full = gathered[:, :row_count].reshape(n_prow * row_count, width)]
    unnamed x30 -> x26, local copies, waits for them, and re-layouts: 13.6 us -> 12.5 us
where the time goes in v14:
time: 204 us; the launch traced here: 203 us
  waiting for transfers between devices  78.6 us (39%)
  starting transfers between devices  53.2 us (26%)
  local copies, waits for them, and re-layouts  26.3 us (13%)
  other arithmetic  17.1 us (8%)
  between operations  14.7 us (7%)
  matrix products  13 us (6%)
    ppermute x6, starting transfers between devices, level0_shift(): return lax.ppermute(x, all_axes, pairs)  31.1 us
    all_to_all x4, waiting for transfers between devices, per_device(): lax.all_to_all(sending, ('lvl', 'pcol'), split_axis=0, concat_axis=0, til...  26.9 us
    all_gather x1, waiting for transfers between devices, per_device(): gathered = lax.all_gather(jnp.stack([inverse, tiles_used]), 'prow', axis=1)  20.8 us
    all_to_all x4, starting transfers between devices, per_device(): lax.all_to_all(sending, ('lvl', 'pcol'), split_axis=0, concat_axis=0, til...  14.5 us
    all_to_all x1, waiting for transfers between devices, per_device(): lax.all_to_all(final, 'prow', split_axis=0, concat_axis=0, tiled=True)  13.8 us
    unnamed x26, local copies, waits for them, and re-layouts  12.5 us
    all_to_all x1, waiting for transfers between devices, per_device(): lax.all_to_all(jnp.broadcast_to(meta[None], (devices,) + meta.shape), ('l...  11.7 us
    dot_general x3, matrix products, per_device(): jnp.dot(inv_full, right.astype(jnp.bfloat16), preferred_element_type=jnp....  7.79 us
  transfers between devices with their start and end apart: 13, of which 9 were waited for; matrix products, arithmetic and copies ran while one was open for 5% of the time, Pallas kernels for 0%

profile of v14, /device:TPU:0, one launch (start us, length us, event | category | flops | bytes accessed | tf_op | source)
XLA Modules:
  0.0 202.9 jit_solution(793355765273805660)
XLA Ops:
  7.2 0.7 select_reduce_fusion.1
  8.0 0.7 select_reduce_fusion.3
  8.7 0.9 select_reduce_fusion.4
  9.7 1.1 bitcast_select_fusion
  10.9 1.3 compare_select_fusion
  12.2 1.1 pad_maximum_fusion
  13.4 1.1 fusion.53
  14.4 6.9 %collective-permute-start.2 = (bf16[256,256]{1,0:T(8,128)(2,1)S(1)}, bf16[256,256]{1,0:T(8,128)(2,1)S(1)}, u32[]{:S(2)}, u32[]{:S(2)}) collective-permute-start(bf16[256,256]{1,0:T(8,128)(2,1)S(1)} %get-tuple-element.36), channel_id=1, source_target_pairs={{0,6},{1,7},{2,0},{3,1},{4,2},{5,3},{6,4},{7,5}} | collective-permute-start | bytes 393224 | tf_op jit(solution)/shard_map/ppermute | solution.py:74
  21.4 1.9 collective-permute-start.1
  23.3 2.9 %collective-permute-start = (bf16[256,256]{1,0:T(8,128)(2,1)S(1)}, bf16[256,256]{1,0:T(8,128)(2,1)S(1)}, u32[]{:S(2)}, u32[]{:S(2)}) collective-permute-start(bf16[256,256]{1,0:T(8,128)(2,1)S(1)} %get-tuple-element.36), channel_id=1, source_target_pairs={{0,2},{1,3},{2,4},{3,5},{4,6},{5,7},{6,0},{7,1}} | collective-permute-start | bytes 393224 | tf_op jit(solution)/shard_map/ppermute | solution.py:74
  26.3 0.6 broadcast_in_dim.156
  26.9 3.2 %all-to-all-start = ((s32[32,2,8]{2,1,0:T(2,128)}), s32[32,2,8]{2,1,0:T(2,128)S(1)}, u32[]{:S(2)}, u32[]{:S(2)}) async-start(s32[32,2,8]{2,1,0:T(2,128)} %broadcast_in_dim.156), calls=%async_computation | async-start | bytes 65536 | tf_op jit(solution)/shard_map/all_to_all | solution.py:106
  30.3 11.7 %all-to-all-done = s32[32,2,8]{2,1,0:T(2,128)S(1)} async-done(((s32[32,2,8]{2,1,0:T(2,128)}), s32[32,2,8]{2,1,0:T(2,128)S(1)}, u32[]{:S(2)}, u32[]{:S(2)}) %all-to-all-start) | async-done | bytes 2080 | tf_op jit(solution)/shard_map/all_to_all | solution.py:106
  43.3 0.6 gather_fusion
  43.9 0.4 convolution_convert_fusion.3
  44.3 14.4 %collective-permute-start.5 = (bf16[256,64]{0,1:T(8,128)(2,1)S(1)}, bf16[256,64]{0,1:T(8,128)(2,1)S(1)}, u32[]{:S(2)}, u32[]{:S(2)}) collective-permute-start(bf16[256,64]{0,1:T(8,128)(2,1)S(1)} %get-tuple-element.27), channel_id=1, source_target_pairs={{0,6},{1,7},{2,0},{3,1},{4,2},{5,3},{6,4},{7,5}} | collective-permute-start | bytes 98312 | tf_op jit(solution)/shard_map/ppermute | solution.py:74
  58.7 1.9 collective-permute-start.4
  60.7 2.9 %collective-permute-start.3 = (bf16[256,64]{0,1:T(8,128)(2,1)S(1)}, bf16[256,64]{0,1:T(8,128)(2,1)S(1)}, u32[]{:S(2)}, u32[]{:S(2)}) collective-permute-start(bf16[256,64]{0,1:T(8,128)(2,1)S(1)} %get-tuple-element.29), channel_id=1, source_target_pairs={{0,2},{1,3},{2,4},{3,5},{4,6},{5,7},{6,0},{7,1}} | collective-permute-start | bytes 98312 | tf_op jit(solution)/shard_map/ppermute | solution.py:74
  63.6 2.8 %collective-permute-done.4 = bf16[256,64]{0,1:T(8,128)(2,1)S(1)} collective-permute-done((bf16[256,64]{0,1:T(8,128)(2,1)S(1)}, bf16[256,64]{0,1:T(8,128)(2,1)S(1)}, u32[]{:S(2)}, u32[]{:S(2)}) %collective-permute-start.4) | collective-permute-done | bytes 32800 | tf_op jit(solution)/shard_map/ppermute | solution.py:74
  66.5 2.5 %collective-permute-done.3 = bf16[256,64]{0,1:T(8,128)(2,1)S(1)} collective-permute-done((bf16[256,64]{0,1:T(8,128)(2,1)S(1)}, bf16[256,64]{0,1:T(8,128)(2,1)S(1)}, u32[]{:S(2)}, u32[]{:S(2)}) %collective-permute-start.3) | collective-permute-done | bytes 32800 | tf_op jit(solution)/shard_map/ppermute | solution.py:74
  69.0 0.6 gather_fusion.1
  69.8 0.7 gather_fusion.2
  70.4 1.1 reshape.691
  71.5 3.4 %all-to-all-start.1 = ((bf16[8,2,8192]{2,1,0:T(2,128)(2,1)}), bf16[8,2,8192]{2,1,0:T(2,128)(2,1)S(1)}, u32[]{:S(2)}, u32[]{:S(2)}) async-start(bf16[8,2,8192]{2,1,0:T(2,128)(2,1)} %reshape.691), calls=%async_computation.1 | async-start | bytes 524288 | tf_op jit(solution)/shard_map/all_to_all | solution.py:162
  75.1 6.8 %all-to-all-done.1 = bf16[8,2,8192]{2,1,0:T(2,128)(2,1)S(1)} async-done(((bf16[8,2,8192]{2,1,0:T(2,128)(2,1)}), bf16[8,2,8192]{2,1,0:T(2,128)(2,1)S(1)}, u32[]{:S(2)}, u32[]{:S(2)}) %all-to-all-start.1) | async-done | bytes 262176 | tf_op jit(solution)/shard_map/all_to_all | solution.py:162
  81.8 0.3 reshape.692
  82.3 1.2 scatter_fusion
  83.5 0.8 slice.111
  84.3 20.8 %all-gather.3.cloned.1.call-done = bf16[2,1024,1024]{2,1,0:T(8,128)(2,1)} async-done(((bf16[2,256,1024]{2,1,0:T(8,128)(2,1)}), bf16[2,1024,1024]{2,1,0:T(8,128)(2,1)}) %all-gather.3.cloned.1.call-update) | async-done | bytes 4194320 | tf_op jit(solution)/shard_map/all_gather | solution.py:54
  105.2 1.9 slice_bitcast_fusion
  107.1 0.9 copy-done
  108.0 2.0 %fusion.5 = f32[1024,64]{0,1:T(8,128)S(1)} fusion(bf16[2,1024,1024]{2,1,0:T(8,128)(2,1)S(1)} %copy-done, f32[1,1,1024,64]{3,2,1,0:T(8,128)} %bitcast.114, f32[1,1,1024,256]{3,2,1,0:T(8,128)} %param.9, s32[]{:T(128)S(6)} %select_n.247), kind=kOutput, calls=%fused_computation.20 | convolution fusion | flops 134348800 | bytes 3407876 | tf_op jit(solution)/shard_map/dot_general | solution.py:153
  110.0 1.5 convolution_convert_fusion.2
  111.5 1.1 copy.64
  112.6 1.4 gather_fusion.3
  114.0 2.1 %reshape.693 = bf16[8,2,8192]{2,1,0:T(2,128)(2,1)} reshape(bf16[64,32,64]{2,1,0:T(8,128)(2,1)} %gather_fusion.3) | data formatting | bytes 524288
  116.2 3.4 %all-to-all-start.2 = ((bf16[8,2,8192]{2,1,0:T(2,128)(2,1)}), bf16[8,2,8192]{2,1,0:T(2,128)(2,1)S(1)}, u32[]{:S(2)}, u32[]{:S(2)}) async-start(bf16[8,2,8192]{2,1,0:T(2,128)(2,1)} %reshape.693), calls=%async_computation.2 | async-start | bytes 524288 | tf_op jit(solution)/shard_map/all_to_all | solution.py:162
  119.8 6.7 %all-to-all-done.2 = bf16[8,2,8192]{2,1,0:T(2,128)(2,1)S(1)} async-done(((bf16[8,2,8192]{2,1,0:T(2,128)(2,1)}), bf16[8,2,8192]{2,1,0:T(2,128)(2,1)S(1)}, u32[]{:S(2)}, u32[]{:S(2)}) %all-to-all-start.2) | async-done | bytes 262176 | tf_op jit(solution)/shard_map/all_to_all | solution.py:162
  126.4 1.2 reshape.694
  127.6 0.9 slice_convert_fusion.3
  128.5 1.2 scatter_fusion.1
  129.8 2.5 %fusion.4 = f32[1024,64]{0,1:T(8,128)S(1)} fusion(bf16[2,1024,1024]{2,1,0:T(8,128)(2,1)} %all-gather.3.cloned.1.call-done, f32[1,1,1024,64]{3,2,1,0:T(8,128)S(1)} %bitcast.115, f32[1,1,1024,256]{3,2,1,0:T(8,128)} %param.9, s32[]{:T(128)S(6)} %select_n.247), kind=kOutput, calls=%fused_computation.19 | convolution fusion | flops 134348800 | bytes 3145732 | tf_op jit(solution)/shard_map/dot_general | solution.py:153
  132.3 1.5 convolution_convert_fusion.1
  133.8 1.7 copy.65
  135.5 2.4 %gather_fusion.4 = bf16[64,32,64]{2,1,0:T(8,128)(2,1)} fusion(bf16[33,32,64]{2,1,0:T(8,128)(2,1)} %bitcast.109, s32[1024]{0:T(1024)S(1)} %pad_clamp_fusion), kind=kCustom, calls=%fused_computation.4 | custom fusion | bytes 524544 | tf_op jit(solution)/shard_map/jit(_take)/gather | solution.py:161
  137.9 2.1 %reshape.695 = bf16[8,2,8192]{2,1,0:T(2,128)(2,1)} reshape(bf16[64,32,64]{2,1,0:T(8,128)(2,1)} %gather_fusion.4) | data formatting | bytes 524288
  140.0 4.3 %all-to-all-start.3 = ((bf16[8,2,8192]{2,1,0:T(2,128)(2,1)}), bf16[8,2,8192]{2,1,0:T(2,128)(2,1)}, u32[]{:S(2)}, u32[]{:S(2)}) async-start(bf16[8,2,8192]{2,1,0:T(2,128)(2,1)} %reshape.695), calls=%async_computation.3 | async-start | bytes 524288 | tf_op jit(solution)/shard_map/all_to_all | solution.py:162
  144.4 6.7 %all-to-all-done.3 = bf16[8,2,8192]{2,1,0:T(2,128)(2,1)} async-done(((bf16[8,2,8192]{2,1,0:T(2,128)(2,1)}), bf16[8,2,8192]{2,1,0:T(2,128)(2,1)}, u32[]{:S(2)}, u32[]{:S(2)}) %all-to-all-start.3) | async-done | bytes 262176 | tf_op jit(solution)/shard_map/all_to_all | solution.py:162
  151.0 2.1 %reshape.696 = bf16[64,32,64]{2,1,0:T(8,128)(2,1)} reshape(bf16[8,2,8192]{2,1,0:T(2,128)(2,1)} %all-to-all-done.3) | data formatting | bytes 524288
  153.2 1.6 slice_convert_fusion.2
  154.8 2.0 scatter_fusion.2
  156.8 3.2 %select_select_fusion = (f32[1024,64]{0,1:T(8,128)}, bf16[1024,64]{0,1:T(8,128)(2,1)S(1)}) fusion(f32[1024,64]{0,1:T(8,128)S(1)} %fusion.4, f32[1024,64]{0,1:T(8,128)S(1)} %fusion.5, pred[]{:T(512)S(6)} %eq.214, pred[]{:T(512)S(6)} %eq.213, pred[]{:T(512)S(6)} %eq.188, f32[1,1,1024,64]{3,2,1,0:T(8,128)S(1)} %bitcast.110, f32[1,1,1024,256]{3,2,1,0:T(8,128)} %param.9, ...), kind=kOutput, calls=%fused_computation.47 | convolution fusion | flops 134610944 | bytes 3801095 | tf_op jit(solution)/shard_map/dot_general | solution.py:153
  160.0 0.8 convolution_convert_fusion
  161.0 0.7 gather_fusion.5
  161.7 1.1 reshape.697
  162.8 3.4 %all-to-all-start.4 = ((bf16[8,2,8192]{2,1,0:T(2,128)(2,1)}), bf16[8,2,8192]{2,1,0:T(2,128)(2,1)S(1)}, u32[]{:S(2)}, u32[]{:S(2)}) async-start(bf16[8,2,8192]{2,1,0:T(2,128)(2,1)} %reshape.697), calls=%async_computation.4 | async-start | bytes 524288 | tf_op jit(solution)/shard_map/all_to_all | solution.py:162
  166.3 6.8 %all-to-all-done.4 = bf16[8,2,8192]{2,1,0:T(2,128)(2,1)S(1)} async-done(((bf16[8,2,8192]{2,1,0:T(2,128)(2,1)}), bf16[8,2,8192]{2,1,0:T(2,128)(2,1)S(1)}, u32[]{:S(2)}, u32[]{:S(2)}) %all-to-all-start.4) | async-done | bytes 262176 | tf_op jit(solution)/shard_map/all_to_all | solution.py:162
  173.1 0.3 reshape.698
  173.5 1.2 scatter_fusion.3
  174.8 0.9 pad_maximum_fusion.2
  175.7 4.4 %all-to-all-start.5 = ((bf16[4,1024,64]{1,2,0:T(8,128)(2,1)}), bf16[4,1024,64]{1,2,0:T(8,128)(2,1)S(1)}, u32[]{:S(2)}, u32[]{:S(2)}) async-start(bf16[4,1024,64]{1,2,0:T(8,128)(2,1)} %pad_maximum_fusion.2), calls=%async_computation.5 | async-start | bytes 1048576 | tf_op jit(solution)/shard_map/all_to_all | solution.py:180
  180.1 13.8 %all-to-all-done.5 = bf16[4,1024,64]{1,2,0:T(8,128)(2,1)S(1)} async-done(((bf16[4,1024,64]{1,2,0:T(8,128)(2,1)}), bf16[4,1024,64]{1,2,0:T(8,128)(2,1)S(1)}, u32[]{:S(2)}, u32[]{:S(2)}) %all-to-all-start.5) | async-done | bytes 524320 | tf_op jit(solution)/shard_map/all_to_all | solution.py:180
  194.3 1.0 copy.71
  195.3 0.7 select_bitcast_fusion
  (78 shorter events, 3.1 us)
Async XLA Ops:
  7.2 98.0 %all-gather.3.cloned.1.call-start = ((), (), s32[]{:S(2)}) async-start(), calls=%async_computation.6 | async-start | bytes 5242880 | tf_op jit(solution)/shard_map/all_gather | solution.py:54
  10.8 2.5 %copy-start.1 = (f32[1,1,1024,256]{3,2,1,0:T(8,128)S(1)}, f32[1,1,1024,256]{3,2,1,0:T(8,128)}, u32[]{:S(2)}) copy-start(f32[1,1,1024,256]{3,2,1,0:T(8,128)} %param.9) | copy-start | bytes 3145732
  10.8 2.5 %copy-start.2 = (bf16[1,1,256,1024]{3,2,1,0:T(8,128)(2,1)S(1)}, bf16[1,1,256,1024]{3,2,1,0:T(8,128)(2,1)}, u32[]{:S(2)}) copy-start(bf16[1,1,256,1024]{3,2,1,0:T(8,128)(2,1)} %param.10) | copy-start | bytes 1572868
  12.2 14.0 %copy-start.6 = (s32[1,1,8]{2,1,0:T(1,128)S(1)}, s32[1,1,8]{2,1,0:T(1,128)}, u32[]{:S(2)}) copy-start(s32[1,1,8]{2,1,0:T(1,128)} %param.14) | copy-start | bytes 100
  12.2 14.0 %copy-start.7 = (s32[1,1,8]{2,1,0:T(1,128)S(1)}, s32[1,1,8]{2,1,0:T(1,128)}, u32[]{:S(2)}) copy-start(s32[1,1,8]{2,1,0:T(1,128)} %param.13) | copy-start | bytes 100
  12.2 18.0 %copy-start.3 = (bf16[1,1,8,32,1024]{4,3,2,1,0:T(8,128)(2,1)S(1)}, bf16[1,1,8,32,1024]{4,3,2,1,0:T(8,128)(2,1)}, u32[]{:S(2)}) copy-start(bf16[1,1,8,32,1024]{4,3,2,1,0:T(8,128)(2,1)} %param.11) | copy-start | bytes 1572868
  14.4 28.8 %collective-permute-start.2 = (bf16[256,256]{1,0:T(8,128)(2,1)S(1)}, bf16[256,256]{1,0:T(8,128)(2,1)S(1)}, u32[]{:S(2)}, u32[]{:S(2)}) collective-permute-start(bf16[256,256]{1,0:T(8,128)(2,1)S(1)} %get-tuple-element.36), channel_id=1, source_target_pairs={{0,6},{1,7},{2,0},{3,1},{4,2},{5,3},{6,4},{7,5}} | collective-permute-start | bytes 393224 | tf_op jit(solution)/shard_map/ppermute | solution.py:74
  21.4 21.9 %collective-permute-start.1 = (bf16[256,256]{1,0:T(8,128)(2,1)S(1)}, bf16[256,256]{1,0:T(8,128)(2,1)S(1)}, u32[]{:S(2)}, u32[]{:S(2)}) collective-permute-start(bf16[256,256]{1,0:T(8,128)(2,1)S(1)} %get-tuple-element.36), channel_id=1, source_target_pairs={{0,4},{1,5},{2,6},{3,7},{4,0},{5,1},{6,2},{7,3}} | collective-permute-start | bytes 393224 | tf_op jit(solution)/shard_map/ppermute | solution.py:74
  23.3 19.9 %collective-permute-start = (bf16[256,256]{1,0:T(8,128)(2,1)S(1)}, bf16[256,256]{1,0:T(8,128)(2,1)S(1)}, u32[]{:S(2)}, u32[]{:S(2)}) collective-permute-start(bf16[256,256]{1,0:T(8,128)(2,1)S(1)} %get-tuple-element.36), channel_id=1, source_target_pairs={{0,2},{1,3},{2,4},{3,5},{4,6},{5,7},{6,0},{7,1}} | collective-permute-start | bytes 393224 | tf_op jit(solution)/shard_map/ppermute | solution.py:74
  26.9 15.1 %all-to-all-start = ((s32[32,2,8]{2,1,0:T(2,128)}), s32[32,2,8]{2,1,0:T(2,128)S(1)}, u32[]{:S(2)}, u32[]{:S(2)}) async-start(s32[32,2,8]{2,1,0:T(2,128)} %broadcast_in_dim.156), calls=%async_computation | async-start | bytes 65536 | tf_op jit(solution)/shard_map/all_to_all | solution.py:106
  44.3 19.3 %collective-permute-start.5 = (bf16[256,64]{0,1:T(8,128)(2,1)S(1)}, bf16[256,64]{0,1:T(8,128)(2,1)S(1)}, u32[]{:S(2)}, u32[]{:S(2)}) collective-permute-start(bf16[256,64]{0,1:T(8,128)(2,1)S(1)} %get-tuple-element.27), channel_id=1, source_target_pairs={{0,6},{1,7},{2,0},{3,1},{4,2},{5,3},{6,4},{7,5}} | collective-permute-start | bytes 98312 | tf_op jit(solution)/shard_map/ppermute | solution.py:74
  58.7 7.7 %collective-permute-start.4 = (bf16[256,64]{0,1:T(8,128)(2,1)S(1)}, bf16[256,64]{0,1:T(8,128)(2,1)S(1)}, u32[]{:S(2)}, u32[]{:S(2)}) collective-permute-start(bf16[256,64]{0,1:T(8,128)(2,1)S(1)} %get-tuple-element.28), channel_id=1, source_target_pairs={{0,4},{1,5},{2,6},{3,7},{4,0},{5,1},{6,2},{7,3}} | collective-permute-start | bytes 98312 | tf_op jit(solution)/shard_map/ppermute | solution.py:74
  60.7 8.3 %collective-permute-start.3 = (bf16[256,64]{0,1:T(8,128)(2,1)S(1)}, bf16[256,64]{0,1:T(8,128)(2,1)S(1)}, u32[]{:S(2)}, u32[]{:S(2)}) collective-permute-start(bf16[256,64]{0,1:T(8,128)(2,1)S(1)} %get-tuple-element.29), channel_id=1, source_target_pairs={{0,2},{1,3},{2,4},{3,5},{4,6},{5,7},{6,0},{7,1}} | collective-permute-start | bytes 98312 | tf_op jit(solution)/shard_map/ppermute | solution.py:74
  71.5 10.3 %all-to-all-start.1 = ((bf16[8,2,8192]{2,1,0:T(2,128)(2,1)}), bf16[8,2,8192]{2,1,0:T(2,128)(2,1)S(1)}, u32[]{:S(2)}, u32[]{:S(2)}) async-start(bf16[8,2,8192]{2,1,0:T(2,128)(2,1)} %reshape.691), calls=%async_computation.1 | async-start | bytes 524288 | tf_op jit(solution)/shard_map/all_to_all | solution.py:162
  105.2 2.8 %copy-start = (bf16[2,1024,1024]{2,1,0:T(8,128)(2,1)S(1)}, bf16[2,1024,1024]{2,1,0:T(8,128)(2,1)}, u32[]{:S(2)}) copy-start(bf16[2,1024,1024]{2,1,0:T(8,128)(2,1)} %all-gather.3.cloned.1.call-done) | copy-start | bytes 12582916
  116.2 10.3 %all-to-all-start.2 = ((bf16[8,2,8192]{2,1,0:T(2,128)(2,1)}), bf16[8,2,8192]{2,1,0:T(2,128)(2,1)S(1)}, u32[]{:S(2)}, u32[]{:S(2)}) async-start(bf16[8,2,8192]{2,1,0:T(2,128)(2,1)} %reshape.693), calls=%async_computation.2 | async-start | bytes 524288 | tf_op jit(solution)/shard_map/all_to_all | solution.py:162
  140.0 11.0 %all-to-all-start.3 = ((bf16[8,2,8192]{2,1,0:T(2,128)(2,1)}), bf16[8,2,8192]{2,1,0:T(2,128)(2,1)}, u32[]{:S(2)}, u32[]{:S(2)}) async-start(bf16[8,2,8192]{2,1,0:T(2,128)(2,1)} %reshape.695), calls=%async_computation.3 | async-start | bytes 524288 | tf_op jit(solution)/shard_map/all_to_all | solution.py:162
  160.0 6.2 %copy-start.4 = (f32[1024,64]{0,1:T(8,128)S(1)}, f32[1024,64]{0,1:T(8,128)}, u32[]{:S(2)}) copy-start(f32[1024,64]{0,1:T(8,128)} %get-tuple-element.38) | copy-start | bytes 786436
  162.8 10.3 %all-to-all-start.4 = ((bf16[8,2,8192]{2,1,0:T(2,128)(2,1)}), bf16[8,2,8192]{2,1,0:T(2,128)(2,1)S(1)}, u32[]{:S(2)}, u32[]{:S(2)}) async-start(bf16[8,2,8192]{2,1,0:T(2,128)(2,1)} %reshape.697), calls=%async_computation.4 | async-start | bytes 524288 | tf_op jit(solution)/shard_map/all_to_all | solution.py:162
  175.7 18.2 %all-to-all-start.5 = ((bf16[4,1024,64]{1,2,0:T(8,128)(2,1)}), bf16[4,1024,64]{1,2,0:T(8,128)(2,1)S(1)}, u32[]{:S(2)}, u32[]{:S(2)}) async-start(bf16[4,1024,64]{1,2,0:T(8,128)(2,1)} %pad_maximum_fusion.2), calls=%async_computation.5 | async-start | bytes 1048576 | tf_op jit(solution)/shard_map/all_to_all | solution.py:180
  180.1 15.2 %copy-start.5 = (f32[256,256]{1,0:T(8,128)S(1)}, f32[256,256]{1,0:T(8,128)}, u32[]{:S(2)}) copy-start(f32[256,256]{1,0:T(8,128)} %get-tuple-element.37) | copy-start | bytes 786436
Sparse Core Ops, SparseCore 0:
  13.5 91.6 all-gather.2

commit v15 on v8

--- a/solution.py
+++ b/solution.py
@@ -161,14 +161,16 @@
         acc = acc.at[recv_block[section]].add(incoming.astype(jnp.float32), mode="clip")
     outer = acc[window_blocks:NT].reshape(ABOVE, cols)
 
+    solved_blocks = solved.reshape(n_prow, rows_out, cols)
     final = jnp.concatenate(
         [
-            solved.reshape(n_prow, rows_out, cols),
-            jnp.broadcast_to(outer[None], (n_prow, ABOVE, cols)),
+            solved_blocks.astype(jnp.bfloat16),
+            jnp.broadcast_to(outer.astype(jnp.bfloat16)[None], (n_prow, ABOVE, cols)),
         ],
         axis=1,
     )
     final = lax.all_to_all(final, "prow", split_axis=0, concat_axis=0, tiled=True)
+    final = final.astype(jnp.float32)
     solution_rows = jnp.transpose(final[:, :rows_out], (1, 0, 2)).reshape(rows_out, columns_all)
     solution_rows = jnp.where(level_index == 0, first_rows, solution_rows)
     outer_all = jnp.transpose(final[:, rows_out:], (1, 0, 2)).reshape(ABOVE, columns_all)

time: 210 us -> 195 us (0.929)
  waiting for transfers between devices: 84.8 us -> 76.5 us
  local copies, waits for them, and re-layouts: 28.3 us -> 24.9 us
    all_to_all x1, waiting for transfers between devices: 19.4 us -> 11 us  [per_device(): lax.all_to_all(final, 'prow', split_axis=0, concat_axis=0, tiled=True)]
    unnamed x30 -> x36, local copies, waits for them, and re-layouts: 13.6 us -> 12.7 us
where the time goes in v15:
time: 195 us; the launch traced here: 194 us
  waiting for transfers between devices  76.5 us (39%)
  starting transfers between devices  52.1 us (27%)
  local copies, waits for them, and re-layouts  24.9 us (13%)
  between operations  14.8 us (8%)
  other arithmetic  14.4 us (7%)
  matrix products  11 us (6%)
    ppermute x6, starting transfers between devices, level0_shift(): return lax.ppermute(x, all_axes, pairs)  30.5 us
    all_to_all x4, waiting for transfers between devices, per_device(): lax.all_to_all(sending, ('lvl', 'pcol'), split_axis=0, concat_axis=0, til...  26.3 us
    all_gather x1, waiting for transfers between devices, per_device(): gathered = lax.all_gather(both, 'prow', axis=0)  21.6 us
    all_to_all x4, starting transfers between devices, per_device(): lax.all_to_all(sending, ('lvl', 'pcol'), split_axis=0, concat_axis=0, til...  13.8 us
    unnamed x36, local copies, waits for them, and re-layouts  12.7 us
    all_to_all x1, waiting for transfers between devices, per_device(): lax.all_to_all(jnp.broadcast_to(meta[None], (devices,) + meta.shape), ('l...  12.3 us
    all_to_all x1, waiting for transfers between devices, per_device(): lax.all_to_all(final, 'prow', split_axis=0, concat_axis=0, tiled=True)  11 us
    dot_general x3, matrix products, per_device(): jnp.dot(inv_full, right.astype(jnp.bfloat16), preferred_element_type=jnp....  6.53 us
  transfers between devices with their start and end apart: 13, of which 9 were waited for; matrix products, arithmetic and copies ran while one was open for 5% of the time, Pallas kernels for 0%

profile of v15, /device:TPU:0, one launch (start us, length us, event | category | flops | bytes accessed | tf_op | source)
XLA Modules:
  0.0 193.6 jit_solution(3008463902809049590)
XLA Ops:
  7.2 0.7 select_reduce_fusion.1
  8.0 0.7 select_reduce_fusion.3
  8.7 0.9 select_reduce_fusion.4
  9.7 1.4 bitcast_select_fusion
  11.1 1.0 pad_maximum_fusion
  12.2 0.5 copy-done.1
  12.8 1.1 fusion.53
  13.9 6.9 %collective-permute-start.2 = (bf16[256,256]{1,0:T(8,128)(2,1)S(1)}, bf16[256,256]{1,0:T(8,128)(2,1)S(1)}, u32[]{:S(2)}, u32[]{:S(2)}) collective-permute-start(bf16[256,256]{1,0:T(8,128)(2,1)S(1)} %get-tuple-element.36), channel_id=1, source_target_pairs={{0,6},{1,7},{2,0},{3,1},{4,2},{5,3},{6,4},{7,5}} | collective-permute-start | bytes 393224 | tf_op jit(solution)/shard_map/ppermute | solution.py:69
  20.9 1.9 collective-permute-start.1
  22.8 2.9 %collective-permute-start = (bf16[256,256]{1,0:T(8,128)(2,1)S(1)}, bf16[256,256]{1,0:T(8,128)(2,1)S(1)}, u32[]{:S(2)}, u32[]{:S(2)}) collective-permute-start(bf16[256,256]{1,0:T(8,128)(2,1)S(1)} %get-tuple-element.36), channel_id=1, source_target_pairs={{0,2},{1,3},{2,4},{3,5},{4,6},{5,7},{6,0},{7,1}} | collective-permute-start | bytes 393224 | tf_op jit(solution)/shard_map/ppermute | solution.py:69
  25.7 0.6 broadcast_in_dim.156
  26.4 3.2 %all-to-all-start = ((s32[32,2,8]{2,1,0:T(2,128)}), s32[32,2,8]{2,1,0:T(2,128)S(1)}, u32[]{:S(2)}, u32[]{:S(2)}) async-start(s32[32,2,8]{2,1,0:T(2,128)} %broadcast_in_dim.156), calls=%async_computation | async-start | bytes 65536 | tf_op jit(solution)/shard_map/all_to_all | solution.py:101
  29.8 12.3 %all-to-all-done = s32[32,2,8]{2,1,0:T(2,128)S(1)} async-done(((s32[32,2,8]{2,1,0:T(2,128)}), s32[32,2,8]{2,1,0:T(2,128)S(1)}, u32[]{:S(2)}, u32[]{:S(2)}) %all-to-all-start) | async-done | bytes 2080 | tf_op jit(solution)/shard_map/all_to_all | solution.py:101
  42.3 0.3 convert_reduce_fusion
  43.4 0.6 gather_fusion
  44.0 0.4 convolution_convert_fusion.3
  44.4 13.8 %collective-permute-start.5 = (bf16[256,64]{0,1:T(8,128)(2,1)S(1)}, bf16[256,64]{0,1:T(8,128)(2,1)S(1)}, u32[]{:S(2)}, u32[]{:S(2)}) collective-permute-start(bf16[256,64]{0,1:T(8,128)(2,1)S(1)} %get-tuple-element.27), channel_id=1, source_target_pairs={{0,6},{1,7},{2,0},{3,1},{4,2},{5,3},{6,4},{7,5}} | collective-permute-start | bytes 98312 | tf_op jit(solution)/shard_map/ppermute | solution.py:69
  58.2 1.9 collective-permute-start.4
  60.1 2.9 %collective-permute-start.3 = (bf16[256,64]{0,1:T(8,128)(2,1)S(1)}, bf16[256,64]{0,1:T(8,128)(2,1)S(1)}, u32[]{:S(2)}, u32[]{:S(2)}) collective-permute-start(bf16[256,64]{0,1:T(8,128)(2,1)S(1)} %get-tuple-element.29), channel_id=1, source_target_pairs={{0,2},{1,3},{2,4},{3,5},{4,6},{5,7},{6,0},{7,1}} | collective-permute-start | bytes 98312 | tf_op jit(solution)/shard_map/ppermute | solution.py:69
  63.1 2.6 %collective-permute-done.4 = bf16[256,64]{0,1:T(8,128)(2,1)S(1)} collective-permute-done((bf16[256,64]{0,1:T(8,128)(2,1)S(1)}, bf16[256,64]{0,1:T(8,128)(2,1)S(1)}, u32[]{:S(2)}, u32[]{:S(2)}) %collective-permute-start.4) | collective-permute-done | bytes 32800 | tf_op jit(solution)/shard_map/ppermute | solution.py:69
  65.8 2.7 %collective-permute-done.3 = bf16[256,64]{0,1:T(8,128)(2,1)S(1)} collective-permute-done((bf16[256,64]{0,1:T(8,128)(2,1)S(1)}, bf16[256,64]{0,1:T(8,128)(2,1)S(1)}, u32[]{:S(2)}, u32[]{:S(2)}) %collective-permute-start.3) | collective-permute-done | bytes 32800 | tf_op jit(solution)/shard_map/ppermute | solution.py:69
  68.4 0.6 gather_fusion.1
  69.2 0.7 gather_fusion.2
  69.9 1.1 reshape.625
  71.0 3.4 %all-to-all-start.1 = ((bf16[8,2,8192]{2,1,0:T(2,128)(2,1)}), bf16[8,2,8192]{2,1,0:T(2,128)(2,1)S(1)}, u32[]{:S(2)}, u32[]{:S(2)}) async-start(bf16[8,2,8192]{2,1,0:T(2,128)(2,1)} %reshape.625), calls=%async_computation.1 | async-start | bytes 524288 | tf_op jit(solution)/shard_map/all_to_all | solution.py:157
  74.4 0.6 fusion.52
  75.1 6.2 %all-to-all-done.1 = bf16[8,2,8192]{2,1,0:T(2,128)(2,1)S(1)} async-done(((bf16[8,2,8192]{2,1,0:T(2,128)(2,1)}), bf16[8,2,8192]{2,1,0:T(2,128)(2,1)S(1)}, u32[]{:S(2)}, u32[]{:S(2)}) %all-to-all-start.1) | async-done | bytes 262176 | tf_op jit(solution)/shard_map/all_to_all | solution.py:157
  81.3 0.3 reshape.626
  81.8 1.2 scatter_fusion
  83.0 21.6 %all-gather.3.cloned.1.call-done = bf16[2048,1024]{1,0:T(8,128)(2,1)} async-done(((bf16[512,1024]{1,0:T(8,128)(2,1)}), bf16[2048,1024]{1,0:T(8,128)(2,1)}) %all-gather.3.cloned.1.call-update) | async-done | bytes 4194320 | tf_op jit(solution)/shard_map/all_gather | solution.py:54
  104.7 2.8 %fusion.50 = (bf16[4,256,1024]{2,1,0:T(8,128)(2,1)S(1)}, bf16[4,256,1024]{2,1,0:T(8,128)(2,1)S(1)}) fusion(bf16[4,512,1024]{2,1,0:T(8,128)(2,1)} %bitcast.110), kind=kLoop, calls=%fused_computation.128 | loop fusion | bytes 8388608 | tf_op jit(solution)/shard_map/slice | solution.py:55
  107.5 1.3 copy-done
  108.8 0.8 fusion.11
  109.7 0.8 convolution_convert_fusion.2
  110.7 1.5 gather_fusion.3
  112.2 2.1 %reshape.627 = bf16[8,2,8192]{2,1,0:T(2,128)(2,1)} reshape(bf16[64,32,64]{2,1,0:T(8,128)(2,1)} %gather_fusion.3) | data formatting | bytes 524288
  114.3 3.4 %all-to-all-start.2 = ((bf16[8,2,8192]{2,1,0:T(2,128)(2,1)}), bf16[8,2,8192]{2,1,0:T(2,128)(2,1)S(1)}, u32[]{:S(2)}, u32[]{:S(2)}) async-start(bf16[8,2,8192]{2,1,0:T(2,128)(2,1)} %reshape.627), calls=%async_computation.2 | async-start | bytes 524288 | tf_op jit(solution)/shard_map/all_to_all | solution.py:157
  117.8 6.8 %all-to-all-done.2 = bf16[8,2,8192]{2,1,0:T(2,128)(2,1)S(1)} async-done(((bf16[8,2,8192]{2,1,0:T(2,128)(2,1)}), bf16[8,2,8192]{2,1,0:T(2,128)(2,1)S(1)}, u32[]{:S(2)}, u32[]{:S(2)}) %all-to-all-start.2) | async-done | bytes 262176 | tf_op jit(solution)/shard_map/all_to_all | solution.py:157
  124.6 1.2 reshape.628
  125.8 0.9 slice_convert_fusion.3
  126.7 1.2 scatter_fusion.1
  128.0 2.5 %fusion.14 = bf16[1024,64]{0,1:T(8,128)(2,1)S(1)} fusion(bf16[1024,1024]{1,0:T(8,128)(2,1)} %bitcast.108, f32[1,1,1024,64]{3,2,1,0:T(8,128)S(1)} %bitcast.120, f32[1,1,1024,256]{3,2,1,0:T(8,128)} %param.9, s32[]{:T(128)S(6)} %select_n.233), kind=kOutput, calls=%fused_computation.36 | convolution fusion | flops 134348800 | bytes 3014660 | tf_op jit(solution)/shard_map/dot_general | solution.py:148
  130.5 1.5 convolution_convert_fusion.1
  131.9 1.1 copy.60
  133.0 1.5 gather_fusion.4
  134.6 2.1 %reshape.629 = bf16[8,2,8192]{2,1,0:T(2,128)(2,1)} reshape(bf16[64,32,64]{2,1,0:T(8,128)(2,1)} %gather_fusion.4) | data formatting | bytes 524288
  136.7 3.6 %all-to-all-start.3 = ((bf16[8,2,8192]{2,1,0:T(2,128)(2,1)}), bf16[8,2,8192]{2,1,0:T(2,128)(2,1)S(1)}, u32[]{:S(2)}, u32[]{:S(2)}) async-start(bf16[8,2,8192]{2,1,0:T(2,128)(2,1)} %reshape.629), calls=%async_computation.3 | async-start | bytes 524288 | tf_op jit(solution)/shard_map/all_to_all | solution.py:157
  140.4 6.6 %all-to-all-done.3 = bf16[8,2,8192]{2,1,0:T(2,128)(2,1)S(1)} async-done(((bf16[8,2,8192]{2,1,0:T(2,128)(2,1)}), bf16[8,2,8192]{2,1,0:T(2,128)(2,1)S(1)}, u32[]{:S(2)}, u32[]{:S(2)}) %all-to-all-start.3) | async-done | bytes 262176 | tf_op jit(solution)/shard_map/all_to_all | solution.py:157
  147.0 1.2 reshape.630
  148.2 0.9 slice_convert_fusion.2
  149.1 1.2 scatter_fusion.2
  150.3 3.2 %select_convert_fusion = (bf16[1024,64]{0,1:T(8,128)(2,1)}, bf16[1024,64]{0,1:T(8,128)(2,1)S(1)}) fusion(bf16[1024,64]{0,1:T(8,128)(2,1)S(1)} %fusion.14, bf16[1024,64]{0,1:T(8,128)(2,1)S(1)} %fusion.11, pred[]{:T(512)S(6)} %eq.207, pred[]{:T(512)S(6)} %eq.206, pred[]{:T(512)S(6)} %eq.181, bf16[1024,1024]{1,0:T(8,128)(2,1)} %bitcast.109, ...), kind=kOutput, calls=%fused_computation.41 | convolution fusion | flops 134545408 | bytes 3407879 | tf_op jit(solution)/shard_map/dot_general | solution.py:148
  153.5 0.8 convolution_convert_fusion
  154.5 0.8 gather_fusion.5
  155.3 1.1 reshape.631
  156.4 3.4 %all-to-all-start.4 = ((bf16[8,2,8192]{2,1,0:T(2,128)(2,1)}), bf16[8,2,8192]{2,1,0:T(2,128)(2,1)S(1)}, u32[]{:S(2)}, u32[]{:S(2)}) async-start(bf16[8,2,8192]{2,1,0:T(2,128)(2,1)} %reshape.631), calls=%async_computation.4 | async-start | bytes 524288 | tf_op jit(solution)/shard_map/all_to_all | solution.py:157
  160.0 6.7 %all-to-all-done.4 = bf16[8,2,8192]{2,1,0:T(2,128)(2,1)S(1)} async-done(((bf16[8,2,8192]{2,1,0:T(2,128)(2,1)}), bf16[8,2,8192]{2,1,0:T(2,128)(2,1)S(1)}, u32[]{:S(2)}, u32[]{:S(2)}) %all-to-all-start.4) | async-done | bytes 262176 | tf_op jit(solution)/shard_map/all_to_all | solution.py:157
  166.7 0.3 reshape.632
  167.1 1.2 scatter_fusion.3
  168.5 0.8 pad_maximum_fusion.2
  169.2 4.6 %all-to-all-start.5 = ((bf16[4,768,64]{1,2,0:T(8,128)(2,1)}), bf16[4,768,64]{1,2,0:T(8,128)(2,1)S(1)}, u32[]{:S(2)}, u32[]{:S(2)}) async-start(bf16[4,768,64]{1,2,0:T(8,128)(2,1)} %pad_maximum_fusion.2), calls=%async_computation.5 | async-start | bytes 786432 | tf_op jit(solution)/shard_map/all_to_all | solution.py:172
  173.8 11.0 %all-to-all-done.5 = bf16[4,768,64]{1,2,0:T(8,128)(2,1)S(1)} async-done(((bf16[4,768,64]{1,2,0:T(8,128)(2,1)}), bf16[4,768,64]{1,2,0:T(8,128)(2,1)S(1)}, u32[]{:S(2)}, u32[]{:S(2)}) %all-to-all-start.5) | async-done | bytes 393248 | tf_op jit(solution)/shard_map/all_to_all | solution.py:172
  185.0 1.0 copy.65
  186.0 0.7 select_bitcast_fusion
  (85 shorter events, 3.0 us)
Async XLA Ops:
  7.2 97.5 %all-gather.3.cloned.1.call-start = ((), (), s32[]{:S(2)}) async-start(), calls=%async_computation.6 | async-start | bytes 5242880 | tf_op jit(solution)/shard_map/all_gather | solution.py:54
  11.1 1.6 copy-start.1
  11.1 1.7 copy-start.3
  11.1 14.6 %copy-start.11 = (s32[1,1,8]{2,1,0:T(1,128)S(1)}, s32[1,1,8]{2,1,0:T(1,128)}, u32[]{:S(2)}) copy-start(s32[1,1,8]{2,1,0:T(1,128)} %param.14) | copy-start | bytes 100
  11.1 14.6 %copy-start.12 = (s32[1,1,8]{2,1,0:T(1,128)S(1)}, s32[1,1,8]{2,1,0:T(1,128)}, u32[]{:S(2)}) copy-start(s32[1,1,8]{2,1,0:T(1,128)} %param.13) | copy-start | bytes 100
  12.2 17.5 %copy-start.4 = (bf16[1,1,8,32,1024]{4,3,2,1,0:T(8,128)(2,1)S(1)}, bf16[1,1,8,32,1024]{4,3,2,1,0:T(8,128)(2,1)}, u32[]{:S(2)}) copy-start(bf16[1,1,8,32,1024]{4,3,2,1,0:T(8,128)(2,1)} %param.11) | copy-start | bytes 1572868
  13.9 29.4 %collective-permute-start.2 = (bf16[256,256]{1,0:T(8,128)(2,1)S(1)}, bf16[256,256]{1,0:T(8,128)(2,1)S(1)}, u32[]{:S(2)}, u32[]{:S(2)}) collective-permute-start(bf16[256,256]{1,0:T(8,128)(2,1)S(1)} %get-tuple-element.36), channel_id=1, source_target_pairs={{0,6},{1,7},{2,0},{3,1},{4,2},{5,3},{6,4},{7,5}} | collective-permute-start | bytes 393224 | tf_op jit(solution)/shard_map/ppermute | solution.py:69
  20.9 22.4 %collective-permute-start.1 = (bf16[256,256]{1,0:T(8,128)(2,1)S(1)}, bf16[256,256]{1,0:T(8,128)(2,1)S(1)}, u32[]{:S(2)}, u32[]{:S(2)}) collective-permute-start(bf16[256,256]{1,0:T(8,128)(2,1)S(1)} %get-tuple-element.36), channel_id=1, source_target_pairs={{0,4},{1,5},{2,6},{3,7},{4,0},{5,1},{6,2},{7,3}} | collective-permute-start | bytes 393224 | tf_op jit(solution)/shard_map/ppermute | solution.py:69
  22.8 20.5 %collective-permute-start = (bf16[256,256]{1,0:T(8,128)(2,1)S(1)}, bf16[256,256]{1,0:T(8,128)(2,1)S(1)}, u32[]{:S(2)}, u32[]{:S(2)}) collective-permute-start(bf16[256,256]{1,0:T(8,128)(2,1)S(1)} %get-tuple-element.36), channel_id=1, source_target_pairs={{0,2},{1,3},{2,4},{3,5},{4,6},{5,7},{6,0},{7,1}} | collective-permute-start | bytes 393224 | tf_op jit(solution)/shard_map/ppermute | solution.py:69
  26.4 15.7 %all-to-all-start = ((s32[32,2,8]{2,1,0:T(2,128)}), s32[32,2,8]{2,1,0:T(2,128)S(1)}, u32[]{:S(2)}, u32[]{:S(2)}) async-start(s32[32,2,8]{2,1,0:T(2,128)} %broadcast_in_dim.156), calls=%async_computation | async-start | bytes 65536 | tf_op jit(solution)/shard_map/all_to_all | solution.py:101
  44.4 18.8 %collective-permute-start.5 = (bf16[256,64]{0,1:T(8,128)(2,1)S(1)}, bf16[256,64]{0,1:T(8,128)(2,1)S(1)}, u32[]{:S(2)}, u32[]{:S(2)}) collective-permute-start(bf16[256,64]{0,1:T(8,128)(2,1)S(1)} %get-tuple-element.27), channel_id=1, source_target_pairs={{0,6},{1,7},{2,0},{3,1},{4,2},{5,3},{6,4},{7,5}} | collective-permute-start | bytes 98312 | tf_op jit(solution)/shard_map/ppermute | solution.py:69
  58.2 7.5 %collective-permute-start.4 = (bf16[256,64]{0,1:T(8,128)(2,1)S(1)}, bf16[256,64]{0,1:T(8,128)(2,1)S(1)}, u32[]{:S(2)}, u32[]{:S(2)}) collective-permute-start(bf16[256,64]{0,1:T(8,128)(2,1)S(1)} %get-tuple-element.28), channel_id=1, source_target_pairs={{0,4},{1,5},{2,6},{3,7},{4,0},{5,1},{6,2},{7,3}} | collective-permute-start | bytes 98312 | tf_op jit(solution)/shard_map/ppermute | solution.py:69
  60.1 8.3 %collective-permute-start.3 = (bf16[256,64]{0,1:T(8,128)(2,1)S(1)}, bf16[256,64]{0,1:T(8,128)(2,1)S(1)}, u32[]{:S(2)}, u32[]{:S(2)}) collective-permute-start(bf16[256,64]{0,1:T(8,128)(2,1)S(1)} %get-tuple-element.29), channel_id=1, source_target_pairs={{0,2},{1,3},{2,4},{3,5},{4,6},{5,7},{6,0},{7,1}} | collective-permute-start | bytes 98312 | tf_op jit(solution)/shard_map/ppermute | solution.py:69
  63.1 18.6 %copy-start.7 = (s32[1024]{0:T(1024)}, s32[1024]{0:T(1024)S(1)}, u32[]{:S(2)}) copy-start(s32[1024]{0:T(1024)S(1)} %pad_clamp_fusion) | copy-start | bytes 12292
  71.0 10.3 %all-to-all-start.1 = ((bf16[8,2,8192]{2,1,0:T(2,128)(2,1)}), bf16[8,2,8192]{2,1,0:T(2,128)(2,1)S(1)}, u32[]{:S(2)}, u32[]{:S(2)}) async-start(bf16[8,2,8192]{2,1,0:T(2,128)(2,1)} %reshape.625), calls=%async_computation.1 | async-start | bytes 524288 | tf_op jit(solution)/shard_map/all_to_all | solution.py:157
  104.7 4.1 %copy-start.2 = (f32[1,1,1024,256]{3,2,1,0:T(8,128)S(1)}, f32[1,1,1024,256]{3,2,1,0:T(8,128)}, u32[]{:S(2)}) copy-start(f32[1,1,1024,256]{3,2,1,0:T(8,128)} %param.9) | copy-start | bytes 3145732
  107.4 1.4 copy-start
  109.6 8.1 %copy-start.10 = (s32[2,8]{1,0:T(2,128)S(1)}, s32[2,8]{1,0:T(2,128)}, u32[]{:S(2)}) copy-start(s32[2,8]{1,0:T(2,128)} %get-tuple-element.34) | copy-start | bytes 196
  114.3 10.3 %all-to-all-start.2 = ((bf16[8,2,8192]{2,1,0:T(2,128)(2,1)}), bf16[8,2,8192]{2,1,0:T(2,128)(2,1)S(1)}, u32[]{:S(2)}, u32[]{:S(2)}) async-start(bf16[8,2,8192]{2,1,0:T(2,128)(2,1)} %reshape.627), calls=%async_computation.2 | async-start | bytes 524288 | tf_op jit(solution)/shard_map/all_to_all | solution.py:157
  130.5 9.9 %copy-start.9 = (s32[2,8]{1,0:T(2,128)S(1)}, s32[2,8]{1,0:T(2,128)}, u32[]{:S(2)}) copy-start(s32[2,8]{1,0:T(2,128)} %get-tuple-element.33) | copy-start | bytes 196
  136.7 10.3 %all-to-all-start.3 = ((bf16[8,2,8192]{2,1,0:T(2,128)(2,1)}), bf16[8,2,8192]{2,1,0:T(2,128)(2,1)S(1)}, u32[]{:S(2)}, u32[]{:S(2)}) async-start(bf16[8,2,8192]{2,1,0:T(2,128)(2,1)} %reshape.629), calls=%async_computation.3 | async-start | bytes 524288 | tf_op jit(solution)/shard_map/all_to_all | solution.py:157
  153.5 6.3 %copy-start.8 = (s32[2,8]{1,0:T(2,128)S(1)}, s32[2,8]{1,0:T(2,128)}, u32[]{:S(2)}) copy-start(s32[2,8]{1,0:T(2,128)} %get-tuple-element.32) | copy-start | bytes 196
  153.5 6.4 %copy-start.6 = (bf16[1024,64]{0,1:T(8,128)(2,1)S(1)}, bf16[1024,64]{0,1:T(8,128)(2,1)}, u32[]{:S(2)}) copy-start(bf16[1024,64]{0,1:T(8,128)(2,1)} %get-tuple-element.38) | copy-start | bytes 393220
  156.4 10.3 %all-to-all-start.4 = ((bf16[8,2,8192]{2,1,0:T(2,128)(2,1)}), bf16[8,2,8192]{2,1,0:T(2,128)(2,1)S(1)}, u32[]{:S(2)}, u32[]{:S(2)}) async-start(bf16[8,2,8192]{2,1,0:T(2,128)(2,1)} %reshape.631), calls=%async_computation.4 | async-start | bytes 524288 | tf_op jit(solution)/shard_map/all_to_all | solution.py:157
  169.2 16.8 %copy-start.5 = (f32[256,256]{1,0:T(8,128)S(1)}, f32[256,256]{1,0:T(8,128)}, u32[]{:S(2)}) copy-start(f32[256,256]{1,0:T(8,128)} %get-tuple-element.37) | copy-start | bytes 786436
  169.2 15.6 %all-to-all-start.5 = ((bf16[4,768,64]{1,2,0:T(8,128)(2,1)}), bf16[4,768,64]{1,2,0:T(8,128)(2,1)S(1)}, u32[]{:S(2)}, u32[]{:S(2)}) async-start(bf16[4,768,64]{1,2,0:T(8,128)(2,1)} %pad_maximum_fusion.2), calls=%async_computation.5 | async-start | bytes 786432 | tf_op jit(solution)/shard_map/all_to_all | solution.py:172
Sparse Core Ops, SparseCore 0:
  12.3 92.2 all-gather.2

commit v16 on v15

--- a/solution.py
+++ b/solution.py
@@ -139,7 +139,7 @@
     rhs_cols = lax.dynamic_slice_in_dim(rhs[0, 0], row_index * cols, cols, axis=1)
     window_blocks = width // block_rows
     acc = jnp.zeros((NT + 1, block_rows, cols), jnp.float32)
-    solved = jnp.zeros((width, cols), jnp.float32)
+    solved = jnp.zeros((width, cols), jnp.bfloat16)
     for section in range(n_lvl):
         if section == 0:
             updates = first_cols
@@ -148,9 +148,10 @@
             solved_now = jnp.dot(
                 inv_full, right.astype(jnp.bfloat16), preferred_element_type=jnp.float32
             )
-            solved = jnp.where(level_index == section, solved_now, solved)
+            solved_half = solved_now.astype(jnp.bfloat16)
+            solved = jnp.where(level_index == section, solved_half, solved)
             updates = jnp.dot(
-                tiles_full, solved_now.astype(jnp.bfloat16), preferred_element_type=jnp.float32
+                tiles_full, solved_half, preferred_element_type=jnp.float32
             ).astype(jnp.bfloat16)
         updates = updates.reshape(group_tiles + 1, block_rows, cols)
         sending = jnp.take(updates, send_index, axis=0, mode="clip")
@@ -164,7 +165,7 @@
     solved_blocks = solved.reshape(n_prow, rows_out, cols)
     final = jnp.concatenate(
         [
-            solved_blocks.astype(jnp.bfloat16),
+            solved_blocks,
             jnp.broadcast_to(outer.astype(jnp.bfloat16)[None], (n_prow, ABOVE, cols)),
         ],
         axis=1,

time: 195 us -> 195 us (level)
  no operation moved by 1% of the time
where the time goes in v16:
time: 195 us; the launch traced here: 194 us
  waiting for transfers between devices  76.5 us (39%)
  starting transfers between devices  52.1 us (27%)
  local copies, waits for them, and re-layouts  24.9 us (13%)
  between operations  14.8 us (8%)
  other arithmetic  14.4 us (7%)
  matrix products  11 us (6%)
    ppermute x6, starting transfers between devices, level0_shift(): return lax.ppermute(x, all_axes, pairs)  30.5 us
    all_to_all x4, waiting for transfers between devices, per_device(): lax.all_to_all(sending, ('lvl', 'pcol'), split_axis=0, concat_axis=0, til...  26.3 us
    all_gather x1, waiting for transfers between devices, per_device(): gathered = lax.all_gather(both, 'prow', axis=0)  21.6 us
    all_to_all x4, starting transfers between devices, per_device(): lax.all_to_all(sending, ('lvl', 'pcol'), split_axis=0, concat_axis=0, til...  13.8 us
    unnamed x36, local copies, waits for them, and re-layouts  12.7 us
    all_to_all x1, waiting for transfers between devices, per_device(): lax.all_to_all(jnp.broadcast_to(meta[None], (devices,) + meta.shape), ('l...  12.3 us
    all_to_all x1, waiting for transfers between devices, per_device(): lax.all_to_all(final, 'prow', split_axis=0, concat_axis=0, tiled=True)  11 us
    dot_general x3, matrix products, per_device(): jnp.dot(inv_full, right.astype(jnp.bfloat16), preferred_element_type=jnp....  6.53 us
  transfers between devices with their start and end apart: 13, of which 9 were waited for; matrix products, arithmetic and copies ran while one was open for 5% of the time, Pallas kernels for 0%

profile of v16, /device:TPU:0, one launch (start us, length us, event | category | flops | bytes accessed | tf_op | source)
XLA Modules:
  0.0 193.6 jit_solution(11278334280521298641)
XLA Ops:
  7.2 0.7 select_reduce_fusion.1
  8.0 0.7 select_reduce_fusion.3
  8.7 0.9 select_reduce_fusion.4
  9.7 1.4 bitcast_select_fusion
  11.1 1.0 pad_maximum_fusion
  12.2 0.5 copy-done.1
  12.8 1.1 fusion.47
  13.9 6.9 %collective-permute-start.2 = (bf16[256,256]{1,0:T(8,128)(2,1)S(1)}, bf16[256,256]{1,0:T(8,128)(2,1)S(1)}, u32[]{:S(2)}, u32[]{:S(2)}) collective-permute-start(bf16[256,256]{1,0:T(8,128)(2,1)S(1)} %get-tuple-element.36), channel_id=1, source_target_pairs={{0,6},{1,7},{2,0},{3,1},{4,2},{5,3},{6,4},{7,5}} | collective-permute-start | bytes 393224 | tf_op jit(solution)/shard_map/ppermute | solution.py:69
  20.9 1.9 collective-permute-start.1
  22.8 2.9 %collective-permute-start = (bf16[256,256]{1,0:T(8,128)(2,1)S(1)}, bf16[256,256]{1,0:T(8,128)(2,1)S(1)}, u32[]{:S(2)}, u32[]{:S(2)}) collective-permute-start(bf16[256,256]{1,0:T(8,128)(2,1)S(1)} %get-tuple-element.36), channel_id=1, source_target_pairs={{0,2},{1,3},{2,4},{3,5},{4,6},{5,7},{6,0},{7,1}} | collective-permute-start | bytes 393224 | tf_op jit(solution)/shard_map/ppermute | solution.py:69
  25.7 0.6 broadcast_in_dim.156
  26.4 3.2 %all-to-all-start = ((s32[32,2,8]{2,1,0:T(2,128)}), s32[32,2,8]{2,1,0:T(2,128)S(1)}, u32[]{:S(2)}, u32[]{:S(2)}) async-start(s32[32,2,8]{2,1,0:T(2,128)} %broadcast_in_dim.156), calls=%async_computation | async-start | bytes 65536 | tf_op jit(solution)/shard_map/all_to_all | solution.py:101
  29.8 12.3 %all-to-all-done = s32[32,2,8]{2,1,0:T(2,128)S(1)} async-done(((s32[32,2,8]{2,1,0:T(2,128)}), s32[32,2,8]{2,1,0:T(2,128)S(1)}, u32[]{:S(2)}, u32[]{:S(2)}) %all-to-all-start) | async-done | bytes 2080 | tf_op jit(solution)/shard_map/all_to_all | solution.py:101
  42.3 0.3 convert_reduce_fusion
  43.4 0.6 gather_fusion
  44.0 0.4 convolution_convert_fusion.6
  44.4 13.8 %collective-permute-start.5 = (bf16[256,64]{0,1:T(8,128)(2,1)S(1)}, bf16[256,64]{0,1:T(8,128)(2,1)S(1)}, u32[]{:S(2)}, u32[]{:S(2)}) collective-permute-start(bf16[256,64]{0,1:T(8,128)(2,1)S(1)} %get-tuple-element.27), channel_id=1, source_target_pairs={{0,6},{1,7},{2,0},{3,1},{4,2},{5,3},{6,4},{7,5}} | collective-permute-start | bytes 98312 | tf_op jit(solution)/shard_map/ppermute | solution.py:69
  58.2 1.9 collective-permute-start.4
  60.1 2.9 %collective-permute-start.3 = (bf16[256,64]{0,1:T(8,128)(2,1)S(1)}, bf16[256,64]{0,1:T(8,128)(2,1)S(1)}, u32[]{:S(2)}, u32[]{:S(2)}) collective-permute-start(bf16[256,64]{0,1:T(8,128)(2,1)S(1)} %get-tuple-element.29), channel_id=1, source_target_pairs={{0,2},{1,3},{2,4},{3,5},{4,6},{5,7},{6,0},{7,1}} | collective-permute-start | bytes 98312 | tf_op jit(solution)/shard_map/ppermute | solution.py:69
  63.1 2.6 %collective-permute-done.4 = bf16[256,64]{0,1:T(8,128)(2,1)S(1)} collective-permute-done((bf16[256,64]{0,1:T(8,128)(2,1)S(1)}, bf16[256,64]{0,1:T(8,128)(2,1)S(1)}, u32[]{:S(2)}, u32[]{:S(2)}) %collective-permute-start.4) | collective-permute-done | bytes 32800 | tf_op jit(solution)/shard_map/ppermute | solution.py:69
  65.8 2.7 %collective-permute-done.3 = bf16[256,64]{0,1:T(8,128)(2,1)S(1)} collective-permute-done((bf16[256,64]{0,1:T(8,128)(2,1)S(1)}, bf16[256,64]{0,1:T(8,128)(2,1)S(1)}, u32[]{:S(2)}, u32[]{:S(2)}) %collective-permute-start.3) | collective-permute-done | bytes 32800 | tf_op jit(solution)/shard_map/ppermute | solution.py:69
  68.4 0.6 gather_fusion.1
  69.2 0.7 gather_fusion.2
  69.9 1.1 reshape.627
  71.0 3.4 %all-to-all-start.1 = ((bf16[8,2,8192]{2,1,0:T(2,128)(2,1)}), bf16[8,2,8192]{2,1,0:T(2,128)(2,1)S(1)}, u32[]{:S(2)}, u32[]{:S(2)}) async-start(bf16[8,2,8192]{2,1,0:T(2,128)(2,1)} %reshape.627), calls=%async_computation.1 | async-start | bytes 524288 | tf_op jit(solution)/shard_map/all_to_all | solution.py:158
  74.4 0.6 fusion.46
  75.1 6.2 %all-to-all-done.1 = bf16[8,2,8192]{2,1,0:T(2,128)(2,1)S(1)} async-done(((bf16[8,2,8192]{2,1,0:T(2,128)(2,1)}), bf16[8,2,8192]{2,1,0:T(2,128)(2,1)S(1)}, u32[]{:S(2)}, u32[]{:S(2)}) %all-to-all-start.1) | async-done | bytes 262176 | tf_op jit(solution)/shard_map/all_to_all | solution.py:158
  81.3 0.3 reshape.628
  81.8 1.2 scatter_fusion
  83.0 21.6 %all-gather.3.cloned.1.call-done = bf16[2048,1024]{1,0:T(8,128)(2,1)} async-done(((bf16[512,1024]{1,0:T(8,128)(2,1)}), bf16[2048,1024]{1,0:T(8,128)(2,1)}) %all-gather.3.cloned.1.call-update) | async-done | bytes 4194320 | tf_op jit(solution)/shard_map/all_gather | solution.py:54
  104.7 2.8 %fusion.44 = (bf16[4,256,1024]{2,1,0:T(8,128)(2,1)S(1)}, bf16[4,256,1024]{2,1,0:T(8,128)(2,1)S(1)}) fusion(bf16[4,512,1024]{2,1,0:T(8,128)(2,1)} %bitcast.110), kind=kLoop, calls=%fused_computation.125 | loop fusion | bytes 8388608 | tf_op jit(solution)/shard_map/slice | solution.py:56
  107.5 1.3 copy-done
  108.8 0.8 convolution_convert_fusion.5
  109.7 0.8 convolution_convert_fusion.2
  110.7 1.5 gather_fusion.3
  112.2 2.1 %reshape.629 = bf16[8,2,8192]{2,1,0:T(2,128)(2,1)} reshape(bf16[64,32,64]{2,1,0:T(8,128)(2,1)} %gather_fusion.3) | data formatting | bytes 524288
  114.3 3.4 %all-to-all-start.2 = ((bf16[8,2,8192]{2,1,0:T(2,128)(2,1)}), bf16[8,2,8192]{2,1,0:T(2,128)(2,1)S(1)}, u32[]{:S(2)}, u32[]{:S(2)}) async-start(bf16[8,2,8192]{2,1,0:T(2,128)(2,1)} %reshape.629), calls=%async_computation.2 | async-start | bytes 524288 | tf_op jit(solution)/shard_map/all_to_all | solution.py:158
  117.8 6.8 %all-to-all-done.2 = bf16[8,2,8192]{2,1,0:T(2,128)(2,1)S(1)} async-done(((bf16[8,2,8192]{2,1,0:T(2,128)(2,1)}), bf16[8,2,8192]{2,1,0:T(2,128)(2,1)S(1)}, u32[]{:S(2)}, u32[]{:S(2)}) %all-to-all-start.2) | async-done | bytes 262176 | tf_op jit(solution)/shard_map/all_to_all | solution.py:158
  124.6 1.2 reshape.630
  125.8 0.9 slice_convert_fusion.3
  126.7 1.2 scatter_fusion.1
  128.0 2.5 %convolution_convert_fusion.4 = bf16[1024,64]{0,1:T(8,128)(2,1)S(1)} fusion(bf16[1024,1024]{1,0:T(8,128)(2,1)} %bitcast.108, f32[1,1,1024,64]{3,2,1,0:T(8,128)S(1)} %bitcast.120, f32[1,1,1024,256]{3,2,1,0:T(8,128)} %param.9, s32[]{:T(128)S(6)} %select_n.233), kind=kOutput, calls=%fused_computation.17 | convolution fusion | flops 134414336 | bytes 3014660 | tf_op jit(solution)/shard_map/dot_general | solution.py:148
  130.5 1.5 convolution_convert_fusion.1
  131.9 1.1 copy.60
  133.0 1.5 gather_fusion.4
  134.6 2.1 %reshape.631 = bf16[8,2,8192]{2,1,0:T(2,128)(2,1)} reshape(bf16[64,32,64]{2,1,0:T(8,128)(2,1)} %gather_fusion.4) | data formatting | bytes 524288
  136.7 3.6 %all-to-all-start.3 = ((bf16[8,2,8192]{2,1,0:T(2,128)(2,1)}), bf16[8,2,8192]{2,1,0:T(2,128)(2,1)S(1)}, u32[]{:S(2)}, u32[]{:S(2)}) async-start(bf16[8,2,8192]{2,1,0:T(2,128)(2,1)} %reshape.631), calls=%async_computation.3 | async-start | bytes 524288 | tf_op jit(solution)/shard_map/all_to_all | solution.py:158
  140.4 6.6 %all-to-all-done.3 = bf16[8,2,8192]{2,1,0:T(2,128)(2,1)S(1)} async-done(((bf16[8,2,8192]{2,1,0:T(2,128)(2,1)}), bf16[8,2,8192]{2,1,0:T(2,128)(2,1)S(1)}, u32[]{:S(2)}, u32[]{:S(2)}) %all-to-all-start.3) | async-done | bytes 262176 | tf_op jit(solution)/shard_map/all_to_all | solution.py:158
  147.0 1.2 reshape.632
  148.2 0.9 slice_convert_fusion.2
  149.1 1.2 scatter_fusion.2
  150.3 3.2 %select_select_fusion = (bf16[1024,64]{0,1:T(8,128)(2,1)}, bf16[1024,64]{0,1:T(8,128)(2,1)S(1)}) fusion(bf16[1024,64]{0,1:T(8,128)(2,1)S(1)} %convolution_convert_fusion.4, bf16[1024,64]{0,1:T(8,128)(2,1)S(1)} %convolution_convert_fusion.5, pred[]{:T(512)S(6)} %eq.207, pred[]{:T(512)S(6)} %eq.206, pred[]{:T(512)S(6)} %eq.181, ...), kind=kOutput, calls=%fused_computation.48 | convolution fusion | flops 134610944 | bytes 3407879 | tf_op jit(solution)/shard_map/dot_general | solution.py:148
  153.5 0.8 convolution_convert_fusion
  154.5 0.8 gather_fusion.5
  155.3 1.1 reshape.633
  156.4 3.4 %all-to-all-start.4 = ((bf16[8,2,8192]{2,1,0:T(2,128)(2,1)}), bf16[8,2,8192]{2,1,0:T(2,128)(2,1)S(1)}, u32[]{:S(2)}, u32[]{:S(2)}) async-start(bf16[8,2,8192]{2,1,0:T(2,128)(2,1)} %reshape.633), calls=%async_computation.4 | async-start | bytes 524288 | tf_op jit(solution)/shard_map/all_to_all | solution.py:158
  160.0 6.7 %all-to-all-done.4 = bf16[8,2,8192]{2,1,0:T(2,128)(2,1)S(1)} async-done(((bf16[8,2,8192]{2,1,0:T(2,128)(2,1)}), bf16[8,2,8192]{2,1,0:T(2,128)(2,1)S(1)}, u32[]{:S(2)}, u32[]{:S(2)}) %all-to-all-start.4) | async-done | bytes 262176 | tf_op jit(solution)/shard_map/all_to_all | solution.py:158
  166.7 0.3 reshape.634
  167.1 1.2 scatter_fusion.3
  168.5 0.8 pad_maximum_fusion.2
  169.2 4.6 %all-to-all-start.5 = ((bf16[4,768,64]{1,2,0:T(8,128)(2,1)}), bf16[4,768,64]{1,2,0:T(8,128)(2,1)S(1)}, u32[]{:S(2)}, u32[]{:S(2)}) async-start(bf16[4,768,64]{1,2,0:T(8,128)(2,1)} %pad_maximum_fusion.2), calls=%async_computation.5 | async-start | bytes 786432 | tf_op jit(solution)/shard_map/all_to_all | solution.py:173
  173.8 11.0 %all-to-all-done.5 = bf16[4,768,64]{1,2,0:T(8,128)(2,1)S(1)} async-done(((bf16[4,768,64]{1,2,0:T(8,128)(2,1)}), bf16[4,768,64]{1,2,0:T(8,128)(2,1)S(1)}, u32[]{:S(2)}, u32[]{:S(2)}) %all-to-all-start.5) | async-done | bytes 393248 | tf_op jit(solution)/shard_map/all_to_all | solution.py:173
  185.0 1.0 copy.65
  186.0 0.7 select_bitcast_fusion
  (85 shorter events, 3.0 us)
Async XLA Ops:
  7.2 97.5 %all-gather.3.cloned.1.call-start = ((), (), s32[]{:S(2)}) async-start(), calls=%async_computation.6 | async-start | bytes 5242880 | tf_op jit(solution)/shard_map/all_gather | solution.py:54
  11.1 1.6 copy-start.1
  11.1 1.7 copy-start.3
  11.1 14.6 %copy-start.11 = (s32[1,1,8]{2,1,0:T(1,128)S(1)}, s32[1,1,8]{2,1,0:T(1,128)}, u32[]{:S(2)}) copy-start(s32[1,1,8]{2,1,0:T(1,128)} %param.14) | copy-start | bytes 100
  11.1 14.6 %copy-start.12 = (s32[1,1,8]{2,1,0:T(1,128)S(1)}, s32[1,1,8]{2,1,0:T(1,128)}, u32[]{:S(2)}) copy-start(s32[1,1,8]{2,1,0:T(1,128)} %param.13) | copy-start | bytes 100
  12.2 17.5 %copy-start.4 = (bf16[1,1,8,32,1024]{4,3,2,1,0:T(8,128)(2,1)S(1)}, bf16[1,1,8,32,1024]{4,3,2,1,0:T(8,128)(2,1)}, u32[]{:S(2)}) copy-start(bf16[1,1,8,32,1024]{4,3,2,1,0:T(8,128)(2,1)} %param.11) | copy-start | bytes 1572868
  13.9 29.4 %collective-permute-start.2 = (bf16[256,256]{1,0:T(8,128)(2,1)S(1)}, bf16[256,256]{1,0:T(8,128)(2,1)S(1)}, u32[]{:S(2)}, u32[]{:S(2)}) collective-permute-start(bf16[256,256]{1,0:T(8,128)(2,1)S(1)} %get-tuple-element.36), channel_id=1, source_target_pairs={{0,6},{1,7},{2,0},{3,1},{4,2},{5,3},{6,4},{7,5}} | collective-permute-start | bytes 393224 | tf_op jit(solution)/shard_map/ppermute | solution.py:69
  20.9 22.4 %collective-permute-start.1 = (bf16[256,256]{1,0:T(8,128)(2,1)S(1)}, bf16[256,256]{1,0:T(8,128)(2,1)S(1)}, u32[]{:S(2)}, u32[]{:S(2)}) collective-permute-start(bf16[256,256]{1,0:T(8,128)(2,1)S(1)} %get-tuple-element.36), channel_id=1, source_target_pairs={{0,4},{1,5},{2,6},{3,7},{4,0},{5,1},{6,2},{7,3}} | collective-permute-start | bytes 393224 | tf_op jit(solution)/shard_map/ppermute | solution.py:69
  22.8 20.5 %collective-permute-start = (bf16[256,256]{1,0:T(8,128)(2,1)S(1)}, bf16[256,256]{1,0:T(8,128)(2,1)S(1)}, u32[]{:S(2)}, u32[]{:S(2)}) collective-permute-start(bf16[256,256]{1,0:T(8,128)(2,1)S(1)} %get-tuple-element.36), channel_id=1, source_target_pairs={{0,2},{1,3},{2,4},{3,5},{4,6},{5,7},{6,0},{7,1}} | collective-permute-start | bytes 393224 | tf_op jit(solution)/shard_map/ppermute | solution.py:69
  26.4 15.7 %all-to-all-start = ((s32[32,2,8]{2,1,0:T(2,128)}), s32[32,2,8]{2,1,0:T(2,128)S(1)}, u32[]{:S(2)}, u32[]{:S(2)}) async-start(s32[32,2,8]{2,1,0:T(2,128)} %broadcast_in_dim.156), calls=%async_computation | async-start | bytes 65536 | tf_op jit(solution)/shard_map/all_to_all | solution.py:101
  44.4 18.8 %collective-permute-start.5 = (bf16[256,64]{0,1:T(8,128)(2,1)S(1)}, bf16[256,64]{0,1:T(8,128)(2,1)S(1)}, u32[]{:S(2)}, u32[]{:S(2)}) collective-permute-start(bf16[256,64]{0,1:T(8,128)(2,1)S(1)} %get-tuple-element.27), channel_id=1, source_target_pairs={{0,6},{1,7},{2,0},{3,1},{4,2},{5,3},{6,4},{7,5}} | collective-permute-start | bytes 98312 | tf_op jit(solution)/shard_map/ppermute | solution.py:69
  58.2 7.5 %collective-permute-start.4 = (bf16[256,64]{0,1:T(8,128)(2,1)S(1)}, bf16[256,64]{0,1:T(8,128)(2,1)S(1)}, u32[]{:S(2)}, u32[]{:S(2)}) collective-permute-start(bf16[256,64]{0,1:T(8,128)(2,1)S(1)} %get-tuple-element.28), channel_id=1, source_target_pairs={{0,4},{1,5},{2,6},{3,7},{4,0},{5,1},{6,2},{7,3}} | collective-permute-start | bytes 98312 | tf_op jit(solution)/shard_map/ppermute | solution.py:69
  60.1 8.3 %collective-permute-start.3 = (bf16[256,64]{0,1:T(8,128)(2,1)S(1)}, bf16[256,64]{0,1:T(8,128)(2,1)S(1)}, u32[]{:S(2)}, u32[]{:S(2)}) collective-permute-start(bf16[256,64]{0,1:T(8,128)(2,1)S(1)} %get-tuple-element.29), channel_id=1, source_target_pairs={{0,2},{1,3},{2,4},{3,5},{4,6},{5,7},{6,0},{7,1}} | collective-permute-start | bytes 98312 | tf_op jit(solution)/shard_map/ppermute | solution.py:69
  63.1 18.6 %copy-start.7 = (s32[1024]{0:T(1024)}, s32[1024]{0:T(1024)S(1)}, u32[]{:S(2)}) copy-start(s32[1024]{0:T(1024)S(1)} %pad_clamp_fusion) | copy-start | bytes 12292
  71.0 10.3 %all-to-all-start.1 = ((bf16[8,2,8192]{2,1,0:T(2,128)(2,1)}), bf16[8,2,8192]{2,1,0:T(2,128)(2,1)S(1)}, u32[]{:S(2)}, u32[]{:S(2)}) async-start(bf16[8,2,8192]{2,1,0:T(2,128)(2,1)} %reshape.627), calls=%async_computation.1 | async-start | bytes 524288 | tf_op jit(solution)/shard_map/all_to_all | solution.py:158
  104.7 4.1 %copy-start.2 = (f32[1,1,1024,256]{3,2,1,0:T(8,128)S(1)}, f32[1,1,1024,256]{3,2,1,0:T(8,128)}, u32[]{:S(2)}) copy-start(f32[1,1,1024,256]{3,2,1,0:T(8,128)} %param.9) | copy-start | bytes 3145732
  107.4 1.4 copy-start
  109.6 8.1 %copy-start.10 = (s32[2,8]{1,0:T(2,128)S(1)}, s32[2,8]{1,0:T(2,128)}, u32[]{:S(2)}) copy-start(s32[2,8]{1,0:T(2,128)} %get-tuple-element.34) | copy-start | bytes 196
  114.3 10.3 %all-to-all-start.2 = ((bf16[8,2,8192]{2,1,0:T(2,128)(2,1)}), bf16[8,2,8192]{2,1,0:T(2,128)(2,1)S(1)}, u32[]{:S(2)}, u32[]{:S(2)}) async-start(bf16[8,2,8192]{2,1,0:T(2,128)(2,1)} %reshape.629), calls=%async_computation.2 | async-start | bytes 524288 | tf_op jit(solution)/shard_map/all_to_all | solution.py:158
  130.5 9.9 %copy-start.9 = (s32[2,8]{1,0:T(2,128)S(1)}, s32[2,8]{1,0:T(2,128)}, u32[]{:S(2)}) copy-start(s32[2,8]{1,0:T(2,128)} %get-tuple-element.33) | copy-start | bytes 196
  136.7 10.3 %all-to-all-start.3 = ((bf16[8,2,8192]{2,1,0:T(2,128)(2,1)}), bf16[8,2,8192]{2,1,0:T(2,128)(2,1)S(1)}, u32[]{:S(2)}, u32[]{:S(2)}) async-start(bf16[8,2,8192]{2,1,0:T(2,128)(2,1)} %reshape.631), calls=%async_computation.3 | async-start | bytes 524288 | tf_op jit(solution)/shard_map/all_to_all | solution.py:158
  153.5 6.3 %copy-start.8 = (s32[2,8]{1,0:T(2,128)S(1)}, s32[2,8]{1,0:T(2,128)}, u32[]{:S(2)}) copy-start(s32[2,8]{1,0:T(2,128)} %get-tuple-element.32) | copy-start | bytes 196
  153.5 6.4 %copy-start.6 = (bf16[1024,64]{0,1:T(8,128)(2,1)S(1)}, bf16[1024,64]{0,1:T(8,128)(2,1)}, u32[]{:S(2)}) copy-start(bf16[1024,64]{0,1:T(8,128)(2,1)} %get-tuple-element.38) | copy-start | bytes 393220
  156.4 10.3 %all-to-all-start.4 = ((bf16[8,2,8192]{2,1,0:T(2,128)(2,1)}), bf16[8,2,8192]{2,1,0:T(2,128)(2,1)S(1)}, u32[]{:S(2)}, u32[]{:S(2)}) async-start(bf16[8,2,8192]{2,1,0:T(2,128)(2,1)} %reshape.633), calls=%async_computation.4 | async-start | bytes 524288 | tf_op jit(solution)/shard_map/all_to_all | solution.py:158
  169.2 16.8 %copy-start.5 = (f32[256,256]{1,0:T(8,128)S(1)}, f32[256,256]{1,0:T(8,128)}, u32[]{:S(2)}) copy-start(f32[256,256]{1,0:T(8,128)} %get-tuple-element.37) | copy-start | bytes 786436
  169.2 15.6 %all-to-all-start.5 = ((bf16[4,768,64]{1,2,0:T(8,128)(2,1)}), bf16[4,768,64]{1,2,0:T(8,128)(2,1)S(1)}, u32[]{:S(2)}, u32[]{:S(2)}) async-start(bf16[4,768,64]{1,2,0:T(8,128)(2,1)} %pad_maximum_fusion.2), calls=%async_computation.5 | async-start | bytes 786432 | tf_op jit(solution)/shard_map/all_to_all | solution.py:173
Sparse Core Ops, SparseCore 0:
  12.3 92.2 all-gather.2

commit v17 on v15

--- a/solution.py
+++ b/solution.py
@@ -50,12 +50,15 @@
         jnp.zeros((), jnp.bfloat16),
     ).reshape(tile_count * block_rows, width)
 
-    both = jnp.concatenate([inverse, tiles_used], axis=0)
-    gathered = lax.all_gather(both, "prow", axis=0)
-    inv_full = gathered[:, :row_count].reshape(n_prow * row_count, width)
-    tiles_full = gathered[:, row_count:].reshape(group_tiles * block_rows, width)
-    tiles_full = jnp.concatenate(
-        [tiles_full, jnp.zeros((block_rows, width), jnp.bfloat16)], axis=0
+    raw = jnp.concatenate(
+        [diag_inverse[0, 0], off_tiles[0, 0].reshape(tile_count * block_rows, width)], axis=0
+    )
+    gathered = lax.all_gather(raw, "prow", axis=0)
+    zero = jnp.zeros((), jnp.bfloat16)
+    inv_full = jnp.where(
+        col_super[:, None] == col_super[None, :],
+        gathered[:, :row_count].reshape(n_prow * row_count, width),
+        zero,
     )
 
     all_axes = ("lvl", "prow", "pcol")
@@ -96,7 +99,7 @@
         [first_cols, jnp.zeros((block_rows, cols), jnp.bfloat16)], axis=0
     )
 
-    meta = jnp.stack([off_device[0, 0], off_block[0, 0]], axis=0)
+    meta = jnp.stack([off_device[0, 0], off_block[0, 0], offdiag_block_panel[0, 0]], axis=0)
     devices = n_lvl * n_prow * n_pcol
     meta = lax.all_to_all(
         jnp.broadcast_to(meta[None], (devices,) + meta.shape),
@@ -105,9 +108,18 @@
         concat_axis=0,
         tiled=True,
     )
-    meta = meta.reshape(n_lvl, n_prow, n_pcol, 2, tile_count)
-    meta = jnp.transpose(meta, (0, 2, 1, 3, 4)).reshape(groups, n_prow, 2, tile_count)
+    meta = meta.reshape(n_lvl, n_prow, n_pcol, 3, tile_count)
+    meta = jnp.transpose(meta, (0, 2, 1, 3, 4)).reshape(groups, n_prow, 3, tile_count)
     target = meta[:, :, 0, :].reshape(groups, group_tiles)
+    group_panels = jnp.take(meta[:, :, 2, :].reshape(groups, group_tiles), my_group, axis=0)
+    tiles_full = jnp.where(
+        col_super[None, None, :] == super_of(group_panels)[:, None, None],
+        gathered[:, row_count:].reshape(group_tiles, block_rows, width),
+        zero,
+    ).reshape(group_tiles * block_rows, width)
+    tiles_full = jnp.concatenate(
+        [tiles_full, jnp.zeros((block_rows, width), jnp.bfloat16)], axis=0
+    )
     block = meta[:, :, 1, :].reshape(groups, group_tiles)
     tile_ids = jnp.arange(group_tiles, dtype=jnp.int32)
     source_row = tile_ids // tile_count

time: 195 us -> 191 us (0.979)
  local copies, waits for them, and re-layouts: 24.9 us -> 21.2 us
    select_n x0 -> x3, other arithmetic: none -> 2.89 us  [the longest x1 2.53 us: per_device(): jnp.where(col_super[:, None] == col_super[None, :], gathered[:, :row_coun...]
    slice x1 -> x2, local copies, waits for them, and re-layouts: 2.78 us -> 0.01 us  [per_device(): meta[:, :, 2, :].reshape(groups, group_tiles)]
    unnamed x36 -> x42, local copies, waits for them, and re-layouts: 12.7 us -> 11.6 us
where the time goes in v17:
time: 191 us; the launch traced here: 189 us
  waiting for transfers between devices  76.2 us (40%)
  starting transfers between devices  52.4 us (27%)
  local copies, waits for them, and re-layouts  21.2 us (11%)
  other arithmetic  15.3 us (8%)
  between operations  14.9 us (8%)
  matrix products  9.4 us (5%)
    ppermute x6, starting transfers between devices, level0_shift(): return lax.ppermute(x, all_axes, pairs)  30.7 us
    all_to_all x4, waiting for transfers between devices, per_device(): lax.all_to_all(sending, ('lvl', 'pcol'), split_axis=0, concat_axis=0, til...  26.8 us
    all_gather x1, waiting for transfers between devices, per_device(): gathered = lax.all_gather(raw, 'prow', axis=0)  20.4 us
    all_to_all x4, starting transfers between devices, per_device(): lax.all_to_all(sending, ('lvl', 'pcol'), split_axis=0, concat_axis=0, til...  13.8 us
    all_to_all x1, waiting for transfers between devices, per_device(): lax.all_to_all(jnp.broadcast_to(meta[None], (devices,) + meta.shape), ('l...  12.4 us
    unnamed x42, local copies, waits for them, and re-layouts  11.6 us
    all_to_all x1, waiting for transfers between devices, per_device(): lax.all_to_all(final, 'prow', split_axis=0, concat_axis=0, tiled=True)  11 us
    ppermute x6, waiting for transfers between devices, level0_shift(): return lax.ppermute(x, all_axes, pairs)  5.61 us
  transfers between devices with their start and end apart: 13, of which 9 were waited for; matrix products, arithmetic and copies ran while one was open for 5% of the time, Pallas kernels for 0%

profile of v17, /device:TPU:0, one launch (start us, length us, event | category | flops | bytes accessed | tf_op | source)
XLA Modules:
  0.0 189.4 jit_solution(12462553433890804793)
XLA Ops:
  7.3 2.3 %pad_maximum_fusion = bf16[512,1024]{1,0:T(8,128)(2,1)} fusion(bf16[256,1024]{1,0:T(8,128)(2,1)} %bitcast.121, bf16[256,1024]{1,0:T(8,128)(2,1)} %bitcast.117), kind=kLoop, calls=%fused_computation.19 | loop fusion | flops 2097152 | bytes 2097152 | tf_op jit(solution)/shard_map/concatenate | solution.py:53
  9.9 1.1 fusion.53
  10.9 6.9 %collective-permute-start.2 = (bf16[256,256]{1,0:T(8,128)(2,1)S(1)}, bf16[256,256]{1,0:T(8,128)(2,1)S(1)}, u32[]{:S(2)}, u32[]{:S(2)}) collective-permute-start(bf16[256,256]{1,0:T(8,128)(2,1)S(1)} %get-tuple-element.37), channel_id=1, source_target_pairs={{0,6},{1,7},{2,0},{3,1},{4,2},{5,3},{6,4},{7,5}} | collective-permute-start | bytes 393224 | tf_op jit(solution)/shard_map/ppermute | solution.py:72
  17.9 1.9 %collective-permute-start.1 = (bf16[256,256]{1,0:T(8,128)(2,1)S(1)}, bf16[256,256]{1,0:T(8,128)(2,1)S(1)}, u32[]{:S(2)}, u32[]{:S(2)}) collective-permute-start(bf16[256,256]{1,0:T(8,128)(2,1)S(1)} %get-tuple-element.37), channel_id=1, source_target_pairs={{0,4},{1,5},{2,6},{3,7},{4,0},{5,1},{6,2},{7,3}} | collective-permute-start | bytes 393224 | tf_op jit(solution)/shard_map/ppermute | solution.py:72
  19.8 2.9 %collective-permute-start = (bf16[256,256]{1,0:T(8,128)(2,1)S(1)}, bf16[256,256]{1,0:T(8,128)(2,1)S(1)}, u32[]{:S(2)}, u32[]{:S(2)}) collective-permute-start(bf16[256,256]{1,0:T(8,128)(2,1)S(1)} %get-tuple-element.37), channel_id=1, source_target_pairs={{0,2},{1,3},{2,4},{3,5},{4,6},{5,7},{6,0},{7,1}} | collective-permute-start | bytes 393224 | tf_op jit(solution)/shard_map/ppermute | solution.py:72
  22.8 0.6 broadcast_in_dim.180
  23.4 3.2 %all-to-all-start = ((s32[32,3,8]{2,1,0:T(4,128)}), s32[32,3,8]{2,1,0:T(4,128)S(1)}, u32[]{:S(2)}, u32[]{:S(2)}) async-start(s32[32,3,8]{2,1,0:T(4,128)} %broadcast_in_dim.180), calls=%async_computation | async-start | bytes 131072 | tf_op jit(solution)/shard_map/all_to_all | solution.py:104
  27.2 12.4 %all-to-all-done = s32[32,3,8]{2,1,0:T(4,128)S(1)} async-done(((s32[32,3,8]{2,1,0:T(4,128)}), s32[32,3,8]{2,1,0:T(4,128)S(1)}, u32[]{:S(2)}, u32[]{:S(2)}) %all-to-all-start) | async-done | bytes 3104 | tf_op jit(solution)/shard_map/all_to_all | solution.py:104
  39.8 0.3 convert_reduce_fusion
  40.1 0.2 fusion.24
  40.3 0.2 select_reduce_fusion
  40.6 0.6 fusion.52
  41.7 0.6 gather_fusion
  42.3 0.4 convolution_convert_fusion.3
  42.7 14.3 %collective-permute-start.5 = (bf16[256,64]{0,1:T(8,128)(2,1)S(1)}, bf16[256,64]{0,1:T(8,128)(2,1)S(1)}, u32[]{:S(2)}, u32[]{:S(2)}) collective-permute-start(bf16[256,64]{0,1:T(8,128)(2,1)S(1)} %get-tuple-element.27), channel_id=1, source_target_pairs={{0,6},{1,7},{2,0},{3,1},{4,2},{5,3},{6,4},{7,5}} | collective-permute-start | bytes 98312 | tf_op jit(solution)/shard_map/ppermute | solution.py:72
  57.0 1.9 %collective-permute-start.4 = (bf16[256,64]{0,1:T(8,128)(2,1)S(1)}, bf16[256,64]{0,1:T(8,128)(2,1)S(1)}, u32[]{:S(2)}, u32[]{:S(2)}) collective-permute-start(bf16[256,64]{0,1:T(8,128)(2,1)S(1)} %get-tuple-element.28), channel_id=1, source_target_pairs={{0,4},{1,5},{2,6},{3,7},{4,0},{5,1},{6,2},{7,3}} | collective-permute-start | bytes 98312 | tf_op jit(solution)/shard_map/ppermute | solution.py:72
  58.9 2.7 %collective-permute-start.3 = (bf16[256,64]{0,1:T(8,128)(2,1)S(1)}, bf16[256,64]{0,1:T(8,128)(2,1)S(1)}, u32[]{:S(2)}, u32[]{:S(2)}) collective-permute-start(bf16[256,64]{0,1:T(8,128)(2,1)S(1)} %get-tuple-element.29), channel_id=1, source_target_pairs={{0,2},{1,3},{2,4},{3,5},{4,6},{5,7},{6,0},{7,1}} | collective-permute-start | bytes 98312 | tf_op jit(solution)/shard_map/ppermute | solution.py:72
  61.7 2.8 %collective-permute-done.4 = bf16[256,64]{0,1:T(8,128)(2,1)S(1)} collective-permute-done((bf16[256,64]{0,1:T(8,128)(2,1)S(1)}, bf16[256,64]{0,1:T(8,128)(2,1)S(1)}, u32[]{:S(2)}, u32[]{:S(2)}) %collective-permute-start.4) | collective-permute-done | bytes 32800 | tf_op jit(solution)/shard_map/ppermute | solution.py:72
  64.4 2.8 %collective-permute-done.3 = bf16[256,64]{0,1:T(8,128)(2,1)S(1)} collective-permute-done((bf16[256,64]{0,1:T(8,128)(2,1)S(1)}, bf16[256,64]{0,1:T(8,128)(2,1)S(1)}, u32[]{:S(2)}, u32[]{:S(2)}) %collective-permute-start.3) | collective-permute-done | bytes 32800 | tf_op jit(solution)/shard_map/ppermute | solution.py:72
  67.3 0.6 gather_fusion.1
  68.1 0.7 gather_fusion.2
  68.8 1.1 reshape.696
  69.9 3.4 %all-to-all-start.1 = ((bf16[8,2,8192]{2,1,0:T(2,128)(2,1)}), bf16[8,2,8192]{2,1,0:T(2,128)(2,1)S(1)}, u32[]{:S(2)}, u32[]{:S(2)}) async-start(bf16[8,2,8192]{2,1,0:T(2,128)(2,1)} %reshape.696), calls=%async_computation.1 | async-start | bytes 524288 | tf_op jit(solution)/shard_map/all_to_all | solution.py:169
  73.5 6.7 %all-to-all-done.1 = bf16[8,2,8192]{2,1,0:T(2,128)(2,1)S(1)} async-done(((bf16[8,2,8192]{2,1,0:T(2,128)(2,1)}), bf16[8,2,8192]{2,1,0:T(2,128)(2,1)S(1)}, u32[]{:S(2)}, u32[]{:S(2)}) %all-to-all-start.1) | async-done | bytes 262176 | tf_op jit(solution)/shard_map/all_to_all | solution.py:169
  80.2 0.3 reshape.697
  80.6 1.2 scatter_fusion
  81.9 20.4 %all-gather.3.cloned.1.call-done = bf16[2048,1024]{1,0:T(8,128)(2,1)} async-done(((bf16[512,1024]{1,0:T(8,128)(2,1)}), bf16[2048,1024]{1,0:T(8,128)(2,1)}) %all-gather.3.cloned.1.call-update) | async-done | bytes 4194320 | tf_op jit(solution)/shard_map/all_gather | solution.py:56
  102.3 2.5 %compare_select_fusion = (bf16[4,256,1024]{2,1,0:T(8,128)(2,1)S(1)}, bf16[4,256,1024]{2,1,0:T(8,128)(2,1)S(1)}) fusion(bf16[4,512,1024]{2,1,0:T(8,128)(2,1)} %bitcast.111, s32[1024]{0:T(1024)S(1)} %select_reduce_fusion.1, s32[4,256]{1,0:T(4,128)S(1)} %eq.225), kind=kLoop, calls=%fused_computation.11 | loop fusion | flops 2097152 | bytes 8396800 | tf_op jit(solution)/shard_map/jit(_where)/select_n | solution.py:58
  104.9 0.3 bitcast_select_fusion
  105.2 0.9 copy-done.4
  106.1 0.8 fusion.11
  106.9 0.8 convolution_convert_fusion.2
  107.8 0.2 copy.62
  107.9 1.5 gather_fusion.3
  109.5 2.1 %reshape.698 = bf16[8,2,8192]{2,1,0:T(2,128)(2,1)} reshape(bf16[64,32,64]{2,1,0:T(8,128)(2,1)} %gather_fusion.3) | data formatting | bytes 524288
  111.6 3.4 %all-to-all-start.2 = ((bf16[8,2,8192]{2,1,0:T(2,128)(2,1)}), bf16[8,2,8192]{2,1,0:T(2,128)(2,1)S(1)}, u32[]{:S(2)}, u32[]{:S(2)}) async-start(bf16[8,2,8192]{2,1,0:T(2,128)(2,1)} %reshape.698), calls=%async_computation.2 | async-start | bytes 524288 | tf_op jit(solution)/shard_map/all_to_all | solution.py:169
  115.2 6.8 %all-to-all-done.2 = bf16[8,2,8192]{2,1,0:T(2,128)(2,1)S(1)} async-done(((bf16[8,2,8192]{2,1,0:T(2,128)(2,1)}), bf16[8,2,8192]{2,1,0:T(2,128)(2,1)S(1)}, u32[]{:S(2)}, u32[]{:S(2)}) %all-to-all-start.2) | async-done | bytes 262176 | tf_op jit(solution)/shard_map/all_to_all | solution.py:169
  121.9 1.2 reshape.699
  123.1 0.9 slice_convert_fusion.3
  124.0 1.2 scatter_fusion.1
  125.3 2.0 %fusion.14 = bf16[1024,64]{0,1:T(8,128)(2,1)S(1)} fusion(bf16[1024,1024]{1,0:T(8,128)(2,1)S(1)} %bitcast.109, f32[1,1,1024,64]{3,2,1,0:T(8,128)S(1)} %bitcast.123, f32[1,1,1024,256]{3,2,1,0:T(8,128)} %param.9, s32[]{:T(128)S(6)} %select_n.246), kind=kOutput, calls=%fused_computation.36 | convolution fusion | flops 134348800 | bytes 3014660 | tf_op jit(solution)/shard_map/dot_general | solution.py:160
  127.3 1.5 convolution_convert_fusion.1
  128.8 1.1 copy.63
  129.9 1.5 gather_fusion.4
  131.4 2.1 %reshape.700 = bf16[8,2,8192]{2,1,0:T(2,128)(2,1)} reshape(bf16[64,32,64]{2,1,0:T(8,128)(2,1)} %gather_fusion.4) | data formatting | bytes 524288
  133.6 3.6 %all-to-all-start.3 = ((bf16[8,2,8192]{2,1,0:T(2,128)(2,1)}), bf16[8,2,8192]{2,1,0:T(2,128)(2,1)S(1)}, u32[]{:S(2)}, u32[]{:S(2)}) async-start(bf16[8,2,8192]{2,1,0:T(2,128)(2,1)} %reshape.700), calls=%async_computation.3 | async-start | bytes 524288 | tf_op jit(solution)/shard_map/all_to_all | solution.py:169
  137.3 6.6 %all-to-all-done.3 = bf16[8,2,8192]{2,1,0:T(2,128)(2,1)S(1)} async-done(((bf16[8,2,8192]{2,1,0:T(2,128)(2,1)}), bf16[8,2,8192]{2,1,0:T(2,128)(2,1)S(1)}, u32[]{:S(2)}, u32[]{:S(2)}) %all-to-all-start.3) | async-done | bytes 262176 | tf_op jit(solution)/shard_map/all_to_all | solution.py:169
  143.9 1.2 reshape.701
  145.0 0.9 slice_convert_fusion.2
  145.9 1.2 scatter_fusion.2
  147.2 2.0 %select_convert_fusion = (bf16[1024,64]{0,1:T(8,128)(2,1)S(1)}, bf16[1024,64]{0,1:T(8,128)(2,1)S(1)}) fusion(bf16[1024,64]{0,1:T(8,128)(2,1)S(1)} %fusion.14, bf16[1024,64]{0,1:T(8,128)(2,1)S(1)} %fusion.11, pred[]{:T(512)S(6)} %eq.257, pred[]{:T(512)S(6)} %eq.256, pred[]{:T(512)S(6)} %eq.224, bf16[1024,1024]{1,0:T(8,128)(2,1)S(1)} %bitcast.110, ...), kind=kOutput, calls=%fused_computation.41 | convolution fusion | flops 134545408 | bytes 3407879 | tf_op jit(solution)/shard_map/dot_general | solution.py:160
  149.3 0.8 convolution_convert_fusion
  150.1 0.2 copy.64
  150.3 0.8 gather_fusion.5
  151.0 1.1 reshape.702
  152.2 3.4 %all-to-all-start.4 = ((bf16[8,2,8192]{2,1,0:T(2,128)(2,1)}), bf16[8,2,8192]{2,1,0:T(2,128)(2,1)S(1)}, u32[]{:S(2)}, u32[]{:S(2)}) async-start(bf16[8,2,8192]{2,1,0:T(2,128)(2,1)} %reshape.702), calls=%async_computation.4 | async-start | bytes 524288 | tf_op jit(solution)/shard_map/all_to_all | solution.py:169
  155.7 6.8 %all-to-all-done.4 = bf16[8,2,8192]{2,1,0:T(2,128)(2,1)S(1)} async-done(((bf16[8,2,8192]{2,1,0:T(2,128)(2,1)}), bf16[8,2,8192]{2,1,0:T(2,128)(2,1)S(1)}, u32[]{:S(2)}, u32[]{:S(2)}) %all-to-all-start.4) | async-done | bytes 262176 | tf_op jit(solution)/shard_map/all_to_all | solution.py:169
  162.4 0.3 reshape.703
  162.8 1.2 scatter_fusion.3
  164.2 0.8 pad_maximum_fusion.2
  165.0 4.6 %all-to-all-start.5 = ((bf16[4,768,64]{1,2,0:T(8,128)(2,1)}), bf16[4,768,64]{1,2,0:T(8,128)(2,1)S(1)}, u32[]{:S(2)}, u32[]{:S(2)}) async-start(bf16[4,768,64]{1,2,0:T(8,128)(2,1)} %pad_maximum_fusion.2), calls=%async_computation.5 | async-start | bytes 786432 | tf_op jit(solution)/shard_map/all_to_all | solution.py:184
  169.6 11.0 %all-to-all-done.5 = bf16[4,768,64]{1,2,0:T(8,128)(2,1)S(1)} async-done(((bf16[4,768,64]{1,2,0:T(8,128)(2,1)}), bf16[4,768,64]{1,2,0:T(8,128)(2,1)S(1)}, u32[]{:S(2)}, u32[]{:S(2)}) %all-to-all-start.5) | async-done | bytes 393248 | tf_op jit(solution)/shard_map/all_to_all | solution.py:184
  180.8 1.0 copy.68
  181.8 0.7 select_bitcast_fusion
  (97 shorter events, 2.7 us)
Async XLA Ops:
  7.2 2.7 %copy-start.5 = (bf16[1,1,256,1024]{3,2,1,0:T(8,128)(2,1)S(1)}, bf16[1,1,256,1024]{3,2,1,0:T(8,128)(2,1)}, u32[]{:S(2)}) copy-start(bf16[1,1,256,1024]{3,2,1,0:T(8,128)(2,1)} %param.10) | copy-start | bytes 1572868
  7.2 2.5 %copy-start.9 = (s32[1,1,8]{2,1,0:T(1,128)S(1)}, s32[1,1,8]{2,1,0:T(1,128)}, u32[]{:S(2)}) copy-start(s32[1,1,8]{2,1,0:T(1,128)} %param.12) | copy-start | bytes 100
  7.2 2.7 %copy-start.3 = (f32[1,1,1024,256]{3,2,1,0:T(8,128)S(1)}, f32[1,1,1024,256]{3,2,1,0:T(8,128)}, u32[]{:S(2)}) copy-start(f32[1,1,1024,256]{3,2,1,0:T(8,128)} %param.9) | copy-start | bytes 3145732
  7.2 95.1 %all-gather.3.cloned.1.call-start = ((), (), s32[]{:S(2)}) async-start(), calls=%async_computation.6 | async-start | bytes 5242880 | tf_op jit(solution)/shard_map/all_gather | solution.py:56
  7.2 15.5 %copy-start.13 = (s32[1,1,8]{2,1,0:T(1,128)S(1)}, s32[1,1,8]{2,1,0:T(1,128)}, u32[]{:S(2)}) copy-start(s32[1,1,8]{2,1,0:T(1,128)} %param.14) | copy-start | bytes 100
  7.3 15.5 %copy-start.14 = (s32[1,1,8]{2,1,0:T(1,128)S(1)}, s32[1,1,8]{2,1,0:T(1,128)}, u32[]{:S(2)}) copy-start(s32[1,1,8]{2,1,0:T(1,128)} %param.13) | copy-start | bytes 100
  7.3 15.5 %copy-start.15 = (s32[1,1,8]{2,1,0:T(1,128)S(1)}, s32[1,1,8]{2,1,0:T(1,128)}, u32[]{:S(2)}) copy-start(s32[1,1,8]{2,1,0:T(1,128)} %param.15) | copy-start | bytes 100
  9.6 17.4 %copy-start.6 = (bf16[1,1,8,32,1024]{4,3,2,1,0:T(8,128)(2,1)S(1)}, bf16[1,1,8,32,1024]{4,3,2,1,0:T(8,128)(2,1)}, u32[]{:S(2)}) copy-start(bf16[1,1,8,32,1024]{4,3,2,1,0:T(8,128)(2,1)} %param.11) | copy-start | bytes 1572868
  10.9 30.6 %collective-permute-start.2 = (bf16[256,256]{1,0:T(8,128)(2,1)S(1)}, bf16[256,256]{1,0:T(8,128)(2,1)S(1)}, u32[]{:S(2)}, u32[]{:S(2)}) collective-permute-start(bf16[256,256]{1,0:T(8,128)(2,1)S(1)} %get-tuple-element.37), channel_id=1, source_target_pairs={{0,6},{1,7},{2,0},{3,1},{4,2},{5,3},{6,4},{7,5}} | collective-permute-start | bytes 393224 | tf_op jit(solution)/shard_map/ppermute | solution.py:72
  17.9 23.7 %collective-permute-start.1 = (bf16[256,256]{1,0:T(8,128)(2,1)S(1)}, bf16[256,256]{1,0:T(8,128)(2,1)S(1)}, u32[]{:S(2)}, u32[]{:S(2)}) collective-permute-start(bf16[256,256]{1,0:T(8,128)(2,1)S(1)} %get-tuple-element.37), channel_id=1, source_target_pairs={{0,4},{1,5},{2,6},{3,7},{4,0},{5,1},{6,2},{7,3}} | collective-permute-start | bytes 393224 | tf_op jit(solution)/shard_map/ppermute | solution.py:72
  19.8 21.8 %collective-permute-start = (bf16[256,256]{1,0:T(8,128)(2,1)S(1)}, bf16[256,256]{1,0:T(8,128)(2,1)S(1)}, u32[]{:S(2)}, u32[]{:S(2)}) collective-permute-start(bf16[256,256]{1,0:T(8,128)(2,1)S(1)} %get-tuple-element.37), channel_id=1, source_target_pairs={{0,2},{1,3},{2,4},{3,5},{4,6},{5,7},{6,0},{7,1}} | collective-permute-start | bytes 393224 | tf_op jit(solution)/shard_map/ppermute | solution.py:72
  23.4 16.1 %all-to-all-start = ((s32[32,3,8]{2,1,0:T(4,128)}), s32[32,3,8]{2,1,0:T(4,128)S(1)}, u32[]{:S(2)}, u32[]{:S(2)}) async-start(s32[32,3,8]{2,1,0:T(4,128)} %broadcast_in_dim.180), calls=%async_computation | async-start | bytes 131072 | tf_op jit(solution)/shard_map/all_to_all | solution.py:104
  41.6 26.5 %copy-start.8 = (s32[1024]{0:T(1024)}, s32[1024]{0:T(1024)S(1)}, u32[]{:S(2)}) copy-start(s32[1024]{0:T(1024)S(1)} %pad_clamp_fusion) | copy-start | bytes 12292
  42.7 19.0 %collective-permute-start.5 = (bf16[256,64]{0,1:T(8,128)(2,1)S(1)}, bf16[256,64]{0,1:T(8,128)(2,1)S(1)}, u32[]{:S(2)}, u32[]{:S(2)}) collective-permute-start(bf16[256,64]{0,1:T(8,128)(2,1)S(1)} %get-tuple-element.27), channel_id=1, source_target_pairs={{0,6},{1,7},{2,0},{3,1},{4,2},{5,3},{6,4},{7,5}} | collective-permute-start | bytes 98312 | tf_op jit(solution)/shard_map/ppermute | solution.py:72
  57.0 7.4 %collective-permute-start.4 = (bf16[256,64]{0,1:T(8,128)(2,1)S(1)}, bf16[256,64]{0,1:T(8,128)(2,1)S(1)}, u32[]{:S(2)}, u32[]{:S(2)}) collective-permute-start(bf16[256,64]{0,1:T(8,128)(2,1)S(1)} %get-tuple-element.28), channel_id=1, source_target_pairs={{0,4},{1,5},{2,6},{3,7},{4,0},{5,1},{6,2},{7,3}} | collective-permute-start | bytes 98312 | tf_op jit(solution)/shard_map/ppermute | solution.py:72
  58.9 8.3 %collective-permute-start.3 = (bf16[256,64]{0,1:T(8,128)(2,1)S(1)}, bf16[256,64]{0,1:T(8,128)(2,1)S(1)}, u32[]{:S(2)}, u32[]{:S(2)}) collective-permute-start(bf16[256,64]{0,1:T(8,128)(2,1)S(1)} %get-tuple-element.29), channel_id=1, source_target_pairs={{0,2},{1,3},{2,4},{3,5},{4,6},{5,7},{6,0},{7,1}} | collective-permute-start | bytes 98312 | tf_op jit(solution)/shard_map/ppermute | solution.py:72
  69.9 10.3 %all-to-all-start.1 = ((bf16[8,2,8192]{2,1,0:T(2,128)(2,1)}), bf16[8,2,8192]{2,1,0:T(2,128)(2,1)S(1)}, u32[]{:S(2)}, u32[]{:S(2)}) async-start(bf16[8,2,8192]{2,1,0:T(2,128)(2,1)} %reshape.696), calls=%async_computation.1 | async-start | bytes 524288 | tf_op jit(solution)/shard_map/all_to_all | solution.py:169
  104.9 1.2 copy-start.4
  105.2 1.7 copy-start
  106.9 8.1 %copy-start.12 = (s32[2,8]{1,0:T(2,128)S(1)}, s32[2,8]{1,0:T(2,128)}, u32[]{:S(2)}) copy-start(s32[2,8]{1,0:T(2,128)} %get-tuple-element.35) | copy-start | bytes 196
  111.6 10.3 %all-to-all-start.2 = ((bf16[8,2,8192]{2,1,0:T(2,128)(2,1)}), bf16[8,2,8192]{2,1,0:T(2,128)(2,1)S(1)}, u32[]{:S(2)}, u32[]{:S(2)}) async-start(bf16[8,2,8192]{2,1,0:T(2,128)(2,1)} %reshape.698), calls=%async_computation.2 | async-start | bytes 524288 | tf_op jit(solution)/shard_map/all_to_all | solution.py:169
  125.2 2.1 %copy-start.1 = (bf16[1024,1024]{1,0:T(8,128)(2,1)S(1)}, bf16[1024,1024]{1,0:T(8,128)(2,1)}, u32[]{:S(2)}) copy-start(bf16[1024,1024]{1,0:T(8,128)(2,1)} %copy-done) | copy-start | bytes 6291460
  127.3 9.9 %copy-start.11 = (s32[2,8]{1,0:T(2,128)S(1)}, s32[2,8]{1,0:T(2,128)}, u32[]{:S(2)}) copy-start(s32[2,8]{1,0:T(2,128)} %get-tuple-element.34) | copy-start | bytes 196
  133.6 10.3 %all-to-all-start.3 = ((bf16[8,2,8192]{2,1,0:T(2,128)(2,1)}), bf16[8,2,8192]{2,1,0:T(2,128)(2,1)S(1)}, u32[]{:S(2)}, u32[]{:S(2)}) async-start(bf16[8,2,8192]{2,1,0:T(2,128)(2,1)} %reshape.700), calls=%async_computation.3 | async-start | bytes 524288 | tf_op jit(solution)/shard_map/all_to_all | solution.py:169
  147.2 2.1 %copy-start.2 = (bf16[1024,1024]{1,0:T(8,128)(2,1)S(1)}, bf16[1024,1024]{1,0:T(8,128)(2,1)}, u32[]{:S(2)}) copy-start(bf16[1024,1024]{1,0:T(8,128)(2,1)} %copy-done) | copy-start | bytes 6291460
  149.2 6.3 %copy-start.10 = (s32[2,8]{1,0:T(2,128)S(1)}, s32[2,8]{1,0:T(2,128)}, u32[]{:S(2)}) copy-start(s32[2,8]{1,0:T(2,128)} %get-tuple-element.33) | copy-start | bytes 196
  152.2 10.3 %all-to-all-start.4 = ((bf16[8,2,8192]{2,1,0:T(2,128)(2,1)}), bf16[8,2,8192]{2,1,0:T(2,128)(2,1)S(1)}, u32[]{:S(2)}, u32[]{:S(2)}) async-start(bf16[8,2,8192]{2,1,0:T(2,128)(2,1)} %reshape.702), calls=%async_computation.4 | async-start | bytes 524288 | tf_op jit(solution)/shard_map/all_to_all | solution.py:169
  165.0 16.8 %copy-start.7 = (f32[256,256]{1,0:T(8,128)S(1)}, f32[256,256]{1,0:T(8,128)}, u32[]{:S(2)}) copy-start(f32[256,256]{1,0:T(8,128)} %get-tuple-element.38) | copy-start | bytes 786436
  165.0 15.6 %all-to-all-start.5 = ((bf16[4,768,64]{1,2,0:T(8,128)(2,1)}), bf16[4,768,64]{1,2,0:T(8,128)(2,1)S(1)}, u32[]{:S(2)}, u32[]{:S(2)}) async-start(bf16[4,768,64]{1,2,0:T(8,128)(2,1)} %pad_maximum_fusion.2), calls=%async_computation.5 | async-start | bytes 786432 | tf_op jit(solution)/shard_map/all_to_all | solution.py:184
Sparse Core Ops, SparseCore 0:
  9.8 92.5 all-gather.2

commit v18 on v17

--- a/solution.py
+++ b/solution.py
@@ -50,16 +50,11 @@
         jnp.zeros((), jnp.bfloat16),
     ).reshape(tile_count * block_rows, width)
 
-    raw = jnp.concatenate(
-        [diag_inverse[0, 0], off_tiles[0, 0].reshape(tile_count * block_rows, width)], axis=0
-    )
-    gathered = lax.all_gather(raw, "prow", axis=0)
+    inv_raw, tiles_raw = lax.all_gather(
+        (diag_inverse[0, 0], off_tiles[0, 0]), "prow", axis=0, tiled=True
+    )
     zero = jnp.zeros((), jnp.bfloat16)
-    inv_full = jnp.where(
-        col_super[:, None] == col_super[None, :],
-        gathered[:, :row_count].reshape(n_prow * row_count, width),
-        zero,
-    )
+    inv_full = jnp.where(col_super[:, None] == col_super[None, :], inv_raw, zero)
 
     all_axes = ("lvl", "prow", "pcol")
 
@@ -114,7 +109,7 @@
     group_panels = jnp.take(meta[:, :, 2, :].reshape(groups, group_tiles), my_group, axis=0)
     tiles_full = jnp.where(
         col_super[None, None, :] == super_of(group_panels)[:, None, None],
-        gathered[:, row_count:].reshape(group_tiles, block_rows, width),
+        tiles_raw,
         zero,
     ).reshape(group_tiles * block_rows, width)
     tiles_full = jnp.concatenate(

time: 191 us -> 203 us (1.063)
  waiting for transfers between devices: 76.2 us -> 90.7 us
  starting transfers between devices: 52.4 us -> 48.3 us
  other arithmetic: 15.3 us -> 18.4 us
    all_gather x1 -> x2, waiting for transfers between devices: 20.4 us -> 32 us  [per_device(): lax.all_gather((diag_inverse[0, 0], off_tiles[0, 0]), 'prow', axis=0, til...]
    ppermute x6, starting transfers between devices: 30.7 us -> 27.3 us  [level0_shift(): return lax.ppermute(x, all_axes, pairs)]
    convert_element_type x0 -> x3, other arithmetic: none -> 3.07 us  [per_device(): right.astype(jnp.bfloat16)]
    concatenate x1 -> x0, other arithmetic: 2.35 us -> none  [per_device(): jnp.concatenate([diag_inverse[0, 0], off_tiles[0, 0].reshape(tile_count *...]
    unnamed x42 -> x32, local copies, waits for them, and re-layouts: 11.6 us -> 12.1 us
  transfers between devices with their start and end apart: 13 -> 14, of which waited for: 9 -> 9; matrix products, arithmetic and copies ran while one was open for 5% -> 8% of each run, Pallas kernels for 0% -> 0%
where the time goes in v18:
time: 203 us; the launch traced here: 202 us
  waiting for transfers between devices  90.7 us (45%)
  starting transfers between devices  48.3 us (24%)
  local copies, waits for them, and re-layouts  20.7 us (10%)
  other arithmetic  18.4 us (9%)
  between operations  14.8 us (7%)
  matrix products  8.84 us (4%)
    all_gather x2, waiting for transfers between devices, per_device(): lax.all_gather((diag_inverse[0, 0], off_tiles[0, 0]), 'prow', axis=0, til...  32 us
    ppermute x6, starting transfers between devices, level0_shift(): return lax.ppermute(x, all_axes, pairs)  27.3 us
    all_to_all x4, waiting for transfers between devices, per_device(): lax.all_to_all(sending, ('lvl', 'pcol'), split_axis=0, concat_axis=0, til...  26.9 us
    all_to_all x4, starting transfers between devices, per_device(): lax.all_to_all(sending, ('lvl', 'pcol'), split_axis=0, concat_axis=0, til...  14.1 us
    all_to_all x1, waiting for transfers between devices, per_device(): lax.all_to_all(jnp.broadcast_to(meta[None], (devices,) + meta.shape), ('l...  13.7 us
    unnamed x32, local copies, waits for them, and re-layouts  12.1 us
    all_to_all x1, waiting for transfers between devices, per_device(): lax.all_to_all(final, 'prow', split_axis=0, concat_axis=0, tiled=True)  11.3 us
    ppermute x6, waiting for transfers between devices, level0_shift(): return lax.ppermute(x, all_axes, pairs)  5.55 us
  transfers between devices with their start and end apart: 14, of which 9 were waited for; matrix products, arithmetic and copies ran while one was open for 8% of the time, Pallas kernels for 0%

profile of v18, /device:TPU:0, one launch (start us, length us, event | category | flops | bytes accessed | tf_op | source)
XLA Modules:
  0.0 201.8 jit_solution(12869565220028210981)
XLA Ops:
  7.3 0.7 all-gather.5.cloned.1.call-update
  8.0 0.7 select_reduce_fusion.3
  8.7 0.7 select_reduce_fusion.1
  9.5 2.4 %fusion.44 = (bf16[256,256]{1,0:T(8,128)(2,1)S(1)}, f32[256,256]{1,0:T(8,128)}) fusion(f32[1,1,1024,256]{3,2,1,0:T(8,128)} %param.9, bf16[1,1,256,1024]{3,2,1,0:T(8,128)(2,1)} %param.10, s32[1024]{0:T(1024)S(1)} %select_reduce_fusion.1, s32[256]{0:T(256)S(1)} %select_reduce_fusion.3), kind=kOutput, calls=%fused_computation.129 | convolution fusion | flops 135069696 | bytes 1971200 | tf_op jit(solution)/shard_map/dot_general | solution.py:75
  11.9 6.9 %collective-permute-start.2 = (bf16[256,256]{1,0:T(8,128)(2,1)S(1)}, bf16[256,256]{1,0:T(8,128)(2,1)S(1)}, u32[]{:S(2)}, u32[]{:S(2)}) collective-permute-start(bf16[256,256]{1,0:T(8,128)(2,1)S(1)} %get-tuple-element.35), channel_id=1, source_target_pairs={{0,6},{1,7},{2,0},{3,1},{4,2},{5,3},{6,4},{7,5}} | collective-permute-start | bytes 393224 | tf_op jit(solution)/shard_map/ppermute | solution.py:67
  18.9 1.9 collective-permute-start.1
  20.8 2.9 %collective-permute-start = (bf16[256,256]{1,0:T(8,128)(2,1)S(1)}, bf16[256,256]{1,0:T(8,128)(2,1)S(1)}, u32[]{:S(2)}, u32[]{:S(2)}) collective-permute-start(bf16[256,256]{1,0:T(8,128)(2,1)S(1)} %get-tuple-element.35), channel_id=1, source_target_pairs={{0,2},{1,3},{2,4},{3,5},{4,6},{5,7},{6,0},{7,1}} | collective-permute-start | bytes 393224 | tf_op jit(solution)/shard_map/ppermute | solution.py:67
  23.8 0.6 broadcast_in_dim.178
  24.4 3.2 %all-to-all-start = ((s32[32,3,8]{2,1,0:T(4,128)}), s32[32,3,8]{2,1,0:T(4,128)S(1)}, u32[]{:S(2)}, u32[]{:S(2)}) async-start(s32[32,3,8]{2,1,0:T(4,128)} %broadcast_in_dim.178), calls=%async_computation | async-start | bytes 131072 | tf_op jit(solution)/shard_map/all_to_all | solution.py:99
  27.6 0.7 all-gather.7.cloned.1.call-update
  28.9 13.7 %all-to-all-done = s32[32,3,8]{2,1,0:T(4,128)S(1)} async-done(((s32[32,3,8]{2,1,0:T(4,128)}), s32[32,3,8]{2,1,0:T(4,128)S(1)}, u32[]{:S(2)}, u32[]{:S(2)}) %all-to-all-start) | async-done | bytes 3104 | tf_op jit(solution)/shard_map/all_to_all | solution.py:99
  42.8 0.3 convert_reduce_fusion
  44.1 0.6 gather_fusion
  44.7 0.4 convolution_convert_fusion.3
  45.1 10.9 %collective-permute-start.5 = (bf16[256,64]{0,1:T(8,128)(2,1)S(1)}, bf16[256,64]{0,1:T(8,128)(2,1)S(1)}, u32[]{:S(2)}, u32[]{:S(2)}) collective-permute-start(bf16[256,64]{0,1:T(8,128)(2,1)S(1)} %get-tuple-element.25), channel_id=1, source_target_pairs={{0,6},{1,7},{2,0},{3,1},{4,2},{5,3},{6,4},{7,5}} | collective-permute-start | bytes 98312 | tf_op jit(solution)/shard_map/ppermute | solution.py:67
  56.0 1.9 collective-permute-start.4
  57.9 2.7 %collective-permute-start.3 = (bf16[256,64]{0,1:T(8,128)(2,1)S(1)}, bf16[256,64]{0,1:T(8,128)(2,1)S(1)}, u32[]{:S(2)}, u32[]{:S(2)}) collective-permute-start(bf16[256,64]{0,1:T(8,128)(2,1)S(1)} %get-tuple-element.27), channel_id=1, source_target_pairs={{0,2},{1,3},{2,4},{3,5},{4,6},{5,7},{6,0},{7,1}} | collective-permute-start | bytes 98312 | tf_op jit(solution)/shard_map/ppermute | solution.py:67
  60.6 4.8 %collective-permute-done.4 = bf16[256,64]{0,1:T(8,128)(2,1)S(1)} collective-permute-done((bf16[256,64]{0,1:T(8,128)(2,1)S(1)}, bf16[256,64]{0,1:T(8,128)(2,1)S(1)}, u32[]{:S(2)}, u32[]{:S(2)}) %collective-permute-start.4) | collective-permute-done | bytes 32800 | tf_op jit(solution)/shard_map/ppermute | solution.py:67
  65.4 0.7 collective-permute-done.3
  66.2 0.6 gather_fusion.1
  67.0 0.7 gather_fusion.2
  67.7 1.1 reshape.659
  68.8 3.5 %all-to-all-start.1 = ((bf16[8,2,8192]{2,1,0:T(2,128)(2,1)}), bf16[8,2,8192]{2,1,0:T(2,128)(2,1)S(1)}, u32[]{:S(2)}, u32[]{:S(2)}) async-start(bf16[8,2,8192]{2,1,0:T(2,128)(2,1)} %reshape.659), calls=%async_computation.1 | async-start | bytes 524288 | tf_op jit(solution)/shard_map/all_to_all | solution.py:164
  72.5 6.7 %all-to-all-done.1 = bf16[8,2,8192]{2,1,0:T(2,128)(2,1)S(1)} async-done(((bf16[8,2,8192]{2,1,0:T(2,128)(2,1)}), bf16[8,2,8192]{2,1,0:T(2,128)(2,1)S(1)}, u32[]{:S(2)}, u32[]{:S(2)}) %all-to-all-start.1) | async-done | bytes 262176 | tf_op jit(solution)/shard_map/all_to_all | solution.py:164
  79.2 0.3 reshape.660
  79.7 1.2 scatter_fusion
  81.2 2.1 %compare_select_fusion = bf16[1024,1024]{1,0:T(8,128)(2,1)S(1)} fusion(bf16[1,1,1024,1024]{3,2,1,0:T(8,128)(2,1)} %all-gather.5.cloned.1.call-done, s32[1024]{0:T(1024)S(1)} %select_reduce_fusion.1), kind=kLoop, calls=%fused_computation.10 | loop fusion | flops 2097152 | bytes 4198400 | tf_op jit(solution)/shard_map/jit(_where)/select_n | solution.py:57
  83.3 0.8 fusion.45
  84.1 32.0 %all-gather.7.cloned.1.call-done = bf16[1,1,32,32,1024]{4,3,1,0,2:T(8,128)(2,1)} async-done(((bf16[1,1,8,32,1024]{4,3,1,0,2:T(8,128)(2,1)}), bf16[1,1,32,32,1024]{4,3,1,0,2:T(8,128)(2,1)}) %all-gather.7.cloned.1.call-update) | async-done | bytes 2097168 | tf_op jit(solution)/shard_map/all_gather | solution.py:53
  116.0 1.8 bitcast_select_fusion
  117.8 1.3 copy-done
  119.2 0.8 convolution_convert_fusion.2
  120.2 1.4 gather_fusion.3
  121.6 2.2 %reshape.661 = bf16[8,2,8192]{2,1,0:T(2,128)(2,1)} reshape(bf16[64,32,64]{2,1,0:T(8,128)(2,1)} %gather_fusion.3) | data formatting | bytes 524288
  123.8 3.6 %all-to-all-start.2 = ((bf16[8,2,8192]{2,1,0:T(2,128)(2,1)}), bf16[8,2,8192]{2,1,0:T(2,128)(2,1)S(1)}, u32[]{:S(2)}, u32[]{:S(2)}) async-start(bf16[8,2,8192]{2,1,0:T(2,128)(2,1)} %reshape.661), calls=%async_computation.2 | async-start | bytes 524288 | tf_op jit(solution)/shard_map/all_to_all | solution.py:164
  127.4 6.8 %all-to-all-done.2 = bf16[8,2,8192]{2,1,0:T(2,128)(2,1)S(1)} async-done(((bf16[8,2,8192]{2,1,0:T(2,128)(2,1)}), bf16[8,2,8192]{2,1,0:T(2,128)(2,1)S(1)}, u32[]{:S(2)}, u32[]{:S(2)}) %all-to-all-start.2) | async-done | bytes 262176 | tf_op jit(solution)/shard_map/all_to_all | solution.py:164
  134.3 1.2 reshape.662
  135.4 0.9 slice_convert_fusion.3
  136.4 1.2 scatter_fusion.1
  137.6 1.4 fusion.7
  139.1 0.8 fusion.46
  139.8 1.5 convolution_convert_fusion.1
  141.3 1.1 copy.65
  142.4 1.4 gather_fusion.4
  143.8 2.2 %reshape.663 = bf16[8,2,8192]{2,1,0:T(2,128)(2,1)} reshape(bf16[64,32,64]{2,1,0:T(8,128)(2,1)} %gather_fusion.4) | data formatting | bytes 524288
  146.0 3.6 %all-to-all-start.3 = ((bf16[8,2,8192]{2,1,0:T(2,128)(2,1)}), bf16[8,2,8192]{2,1,0:T(2,128)(2,1)S(1)}, u32[]{:S(2)}, u32[]{:S(2)}) async-start(bf16[8,2,8192]{2,1,0:T(2,128)(2,1)} %reshape.663), calls=%async_computation.3 | async-start | bytes 524288 | tf_op jit(solution)/shard_map/all_to_all | solution.py:164
  149.7 6.6 %all-to-all-done.3 = bf16[8,2,8192]{2,1,0:T(2,128)(2,1)S(1)} async-done(((bf16[8,2,8192]{2,1,0:T(2,128)(2,1)}), bf16[8,2,8192]{2,1,0:T(2,128)(2,1)S(1)}, u32[]{:S(2)}, u32[]{:S(2)}) %all-to-all-start.3) | async-done | bytes 262176 | tf_op jit(solution)/shard_map/all_to_all | solution.py:164
  156.3 1.2 reshape.664
  157.4 0.9 slice_convert_fusion.2
  158.3 1.2 scatter_fusion.2
  159.6 1.4 fusion.6
  161.1 1.4 select_convert_fusion
  162.5 0.8 convolution_convert_fusion
  163.5 0.7 gather_fusion.5
  164.2 1.1 reshape.665
  165.3 3.4 %all-to-all-start.4 = ((bf16[8,2,8192]{2,1,0:T(2,128)(2,1)}), bf16[8,2,8192]{2,1,0:T(2,128)(2,1)S(1)}, u32[]{:S(2)}, u32[]{:S(2)}) async-start(bf16[8,2,8192]{2,1,0:T(2,128)(2,1)} %reshape.665), calls=%async_computation.4 | async-start | bytes 524288 | tf_op jit(solution)/shard_map/all_to_all | solution.py:164
  168.8 6.8 %all-to-all-done.4 = bf16[8,2,8192]{2,1,0:T(2,128)(2,1)S(1)} async-done(((bf16[8,2,8192]{2,1,0:T(2,128)(2,1)}), bf16[8,2,8192]{2,1,0:T(2,128)(2,1)S(1)}, u32[]{:S(2)}, u32[]{:S(2)}) %all-to-all-start.4) | async-done | bytes 262176 | tf_op jit(solution)/shard_map/all_to_all | solution.py:164
  175.6 0.3 reshape.666
  175.9 1.2 scatter_fusion.3
  177.3 0.8 pad_maximum_fusion.1
  178.1 3.6 %all-to-all-start.5 = ((bf16[4,768,64]{1,2,0:T(8,128)(2,1)}), bf16[4,768,64]{1,2,0:T(8,128)(2,1)S(1)}, u32[]{:S(2)}, u32[]{:S(2)}) async-start(bf16[4,768,64]{1,2,0:T(8,128)(2,1)} %pad_maximum_fusion.1), calls=%async_computation.5 | async-start | bytes 786432 | tf_op jit(solution)/shard_map/all_to_all | solution.py:179
  181.7 11.3 %all-to-all-done.5 = bf16[4,768,64]{1,2,0:T(8,128)(2,1)S(1)} async-done(((bf16[4,768,64]{1,2,0:T(8,128)(2,1)}), bf16[4,768,64]{1,2,0:T(8,128)(2,1)S(1)}, u32[]{:S(2)}, u32[]{:S(2)}) %all-to-all-start.5) | async-done | bytes 393248 | tf_op jit(solution)/shard_map/all_to_all | solution.py:179
  193.2 1.0 copy.70
  194.2 0.7 select_bitcast_fusion
  (91 shorter events, 3.6 us)
Async XLA Ops:
  7.2 21.2 %copy-start.7 = (s32[1,1,8]{2,1,0:T(1,128)S(1)}, s32[1,1,8]{2,1,0:T(1,128)}, u32[]{:S(2)}) copy-start(s32[1,1,8]{2,1,0:T(1,128)} %param.12) | copy-start | bytes 100
  7.2 16.5 %copy-start.10 = (s32[1,1,8]{2,1,0:T(1,128)S(1)}, s32[1,1,8]{2,1,0:T(1,128)}, u32[]{:S(2)}) copy-start(s32[1,1,8]{2,1,0:T(1,128)} %param.15) | copy-start | bytes 100
  7.2 16.5 %copy-start.8 = (s32[1,1,8]{2,1,0:T(1,128)S(1)}, s32[1,1,8]{2,1,0:T(1,128)}, u32[]{:S(2)}) copy-start(s32[1,1,8]{2,1,0:T(1,128)} %param.14) | copy-start | bytes 100
  7.2 16.5 %copy-start.9 = (s32[1,1,8]{2,1,0:T(1,128)S(1)}, s32[1,1,8]{2,1,0:T(1,128)}, u32[]{:S(2)}) copy-start(s32[1,1,8]{2,1,0:T(1,128)} %param.13) | copy-start | bytes 100
  7.2 21.5 %copy-start.4 = (bf16[1,1,8,32,1024]{4,3,2,1,0:T(8,128)(2,1)S(1)}, bf16[1,1,8,32,1024]{4,3,2,1,0:T(8,128)(2,1)}, u32[]{:S(2)}) copy-start(bf16[1,1,8,32,1024]{4,3,2,1,0:T(8,128)(2,1)} %param.11) | copy-start | bytes 1572868
  7.2 74.0 %all-gather.5.cloned.1.call-start = ((), (), s32[]{:S(2)}) async-start(), calls=%async_computation.6 | async-start | bytes 2621440 | tf_op jit(solution)/shard_map/all_gather | solution.py:53
  11.9 32.1 %collective-permute-start.2 = (bf16[256,256]{1,0:T(8,128)(2,1)S(1)}, bf16[256,256]{1,0:T(8,128)(2,1)S(1)}, u32[]{:S(2)}, u32[]{:S(2)}) collective-permute-start(bf16[256,256]{1,0:T(8,128)(2,1)S(1)} %get-tuple-element.35), channel_id=1, source_target_pairs={{0,6},{1,7},{2,0},{3,1},{4,2},{5,3},{6,4},{7,5}} | collective-permute-start | bytes 393224 | tf_op jit(solution)/shard_map/ppermute | solution.py:67
  18.9 25.1 %collective-permute-start.1 = (bf16[256,256]{1,0:T(8,128)(2,1)S(1)}, bf16[256,256]{1,0:T(8,128)(2,1)S(1)}, u32[]{:S(2)}, u32[]{:S(2)}) collective-permute-start(bf16[256,256]{1,0:T(8,128)(2,1)S(1)} %get-tuple-element.35), channel_id=1, source_target_pairs={{0,4},{1,5},{2,6},{3,7},{4,0},{5,1},{6,2},{7,3}} | collective-permute-start | bytes 393224 | tf_op jit(solution)/shard_map/ppermute | solution.py:67
  20.8 23.2 %collective-permute-start = (bf16[256,256]{1,0:T(8,128)(2,1)S(1)}, bf16[256,256]{1,0:T(8,128)(2,1)S(1)}, u32[]{:S(2)}, u32[]{:S(2)}) collective-permute-start(bf16[256,256]{1,0:T(8,128)(2,1)S(1)} %get-tuple-element.35), channel_id=1, source_target_pairs={{0,2},{1,3},{2,4},{3,5},{4,6},{5,7},{6,0},{7,1}} | collective-permute-start | bytes 393224 | tf_op jit(solution)/shard_map/ppermute | solution.py:67
  24.4 18.2 %all-to-all-start = ((s32[32,3,8]{2,1,0:T(4,128)}), s32[32,3,8]{2,1,0:T(4,128)S(1)}, u32[]{:S(2)}, u32[]{:S(2)}) async-start(s32[32,3,8]{2,1,0:T(4,128)} %broadcast_in_dim.178), calls=%async_computation | async-start | bytes 131072 | tf_op jit(solution)/shard_map/all_to_all | solution.py:99
  27.6 88.4 %all-gather.7.cloned.1.call-start = ((), (), s32[]{:S(2)}) async-start(), calls=%async_computation.7 | async-start | bytes 2621440 | tf_op jit(solution)/shard_map/all_gather | solution.py:53
  45.1 15.6 %collective-permute-start.5 = (bf16[256,64]{0,1:T(8,128)(2,1)S(1)}, bf16[256,64]{0,1:T(8,128)(2,1)S(1)}, u32[]{:S(2)}, u32[]{:S(2)}) collective-permute-start(bf16[256,64]{0,1:T(8,128)(2,1)S(1)} %get-tuple-element.25), channel_id=1, source_target_pairs={{0,6},{1,7},{2,0},{3,1},{4,2},{5,3},{6,4},{7,5}} | collective-permute-start | bytes 98312 | tf_op jit(solution)/shard_map/ppermute | solution.py:67
  56.0 9.5 %collective-permute-start.4 = (bf16[256,64]{0,1:T(8,128)(2,1)S(1)}, bf16[256,64]{0,1:T(8,128)(2,1)S(1)}, u32[]{:S(2)}, u32[]{:S(2)}) collective-permute-start(bf16[256,64]{0,1:T(8,128)(2,1)S(1)} %get-tuple-element.26), channel_id=1, source_target_pairs={{0,4},{1,5},{2,6},{3,7},{4,0},{5,1},{6,2},{7,3}} | collective-permute-start | bytes 98312 | tf_op jit(solution)/shard_map/ppermute | solution.py:67
  57.9 8.3 %collective-permute-start.3 = (bf16[256,64]{0,1:T(8,128)(2,1)S(1)}, bf16[256,64]{0,1:T(8,128)(2,1)S(1)}, u32[]{:S(2)}, u32[]{:S(2)}) collective-permute-start(bf16[256,64]{0,1:T(8,128)(2,1)S(1)} %get-tuple-element.27), channel_id=1, source_target_pairs={{0,2},{1,3},{2,4},{3,5},{4,6},{5,7},{6,0},{7,1}} | collective-permute-start | bytes 98312 | tf_op jit(solution)/shard_map/ppermute | solution.py:67
  68.8 12.2 %copy-start.3 = (f32[1,1,1024,256]{3,2,1,0:T(8,128)S(1)}, f32[1,1,1024,256]{3,2,1,0:T(8,128)}, u32[]{:S(2)}) copy-start(f32[1,1,1024,256]{3,2,1,0:T(8,128)} %param.9) | copy-start | bytes 3145732
  68.8 10.4 %all-to-all-start.1 = ((bf16[8,2,8192]{2,1,0:T(2,128)(2,1)}), bf16[8,2,8192]{2,1,0:T(2,128)(2,1)S(1)}, u32[]{:S(2)}, u32[]{:S(2)}) async-start(bf16[8,2,8192]{2,1,0:T(2,128)(2,1)} %reshape.659), calls=%async_computation.1 | async-start | bytes 524288 | tf_op jit(solution)/shard_map/all_to_all | solution.py:164
  117.8 1.3 copy-start
  123.8 10.5 %all-to-all-start.2 = ((bf16[8,2,8192]{2,1,0:T(2,128)(2,1)}), bf16[8,2,8192]{2,1,0:T(2,128)(2,1)S(1)}, u32[]{:S(2)}, u32[]{:S(2)}) async-start(bf16[8,2,8192]{2,1,0:T(2,128)(2,1)} %reshape.661), calls=%async_computation.2 | async-start | bytes 524288 | tf_op jit(solution)/shard_map/all_to_all | solution.py:164
  137.6 2.2 %copy-start.1 = (bf16[32,32,1024]{2,1,0:T(8,128)(2,1)S(1)}, bf16[32,32,1024]{2,1,0:T(8,128)(2,1)}, u32[]{:S(2)}) copy-start(bf16[32,32,1024]{2,1,0:T(8,128)(2,1)} %copy-done) | copy-start | bytes 6291460
  146.0 10.3 %all-to-all-start.3 = ((bf16[8,2,8192]{2,1,0:T(2,128)(2,1)}), bf16[8,2,8192]{2,1,0:T(2,128)(2,1)S(1)}, u32[]{:S(2)}, u32[]{:S(2)}) async-start(bf16[8,2,8192]{2,1,0:T(2,128)(2,1)} %reshape.663), calls=%async_computation.3 | async-start | bytes 524288 | tf_op jit(solution)/shard_map/all_to_all | solution.py:164
  159.6 2.9 %copy-start.2 = (bf16[32,32,1024]{2,1,0:T(8,128)(2,1)S(1)}, bf16[32,32,1024]{2,1,0:T(8,128)(2,1)}, u32[]{:S(2)}) copy-start(bf16[32,32,1024]{2,1,0:T(8,128)(2,1)} %copy-done) | copy-start | bytes 6291460
  162.5 6.3 %copy-start.6 = (bf16[1024,64]{0,1:T(8,128)(2,1)S(1)}, bf16[1024,64]{0,1:T(8,128)(2,1)}, u32[]{:S(2)}) copy-start(bf16[1024,64]{0,1:T(8,128)(2,1)} %get-tuple-element.37) | copy-start | bytes 393220
  165.3 10.3 %all-to-all-start.4 = ((bf16[8,2,8192]{2,1,0:T(2,128)(2,1)}), bf16[8,2,8192]{2,1,0:T(2,128)(2,1)S(1)}, u32[]{:S(2)}, u32[]{:S(2)}) async-start(bf16[8,2,8192]{2,1,0:T(2,128)(2,1)} %reshape.665), calls=%async_computation.4 | async-start | bytes 524288 | tf_op jit(solution)/shard_map/all_to_all | solution.py:164
  178.1 16.1 %copy-start.5 = (f32[256,256]{1,0:T(8,128)S(1)}, f32[256,256]{1,0:T(8,128)}, u32[]{:S(2)}) copy-start(f32[256,256]{1,0:T(8,128)} %get-tuple-element.36) | copy-start | bytes 786436
  178.1 14.9 %all-to-all-start.5 = ((bf16[4,768,64]{1,2,0:T(8,128)(2,1)}), bf16[4,768,64]{1,2,0:T(8,128)(2,1)S(1)}, u32[]{:S(2)}, u32[]{:S(2)}) async-start(bf16[4,768,64]{1,2,0:T(8,128)(2,1)} %pad_maximum_fusion.1), calls=%async_computation.5 | async-start | bytes 786432 | tf_op jit(solution)/shard_map/all_to_all | solution.py:179
Sparse Core Ops, SparseCore 0:
  9.6 59.7 all-gather.4
  71.0 44.9 all-gather.6

commit v19 on v17

--- a/solution.py
+++ b/solution.py
@@ -181,7 +181,10 @@
         ],
         axis=1,
     )
-    final = lax.all_to_all(final, "prow", split_axis=0, concat_axis=0, tiled=True)
+    final_shape = final.shape
+    final = lax.all_to_all(
+        final.reshape(n_prow, -1), "prow", split_axis=0, concat_axis=0, tiled=True
+    ).reshape(final_shape)
     final = final.astype(jnp.float32)
     solution_rows = jnp.transpose(final[:, :rows_out], (1, 0, 2)).reshape(rows_out, columns_all)
     solution_rows = jnp.where(level_index == 0, first_rows, solution_rows)

time: 191 us -> 199 us (1.042)
  other arithmetic: 15.3 us -> 20.2 us
  local copies, waits for them, and re-layouts: 21.2 us -> 25.2 us
    all_to_all x0 -> x1, other arithmetic: none -> 3.17 us  [per_device(): lax.all_to_all(final.reshape(n_prow, -1), 'prow', split_axis=0, concat_ax...]
    convert_element_type x0 -> x1, other arithmetic: none -> 2.37 us  [per_device(): final = final.astype(jnp.float32)]
    unnamed x42 -> x44, local copies, waits for them, and re-layouts: 11.6 us -> 13.2 us
where the time goes in v19:
time: 199 us; the launch traced here: 198 us
  waiting for transfers between devices  76 us (38%)
  starting transfers between devices  52.3 us (26%)
  local copies, waits for them, and re-layouts  25.2 us (13%)
  other arithmetic  20.2 us (10%)
  between operations  14.9 us (7%)
  matrix products  9.4 us (5%)
    ppermute x6, starting transfers between devices, level0_shift(): return lax.ppermute(x, all_axes, pairs)  30.8 us
    all_to_all x4, waiting for transfers between devices, per_device(): lax.all_to_all(sending, ('lvl', 'pcol'), split_axis=0, concat_axis=0, til...  26.6 us
    all_gather x1, waiting for transfers between devices, per_device(): gathered = lax.all_gather(raw, 'prow', axis=0)  20.4 us
    all_to_all x4, starting transfers between devices, per_device(): lax.all_to_all(sending, ('lvl', 'pcol'), split_axis=0, concat_axis=0, til...  13.8 us
    unnamed x44, local copies, waits for them, and re-layouts  13.2 us
    all_to_all x1, waiting for transfers between devices, per_device(): lax.all_to_all(jnp.broadcast_to(meta[None], (devices,) + meta.shape), ('l...  12.4 us
    all_to_all x1, waiting for transfers between devices, per_device(): lax.all_to_all(final.reshape(n_prow, -1), 'prow', split_axis=0, concat_ax...  11 us
    ppermute x6, waiting for transfers between devices, level0_shift(): return lax.ppermute(x, all_axes, pairs)  5.61 us
  transfers between devices with their start and end apart: 13, of which 9 were waited for; matrix products, arithmetic and copies ran while one was open for 5% of the time, Pallas kernels for 0%

profile of v19, /device:TPU:0, one launch (start us, length us, event | category | flops | bytes accessed | tf_op | source)
XLA Modules:
  0.0 198.1 jit_solution(16244576153988295893)
XLA Ops:
  7.3 2.3 %pad_maximum_fusion = bf16[512,1024]{1,0:T(8,128)(2,1)} fusion(bf16[256,1024]{1,0:T(8,128)(2,1)} %bitcast.118, bf16[256,1024]{1,0:T(8,128)(2,1)} %bitcast.115), kind=kLoop, calls=%fused_computation.20 | loop fusion | flops 2097152 | bytes 2097152 | tf_op jit(solution)/shard_map/concatenate | solution.py:53
  9.9 1.1 fusion.53
  10.9 6.9 %collective-permute-start.2 = (bf16[256,256]{1,0:T(8,128)(2,1)S(1)}, bf16[256,256]{1,0:T(8,128)(2,1)S(1)}, u32[]{:S(2)}, u32[]{:S(2)}) collective-permute-start(bf16[256,256]{1,0:T(8,128)(2,1)S(1)} %get-tuple-element.37), channel_id=1, source_target_pairs={{0,6},{1,7},{2,0},{3,1},{4,2},{5,3},{6,4},{7,5}} | collective-permute-start | bytes 393224 | tf_op jit(solution)/shard_map/ppermute | solution.py:72
  17.9 1.9 collective-permute-start.1
  19.8 2.9 %collective-permute-start = (bf16[256,256]{1,0:T(8,128)(2,1)S(1)}, bf16[256,256]{1,0:T(8,128)(2,1)S(1)}, u32[]{:S(2)}, u32[]{:S(2)}) collective-permute-start(bf16[256,256]{1,0:T(8,128)(2,1)S(1)} %get-tuple-element.37), channel_id=1, source_target_pairs={{0,2},{1,3},{2,4},{3,5},{4,6},{5,7},{6,0},{7,1}} | collective-permute-start | bytes 393224 | tf_op jit(solution)/shard_map/ppermute | solution.py:72
  22.8 0.6 broadcast_in_dim.180
  23.4 3.2 %all-to-all-start = ((s32[32,3,8]{2,1,0:T(4,128)}), s32[32,3,8]{2,1,0:T(4,128)S(1)}, u32[]{:S(2)}, u32[]{:S(2)}) async-start(s32[32,3,8]{2,1,0:T(4,128)} %broadcast_in_dim.180), calls=%async_computation | async-start | bytes 131072 | tf_op jit(solution)/shard_map/all_to_all | solution.py:104
  27.2 12.4 %all-to-all-done = s32[32,3,8]{2,1,0:T(4,128)S(1)} async-done(((s32[32,3,8]{2,1,0:T(4,128)}), s32[32,3,8]{2,1,0:T(4,128)S(1)}, u32[]{:S(2)}, u32[]{:S(2)}) %all-to-all-start) | async-done | bytes 3104 | tf_op jit(solution)/shard_map/all_to_all | solution.py:104
  40.6 0.6 fusion.52
  41.7 0.6 gather_fusion
  42.3 0.4 convolution_convert_fusion.3
  42.6 14.4 %collective-permute-start.5 = (bf16[256,64]{0,1:T(8,128)(2,1)S(1)}, bf16[256,64]{0,1:T(8,128)(2,1)S(1)}, u32[]{:S(2)}, u32[]{:S(2)}) collective-permute-start(bf16[256,64]{0,1:T(8,128)(2,1)S(1)} %get-tuple-element.27), channel_id=1, source_target_pairs={{0,6},{1,7},{2,0},{3,1},{4,2},{5,3},{6,4},{7,5}} | collective-permute-start | bytes 98312 | tf_op jit(solution)/shard_map/ppermute | solution.py:72
  57.0 1.9 collective-permute-start.4
  58.9 2.7 %collective-permute-start.3 = (bf16[256,64]{0,1:T(8,128)(2,1)S(1)}, bf16[256,64]{0,1:T(8,128)(2,1)S(1)}, u32[]{:S(2)}, u32[]{:S(2)}) collective-permute-start(bf16[256,64]{0,1:T(8,128)(2,1)S(1)} %get-tuple-element.29), channel_id=1, source_target_pairs={{0,2},{1,3},{2,4},{3,5},{4,6},{5,7},{6,0},{7,1}} | collective-permute-start | bytes 98312 | tf_op jit(solution)/shard_map/ppermute | solution.py:72
  61.7 2.8 %collective-permute-done.4 = bf16[256,64]{0,1:T(8,128)(2,1)S(1)} collective-permute-done((bf16[256,64]{0,1:T(8,128)(2,1)S(1)}, bf16[256,64]{0,1:T(8,128)(2,1)S(1)}, u32[]{:S(2)}, u32[]{:S(2)}) %collective-permute-start.4) | collective-permute-done | bytes 32800 | tf_op jit(solution)/shard_map/ppermute | solution.py:72
  64.4 2.8 %collective-permute-done.3 = bf16[256,64]{0,1:T(8,128)(2,1)S(1)} collective-permute-done((bf16[256,64]{0,1:T(8,128)(2,1)S(1)}, bf16[256,64]{0,1:T(8,128)(2,1)S(1)}, u32[]{:S(2)}, u32[]{:S(2)}) %collective-permute-start.3) | collective-permute-done | bytes 32800 | tf_op jit(solution)/shard_map/ppermute | solution.py:72
  67.3 0.6 gather_fusion.1
  68.1 0.7 gather_fusion.2
  68.8 1.1 reshape.706
  69.9 3.4 %all-to-all-start.1 = ((bf16[8,2,8192]{2,1,0:T(2,128)(2,1)}), bf16[8,2,8192]{2,1,0:T(2,128)(2,1)S(1)}, u32[]{:S(2)}, u32[]{:S(2)}) async-start(bf16[8,2,8192]{2,1,0:T(2,128)(2,1)} %reshape.706), calls=%async_computation.1 | async-start | bytes 524288 | tf_op jit(solution)/shard_map/all_to_all | solution.py:169
  73.5 6.7 %all-to-all-done.1 = bf16[8,2,8192]{2,1,0:T(2,128)(2,1)S(1)} async-done(((bf16[8,2,8192]{2,1,0:T(2,128)(2,1)}), bf16[8,2,8192]{2,1,0:T(2,128)(2,1)S(1)}, u32[]{:S(2)}, u32[]{:S(2)}) %all-to-all-start.1) | async-done | bytes 262176 | tf_op jit(solution)/shard_map/all_to_all | solution.py:169
  80.6 1.2 scatter_fusion
  81.9 20.4 %all-gather.3.cloned.1.call-done = bf16[2048,1024]{1,0:T(8,128)(2,1)} async-done(((bf16[512,1024]{1,0:T(8,128)(2,1)}), bf16[2048,1024]{1,0:T(8,128)(2,1)}) %all-gather.3.cloned.1.call-update) | async-done | bytes 4194320 | tf_op jit(solution)/shard_map/all_gather | solution.py:56
  102.3 2.5 %compare_select_fusion = (bf16[4,256,1024]{2,1,0:T(8,128)(2,1)S(1)}, bf16[4,256,1024]{2,1,0:T(8,128)(2,1)S(1)}) fusion(bf16[4,512,1024]{2,1,0:T(8,128)(2,1)} %bitcast.108, s32[1024]{0:T(1024)S(1)} %select_reduce_fusion.1, s32[4,256]{1,0:T(4,128)S(1)} %eq.225), kind=kLoop, calls=%fused_computation.11 | loop fusion | flops 2097152 | bytes 8396800 | tf_op jit(solution)/shard_map/jit(_where)/select_n | solution.py:58
  104.9 0.3 bitcast_select_fusion
  105.2 0.9 copy-done.4
  106.1 0.8 fusion.11
  106.9 0.8 convolution_convert_fusion.2
  107.9 1.5 gather_fusion.3
  109.5 2.2 %reshape.708 = bf16[8,2,8192]{2,1,0:T(2,128)(2,1)} reshape(bf16[64,32,64]{2,1,0:T(8,128)(2,1)} %gather_fusion.3) | data formatting | bytes 524288
  111.7 3.4 %all-to-all-start.2 = ((bf16[8,2,8192]{2,1,0:T(2,128)(2,1)}), bf16[8,2,8192]{2,1,0:T(2,128)(2,1)S(1)}, u32[]{:S(2)}, u32[]{:S(2)}) async-start(bf16[8,2,8192]{2,1,0:T(2,128)(2,1)} %reshape.708), calls=%async_computation.2 | async-start | bytes 524288 | tf_op jit(solution)/shard_map/all_to_all | solution.py:169
  115.2 6.8 %all-to-all-done.2 = bf16[8,2,8192]{2,1,0:T(2,128)(2,1)S(1)} async-done(((bf16[8,2,8192]{2,1,0:T(2,128)(2,1)}), bf16[8,2,8192]{2,1,0:T(2,128)(2,1)S(1)}, u32[]{:S(2)}, u32[]{:S(2)}) %all-to-all-start.2) | async-done | bytes 262176 | tf_op jit(solution)/shard_map/all_to_all | solution.py:169
  121.9 1.2 reshape.709
  123.1 0.9 slice_convert_fusion.3
  124.0 1.2 scatter_fusion.1
  125.3 2.0 %fusion.14 = bf16[1024,64]{0,1:T(8,128)(2,1)S(1)} fusion(bf16[1024,1024]{1,0:T(8,128)(2,1)S(1)} %bitcast.106, f32[1,1,1024,64]{3,2,1,0:T(8,128)S(1)} %bitcast.120, f32[1,1,1024,256]{3,2,1,0:T(8,128)} %param.9, s32[]{:T(128)S(6)} %select_n.246), kind=kOutput, calls=%fused_computation.39 | convolution fusion | flops 134348800 | bytes 3014660 | tf_op jit(solution)/shard_map/dot_general | solution.py:160
  127.3 1.5 convolution_convert_fusion.1
  128.8 1.1 copy.68
  129.9 1.5 gather_fusion.4
  131.4 2.2 %reshape.710 = bf16[8,2,8192]{2,1,0:T(2,128)(2,1)} reshape(bf16[64,32,64]{2,1,0:T(8,128)(2,1)} %gather_fusion.4) | data formatting | bytes 524288
  133.6 3.6 %all-to-all-start.3 = ((bf16[8,2,8192]{2,1,0:T(2,128)(2,1)}), bf16[8,2,8192]{2,1,0:T(2,128)(2,1)S(1)}, u32[]{:S(2)}, u32[]{:S(2)}) async-start(bf16[8,2,8192]{2,1,0:T(2,128)(2,1)} %reshape.710), calls=%async_computation.3 | async-start | bytes 524288 | tf_op jit(solution)/shard_map/all_to_all | solution.py:169
  137.3 6.6 %all-to-all-done.3 = bf16[8,2,8192]{2,1,0:T(2,128)(2,1)S(1)} async-done(((bf16[8,2,8192]{2,1,0:T(2,128)(2,1)}), bf16[8,2,8192]{2,1,0:T(2,128)(2,1)S(1)}, u32[]{:S(2)}, u32[]{:S(2)}) %all-to-all-start.3) | async-done | bytes 262176 | tf_op jit(solution)/shard_map/all_to_all | solution.py:169
  143.9 1.2 reshape.711
  145.0 0.9 slice_convert_fusion.2
  146.0 1.2 scatter_fusion.2
  147.2 2.0 %select_convert_fusion = (bf16[1024,64]{0,1:T(8,128)(2,1)S(1)}, bf16[1024,64]{0,1:T(8,128)(2,1)S(1)}) fusion(bf16[1024,64]{0,1:T(8,128)(2,1)S(1)} %fusion.14, bf16[1024,64]{0,1:T(8,128)(2,1)S(1)} %fusion.11, pred[]{:T(512)S(6)} %eq.257, pred[]{:T(512)S(6)} %eq.256, pred[]{:T(512)S(6)} %eq.224, bf16[1024,1024]{1,0:T(8,128)(2,1)S(1)} %bitcast.107, ...), kind=kOutput, calls=%fused_computation.44 | convolution fusion | flops 134545408 | bytes 3407879 | tf_op jit(solution)/shard_map/dot_general | solution.py:160
  149.3 0.8 convolution_convert_fusion
  150.3 0.8 gather_fusion.5
  151.1 1.1 reshape.712
  152.2 3.4 %all-to-all-start.4 = ((bf16[8,2,8192]{2,1,0:T(2,128)(2,1)}), bf16[8,2,8192]{2,1,0:T(2,128)(2,1)S(1)}, u32[]{:S(2)}, u32[]{:S(2)}) async-start(bf16[8,2,8192]{2,1,0:T(2,128)(2,1)} %reshape.712), calls=%async_computation.4 | async-start | bytes 524288 | tf_op jit(solution)/shard_map/all_to_all | solution.py:169
  155.9 6.6 %all-to-all-done.4 = bf16[8,2,8192]{2,1,0:T(2,128)(2,1)S(1)} async-done(((bf16[8,2,8192]{2,1,0:T(2,128)(2,1)}), bf16[8,2,8192]{2,1,0:T(2,128)(2,1)S(1)}, u32[]{:S(2)}, u32[]{:S(2)}) %all-to-all-start.4) | async-done | bytes 262176 | tf_op jit(solution)/shard_map/all_to_all | solution.py:169
  162.5 0.3 reshape.713
  162.9 1.2 scatter_fusion.3
  164.4 0.4 all_to_all.28
  164.8 0.5 broadcast.589
  165.3 3.2 %reduce.2 = bf16[4,49152]{1,0:T(4,128)(2,1)S(1)} reduce(bf16[4,1,49152]{2,1,0:T(2,128)(2,1)S(1)} %all_to_all.28, bf16[]{:T(256)} %broadcast.589), dimensions={1}, to_apply=%all_to_all.28.reduce_sub_computation | reduce | bytes 786434 | tf_op jit(solution)/shard_map/all_to_all | solution.py:185
  168.5 1.2 reshape.714
  169.7 4.5 %all-to-all-start.5 = ((bf16[4,2,24576]{2,1,0:T(2,128)(2,1)}), bf16[4,2,24576]{2,1,0:T(2,128)(2,1)S(1)}, u32[]{:S(2)}, u32[]{:S(2)}) async-start(bf16[4,2,24576]{2,1,0:T(2,128)(2,1)} %reshape.714), calls=%async_computation.5 | async-start | bytes 786432 | tf_op jit(solution)/shard_map/all_to_all | solution.py:185
  174.1 11.0 %all-to-all-done.5 = bf16[4,2,24576]{2,1,0:T(2,128)(2,1)S(1)} async-done(((bf16[4,2,24576]{2,1,0:T(2,128)(2,1)}), bf16[4,2,24576]{2,1,0:T(2,128)(2,1)S(1)}, u32[]{:S(2)}, u32[]{:S(2)}) %all-to-all-start.5) | async-done | bytes 393248 | tf_op jit(solution)/shard_map/all_to_all | solution.py:185
  185.2 0.4 reshape.715
  185.6 2.4 %convert_reduce_fusion = f32[4,49152]{1,0:T(4,128)S(1)} fusion(bf16[4,1,49152]{2,1,0:T(2,128)(2,1)S(1)} %reshape.715), kind=kLoop, calls=%fused_computation.23 | loop fusion | flops 196608 | bytes 1179648 | tf_op jit(solution)/shard_map/convert_element_type | solution.py:188
  187.9 0.8 reshape.607
  189.5 1.0 copy.75
  190.5 0.7 select_bitcast_fusion
  (105 shorter events, 5.0 us)
Async XLA Ops:
  7.2 2.7 %copy-start.5 = (bf16[1,1,256,1024]{3,2,1,0:T(8,128)(2,1)S(1)}, bf16[1,1,256,1024]{3,2,1,0:T(8,128)(2,1)}, u32[]{:S(2)}) copy-start(bf16[1,1,256,1024]{3,2,1,0:T(8,128)(2,1)} %param.10) | copy-start | bytes 1572868
  7.2 2.5 %copy-start.9 = (s32[1,1,8]{2,1,0:T(1,128)S(1)}, s32[1,1,8]{2,1,0:T(1,128)}, u32[]{:S(2)}) copy-start(s32[1,1,8]{2,1,0:T(1,128)} %param.12) | copy-start | bytes 100
  7.2 2.7 %copy-start.3 = (f32[1,1,1024,256]{3,2,1,0:T(8,128)S(1)}, f32[1,1,1024,256]{3,2,1,0:T(8,128)}, u32[]{:S(2)}) copy-start(f32[1,1,1024,256]{3,2,1,0:T(8,128)} %param.9) | copy-start | bytes 3145732
  7.2 95.1 %all-gather.3.cloned.1.call-start = ((), (), s32[]{:S(2)}) async-start(), calls=%async_computation.6 | async-start | bytes 5242880 | tf_op jit(solution)/shard_map/all_gather | solution.py:56
  7.2 15.5 %copy-start.13 = (s32[1,1,8]{2,1,0:T(1,128)S(1)}, s32[1,1,8]{2,1,0:T(1,128)}, u32[]{:S(2)}) copy-start(s32[1,1,8]{2,1,0:T(1,128)} %param.14) | copy-start | bytes 100
  7.3 15.5 %copy-start.14 = (s32[1,1,8]{2,1,0:T(1,128)S(1)}, s32[1,1,8]{2,1,0:T(1,128)}, u32[]{:S(2)}) copy-start(s32[1,1,8]{2,1,0:T(1,128)} %param.13) | copy-start | bytes 100
  7.3 15.5 %copy-start.15 = (s32[1,1,8]{2,1,0:T(1,128)S(1)}, s32[1,1,8]{2,1,0:T(1,128)}, u32[]{:S(2)}) copy-start(s32[1,1,8]{2,1,0:T(1,128)} %param.15) | copy-start | bytes 100
  9.6 17.4 %copy-start.6 = (bf16[1,1,8,32,1024]{4,3,2,1,0:T(8,128)(2,1)S(1)}, bf16[1,1,8,32,1024]{4,3,2,1,0:T(8,128)(2,1)}, u32[]{:S(2)}) copy-start(bf16[1,1,8,32,1024]{4,3,2,1,0:T(8,128)(2,1)} %param.11) | copy-start | bytes 1572868
  10.9 30.6 %collective-permute-start.2 = (bf16[256,256]{1,0:T(8,128)(2,1)S(1)}, bf16[256,256]{1,0:T(8,128)(2,1)S(1)}, u32[]{:S(2)}, u32[]{:S(2)}) collective-permute-start(bf16[256,256]{1,0:T(8,128)(2,1)S(1)} %get-tuple-element.37), channel_id=1, source_target_pairs={{0,6},{1,7},{2,0},{3,1},{4,2},{5,3},{6,4},{7,5}} | collective-permute-start | bytes 393224 | tf_op jit(solution)/shard_map/ppermute | solution.py:72
  17.9 23.7 %collective-permute-start.1 = (bf16[256,256]{1,0:T(8,128)(2,1)S(1)}, bf16[256,256]{1,0:T(8,128)(2,1)S(1)}, u32[]{:S(2)}, u32[]{:S(2)}) collective-permute-start(bf16[256,256]{1,0:T(8,128)(2,1)S(1)} %get-tuple-element.37), channel_id=1, source_target_pairs={{0,4},{1,5},{2,6},{3,7},{4,0},{5,1},{6,2},{7,3}} | collective-permute-start | bytes 393224 | tf_op jit(solution)/shard_map/ppermute | solution.py:72
  19.8 21.8 %collective-permute-start = (bf16[256,256]{1,0:T(8,128)(2,1)S(1)}, bf16[256,256]{1,0:T(8,128)(2,1)S(1)}, u32[]{:S(2)}, u32[]{:S(2)}) collective-permute-start(bf16[256,256]{1,0:T(8,128)(2,1)S(1)} %get-tuple-element.37), channel_id=1, source_target_pairs={{0,2},{1,3},{2,4},{3,5},{4,6},{5,7},{6,0},{7,1}} | collective-permute-start | bytes 393224 | tf_op jit(solution)/shard_map/ppermute | solution.py:72
  23.4 16.1 %all-to-all-start = ((s32[32,3,8]{2,1,0:T(4,128)}), s32[32,3,8]{2,1,0:T(4,128)S(1)}, u32[]{:S(2)}, u32[]{:S(2)}) async-start(s32[32,3,8]{2,1,0:T(4,128)} %broadcast_in_dim.180), calls=%async_computation | async-start | bytes 131072 | tf_op jit(solution)/shard_map/all_to_all | solution.py:104
  41.6 26.5 %copy-start.8 = (s32[1024]{0:T(1024)}, s32[1024]{0:T(1024)S(1)}, u32[]{:S(2)}) copy-start(s32[1024]{0:T(1024)S(1)} %pad_clamp_fusion) | copy-start | bytes 12292
  42.6 19.0 %collective-permute-start.5 = (bf16[256,64]{0,1:T(8,128)(2,1)S(1)}, bf16[256,64]{0,1:T(8,128)(2,1)S(1)}, u32[]{:S(2)}, u32[]{:S(2)}) collective-permute-start(bf16[256,64]{0,1:T(8,128)(2,1)S(1)} %get-tuple-element.27), channel_id=1, source_target_pairs={{0,6},{1,7},{2,0},{3,1},{4,2},{5,3},{6,4},{7,5}} | collective-permute-start | bytes 98312 | tf_op jit(solution)/shard_map/ppermute | solution.py:72
  57.0 7.4 %collective-permute-start.4 = (bf16[256,64]{0,1:T(8,128)(2,1)S(1)}, bf16[256,64]{0,1:T(8,128)(2,1)S(1)}, u32[]{:S(2)}, u32[]{:S(2)}) collective-permute-start(bf16[256,64]{0,1:T(8,128)(2,1)S(1)} %get-tuple-element.28), channel_id=1, source_target_pairs={{0,4},{1,5},{2,6},{3,7},{4,0},{5,1},{6,2},{7,3}} | collective-permute-start | bytes 98312 | tf_op jit(solution)/shard_map/ppermute | solution.py:72
  58.9 8.3 %collective-permute-start.3 = (bf16[256,64]{0,1:T(8,128)(2,1)S(1)}, bf16[256,64]{0,1:T(8,128)(2,1)S(1)}, u32[]{:S(2)}, u32[]{:S(2)}) collective-permute-start(bf16[256,64]{0,1:T(8,128)(2,1)S(1)} %get-tuple-element.29), channel_id=1, source_target_pairs={{0,2},{1,3},{2,4},{3,5},{4,6},{5,7},{6,0},{7,1}} | collective-permute-start | bytes 98312 | tf_op jit(solution)/shard_map/ppermute | solution.py:72
  69.9 10.3 %all-to-all-start.1 = ((bf16[8,2,8192]{2,1,0:T(2,128)(2,1)}), bf16[8,2,8192]{2,1,0:T(2,128)(2,1)S(1)}, u32[]{:S(2)}, u32[]{:S(2)}) async-start(bf16[8,2,8192]{2,1,0:T(2,128)(2,1)} %reshape.706), calls=%async_computation.1 | async-start | bytes 524288 | tf_op jit(solution)/shard_map/all_to_all | solution.py:169
  104.9 1.2 copy-start.4
  105.2 1.7 copy-start
  106.9 8.1 %copy-start.12 = (s32[2,8]{1,0:T(2,128)S(1)}, s32[2,8]{1,0:T(2,128)}, u32[]{:S(2)}) copy-start(s32[2,8]{1,0:T(2,128)} %get-tuple-element.35) | copy-start | bytes 196
  111.7 10.3 %all-to-all-start.2 = ((bf16[8,2,8192]{2,1,0:T(2,128)(2,1)}), bf16[8,2,8192]{2,1,0:T(2,128)(2,1)S(1)}, u32[]{:S(2)}, u32[]{:S(2)}) async-start(bf16[8,2,8192]{2,1,0:T(2,128)(2,1)} %reshape.708), calls=%async_computation.2 | async-start | bytes 524288 | tf_op jit(solution)/shard_map/all_to_all | solution.py:169
  125.2 2.1 %copy-start.1 = (bf16[1024,1024]{1,0:T(8,128)(2,1)S(1)}, bf16[1024,1024]{1,0:T(8,128)(2,1)}, u32[]{:S(2)}) copy-start(bf16[1024,1024]{1,0:T(8,128)(2,1)} %copy-done) | copy-start | bytes 6291460
  127.3 9.9 %copy-start.11 = (s32[2,8]{1,0:T(2,128)S(1)}, s32[2,8]{1,0:T(2,128)}, u32[]{:S(2)}) copy-start(s32[2,8]{1,0:T(2,128)} %get-tuple-element.34) | copy-start | bytes 196
  133.6 10.3 %all-to-all-start.3 = ((bf16[8,2,8192]{2,1,0:T(2,128)(2,1)}), bf16[8,2,8192]{2,1,0:T(2,128)(2,1)S(1)}, u32[]{:S(2)}, u32[]{:S(2)}) async-start(bf16[8,2,8192]{2,1,0:T(2,128)(2,1)} %reshape.710), calls=%async_computation.3 | async-start | bytes 524288 | tf_op jit(solution)/shard_map/all_to_all | solution.py:169
  147.2 2.1 %copy-start.2 = (bf16[1024,1024]{1,0:T(8,128)(2,1)S(1)}, bf16[1024,1024]{1,0:T(8,128)(2,1)}, u32[]{:S(2)}) copy-start(bf16[1024,1024]{1,0:T(8,128)(2,1)} %copy-done) | copy-start | bytes 6291460
  149.3 6.3 %copy-start.10 = (s32[2,8]{1,0:T(2,128)S(1)}, s32[2,8]{1,0:T(2,128)}, u32[]{:S(2)}) copy-start(s32[2,8]{1,0:T(2,128)} %get-tuple-element.33) | copy-start | bytes 196
  152.2 10.3 %all-to-all-start.4 = ((bf16[8,2,8192]{2,1,0:T(2,128)(2,1)}), bf16[8,2,8192]{2,1,0:T(2,128)(2,1)S(1)}, u32[]{:S(2)}, u32[]{:S(2)}) async-start(bf16[8,2,8192]{2,1,0:T(2,128)(2,1)} %reshape.712), calls=%async_computation.4 | async-start | bytes 524288 | tf_op jit(solution)/shard_map/all_to_all | solution.py:169
  169.7 15.5 %all-to-all-start.5 = ((bf16[4,2,24576]{2,1,0:T(2,128)(2,1)}), bf16[4,2,24576]{2,1,0:T(2,128)(2,1)S(1)}, u32[]{:S(2)}, u32[]{:S(2)}) async-start(bf16[4,2,24576]{2,1,0:T(2,128)(2,1)} %reshape.714), calls=%async_computation.5 | async-start | bytes 786432 | tf_op jit(solution)/shard_map/all_to_all | solution.py:185
  188.8 1.7 copy-start.7
Sparse Core Ops, SparseCore 0:
  9.8 92.5 all-gather.2

commit v20 on v17

--- a/solution.py
+++ b/solution.py
@@ -164,10 +164,14 @@
             updates = jnp.dot(
                 tiles_full, solved_now.astype(jnp.bfloat16), preferred_element_type=jnp.float32
             ).astype(jnp.bfloat16)
-        updates = updates.reshape(group_tiles + 1, block_rows, cols)
+        updates = updates.reshape(group_tiles + 1, block_rows * cols)
         sending = jnp.take(updates, send_index, axis=0, mode="clip")
         incoming = lax.all_to_all(
-            sending, ("lvl", "pcol"), split_axis=0, concat_axis=0, tiled=True
+            sending.reshape(groups, slots * block_rows * cols),
+            ("lvl", "pcol"),
+            split_axis=0,
+            concat_axis=0,
+            tiled=True,
         )
         incoming = incoming.reshape(n_lvl, n_pcol * slots, block_rows, cols)[section]
         acc = acc.at[recv_block[section]].add(incoming.astype(jnp.float32), mode="clip")

time: 191 us -> 203 us (1.063)
  other arithmetic: 15.3 us -> 27.6 us
  local copies, waits for them, and re-layouts: 21.2 us -> 27.2 us
  waiting for transfers between devices: 76.2 us -> 70.5 us
    all_to_all x0 -> x4, other arithmetic: none -> 10 us  [per_device(): lax.all_to_all(sending.reshape(groups, slots * block_rows * cols), ('lvl'...]
    all_to_all x0 -> x5, local copies, waits for them, and re-layouts: none -> 4.12 us  [per_device(): lax.all_to_all(sending.reshape(groups, slots * block_rows * cols), ('lvl'...]
    all_gather x1, waiting for transfers between devices: 20.4 us -> 16.6 us  [per_device(): gathered = lax.all_gather(raw, 'prow', axis=0)]
  transfers between devices with their start and end apart: 13 -> 13, of which waited for: 9 -> 9; matrix products, arithmetic and copies ran while one was open for 5% -> 8% of each run, Pallas kernels for 0% -> 0%
where the time goes in v20:
time: 203 us; the launch traced here: 202 us
  waiting for transfers between devices  70.5 us (35%)
  starting transfers between devices  52.4 us (26%)
  other arithmetic  27.6 us (14%)
  local copies, waits for them, and re-layouts  27.2 us (13%)
  between operations  14.9 us (7%)
  matrix products  9.4 us (5%)
    ppermute x6, starting transfers between devices, level0_shift(): return lax.ppermute(x, all_axes, pairs)  30.8 us
    all_to_all x4, waiting for transfers between devices, per_device(): lax.all_to_all(sending.reshape(groups, slots * block_rows * cols), ('lvl'...  24.9 us
    all_gather x1, waiting for transfers between devices, per_device(): gathered = lax.all_gather(raw, 'prow', axis=0)  16.6 us
    all_to_all x4, starting transfers between devices, per_device(): lax.all_to_all(sending.reshape(groups, slots * block_rows * cols), ('lvl'...  13.8 us
    all_to_all x1, waiting for transfers between devices, per_device(): lax.all_to_all(jnp.broadcast_to(meta[None], (devices,) + meta.shape), ('l...  12.4 us
    all_to_all x1, waiting for transfers between devices, per_device(): lax.all_to_all(final, 'prow', split_axis=0, concat_axis=0, tiled=True)  11 us
    unnamed x42, local copies, waits for them, and re-layouts  10.1 us
    all_to_all x4, other arithmetic, per_device(): lax.all_to_all(sending.reshape(groups, slots * block_rows * cols), ('lvl'...  10 us
  transfers between devices with their start and end apart: 13, of which 9 were waited for; matrix products, arithmetic and copies ran while one was open for 8% of the time, Pallas kernels for 0%

profile of v20, /device:TPU:0, one launch (start us, length us, event | category | flops | bytes accessed | tf_op | source)
XLA Modules:
  0.0 202.0 jit_solution(3305653307694351727)
XLA Ops:
  7.3 2.3 %pad_maximum_fusion = bf16[512,1024]{1,0:T(8,128)(2,1)} fusion(bf16[256,1024]{1,0:T(8,128)(2,1)} %bitcast.113, bf16[256,1024]{1,0:T(8,128)(2,1)} %bitcast.109), kind=kLoop, calls=%fused_computation.19 | loop fusion | flops 2097152 | bytes 2097152 | tf_op jit(solution)/shard_map/concatenate | solution.py:53
  9.9 1.1 fusion.57
  10.9 6.9 %collective-permute-start.2 = (bf16[256,256]{1,0:T(8,128)(2,1)S(1)}, bf16[256,256]{1,0:T(8,128)(2,1)S(1)}, u32[]{:S(2)}, u32[]{:S(2)}) collective-permute-start(bf16[256,256]{1,0:T(8,128)(2,1)S(1)} %get-tuple-element.37), channel_id=1, source_target_pairs={{0,6},{1,7},{2,0},{3,1},{4,2},{5,3},{6,4},{7,5}} | collective-permute-start | bytes 393224 | tf_op jit(solution)/shard_map/ppermute | solution.py:72
  17.9 1.9 collective-permute-start.1
  19.8 2.9 %collective-permute-start = (bf16[256,256]{1,0:T(8,128)(2,1)S(1)}, bf16[256,256]{1,0:T(8,128)(2,1)S(1)}, u32[]{:S(2)}, u32[]{:S(2)}) collective-permute-start(bf16[256,256]{1,0:T(8,128)(2,1)S(1)} %get-tuple-element.37), channel_id=1, source_target_pairs={{0,2},{1,3},{2,4},{3,5},{4,6},{5,7},{6,0},{7,1}} | collective-permute-start | bytes 393224 | tf_op jit(solution)/shard_map/ppermute | solution.py:72
  22.8 0.6 broadcast_in_dim.180
  23.4 3.2 %all-to-all-start = ((s32[32,3,8]{2,1,0:T(4,128)}), s32[32,3,8]{2,1,0:T(4,128)S(1)}, u32[]{:S(2)}, u32[]{:S(2)}) async-start(s32[32,3,8]{2,1,0:T(4,128)} %broadcast_in_dim.180), calls=%async_computation | async-start | bytes 131072 | tf_op jit(solution)/shard_map/all_to_all | solution.py:104
  27.2 12.4 %all-to-all-done = s32[32,3,8]{2,1,0:T(4,128)S(1)} async-done(((s32[32,3,8]{2,1,0:T(4,128)}), s32[32,3,8]{2,1,0:T(4,128)S(1)}, u32[]{:S(2)}, u32[]{:S(2)}) %all-to-all-start) | async-done | bytes 3104 | tf_op jit(solution)/shard_map/all_to_all | solution.py:104
  40.6 0.6 fusion.56
  41.7 0.6 gather_fusion
  42.6 14.4 %collective-permute-start.5 = (bf16[256,64]{0,1:T(8,128)(2,1)S(1)}, bf16[256,64]{0,1:T(8,128)(2,1)S(1)}, u32[]{:S(2)}, u32[]{:S(2)}) collective-permute-start(bf16[256,64]{0,1:T(8,128)(2,1)S(1)} %get-tuple-element.27), channel_id=1, source_target_pairs={{0,6},{1,7},{2,0},{3,1},{4,2},{5,3},{6,4},{7,5}} | collective-permute-start | bytes 98312 | tf_op jit(solution)/shard_map/ppermute | solution.py:72
  57.0 1.9 collective-permute-start.4
  58.9 2.7 %collective-permute-start.3 = (bf16[256,64]{0,1:T(8,128)(2,1)S(1)}, bf16[256,64]{0,1:T(8,128)(2,1)S(1)}, u32[]{:S(2)}, u32[]{:S(2)}) collective-permute-start(bf16[256,64]{0,1:T(8,128)(2,1)S(1)} %get-tuple-element.29), channel_id=1, source_target_pairs={{0,2},{1,3},{2,4},{3,5},{4,6},{5,7},{6,0},{7,1}} | collective-permute-start | bytes 98312 | tf_op jit(solution)/shard_map/ppermute | solution.py:72
  61.7 2.8 %collective-permute-done.4 = bf16[256,64]{0,1:T(8,128)(2,1)S(1)} collective-permute-done((bf16[256,64]{0,1:T(8,128)(2,1)S(1)}, bf16[256,64]{0,1:T(8,128)(2,1)S(1)}, u32[]{:S(2)}, u32[]{:S(2)}) %collective-permute-start.4) | collective-permute-done | bytes 32800 | tf_op jit(solution)/shard_map/ppermute | solution.py:72
  64.4 2.8 %collective-permute-done.3 = bf16[256,64]{0,1:T(8,128)(2,1)S(1)} collective-permute-done((bf16[256,64]{0,1:T(8,128)(2,1)S(1)}, bf16[256,64]{0,1:T(8,128)(2,1)S(1)}, u32[]{:S(2)}, u32[]{:S(2)}) %collective-permute-start.3) | collective-permute-done | bytes 32800 | tf_op jit(solution)/shard_map/ppermute | solution.py:72
  67.3 0.6 gather_fusion.1
  68.4 0.7 gather_fusion.2
  70.1 2.2 %reduce.8 = bf16[8,16384]{1,0:T(8,128)(2,1)S(1)} reduce(bf16[8,1,16384]{2,1,0:T(2,128)(2,1)S(1)} %all_to_all.40, bf16[]{:T(256)} %broadcast.592), dimensions={1}, to_apply=%all_to_all.40.reduce_sub_computation | reduce | bytes 524290 | tf_op jit(solution)/shard_map/all_to_all | solution.py:169
  72.3 0.9 reshape.736
  73.2 3.4 %all-to-all-start.1 = ((bf16[8,2,8192]{2,1,0:T(2,128)(2,1)}), bf16[8,2,8192]{2,1,0:T(2,128)(2,1)S(1)}, u32[]{:S(2)}, u32[]{:S(2)}) async-start(bf16[8,2,8192]{2,1,0:T(2,128)(2,1)} %reshape.736), calls=%async_computation.1 | async-start | bytes 524288 | tf_op jit(solution)/shard_map/all_to_all | solution.py:169
  76.8 6.7 %all-to-all-done.1 = bf16[8,2,8192]{2,1,0:T(2,128)(2,1)S(1)} async-done(((bf16[8,2,8192]{2,1,0:T(2,128)(2,1)}), bf16[8,2,8192]{2,1,0:T(2,128)(2,1)S(1)}, u32[]{:S(2)}, u32[]{:S(2)}) %all-to-all-start.1) | async-done | bytes 262176 | tf_op jit(solution)/shard_map/all_to_all | solution.py:169
  84.4 1.2 scatter_fusion
  85.7 16.6 %all-gather.3.cloned.1.call-done = bf16[2048,1024]{1,0:T(8,128)(2,1)} async-done(((bf16[512,1024]{1,0:T(8,128)(2,1)}), bf16[2048,1024]{1,0:T(8,128)(2,1)}) %all-gather.3.cloned.1.call-update) | async-done | bytes 4194320 | tf_op jit(solution)/shard_map/all_gather | solution.py:56
  102.3 2.5 %compare_select_fusion = (bf16[4,256,1024]{2,1,0:T(8,128)(2,1)S(1)}, bf16[4,256,1024]{2,1,0:T(8,128)(2,1)S(1)}) fusion(bf16[4,512,1024]{2,1,0:T(8,128)(2,1)} %bitcast.107, s32[1024]{0:T(1024)S(1)} %select_reduce_fusion.1, s32[4,256]{1,0:T(4,128)S(1)} %eq.225), kind=kLoop, calls=%fused_computation.11 | loop fusion | flops 2097152 | bytes 8396800 | tf_op jit(solution)/shard_map/jit(_where)/select_n | solution.py:58
  105.2 0.9 copy-done.4
  106.1 0.8 fusion.11
  106.9 0.8 convolution_convert_fusion.2
  108.2 1.6 gather_fusion.3
  109.8 1.3 all_to_all.41
  111.1 2.9 %reduce.9 = bf16[8,16384]{1,0:T(8,128)(2,1)} reduce(bf16[8,1,16384]{2,1,0:T(2,128)(2,1)S(1)} %all_to_all.41, bf16[]{:T(256)} %broadcast.592), dimensions={1}, to_apply=%all_to_all.41.reduce_sub_computation | reduce | bytes 524290 | tf_op jit(solution)/shard_map/all_to_all | solution.py:169
  114.0 1.9 reshape.738
  115.8 3.6 %all-to-all-start.2 = ((bf16[8,2,8192]{2,1,0:T(2,128)(2,1)}), bf16[8,2,8192]{2,1,0:T(2,128)(2,1)S(1)}, u32[]{:S(2)}, u32[]{:S(2)}) async-start(bf16[8,2,8192]{2,1,0:T(2,128)(2,1)} %reshape.738), calls=%async_computation.2 | async-start | bytes 524288 | tf_op jit(solution)/shard_map/all_to_all | solution.py:169
  119.4 0.8 squeeze.32
  120.2 5.9 %all-to-all-done.2 = bf16[8,2,8192]{2,1,0:T(2,128)(2,1)S(1)} async-done(((bf16[8,2,8192]{2,1,0:T(2,128)(2,1)}), bf16[8,2,8192]{2,1,0:T(2,128)(2,1)S(1)}, u32[]{:S(2)}, u32[]{:S(2)}) %all-to-all-start.2) | async-done | bytes 262176 | tf_op jit(solution)/shard_map/all_to_all | solution.py:169
  126.1 1.0 reshape.739
  127.1 1.3 fusion.22
  128.6 1.2 scatter_fusion.1
  129.9 2.0 %fusion.14 = bf16[1024,64]{0,1:T(8,128)(2,1)S(1)} fusion(bf16[1024,1024]{1,0:T(8,128)(2,1)S(1)} %bitcast.105, f32[1,1,1024,64]{3,2,1,0:T(8,128)S(1)} %bitcast.115, f32[1,1,1024,256]{3,2,1,0:T(8,128)} %param.9, s32[]{:T(128)S(6)} %select_n.246), kind=kOutput, calls=%fused_computation.36 | convolution fusion | flops 134348800 | bytes 3014660 | tf_op jit(solution)/shard_map/dot_general | solution.py:160
  131.9 1.5 convolution_convert_fusion.1
  133.4 1.1 copy.70
  134.7 1.6 gather_fusion.4
  136.3 1.3 all_to_all.42
  137.7 2.9 %reduce.10 = bf16[8,16384]{1,0:T(8,128)(2,1)} reduce(bf16[8,1,16384]{2,1,0:T(2,128)(2,1)S(1)} %all_to_all.42, bf16[]{:T(256)} %broadcast.592), dimensions={1}, to_apply=%all_to_all.42.reduce_sub_computation | reduce | bytes 524290 | tf_op jit(solution)/shard_map/all_to_all | solution.py:169
  140.5 1.9 reshape.740
  142.4 3.4 %all-to-all-start.3 = ((bf16[8,2,8192]{2,1,0:T(2,128)(2,1)}), bf16[8,2,8192]{2,1,0:T(2,128)(2,1)S(1)}, u32[]{:S(2)}, u32[]{:S(2)}) async-start(bf16[8,2,8192]{2,1,0:T(2,128)(2,1)} %reshape.740), calls=%async_computation.3 | async-start | bytes 524288 | tf_op jit(solution)/shard_map/all_to_all | solution.py:169
  145.9 0.8 squeeze.33
  146.6 0.6 fusion.48
  147.2 5.5 %all-to-all-done.3 = bf16[8,2,8192]{2,1,0:T(2,128)(2,1)S(1)} async-done(((bf16[8,2,8192]{2,1,0:T(2,128)(2,1)}), bf16[8,2,8192]{2,1,0:T(2,128)(2,1)S(1)}, u32[]{:S(2)}, u32[]{:S(2)}) %all-to-all-start.3) | async-done | bytes 262176 | tf_op jit(solution)/shard_map/all_to_all | solution.py:169
  152.7 1.0 reshape.741
  153.7 1.3 fusion.21
  155.2 1.3 scatter_fusion.2
  156.6 2.0 %select_convert_fusion = (bf16[1024,64]{0,1:T(8,128)(2,1)S(1)}, bf16[1024,64]{0,1:T(8,128)(2,1)S(1)}) fusion(bf16[1024,64]{0,1:T(8,128)(2,1)S(1)} %copy-done.8, bf16[1024,64]{0,1:T(8,128)(2,1)S(1)} %fusion.11, pred[]{:T(512)S(6)} %eq.257, pred[]{:T(512)S(6)} %eq.256, pred[]{:T(512)S(6)} %eq.224, bf16[1024,1024]{1,0:T(8,128)(2,1)S(1)} %bitcast.106, ...), kind=kOutput, calls=%fused_computation.41 | convolution fusion | flops 134545408 | bytes 3407879 | tf_op jit(solution)/shard_map/dot_general | solution.py:160
  158.7 0.8 convolution_convert_fusion
  159.9 0.9 gather_fusion.5
  161.2 2.2 %reduce.11 = bf16[8,16384]{1,0:T(8,128)(2,1)S(1)} reduce(bf16[8,1,16384]{2,1,0:T(2,128)(2,1)S(1)} %all_to_all.43, bf16[]{:T(256)} %broadcast.592), dimensions={1}, to_apply=%all_to_all.43.reduce_sub_computation | reduce | bytes 524290 | tf_op jit(solution)/shard_map/all_to_all | solution.py:169
  163.4 0.9 reshape.742
  164.3 3.4 %all-to-all-start.4 = ((bf16[8,2,8192]{2,1,0:T(2,128)(2,1)}), bf16[8,2,8192]{2,1,0:T(2,128)(2,1)S(1)}, u32[]{:S(2)}, u32[]{:S(2)}) async-start(bf16[8,2,8192]{2,1,0:T(2,128)(2,1)} %reshape.742), calls=%async_computation.4 | async-start | bytes 524288 | tf_op jit(solution)/shard_map/all_to_all | solution.py:169
  167.8 6.8 %all-to-all-done.4 = bf16[8,2,8192]{2,1,0:T(2,128)(2,1)S(1)} async-done(((bf16[8,2,8192]{2,1,0:T(2,128)(2,1)}), bf16[8,2,8192]{2,1,0:T(2,128)(2,1)S(1)}, u32[]{:S(2)}, u32[]{:S(2)}) %all-to-all-start.4) | async-done | bytes 262176 | tf_op jit(solution)/shard_map/all_to_all | solution.py:169
  175.5 1.2 scatter_fusion.3
  176.8 0.8 pad_maximum_fusion.2
  177.6 4.6 %all-to-all-start.5 = ((bf16[4,768,64]{1,2,0:T(8,128)(2,1)}), bf16[4,768,64]{1,2,0:T(8,128)(2,1)S(1)}, u32[]{:S(2)}, u32[]{:S(2)}) async-start(bf16[4,768,64]{1,2,0:T(8,128)(2,1)} %pad_maximum_fusion.2), calls=%async_computation.5 | async-start | bytes 786432 | tf_op jit(solution)/shard_map/all_to_all | solution.py:188
  182.2 11.0 %all-to-all-done.5 = bf16[4,768,64]{1,2,0:T(8,128)(2,1)S(1)} async-done(((bf16[4,768,64]{1,2,0:T(8,128)(2,1)}), bf16[4,768,64]{1,2,0:T(8,128)(2,1)S(1)}, u32[]{:S(2)}, u32[]{:S(2)}) %all-to-all-start.5) | async-done | bytes 393248 | tf_op jit(solution)/shard_map/all_to_all | solution.py:188
  193.5 1.0 copy.77
  194.5 0.7 select_bitcast_fusion
  (114 shorter events, 8.9 us)
Async XLA Ops:
  7.2 2.7 %copy-start.5 = (bf16[1,1,256,1024]{3,2,1,0:T(8,128)(2,1)S(1)}, bf16[1,1,256,1024]{3,2,1,0:T(8,128)(2,1)}, u32[]{:S(2)}) copy-start(bf16[1,1,256,1024]{3,2,1,0:T(8,128)(2,1)} %param.10) | copy-start | bytes 1572868
  7.2 2.5 %copy-start.11 = (s32[1,1,8]{2,1,0:T(1,128)S(1)}, s32[1,1,8]{2,1,0:T(1,128)}, u32[]{:S(2)}) copy-start(s32[1,1,8]{2,1,0:T(1,128)} %param.12) | copy-start | bytes 100
  7.2 2.7 %copy-start.3 = (f32[1,1,1024,256]{3,2,1,0:T(8,128)S(1)}, f32[1,1,1024,256]{3,2,1,0:T(8,128)}, u32[]{:S(2)}) copy-start(f32[1,1,1024,256]{3,2,1,0:T(8,128)} %param.9) | copy-start | bytes 3145732
  7.2 95.1 %all-gather.3.cloned.1.call-start = ((), (), s32[]{:S(2)}) async-start(), calls=%async_computation.6 | async-start | bytes 5242880 | tf_op jit(solution)/shard_map/all_gather | solution.py:56
  7.2 15.5 %copy-start.13 = (s32[1,1,8]{2,1,0:T(1,128)S(1)}, s32[1,1,8]{2,1,0:T(1,128)}, u32[]{:S(2)}) copy-start(s32[1,1,8]{2,1,0:T(1,128)} %param.14) | copy-start | bytes 100
  7.3 15.5 %copy-start.14 = (s32[1,1,8]{2,1,0:T(1,128)S(1)}, s32[1,1,8]{2,1,0:T(1,128)}, u32[]{:S(2)}) copy-start(s32[1,1,8]{2,1,0:T(1,128)} %param.13) | copy-start | bytes 100
  7.3 15.5 %copy-start.15 = (s32[1,1,8]{2,1,0:T(1,128)S(1)}, s32[1,1,8]{2,1,0:T(1,128)}, u32[]{:S(2)}) copy-start(s32[1,1,8]{2,1,0:T(1,128)} %param.15) | copy-start | bytes 100
  9.6 17.4 %copy-start.6 = (bf16[1,1,8,32,1024]{4,3,2,1,0:T(8,128)(2,1)S(1)}, bf16[1,1,8,32,1024]{4,3,2,1,0:T(8,128)(2,1)}, u32[]{:S(2)}) copy-start(bf16[1,1,8,32,1024]{4,3,2,1,0:T(8,128)(2,1)} %param.11) | copy-start | bytes 1572868
  10.9 30.6 %collective-permute-start.2 = (bf16[256,256]{1,0:T(8,128)(2,1)S(1)}, bf16[256,256]{1,0:T(8,128)(2,1)S(1)}, u32[]{:S(2)}, u32[]{:S(2)}) collective-permute-start(bf16[256,256]{1,0:T(8,128)(2,1)S(1)} %get-tuple-element.37), channel_id=1, source_target_pairs={{0,6},{1,7},{2,0},{3,1},{4,2},{5,3},{6,4},{7,5}} | collective-permute-start | bytes 393224 | tf_op jit(solution)/shard_map/ppermute | solution.py:72
  17.9 23.7 %collective-permute-start.1 = (bf16[256,256]{1,0:T(8,128)(2,1)S(1)}, bf16[256,256]{1,0:T(8,128)(2,1)S(1)}, u32[]{:S(2)}, u32[]{:S(2)}) collective-permute-start(bf16[256,256]{1,0:T(8,128)(2,1)S(1)} %get-tuple-element.37), channel_id=1, source_target_pairs={{0,4},{1,5},{2,6},{3,7},{4,0},{5,1},{6,2},{7,3}} | collective-permute-start | bytes 393224 | tf_op jit(solution)/shard_map/ppermute | solution.py:72
  19.8 21.8 %collective-permute-start = (bf16[256,256]{1,0:T(8,128)(2,1)S(1)}, bf16[256,256]{1,0:T(8,128)(2,1)S(1)}, u32[]{:S(2)}, u32[]{:S(2)}) collective-permute-start(bf16[256,256]{1,0:T(8,128)(2,1)S(1)} %get-tuple-element.37), channel_id=1, source_target_pairs={{0,2},{1,3},{2,4},{3,5},{4,6},{5,7},{6,0},{7,1}} | collective-permute-start | bytes 393224 | tf_op jit(solution)/shard_map/ppermute | solution.py:72
  23.4 16.1 %all-to-all-start = ((s32[32,3,8]{2,1,0:T(4,128)}), s32[32,3,8]{2,1,0:T(4,128)S(1)}, u32[]{:S(2)}, u32[]{:S(2)}) async-start(s32[32,3,8]{2,1,0:T(4,128)} %broadcast_in_dim.180), calls=%async_computation | async-start | bytes 131072 | tf_op jit(solution)/shard_map/all_to_all | solution.py:104
  41.6 26.8 %copy-start.10 = (s32[1024]{0:T(1024)}, s32[1024]{0:T(1024)S(1)}, u32[]{:S(2)}) copy-start(s32[1024]{0:T(1024)S(1)} %pad_clamp_fusion) | copy-start | bytes 12292
  42.6 19.0 %collective-permute-start.5 = (bf16[256,64]{0,1:T(8,128)(2,1)S(1)}, bf16[256,64]{0,1:T(8,128)(2,1)S(1)}, u32[]{:S(2)}, u32[]{:S(2)}) collective-permute-start(bf16[256,64]{0,1:T(8,128)(2,1)S(1)} %get-tuple-element.27), channel_id=1, source_target_pairs={{0,6},{1,7},{2,0},{3,1},{4,2},{5,3},{6,4},{7,5}} | collective-permute-start | bytes 98312 | tf_op jit(solution)/shard_map/ppermute | solution.py:72
  57.0 7.4 %collective-permute-start.4 = (bf16[256,64]{0,1:T(8,128)(2,1)S(1)}, bf16[256,64]{0,1:T(8,128)(2,1)S(1)}, u32[]{:S(2)}, u32[]{:S(2)}) collective-permute-start(bf16[256,64]{0,1:T(8,128)(2,1)S(1)} %get-tuple-element.28), channel_id=1, source_target_pairs={{0,4},{1,5},{2,6},{3,7},{4,0},{5,1},{6,2},{7,3}} | collective-permute-start | bytes 98312 | tf_op jit(solution)/shard_map/ppermute | solution.py:72
  58.9 8.3 %collective-permute-start.3 = (bf16[256,64]{0,1:T(8,128)(2,1)S(1)}, bf16[256,64]{0,1:T(8,128)(2,1)S(1)}, u32[]{:S(2)}, u32[]{:S(2)}) collective-permute-start(bf16[256,64]{0,1:T(8,128)(2,1)S(1)} %get-tuple-element.29), channel_id=1, source_target_pairs={{0,2},{1,3},{2,4},{3,5},{4,6},{5,7},{6,0},{7,1}} | collective-permute-start | bytes 98312 | tf_op jit(solution)/shard_map/ppermute | solution.py:72
  73.2 10.3 %all-to-all-start.1 = ((bf16[8,2,8192]{2,1,0:T(2,128)(2,1)}), bf16[8,2,8192]{2,1,0:T(2,128)(2,1)S(1)}, u32[]{:S(2)}, u32[]{:S(2)}) async-start(bf16[8,2,8192]{2,1,0:T(2,128)(2,1)} %reshape.736), calls=%async_computation.1 | async-start | bytes 524288 | tf_op jit(solution)/shard_map/all_to_all | solution.py:169
  104.9 1.2 copy-start.4
  105.2 1.7 copy-start
  115.8 10.3 %all-to-all-start.2 = ((bf16[8,2,8192]{2,1,0:T(2,128)(2,1)}), bf16[8,2,8192]{2,1,0:T(2,128)(2,1)S(1)}, u32[]{:S(2)}, u32[]{:S(2)}) async-start(bf16[8,2,8192]{2,1,0:T(2,128)(2,1)} %reshape.738), calls=%async_computation.2 | async-start | bytes 524288 | tf_op jit(solution)/shard_map/all_to_all | solution.py:169
  129.8 2.1 %copy-start.1 = (bf16[1024,1024]{1,0:T(8,128)(2,1)S(1)}, bf16[1024,1024]{1,0:T(8,128)(2,1)}, u32[]{:S(2)}) copy-start(bf16[1024,1024]{1,0:T(8,128)(2,1)} %copy-done) | copy-start | bytes 6291460
  131.9 1.5 copy-start.7
  140.5 16.1 %copy-start.8 = (bf16[1024,64]{0,1:T(8,128)(2,1)S(1)}, bf16[1024,64]{0,1:T(8,128)(2,1)}, u32[]{:S(2)}) copy-start(bf16[1024,64]{0,1:T(8,128)(2,1)} %copy-done.7) | copy-start | bytes 393220
  142.4 10.3 %all-to-all-start.3 = ((bf16[8,2,8192]{2,1,0:T(2,128)(2,1)}), bf16[8,2,8192]{2,1,0:T(2,128)(2,1)S(1)}, u32[]{:S(2)}, u32[]{:S(2)}) async-start(bf16[8,2,8192]{2,1,0:T(2,128)(2,1)} %reshape.740), calls=%async_computation.3 | async-start | bytes 524288 | tf_op jit(solution)/shard_map/all_to_all | solution.py:169
  156.6 2.1 %copy-start.2 = (bf16[1024,1024]{1,0:T(8,128)(2,1)S(1)}, bf16[1024,1024]{1,0:T(8,128)(2,1)}, u32[]{:S(2)}) copy-start(bf16[1024,1024]{1,0:T(8,128)(2,1)} %copy-done) | copy-start | bytes 6291460
  159.9 7.8 %copy-start.12 = (s32[2,8]{1,0:T(2,128)S(1)}, s32[2,8]{1,0:T(2,128)}, u32[]{:S(2)}) copy-start(s32[2,8]{1,0:T(2,128)} %get-tuple-element.33) | copy-start | bytes 196
  164.3 10.3 %all-to-all-start.4 = ((bf16[8,2,8192]{2,1,0:T(2,128)(2,1)}), bf16[8,2,8192]{2,1,0:T(2,128)(2,1)S(1)}, u32[]{:S(2)}, u32[]{:S(2)}) async-start(bf16[8,2,8192]{2,1,0:T(2,128)(2,1)} %reshape.742), calls=%async_computation.4 | async-start | bytes 524288 | tf_op jit(solution)/shard_map/all_to_all | solution.py:169
  177.6 16.9 %copy-start.9 = (f32[256,256]{1,0:T(8,128)S(1)}, f32[256,256]{1,0:T(8,128)}, u32[]{:S(2)}) copy-start(f32[256,256]{1,0:T(8,128)} %get-tuple-element.38) | copy-start | bytes 786436
  177.6 15.6 %all-to-all-start.5 = ((bf16[4,768,64]{1,2,0:T(8,128)(2,1)}), bf16[4,768,64]{1,2,0:T(8,128)(2,1)S(1)}, u32[]{:S(2)}, u32[]{:S(2)}) async-start(bf16[4,768,64]{1,2,0:T(8,128)(2,1)} %pad_maximum_fusion.2), calls=%async_computation.5 | async-start | bytes 786432 | tf_op jit(solution)/shard_map/all_to_all | solution.py:188
Sparse Core Ops, SparseCore 0:
  9.8 92.5 all-gather.2

commit v21 on v17

--- a/solution.py
+++ b/solution.py
@@ -151,7 +151,7 @@
     rhs_cols = lax.dynamic_slice_in_dim(rhs[0, 0], row_index * cols, cols, axis=1)
     window_blocks = width // block_rows
     acc = jnp.zeros((NT + 1, block_rows, cols), jnp.float32)
-    solved = jnp.zeros((width, cols), jnp.float32)
+    halves = []
     for section in range(n_lvl):
         if section == 0:
             updates = first_cols
@@ -160,7 +160,7 @@
             solved_now = jnp.dot(
                 inv_full, right.astype(jnp.bfloat16), preferred_element_type=jnp.float32
             )
-            solved = jnp.where(level_index == section, solved_now, solved)
+            halves.append(solved_now.astype(jnp.bfloat16))
             updates = jnp.dot(
                 tiles_full, solved_now.astype(jnp.bfloat16), preferred_element_type=jnp.float32
             ).astype(jnp.bfloat16)
@@ -173,6 +173,9 @@
         acc = acc.at[recv_block[section]].add(incoming.astype(jnp.float32), mode="clip")
     outer = acc[window_blocks:NT].reshape(ABOVE, cols)
 
+    solved = halves[-1]
+    for section in range(n_lvl - 2, 0, -1):
+        solved = jnp.where(level_index == section, halves[section - 1], solved)
     solved_blocks = solved.reshape(n_prow, rows_out, cols)
     final = jnp.concatenate(
         [

time: 191 us -> 191 us (level)
    select_n x1 -> x0, other arithmetic: 2.53 us -> none  [per_device(): jnp.where(col_super[:, None] == col_super[None, :], gathered[:, :row_coun...]
    slice x0 -> x1, other arithmetic: none -> 2.53 us  [per_device(): gathered[:, row_count:].reshape(group_tiles, block_rows, width)]
where the time goes in v21:
time: 191 us; the launch traced here: 189 us
  waiting for transfers between devices  76.2 us (40%)
  starting transfers between devices  52.4 us (27%)
  local copies, waits for them, and re-layouts  21.2 us (11%)
  other arithmetic  15.3 us (8%)
  between operations  14.9 us (8%)
  matrix products  9.39 us (5%)
    ppermute x6, starting transfers between devices, level0_shift(): return lax.ppermute(x, all_axes, pairs)  30.7 us
    all_to_all x4, waiting for transfers between devices, per_device(): lax.all_to_all(sending, ('lvl', 'pcol'), split_axis=0, concat_axis=0, til...  26.8 us
    all_gather x1, waiting for transfers between devices, per_device(): gathered = lax.all_gather(raw, 'prow', axis=0)  20.4 us
    all_to_all x4, starting transfers between devices, per_device(): lax.all_to_all(sending, ('lvl', 'pcol'), split_axis=0, concat_axis=0, til...  13.8 us
    all_to_all x1, waiting for transfers between devices, per_device(): lax.all_to_all(jnp.broadcast_to(meta[None], (devices,) + meta.shape), ('l...  12.4 us
    unnamed x42, local copies, waits for them, and re-layouts  11.6 us
    all_to_all x1, waiting for transfers between devices, per_device(): lax.all_to_all(final, 'prow', split_axis=0, concat_axis=0, tiled=True)  11 us
    ppermute x6, waiting for transfers between devices, level0_shift(): return lax.ppermute(x, all_axes, pairs)  5.61 us
  transfers between devices with their start and end apart: 13, of which 9 were waited for; matrix products, arithmetic and copies ran while one was open for 5% of the time, Pallas kernels for 0%

profile of v21, /device:TPU:0, one launch (start us, length us, event | category | flops | bytes accessed | tf_op | source)
XLA Modules:
  0.0 189.4 jit_solution(17639114493710446803)
XLA Ops:
  7.3 2.3 %pad_maximum_fusion = bf16[512,1024]{1,0:T(8,128)(2,1)} fusion(bf16[256,1024]{1,0:T(8,128)(2,1)} %bitcast.120, bf16[256,1024]{1,0:T(8,128)(2,1)} %bitcast.116), kind=kLoop, calls=%fused_computation.22 | loop fusion | flops 2097152 | bytes 2097152 | tf_op jit(solution)/shard_map/concatenate | solution.py:53
  9.9 1.1 fusion.48
  10.9 6.9 %collective-permute-start.2 = (bf16[256,256]{1,0:T(8,128)(2,1)S(1)}, bf16[256,256]{1,0:T(8,128)(2,1)S(1)}, u32[]{:S(2)}, u32[]{:S(2)}) collective-permute-start(bf16[256,256]{1,0:T(8,128)(2,1)S(1)} %get-tuple-element.37), channel_id=1, source_target_pairs={{0,6},{1,7},{2,0},{3,1},{4,2},{5,3},{6,4},{7,5}} | collective-permute-start | bytes 393224 | tf_op jit(solution)/shard_map/ppermute | solution.py:72
  17.9 1.9 %collective-permute-start.1 = (bf16[256,256]{1,0:T(8,128)(2,1)S(1)}, bf16[256,256]{1,0:T(8,128)(2,1)S(1)}, u32[]{:S(2)}, u32[]{:S(2)}) collective-permute-start(bf16[256,256]{1,0:T(8,128)(2,1)S(1)} %get-tuple-element.37), channel_id=1, source_target_pairs={{0,4},{1,5},{2,6},{3,7},{4,0},{5,1},{6,2},{7,3}} | collective-permute-start | bytes 393224 | tf_op jit(solution)/shard_map/ppermute | solution.py:72
  19.8 2.9 %collective-permute-start = (bf16[256,256]{1,0:T(8,128)(2,1)S(1)}, bf16[256,256]{1,0:T(8,128)(2,1)S(1)}, u32[]{:S(2)}, u32[]{:S(2)}) collective-permute-start(bf16[256,256]{1,0:T(8,128)(2,1)S(1)} %get-tuple-element.37), channel_id=1, source_target_pairs={{0,2},{1,3},{2,4},{3,5},{4,6},{5,7},{6,0},{7,1}} | collective-permute-start | bytes 393224 | tf_op jit(solution)/shard_map/ppermute | solution.py:72
  22.8 0.6 broadcast_in_dim.177
  23.4 3.2 %all-to-all-start = ((s32[32,3,8]{2,1,0:T(4,128)}), s32[32,3,8]{2,1,0:T(4,128)S(1)}, u32[]{:S(2)}, u32[]{:S(2)}) async-start(s32[32,3,8]{2,1,0:T(4,128)} %broadcast_in_dim.177), calls=%async_computation | async-start | bytes 131072 | tf_op jit(solution)/shard_map/all_to_all | solution.py:104
  27.2 12.4 %all-to-all-done = s32[32,3,8]{2,1,0:T(4,128)S(1)} async-done(((s32[32,3,8]{2,1,0:T(4,128)}), s32[32,3,8]{2,1,0:T(4,128)S(1)}, u32[]{:S(2)}, u32[]{:S(2)}) %all-to-all-start) | async-done | bytes 3104 | tf_op jit(solution)/shard_map/all_to_all | solution.py:104
  39.8 0.3 convert_reduce_fusion
  40.1 0.2 fusion.18
  40.3 0.2 select_reduce_fusion
  40.6 0.6 fusion.47
  41.7 0.6 gather_fusion
  42.3 0.4 convolution_convert_fusion.6
  42.7 14.3 %collective-permute-start.5 = (bf16[256,64]{0,1:T(8,128)(2,1)S(1)}, bf16[256,64]{0,1:T(8,128)(2,1)S(1)}, u32[]{:S(2)}, u32[]{:S(2)}) collective-permute-start(bf16[256,64]{0,1:T(8,128)(2,1)S(1)} %get-tuple-element.27), channel_id=1, source_target_pairs={{0,6},{1,7},{2,0},{3,1},{4,2},{5,3},{6,4},{7,5}} | collective-permute-start | bytes 98312 | tf_op jit(solution)/shard_map/ppermute | solution.py:72
  57.0 1.9 %collective-permute-start.4 = (bf16[256,64]{0,1:T(8,128)(2,1)S(1)}, bf16[256,64]{0,1:T(8,128)(2,1)S(1)}, u32[]{:S(2)}, u32[]{:S(2)}) collective-permute-start(bf16[256,64]{0,1:T(8,128)(2,1)S(1)} %get-tuple-element.28), channel_id=1, source_target_pairs={{0,4},{1,5},{2,6},{3,7},{4,0},{5,1},{6,2},{7,3}} | collective-permute-start | bytes 98312 | tf_op jit(solution)/shard_map/ppermute | solution.py:72
  58.9 2.7 %collective-permute-start.3 = (bf16[256,64]{0,1:T(8,128)(2,1)S(1)}, bf16[256,64]{0,1:T(8,128)(2,1)S(1)}, u32[]{:S(2)}, u32[]{:S(2)}) collective-permute-start(bf16[256,64]{0,1:T(8,128)(2,1)S(1)} %get-tuple-element.29), channel_id=1, source_target_pairs={{0,2},{1,3},{2,4},{3,5},{4,6},{5,7},{6,0},{7,1}} | collective-permute-start | bytes 98312 | tf_op jit(solution)/shard_map/ppermute | solution.py:72
  61.7 2.8 %collective-permute-done.4 = bf16[256,64]{0,1:T(8,128)(2,1)S(1)} collective-permute-done((bf16[256,64]{0,1:T(8,128)(2,1)S(1)}, bf16[256,64]{0,1:T(8,128)(2,1)S(1)}, u32[]{:S(2)}, u32[]{:S(2)}) %collective-permute-start.4) | collective-permute-done | bytes 32800 | tf_op jit(solution)/shard_map/ppermute | solution.py:72
  64.4 2.8 %collective-permute-done.3 = bf16[256,64]{0,1:T(8,128)(2,1)S(1)} collective-permute-done((bf16[256,64]{0,1:T(8,128)(2,1)S(1)}, bf16[256,64]{0,1:T(8,128)(2,1)S(1)}, u32[]{:S(2)}, u32[]{:S(2)}) %collective-permute-start.3) | collective-permute-done | bytes 32800 | tf_op jit(solution)/shard_map/ppermute | solution.py:72
  67.3 0.6 gather_fusion.1
  68.1 0.7 gather_fusion.2
  68.8 1.1 reshape.698
  69.9 3.4 %all-to-all-start.1 = ((bf16[8,2,8192]{2,1,0:T(2,128)(2,1)}), bf16[8,2,8192]{2,1,0:T(2,128)(2,1)S(1)}, u32[]{:S(2)}, u32[]{:S(2)}) async-start(bf16[8,2,8192]{2,1,0:T(2,128)(2,1)} %reshape.698), calls=%async_computation.1 | async-start | bytes 524288 | tf_op jit(solution)/shard_map/all_to_all | solution.py:169
  73.5 6.7 %all-to-all-done.1 = bf16[8,2,8192]{2,1,0:T(2,128)(2,1)S(1)} async-done(((bf16[8,2,8192]{2,1,0:T(2,128)(2,1)}), bf16[8,2,8192]{2,1,0:T(2,128)(2,1)S(1)}, u32[]{:S(2)}, u32[]{:S(2)}) %all-to-all-start.1) | async-done | bytes 262176 | tf_op jit(solution)/shard_map/all_to_all | solution.py:169
  80.2 0.3 reshape.699
  80.6 1.2 scatter_fusion
  81.9 20.4 %all-gather.3.cloned.1.call-done = bf16[2048,1024]{1,0:T(8,128)(2,1)} async-done(((bf16[512,1024]{1,0:T(8,128)(2,1)}), bf16[2048,1024]{1,0:T(8,128)(2,1)}) %all-gather.3.cloned.1.call-update) | async-done | bytes 4194320 | tf_op jit(solution)/shard_map/all_gather | solution.py:56
  102.3 2.5 %fusion.45 = (bf16[4,256,1024]{2,1,0:T(8,128)(2,1)S(1)}, bf16[4,256,1024]{2,1,0:T(8,128)(2,1)S(1)}) fusion(bf16[4,512,1024]{2,1,0:T(8,128)(2,1)} %bitcast.111, s32[1024]{0:T(1024)S(1)} %select_reduce_fusion.1, s32[4,256]{1,0:T(4,128)S(1)} %eq.222), kind=kLoop, calls=%fused_computation.131 | loop fusion | flops 2097152 | bytes 8396800 | tf_op jit(solution)/shard_map/slice | solution.py:117
  104.9 0.3 bitcast_select_fusion
  105.2 0.9 copy-done.4
  106.1 0.8 convolution_convert_fusion.5
  106.9 0.8 convolution_convert_fusion.2
  107.8 0.2 copy.62
  107.9 1.5 gather_fusion.3
  109.5 2.1 %reshape.700 = bf16[8,2,8192]{2,1,0:T(2,128)(2,1)} reshape(bf16[64,32,64]{2,1,0:T(8,128)(2,1)} %gather_fusion.3) | data formatting | bytes 524288
  111.6 3.4 %all-to-all-start.2 = ((bf16[8,2,8192]{2,1,0:T(2,128)(2,1)}), bf16[8,2,8192]{2,1,0:T(2,128)(2,1)S(1)}, u32[]{:S(2)}, u32[]{:S(2)}) async-start(bf16[8,2,8192]{2,1,0:T(2,128)(2,1)} %reshape.700), calls=%async_computation.2 | async-start | bytes 524288 | tf_op jit(solution)/shard_map/all_to_all | solution.py:169
  115.2 6.8 %all-to-all-done.2 = bf16[8,2,8192]{2,1,0:T(2,128)(2,1)S(1)} async-done(((bf16[8,2,8192]{2,1,0:T(2,128)(2,1)}), bf16[8,2,8192]{2,1,0:T(2,128)(2,1)S(1)}, u32[]{:S(2)}, u32[]{:S(2)}) %all-to-all-start.2) | async-done | bytes 262176 | tf_op jit(solution)/shard_map/all_to_all | solution.py:169
  121.9 1.2 reshape.701
  123.1 0.9 slice_convert_fusion.3
  124.0 1.2 scatter_fusion.1
  125.3 2.0 %convolution_convert_fusion.4 = bf16[1024,64]{0,1:T(8,128)(2,1)S(1)} fusion(bf16[1024,1024]{1,0:T(8,128)(2,1)S(1)} %bitcast.109, f32[1,1,1024,64]{3,2,1,0:T(8,128)S(1)} %bitcast.123, f32[1,1,1024,256]{3,2,1,0:T(8,128)} %param.9, s32[]{:T(128)S(6)} %select_n.240), kind=kOutput, calls=%fused_computation.19 | convolution fusion | flops 134414336 | bytes 3014660 | tf_op jit(solution)/shard_map/dot_general | solution.py:160
  127.3 1.5 convolution_convert_fusion.1
  128.8 1.1 copy.63
  129.9 1.5 gather_fusion.4
  131.4 2.1 %reshape.702 = bf16[8,2,8192]{2,1,0:T(2,128)(2,1)} reshape(bf16[64,32,64]{2,1,0:T(8,128)(2,1)} %gather_fusion.4) | data formatting | bytes 524288
  133.6 3.6 %all-to-all-start.3 = ((bf16[8,2,8192]{2,1,0:T(2,128)(2,1)}), bf16[8,2,8192]{2,1,0:T(2,128)(2,1)S(1)}, u32[]{:S(2)}, u32[]{:S(2)}) async-start(bf16[8,2,8192]{2,1,0:T(2,128)(2,1)} %reshape.702), calls=%async_computation.3 | async-start | bytes 524288 | tf_op jit(solution)/shard_map/all_to_all | solution.py:169
  137.3 6.6 %all-to-all-done.3 = bf16[8,2,8192]{2,1,0:T(2,128)(2,1)S(1)} async-done(((bf16[8,2,8192]{2,1,0:T(2,128)(2,1)}), bf16[8,2,8192]{2,1,0:T(2,128)(2,1)S(1)}, u32[]{:S(2)}, u32[]{:S(2)}) %all-to-all-start.3) | async-done | bytes 262176 | tf_op jit(solution)/shard_map/all_to_all | solution.py:169
  143.8 1.2 reshape.703
  145.0 0.9 slice_convert_fusion.2
  145.9 1.2 scatter_fusion.2
  147.2 2.0 %select_select_fusion = (bf16[1024,64]{0,1:T(8,128)(2,1)S(1)}, bf16[1024,64]{0,1:T(8,128)(2,1)S(1)}) fusion(bf16[1024,64]{0,1:T(8,128)(2,1)S(1)} %convolution_convert_fusion.5, bf16[1024,64]{0,1:T(8,128)(2,1)S(1)} %convolution_convert_fusion.4, pred[]{:T(512)S(6)} %eq.247, pred[]{:T(512)S(6)} %eq.221, bf16[1024,1024]{1,0:T(8,128)(2,1)S(1)} %bitcast.110, ...), kind=kOutput, calls=%fused_computation.48 | convolution fusion | flops 134545408 | bytes 3407878 | tf_op jit(solution)/shard_map/dot_general | solution.py:160
  149.3 0.8 convolution_convert_fusion
  150.1 0.2 copy.64
  150.3 0.8 gather_fusion.5
  151.0 1.1 reshape.704
  152.1 3.4 %all-to-all-start.4 = ((bf16[8,2,8192]{2,1,0:T(2,128)(2,1)}), bf16[8,2,8192]{2,1,0:T(2,128)(2,1)S(1)}, u32[]{:S(2)}, u32[]{:S(2)}) async-start(bf16[8,2,8192]{2,1,0:T(2,128)(2,1)} %reshape.704), calls=%async_computation.4 | async-start | bytes 524288 | tf_op jit(solution)/shard_map/all_to_all | solution.py:169
  155.7 6.8 %all-to-all-done.4 = bf16[8,2,8192]{2,1,0:T(2,128)(2,1)S(1)} async-done(((bf16[8,2,8192]{2,1,0:T(2,128)(2,1)}), bf16[8,2,8192]{2,1,0:T(2,128)(2,1)S(1)}, u32[]{:S(2)}, u32[]{:S(2)}) %all-to-all-start.4) | async-done | bytes 262176 | tf_op jit(solution)/shard_map/all_to_all | solution.py:169
  162.4 0.3 reshape.705
  162.8 1.2 scatter_fusion.3
  164.2 0.8 pad_maximum_fusion.2
  165.0 4.6 %all-to-all-start.5 = ((bf16[4,768,64]{1,2,0:T(8,128)(2,1)}), bf16[4,768,64]{1,2,0:T(8,128)(2,1)S(1)}, u32[]{:S(2)}, u32[]{:S(2)}) async-start(bf16[4,768,64]{1,2,0:T(8,128)(2,1)} %pad_maximum_fusion.2), calls=%async_computation.5 | async-start | bytes 786432 | tf_op jit(solution)/shard_map/all_to_all | solution.py:187
  169.6 11.0 %all-to-all-done.5 = bf16[4,768,64]{1,2,0:T(8,128)(2,1)S(1)} async-done(((bf16[4,768,64]{1,2,0:T(8,128)(2,1)}), bf16[4,768,64]{1,2,0:T(8,128)(2,1)S(1)}, u32[]{:S(2)}, u32[]{:S(2)}) %all-to-all-start.5) | async-done | bytes 393248 | tf_op jit(solution)/shard_map/all_to_all | solution.py:187
  180.8 1.0 copy.68
  181.8 0.7 select_bitcast_fusion
  (97 shorter events, 2.7 us)
Async XLA Ops:
  7.2 2.7 %copy-start.5 = (bf16[1,1,256,1024]{3,2,1,0:T(8,128)(2,1)S(1)}, bf16[1,1,256,1024]{3,2,1,0:T(8,128)(2,1)}, u32[]{:S(2)}) copy-start(bf16[1,1,256,1024]{3,2,1,0:T(8,128)(2,1)} %param.10) | copy-start | bytes 1572868
  7.2 2.5 %copy-start.9 = (s32[1,1,8]{2,1,0:T(1,128)S(1)}, s32[1,1,8]{2,1,0:T(1,128)}, u32[]{:S(2)}) copy-start(s32[1,1,8]{2,1,0:T(1,128)} %param.12) | copy-start | bytes 100
  7.2 2.7 %copy-start.3 = (f32[1,1,1024,256]{3,2,1,0:T(8,128)S(1)}, f32[1,1,1024,256]{3,2,1,0:T(8,128)}, u32[]{:S(2)}) copy-start(f32[1,1,1024,256]{3,2,1,0:T(8,128)} %param.9) | copy-start | bytes 3145732
  7.2 95.1 %all-gather.3.cloned.1.call-start = ((), (), s32[]{:S(2)}) async-start(), calls=%async_computation.6 | async-start | bytes 5242880 | tf_op jit(solution)/shard_map/all_gather | solution.py:56
  7.2 15.5 %copy-start.13 = (s32[1,1,8]{2,1,0:T(1,128)S(1)}, s32[1,1,8]{2,1,0:T(1,128)}, u32[]{:S(2)}) copy-start(s32[1,1,8]{2,1,0:T(1,128)} %param.14) | copy-start | bytes 100
  7.3 15.5 %copy-start.14 = (s32[1,1,8]{2,1,0:T(1,128)S(1)}, s32[1,1,8]{2,1,0:T(1,128)}, u32[]{:S(2)}) copy-start(s32[1,1,8]{2,1,0:T(1,128)} %param.13) | copy-start | bytes 100
  7.3 15.5 %copy-start.15 = (s32[1,1,8]{2,1,0:T(1,128)S(1)}, s32[1,1,8]{2,1,0:T(1,128)}, u32[]{:S(2)}) copy-start(s32[1,1,8]{2,1,0:T(1,128)} %param.15) | copy-start | bytes 100
  9.6 17.4 %copy-start.6 = (bf16[1,1,8,32,1024]{4,3,2,1,0:T(8,128)(2,1)S(1)}, bf16[1,1,8,32,1024]{4,3,2,1,0:T(8,128)(2,1)}, u32[]{:S(2)}) copy-start(bf16[1,1,8,32,1024]{4,3,2,1,0:T(8,128)(2,1)} %param.11) | copy-start | bytes 1572868
  10.9 30.6 %collective-permute-start.2 = (bf16[256,256]{1,0:T(8,128)(2,1)S(1)}, bf16[256,256]{1,0:T(8,128)(2,1)S(1)}, u32[]{:S(2)}, u32[]{:S(2)}) collective-permute-start(bf16[256,256]{1,0:T(8,128)(2,1)S(1)} %get-tuple-element.37), channel_id=1, source_target_pairs={{0,6},{1,7},{2,0},{3,1},{4,2},{5,3},{6,4},{7,5}} | collective-permute-start | bytes 393224 | tf_op jit(solution)/shard_map/ppermute | solution.py:72
  17.9 23.7 %collective-permute-start.1 = (bf16[256,256]{1,0:T(8,128)(2,1)S(1)}, bf16[256,256]{1,0:T(8,128)(2,1)S(1)}, u32[]{:S(2)}, u32[]{:S(2)}) collective-permute-start(bf16[256,256]{1,0:T(8,128)(2,1)S(1)} %get-tuple-element.37), channel_id=1, source_target_pairs={{0,4},{1,5},{2,6},{3,7},{4,0},{5,1},{6,2},{7,3}} | collective-permute-start | bytes 393224 | tf_op jit(solution)/shard_map/ppermute | solution.py:72
  19.8 21.8 %collective-permute-start = (bf16[256,256]{1,0:T(8,128)(2,1)S(1)}, bf16[256,256]{1,0:T(8,128)(2,1)S(1)}, u32[]{:S(2)}, u32[]{:S(2)}) collective-permute-start(bf16[256,256]{1,0:T(8,128)(2,1)S(1)} %get-tuple-element.37), channel_id=1, source_target_pairs={{0,2},{1,3},{2,4},{3,5},{4,6},{5,7},{6,0},{7,1}} | collective-permute-start | bytes 393224 | tf_op jit(solution)/shard_map/ppermute | solution.py:72
  23.4 16.1 %all-to-all-start = ((s32[32,3,8]{2,1,0:T(4,128)}), s32[32,3,8]{2,1,0:T(4,128)S(1)}, u32[]{:S(2)}, u32[]{:S(2)}) async-start(s32[32,3,8]{2,1,0:T(4,128)} %broadcast_in_dim.177), calls=%async_computation | async-start | bytes 131072 | tf_op jit(solution)/shard_map/all_to_all | solution.py:104
  41.6 26.5 %copy-start.8 = (s32[1024]{0:T(1024)}, s32[1024]{0:T(1024)S(1)}, u32[]{:S(2)}) copy-start(s32[1024]{0:T(1024)S(1)} %pad_clamp_fusion) | copy-start | bytes 12292
  42.7 19.0 %collective-permute-start.5 = (bf16[256,64]{0,1:T(8,128)(2,1)S(1)}, bf16[256,64]{0,1:T(8,128)(2,1)S(1)}, u32[]{:S(2)}, u32[]{:S(2)}) collective-permute-start(bf16[256,64]{0,1:T(8,128)(2,1)S(1)} %get-tuple-element.27), channel_id=1, source_target_pairs={{0,6},{1,7},{2,0},{3,1},{4,2},{5,3},{6,4},{7,5}} | collective-permute-start | bytes 98312 | tf_op jit(solution)/shard_map/ppermute | solution.py:72
  57.0 7.4 %collective-permute-start.4 = (bf16[256,64]{0,1:T(8,128)(2,1)S(1)}, bf16[256,64]{0,1:T(8,128)(2,1)S(1)}, u32[]{:S(2)}, u32[]{:S(2)}) collective-permute-start(bf16[256,64]{0,1:T(8,128)(2,1)S(1)} %get-tuple-element.28), channel_id=1, source_target_pairs={{0,4},{1,5},{2,6},{3,7},{4,0},{5,1},{6,2},{7,3}} | collective-permute-start | bytes 98312 | tf_op jit(solution)/shard_map/ppermute | solution.py:72
  58.9 8.3 %collective-permute-start.3 = (bf16[256,64]{0,1:T(8,128)(2,1)S(1)}, bf16[256,64]{0,1:T(8,128)(2,1)S(1)}, u32[]{:S(2)}, u32[]{:S(2)}) collective-permute-start(bf16[256,64]{0,1:T(8,128)(2,1)S(1)} %get-tuple-element.29), channel_id=1, source_target_pairs={{0,2},{1,3},{2,4},{3,5},{4,6},{5,7},{6,0},{7,1}} | collective-permute-start | bytes 98312 | tf_op jit(solution)/shard_map/ppermute | solution.py:72
  69.9 10.3 %all-to-all-start.1 = ((bf16[8,2,8192]{2,1,0:T(2,128)(2,1)}), bf16[8,2,8192]{2,1,0:T(2,128)(2,1)S(1)}, u32[]{:S(2)}, u32[]{:S(2)}) async-start(bf16[8,2,8192]{2,1,0:T(2,128)(2,1)} %reshape.698), calls=%async_computation.1 | async-start | bytes 524288 | tf_op jit(solution)/shard_map/all_to_all | solution.py:169
  104.9 1.2 copy-start.4
  105.2 1.7 copy-start
  106.9 8.1 %copy-start.12 = (s32[2,8]{1,0:T(2,128)S(1)}, s32[2,8]{1,0:T(2,128)}, u32[]{:S(2)}) copy-start(s32[2,8]{1,0:T(2,128)} %get-tuple-element.35) | copy-start | bytes 196
  111.6 10.3 %all-to-all-start.2 = ((bf16[8,2,8192]{2,1,0:T(2,128)(2,1)}), bf16[8,2,8192]{2,1,0:T(2,128)(2,1)S(1)}, u32[]{:S(2)}, u32[]{:S(2)}) async-start(bf16[8,2,8192]{2,1,0:T(2,128)(2,1)} %reshape.700), calls=%async_computation.2 | async-start | bytes 524288 | tf_op jit(solution)/shard_map/all_to_all | solution.py:169
  125.2 2.1 %copy-start.1 = (bf16[1024,1024]{1,0:T(8,128)(2,1)S(1)}, bf16[1024,1024]{1,0:T(8,128)(2,1)}, u32[]{:S(2)}) copy-start(bf16[1024,1024]{1,0:T(8,128)(2,1)} %copy-done) | copy-start | bytes 6291460
  127.3 9.9 %copy-start.11 = (s32[2,8]{1,0:T(2,128)S(1)}, s32[2,8]{1,0:T(2,128)}, u32[]{:S(2)}) copy-start(s32[2,8]{1,0:T(2,128)} %get-tuple-element.34) | copy-start | bytes 196
  133.6 10.3 %all-to-all-start.3 = ((bf16[8,2,8192]{2,1,0:T(2,128)(2,1)}), bf16[8,2,8192]{2,1,0:T(2,128)(2,1)S(1)}, u32[]{:S(2)}, u32[]{:S(2)}) async-start(bf16[8,2,8192]{2,1,0:T(2,128)(2,1)} %reshape.702), calls=%async_computation.3 | async-start | bytes 524288 | tf_op jit(solution)/shard_map/all_to_all | solution.py:169
  147.2 2.1 %copy-start.2 = (bf16[1024,1024]{1,0:T(8,128)(2,1)S(1)}, bf16[1024,1024]{1,0:T(8,128)(2,1)}, u32[]{:S(2)}) copy-start(bf16[1024,1024]{1,0:T(8,128)(2,1)} %copy-done) | copy-start | bytes 6291460
  149.2 6.3 %copy-start.10 = (s32[2,8]{1,0:T(2,128)S(1)}, s32[2,8]{1,0:T(2,128)}, u32[]{:S(2)}) copy-start(s32[2,8]{1,0:T(2,128)} %get-tuple-element.33) | copy-start | bytes 196
  152.1 10.3 %all-to-all-start.4 = ((bf16[8,2,8192]{2,1,0:T(2,128)(2,1)}), bf16[8,2,8192]{2,1,0:T(2,128)(2,1)S(1)}, u32[]{:S(2)}, u32[]{:S(2)}) async-start(bf16[8,2,8192]{2,1,0:T(2,128)(2,1)} %reshape.704), calls=%async_computation.4 | async-start | bytes 524288 | tf_op jit(solution)/shard_map/all_to_all | solution.py:169
  165.0 16.8 %copy-start.7 = (f32[256,256]{1,0:T(8,128)S(1)}, f32[256,256]{1,0:T(8,128)}, u32[]{:S(2)}) copy-start(f32[256,256]{1,0:T(8,128)} %get-tuple-element.38) | copy-start | bytes 786436
  165.0 15.6 %all-to-all-start.5 = ((bf16[4,768,64]{1,2,0:T(8,128)(2,1)}), bf16[4,768,64]{1,2,0:T(8,128)(2,1)S(1)}, u32[]{:S(2)}, u32[]{:S(2)}) async-start(bf16[4,768,64]{1,2,0:T(8,128)(2,1)} %pad_maximum_fusion.2), calls=%async_computation.5 | async-start | bytes 786432 | tf_op jit(solution)/shard_map/all_to_all | solution.py:187
Sparse Core Ops, SparseCore 0:
  9.8 92.5 all-gather.2

commit v22 on v17

--- a/solution.py
+++ b/solution.py
@@ -100,14 +100,7 @@
     )
 
     meta = jnp.stack([off_device[0, 0], off_block[0, 0], offdiag_block_panel[0, 0]], axis=0)
-    devices = n_lvl * n_prow * n_pcol
-    meta = lax.all_to_all(
-        jnp.broadcast_to(meta[None], (devices,) + meta.shape),
-        ("lvl", "prow", "pcol"),
-        split_axis=0,
-        concat_axis=0,
-        tiled=True,
-    )
+    meta = lax.all_gather(meta, ("lvl", "prow", "pcol"), axis=0)
     meta = meta.reshape(n_lvl, n_prow, n_pcol, 3, tile_count)
     meta = jnp.transpose(meta, (0, 2, 1, 3, 4)).reshape(groups, n_prow, 3, tile_count)
     target = meta[:, :, 0, :].reshape(groups, group_tiles)

time: 191 us -> 193 us (1.010)
  blocking collectives: 0 us -> 48.2 us
  waiting for transfers between devices: 76.2 us -> 44.5 us
  starting transfers between devices: 52.4 us -> 39 us
    all_gather x0 -> x1, blocking collectives: none -> 48.2 us  [per_device(): meta = lax.all_gather(meta, ('lvl', 'prow', 'pcol'), axis=0)]
    all_gather x1, waiting for transfers between devices: 20.4 us -> 0.02 us  [per_device(): gathered = lax.all_gather(raw, 'prow', axis=0)]
    all_to_all x1 -> x0, waiting for transfers between devices: 12.4 us -> none  [per_device(): lax.all_to_all(jnp.broadcast_to(meta[None], (devices,) + meta.shape), ('l...]
    ppermute x6, starting transfers between devices: 30.7 us -> 21.6 us  [level0_shift(): return lax.ppermute(x, all_axes, pairs)]
    all_to_all x1 -> x0, starting transfers between devices: 3.19 us -> none  [per_device(): lax.all_to_all(jnp.broadcast_to(meta[None], (devices,) + meta.shape), ('l...]
  transfers between devices with their start and end apart: 13 -> 12, of which waited for: 9 -> 7; matrix products, arithmetic and copies ran while one was open for 5% -> 5% of each run, Pallas kernels for 0% -> 0%
where the time goes in v22:
time: 193 us; the launch traced here: 192 us
  blocking collectives  48.2 us (25%)
  waiting for transfers between devices  44.5 us (23%)
  starting transfers between devices  39 us (20%)
  local copies, waits for them, and re-layouts  20.6 us (11%)
  other arithmetic  15.3 us (8%)
  between operations  14.8 us (8%)
  matrix products  9.4 us (5%)
    all_gather x1, blocking collectives, per_device(): meta = lax.all_gather(meta, ('lvl', 'prow', 'pcol'), axis=0)  48.2 us
    all_to_all x4, waiting for transfers between devices, per_device(): lax.all_to_all(sending, ('lvl', 'pcol'), split_axis=0, concat_axis=0, til...  26.8 us
    ppermute x6, starting transfers between devices, level0_shift(): return lax.ppermute(x, all_axes, pairs)  21.6 us
    all_to_all x4, starting transfers between devices, per_device(): lax.all_to_all(sending, ('lvl', 'pcol'), split_axis=0, concat_axis=0, til...  13.8 us
    unnamed x42, local copies, waits for them, and re-layouts  11.6 us
    all_to_all x1, waiting for transfers between devices, per_device(): lax.all_to_all(final, 'prow', split_axis=0, concat_axis=0, tiled=True)  11.3 us
    ppermute x6, waiting for transfers between devices, level0_shift(): return lax.ppermute(x, all_axes, pairs)  6.38 us
    dot_general x3, matrix products, per_device(): jnp.dot(inv_full, right.astype(jnp.bfloat16), preferred_element_type=jnp....  4.9 us
  transfers between devices with their start and end apart: 12, of which 7 were waited for; matrix products, arithmetic and copies ran while one was open for 5% of the time, Pallas kernels for 0%

profile of v22, /device:TPU:0, one launch (start us, length us, event | category | flops | bytes accessed | tf_op | source)
XLA Modules:
  0.0 191.8 jit_solution(15605002442555164026)
XLA Ops:
  7.3 2.3 %pad_maximum_fusion = bf16[512,1024]{1,0:T(8,128)(2,1)} fusion(bf16[256,1024]{1,0:T(8,128)(2,1)} %bitcast.123, bf16[256,1024]{1,0:T(8,128)(2,1)} %bitcast.119), kind=kLoop, calls=%fused_computation.19 | loop fusion | flops 2097152 | bytes 2097152 | tf_op jit(solution)/shard_map/concatenate | solution.py:53
  9.9 1.1 fusion.53
  10.9 6.9 %collective-permute-start.2 = (bf16[256,256]{1,0:T(8,128)(2,1)S(1)}, bf16[256,256]{1,0:T(8,128)(2,1)S(1)}, u32[]{:S(2)}, u32[]{:S(2)}) collective-permute-start(bf16[256,256]{1,0:T(8,128)(2,1)S(1)} %get-tuple-element.35), channel_id=1, source_target_pairs={{0,6},{1,7},{2,0},{3,1},{4,2},{5,3},{6,4},{7,5}} | collective-permute-start | bytes 393224 | tf_op jit(solution)/shard_map/ppermute | solution.py:72
  17.9 1.9 %collective-permute-start.1 = (bf16[256,256]{1,0:T(8,128)(2,1)S(1)}, bf16[256,256]{1,0:T(8,128)(2,1)S(1)}, u32[]{:S(2)}, u32[]{:S(2)}) collective-permute-start(bf16[256,256]{1,0:T(8,128)(2,1)S(1)} %get-tuple-element.35), channel_id=1, source_target_pairs={{0,4},{1,5},{2,6},{3,7},{4,0},{5,1},{6,2},{7,3}} | collective-permute-start | bytes 393224 | tf_op jit(solution)/shard_map/ppermute | solution.py:72
  19.8 2.9 %collective-permute-start = (bf16[256,256]{1,0:T(8,128)(2,1)S(1)}, bf16[256,256]{1,0:T(8,128)(2,1)S(1)}, u32[]{:S(2)}, u32[]{:S(2)}) collective-permute-start(bf16[256,256]{1,0:T(8,128)(2,1)S(1)} %get-tuple-element.35), channel_id=1, source_target_pairs={{0,2},{1,3},{2,4},{3,5},{4,6},{5,7},{6,0},{7,1}} | collective-permute-start | bytes 393224 | tf_op jit(solution)/shard_map/ppermute | solution.py:72
  22.8 48.2 %all-gather.2 = s32[32,3,8]{2,1,0:T(4,128)S(1)} all-gather(s32[1,3,8]{2,1,0:T(4,128)S(1)} %add_bitcast_fusion), channel_id=3, replica_groups=mesh['lvl'=4,'prow'=4,'pcol'=2] {'lvl','prow','pcol'}, dimensions={0}, use_global_device_ids=true | all-gather | bytes 3168 | tf_op jit(solution)/shard_map/all_gather | solution.py:103
  71.3 0.3 convert_reduce_fusion
  71.6 0.2 fusion.24
  71.8 0.2 select_reduce_fusion
  72.1 0.6 fusion.52
  73.0 0.2 select_reduce_fusion.5
  73.6 0.6 gather_fusion
  74.2 0.3 convolution_convert_fusion.3
  74.5 2.9 %collective-permute-start.5 = (bf16[256,64]{0,1:T(8,128)(2,1)S(1)}, bf16[256,64]{0,1:T(8,128)(2,1)S(1)}, u32[]{:S(2)}, u32[]{:S(2)}) collective-permute-start(bf16[256,64]{0,1:T(8,128)(2,1)S(1)} %get-tuple-element.25), channel_id=1, source_target_pairs={{0,6},{1,7},{2,0},{3,1},{4,2},{5,3},{6,4},{7,5}} | collective-permute-start | bytes 98312 | tf_op jit(solution)/shard_map/ppermute | solution.py:72
  77.5 5.0 %collective-permute-start.4 = (bf16[256,64]{0,1:T(8,128)(2,1)S(1)}, bf16[256,64]{0,1:T(8,128)(2,1)S(1)}, u32[]{:S(2)}, u32[]{:S(2)}) collective-permute-start(bf16[256,64]{0,1:T(8,128)(2,1)S(1)} %get-tuple-element.26), channel_id=1, source_target_pairs={{0,4},{1,5},{2,6},{3,7},{4,0},{5,1},{6,2},{7,3}} | collective-permute-start | bytes 98312 | tf_op jit(solution)/shard_map/ppermute | solution.py:72
  82.5 1.9 %collective-permute-start.3 = (bf16[256,64]{0,1:T(8,128)(2,1)S(1)}, bf16[256,64]{0,1:T(8,128)(2,1)S(1)}, u32[]{:S(2)}, u32[]{:S(2)}) collective-permute-start(bf16[256,64]{0,1:T(8,128)(2,1)S(1)} %get-tuple-element.27), channel_id=1, source_target_pairs={{0,2},{1,3},{2,4},{3,5},{4,6},{5,7},{6,0},{7,1}} | collective-permute-start | bytes 98312 | tf_op jit(solution)/shard_map/ppermute | solution.py:72
  84.4 5.3 %collective-permute-done.4 = bf16[256,64]{0,1:T(8,128)(2,1)S(1)} collective-permute-done((bf16[256,64]{0,1:T(8,128)(2,1)S(1)}, bf16[256,64]{0,1:T(8,128)(2,1)S(1)}, u32[]{:S(2)}, u32[]{:S(2)}) %collective-permute-start.4) | collective-permute-done | bytes 32800 | tf_op jit(solution)/shard_map/ppermute | solution.py:72
  89.7 1.1 collective-permute-done.3
  90.8 0.6 gather_fusion.1
  91.4 0.2 copy.59
  91.6 0.7 gather_fusion.2
  92.3 1.1 reshape.700
  93.4 3.4 %all-to-all-start = ((bf16[8,2,8192]{2,1,0:T(2,128)(2,1)}), bf16[8,2,8192]{2,1,0:T(2,128)(2,1)S(1)}, u32[]{:S(2)}, u32[]{:S(2)}) async-start(bf16[8,2,8192]{2,1,0:T(2,128)(2,1)} %reshape.700), calls=%async_computation | async-start | bytes 524288 | tf_op jit(solution)/shard_map/all_to_all | solution.py:162
  97.0 6.7 %all-to-all-done = bf16[8,2,8192]{2,1,0:T(2,128)(2,1)S(1)} async-done(((bf16[8,2,8192]{2,1,0:T(2,128)(2,1)}), bf16[8,2,8192]{2,1,0:T(2,128)(2,1)S(1)}, u32[]{:S(2)}, u32[]{:S(2)}) %all-to-all-start) | async-done | bytes 262176 | tf_op jit(solution)/shard_map/all_to_all | solution.py:162
  103.7 0.3 reshape.701
  104.1 1.2 scatter_fusion
  105.4 2.5 %compare_select_fusion = (bf16[4,256,1024]{2,1,0:T(8,128)(2,1)S(1)}, bf16[4,256,1024]{2,1,0:T(8,128)(2,1)S(1)}) fusion(bf16[4,512,1024]{2,1,0:T(8,128)(2,1)} %bitcast.113, s32[1024]{0:T(1024)S(1)} %select_reduce_fusion.1, s32[4,256]{1,0:T(4,128)S(1)} %eq.225), kind=kLoop, calls=%fused_computation.11 | loop fusion | flops 2097152 | bytes 8396800 | tf_op jit(solution)/shard_map/jit(_where)/select_n | solution.py:58
  108.0 0.3 bitcast_select_fusion
  108.4 0.9 copy-done.4
  109.2 0.8 fusion.11
  110.1 0.8 convolution_convert_fusion.2
  110.9 0.2 copy.51
  111.1 1.5 gather_fusion.3
  112.6 2.2 %reshape.702 = bf16[8,2,8192]{2,1,0:T(2,128)(2,1)} reshape(bf16[64,32,64]{2,1,0:T(8,128)(2,1)} %gather_fusion.3) | data formatting | bytes 524288
  114.8 3.4 %all-to-all-start.1 = ((bf16[8,2,8192]{2,1,0:T(2,128)(2,1)}), bf16[8,2,8192]{2,1,0:T(2,128)(2,1)S(1)}, u32[]{:S(2)}, u32[]{:S(2)}) async-start(bf16[8,2,8192]{2,1,0:T(2,128)(2,1)} %reshape.702), calls=%async_computation.1 | async-start | bytes 524288 | tf_op jit(solution)/shard_map/all_to_all | solution.py:162
  118.3 6.8 %all-to-all-done.1 = bf16[8,2,8192]{2,1,0:T(2,128)(2,1)S(1)} async-done(((bf16[8,2,8192]{2,1,0:T(2,128)(2,1)}), bf16[8,2,8192]{2,1,0:T(2,128)(2,1)S(1)}, u32[]{:S(2)}, u32[]{:S(2)}) %all-to-all-start.1) | async-done | bytes 262176 | tf_op jit(solution)/shard_map/all_to_all | solution.py:162
  125.1 1.2 reshape.703
  126.2 0.9 slice_convert_fusion.3
  127.2 1.2 scatter_fusion.1
  128.4 2.0 %fusion.14 = bf16[1024,64]{0,1:T(8,128)(2,1)S(1)} fusion(bf16[1024,1024]{1,0:T(8,128)(2,1)S(1)} %bitcast.111, f32[1,1,1024,64]{3,2,1,0:T(8,128)S(1)} %bitcast.125, f32[1,1,1024,256]{3,2,1,0:T(8,128)} %param.9, s32[]{:T(128)S(6)} %select_n.246), kind=kOutput, calls=%fused_computation.36 | convolution fusion | flops 134348800 | bytes 3014660 | tf_op jit(solution)/shard_map/dot_general | solution.py:153
  130.5 1.5 convolution_convert_fusion.1
  131.9 1.1 copy.52
  133.0 1.5 gather_fusion.4
  134.6 2.2 %reshape.704 = bf16[8,2,8192]{2,1,0:T(2,128)(2,1)} reshape(bf16[64,32,64]{2,1,0:T(8,128)(2,1)} %gather_fusion.4) | data formatting | bytes 524288
  136.7 3.6 %all-to-all-start.2 = ((bf16[8,2,8192]{2,1,0:T(2,128)(2,1)}), bf16[8,2,8192]{2,1,0:T(2,128)(2,1)S(1)}, u32[]{:S(2)}, u32[]{:S(2)}) async-start(bf16[8,2,8192]{2,1,0:T(2,128)(2,1)} %reshape.704), calls=%async_computation.2 | async-start | bytes 524288 | tf_op jit(solution)/shard_map/all_to_all | solution.py:162
  140.4 6.6 %all-to-all-done.2 = bf16[8,2,8192]{2,1,0:T(2,128)(2,1)S(1)} async-done(((bf16[8,2,8192]{2,1,0:T(2,128)(2,1)}), bf16[8,2,8192]{2,1,0:T(2,128)(2,1)S(1)}, u32[]{:S(2)}, u32[]{:S(2)}) %all-to-all-start.2) | async-done | bytes 262176 | tf_op jit(solution)/shard_map/all_to_all | solution.py:162
  147.0 1.2 reshape.705
  148.2 0.9 slice_convert_fusion.2
  149.1 1.2 scatter_fusion.2
  150.4 2.0 %select_convert_fusion = (bf16[1024,64]{0,1:T(8,128)(2,1)S(1)}, bf16[1024,64]{0,1:T(8,128)(2,1)S(1)}) fusion(bf16[1024,64]{0,1:T(8,128)(2,1)S(1)} %fusion.14, bf16[1024,64]{0,1:T(8,128)(2,1)S(1)} %fusion.11, pred[]{:T(512)S(6)} %eq.257, pred[]{:T(512)S(6)} %eq.256, pred[]{:T(512)S(6)} %eq.224, bf16[1024,1024]{1,0:T(8,128)(2,1)S(1)} %bitcast.112, ...), kind=kOutput, calls=%fused_computation.41 | convolution fusion | flops 134545408 | bytes 3407879 | tf_op jit(solution)/shard_map/dot_general | solution.py:153
  152.4 0.8 convolution_convert_fusion
  153.2 0.2 copy.53
  153.4 0.8 gather_fusion.5
  154.2 1.1 reshape.706
  155.3 3.4 %all-to-all-start.3 = ((bf16[8,2,8192]{2,1,0:T(2,128)(2,1)}), bf16[8,2,8192]{2,1,0:T(2,128)(2,1)S(1)}, u32[]{:S(2)}, u32[]{:S(2)}) async-start(bf16[8,2,8192]{2,1,0:T(2,128)(2,1)} %reshape.706), calls=%async_computation.3 | async-start | bytes 524288 | tf_op jit(solution)/shard_map/all_to_all | solution.py:162
  158.9 6.8 %all-to-all-done.3 = bf16[8,2,8192]{2,1,0:T(2,128)(2,1)S(1)} async-done(((bf16[8,2,8192]{2,1,0:T(2,128)(2,1)}), bf16[8,2,8192]{2,1,0:T(2,128)(2,1)S(1)}, u32[]{:S(2)}, u32[]{:S(2)}) %all-to-all-start.3) | async-done | bytes 262176 | tf_op jit(solution)/shard_map/all_to_all | solution.py:162
  165.6 0.3 reshape.707
  166.0 1.2 scatter_fusion.3
  167.4 0.8 pad_maximum_fusion.2
  168.1 3.6 %all-to-all-start.4 = ((bf16[4,768,64]{1,2,0:T(8,128)(2,1)}), bf16[4,768,64]{1,2,0:T(8,128)(2,1)S(1)}, u32[]{:S(2)}, u32[]{:S(2)}) async-start(bf16[4,768,64]{1,2,0:T(8,128)(2,1)} %pad_maximum_fusion.2), calls=%async_computation.4 | async-start | bytes 786432 | tf_op jit(solution)/shard_map/all_to_all | solution.py:177
  171.7 11.3 %all-to-all-done.4 = bf16[4,768,64]{1,2,0:T(8,128)(2,1)S(1)} async-done(((bf16[4,768,64]{1,2,0:T(8,128)(2,1)}), bf16[4,768,64]{1,2,0:T(8,128)(2,1)S(1)}, u32[]{:S(2)}, u32[]{:S(2)}) %all-to-all-start.4) | async-done | bytes 393248 | tf_op jit(solution)/shard_map/all_to_all | solution.py:177
  183.0 0.1 copy.56
  183.2 1.0 copy.57
  184.2 0.7 select_bitcast_fusion
  (94 shorter events, 2.2 us)
Async XLA Ops:
  7.2 2.7 %copy-start.5 = (bf16[1,1,256,1024]{3,2,1,0:T(8,128)(2,1)S(1)}, bf16[1,1,256,1024]{3,2,1,0:T(8,128)(2,1)}, u32[]{:S(2)}) copy-start(bf16[1,1,256,1024]{3,2,1,0:T(8,128)(2,1)} %param.10) | copy-start | bytes 1572868
  7.2 2.5 %copy-start.9 = (s32[1,1,8]{2,1,0:T(1,128)S(1)}, s32[1,1,8]{2,1,0:T(1,128)}, u32[]{:S(2)}) copy-start(s32[1,1,8]{2,1,0:T(1,128)} %param.12) | copy-start | bytes 100
  7.2 2.7 %copy-start.3 = (f32[1,1,1024,256]{3,2,1,0:T(8,128)S(1)}, f32[1,1,1024,256]{3,2,1,0:T(8,128)}, u32[]{:S(2)}) copy-start(f32[1,1,1024,256]{3,2,1,0:T(8,128)} %param.9) | copy-start | bytes 3145732
  7.2 98.2 %all-gather.5.cloned.1.call-start = ((), (), s32[]{:S(2)}) async-start(), calls=%async_computation.5 | async-start | bytes 5242880 | tf_op jit(solution)/shard_map/all_gather | solution.py:56
  7.2 15.5 %copy-start.13 = (s32[1,1,8]{2,1,0:T(1,128)S(1)}, s32[1,1,8]{2,1,0:T(1,128)}, u32[]{:S(2)}) copy-start(s32[1,1,8]{2,1,0:T(1,128)} %param.14) | copy-start | bytes 100
  7.3 15.5 %copy-start.14 = (s32[1,1,8]{2,1,0:T(1,128)S(1)}, s32[1,1,8]{2,1,0:T(1,128)}, u32[]{:S(2)}) copy-start(s32[1,1,8]{2,1,0:T(1,128)} %param.13) | copy-start | bytes 100
  7.3 15.5 %copy-start.15 = (s32[1,1,8]{2,1,0:T(1,128)S(1)}, s32[1,1,8]{2,1,0:T(1,128)}, u32[]{:S(2)}) copy-start(s32[1,1,8]{2,1,0:T(1,128)} %param.15) | copy-start | bytes 100
  9.6 63.6 %copy-start.6 = (bf16[1,1,8,32,1024]{4,3,2,1,0:T(8,128)(2,1)S(1)}, bf16[1,1,8,32,1024]{4,3,2,1,0:T(8,128)(2,1)}, u32[]{:S(2)}) copy-start(bf16[1,1,8,32,1024]{4,3,2,1,0:T(8,128)(2,1)} %param.11) | copy-start | bytes 1572868
  10.9 62.5 %collective-permute-start.2 = (bf16[256,256]{1,0:T(8,128)(2,1)S(1)}, bf16[256,256]{1,0:T(8,128)(2,1)S(1)}, u32[]{:S(2)}, u32[]{:S(2)}) collective-permute-start(bf16[256,256]{1,0:T(8,128)(2,1)S(1)} %get-tuple-element.35), channel_id=1, source_target_pairs={{0,6},{1,7},{2,0},{3,1},{4,2},{5,3},{6,4},{7,5}} | collective-permute-start | bytes 393224 | tf_op jit(solution)/shard_map/ppermute | solution.py:72
  17.9 55.6 %collective-permute-start.1 = (bf16[256,256]{1,0:T(8,128)(2,1)S(1)}, bf16[256,256]{1,0:T(8,128)(2,1)S(1)}, u32[]{:S(2)}, u32[]{:S(2)}) collective-permute-start(bf16[256,256]{1,0:T(8,128)(2,1)S(1)} %get-tuple-element.35), channel_id=1, source_target_pairs={{0,4},{1,5},{2,6},{3,7},{4,0},{5,1},{6,2},{7,3}} | collective-permute-start | bytes 393224 | tf_op jit(solution)/shard_map/ppermute | solution.py:72
  19.8 53.7 %collective-permute-start = (bf16[256,256]{1,0:T(8,128)(2,1)S(1)}, bf16[256,256]{1,0:T(8,128)(2,1)S(1)}, u32[]{:S(2)}, u32[]{:S(2)}) collective-permute-start(bf16[256,256]{1,0:T(8,128)(2,1)S(1)} %get-tuple-element.35), channel_id=1, source_target_pairs={{0,2},{1,3},{2,4},{3,5},{4,6},{5,7},{6,0},{7,1}} | collective-permute-start | bytes 393224 | tf_op jit(solution)/shard_map/ppermute | solution.py:72
  73.5 18.2 %copy-start.8 = (s32[1024]{0:T(1024)}, s32[1024]{0:T(1024)S(1)}, u32[]{:S(2)}) copy-start(s32[1024]{0:T(1024)S(1)} %pad_clamp_fusion) | copy-start | bytes 12292
  74.5 9.9 %collective-permute-start.5 = (bf16[256,64]{0,1:T(8,128)(2,1)S(1)}, bf16[256,64]{0,1:T(8,128)(2,1)S(1)}, u32[]{:S(2)}, u32[]{:S(2)}) collective-permute-start(bf16[256,64]{0,1:T(8,128)(2,1)S(1)} %get-tuple-element.25), channel_id=1, source_target_pairs={{0,6},{1,7},{2,0},{3,1},{4,2},{5,3},{6,4},{7,5}} | collective-permute-start | bytes 98312 | tf_op jit(solution)/shard_map/ppermute | solution.py:72
  77.5 12.2 %collective-permute-start.4 = (bf16[256,64]{0,1:T(8,128)(2,1)S(1)}, bf16[256,64]{0,1:T(8,128)(2,1)S(1)}, u32[]{:S(2)}, u32[]{:S(2)}) collective-permute-start(bf16[256,64]{0,1:T(8,128)(2,1)S(1)} %get-tuple-element.26), channel_id=1, source_target_pairs={{0,4},{1,5},{2,6},{3,7},{4,0},{5,1},{6,2},{7,3}} | collective-permute-start | bytes 98312 | tf_op jit(solution)/shard_map/ppermute | solution.py:72
  82.5 8.3 %collective-permute-start.3 = (bf16[256,64]{0,1:T(8,128)(2,1)S(1)}, bf16[256,64]{0,1:T(8,128)(2,1)S(1)}, u32[]{:S(2)}, u32[]{:S(2)}) collective-permute-start(bf16[256,64]{0,1:T(8,128)(2,1)S(1)} %get-tuple-element.27), channel_id=1, source_target_pairs={{0,2},{1,3},{2,4},{3,5},{4,6},{5,7},{6,0},{7,1}} | collective-permute-start | bytes 98312 | tf_op jit(solution)/shard_map/ppermute | solution.py:72
  93.4 10.3 %all-to-all-start = ((bf16[8,2,8192]{2,1,0:T(2,128)(2,1)}), bf16[8,2,8192]{2,1,0:T(2,128)(2,1)S(1)}, u32[]{:S(2)}, u32[]{:S(2)}) async-start(bf16[8,2,8192]{2,1,0:T(2,128)(2,1)} %reshape.700), calls=%async_computation | async-start | bytes 524288 | tf_op jit(solution)/shard_map/all_to_all | solution.py:162
  108.0 1.2 copy-start.4
  108.4 1.7 copy-start
  110.1 8.1 %copy-start.12 = (s32[2,8]{1,0:T(2,128)S(1)}, s32[2,8]{1,0:T(2,128)}, u32[]{:S(2)}) copy-start(s32[2,8]{1,0:T(2,128)} %get-tuple-element.33) | copy-start | bytes 196
  114.8 10.3 %all-to-all-start.1 = ((bf16[8,2,8192]{2,1,0:T(2,128)(2,1)}), bf16[8,2,8192]{2,1,0:T(2,128)(2,1)S(1)}, u32[]{:S(2)}, u32[]{:S(2)}) async-start(bf16[8,2,8192]{2,1,0:T(2,128)(2,1)} %reshape.702), calls=%async_computation.1 | async-start | bytes 524288 | tf_op jit(solution)/shard_map/all_to_all | solution.py:162
  128.4 2.1 %copy-start.1 = (bf16[1024,1024]{1,0:T(8,128)(2,1)S(1)}, bf16[1024,1024]{1,0:T(8,128)(2,1)}, u32[]{:S(2)}) copy-start(bf16[1024,1024]{1,0:T(8,128)(2,1)} %copy-done) | copy-start | bytes 6291460
  130.5 9.9 %copy-start.11 = (s32[2,8]{1,0:T(2,128)S(1)}, s32[2,8]{1,0:T(2,128)}, u32[]{:S(2)}) copy-start(s32[2,8]{1,0:T(2,128)} %get-tuple-element.32) | copy-start | bytes 196
  136.7 10.3 %all-to-all-start.2 = ((bf16[8,2,8192]{2,1,0:T(2,128)(2,1)}), bf16[8,2,8192]{2,1,0:T(2,128)(2,1)S(1)}, u32[]{:S(2)}, u32[]{:S(2)}) async-start(bf16[8,2,8192]{2,1,0:T(2,128)(2,1)} %reshape.704), calls=%async_computation.2 | async-start | bytes 524288 | tf_op jit(solution)/shard_map/all_to_all | solution.py:162
  150.4 2.1 %copy-start.2 = (bf16[1024,1024]{1,0:T(8,128)(2,1)S(1)}, bf16[1024,1024]{1,0:T(8,128)(2,1)}, u32[]{:S(2)}) copy-start(bf16[1024,1024]{1,0:T(8,128)(2,1)} %copy-done) | copy-start | bytes 6291460
  152.4 6.3 %copy-start.10 = (s32[2,8]{1,0:T(2,128)S(1)}, s32[2,8]{1,0:T(2,128)}, u32[]{:S(2)}) copy-start(s32[2,8]{1,0:T(2,128)} %get-tuple-element.31) | copy-start | bytes 196
  155.3 10.3 %all-to-all-start.3 = ((bf16[8,2,8192]{2,1,0:T(2,128)(2,1)}), bf16[8,2,8192]{2,1,0:T(2,128)(2,1)S(1)}, u32[]{:S(2)}, u32[]{:S(2)}) async-start(bf16[8,2,8192]{2,1,0:T(2,128)(2,1)} %reshape.706), calls=%async_computation.3 | async-start | bytes 524288 | tf_op jit(solution)/shard_map/all_to_all | solution.py:162
  168.1 16.1 %copy-start.7 = (f32[256,256]{1,0:T(8,128)S(1)}, f32[256,256]{1,0:T(8,128)}, u32[]{:S(2)}) copy-start(f32[256,256]{1,0:T(8,128)} %get-tuple-element.36) | copy-start | bytes 786436
  168.1 14.9 %all-to-all-start.4 = ((bf16[4,768,64]{1,2,0:T(8,128)(2,1)}), bf16[4,768,64]{1,2,0:T(8,128)(2,1)S(1)}, u32[]{:S(2)}, u32[]{:S(2)}) async-start(bf16[4,768,64]{1,2,0:T(8,128)(2,1)} %pad_maximum_fusion.2), calls=%async_computation.4 | async-start | bytes 786432 | tf_op jit(solution)/shard_map/all_to_all | solution.py:177
Sparse Core Ops, SparseCore 0:
  9.8 91.6 all-gather.4

commit v23 on v17

--- a/solution.py
+++ b/solution.py
@@ -165,12 +165,12 @@
                 tiles_full, solved_now.astype(jnp.bfloat16), preferred_element_type=jnp.float32
             ).astype(jnp.bfloat16)
         updates = updates.reshape(group_tiles + 1, block_rows, cols)
-        sending = jnp.take(updates, send_index, axis=0, mode="clip")
+        sending = updates.at[send_index].get(mode="promise_in_bounds")
         incoming = lax.all_to_all(
             sending, ("lvl", "pcol"), split_axis=0, concat_axis=0, tiled=True
         )
         incoming = incoming.reshape(n_lvl, n_pcol * slots, block_rows, cols)[section]
-        acc = acc.at[recv_block[section]].add(incoming.astype(jnp.float32), mode="clip")
+        acc = acc.at[recv_block[section]].add(incoming.astype(jnp.float32), mode="promise_in_bounds")
     outer = acc[window_blocks:NT].reshape(ABOVE, cols)
 
     solved_blocks = solved.reshape(n_prow, rows_out, cols)

time: 191 us -> 191 us (level)
  no operation moved by 1% of the time
where the time goes in v23:
time: 191 us; the launch traced here: 189 us
  waiting for transfers between devices  76.2 us (40%)
  starting transfers between devices  52.4 us (27%)
  local copies, waits for them, and re-layouts  21.2 us (11%)
  other arithmetic  15.3 us (8%)
  between operations  14.9 us (8%)
  matrix products  9.4 us (5%)
    ppermute x6, starting transfers between devices, level0_shift(): return lax.ppermute(x, all_axes, pairs)  30.7 us
    all_to_all x4, waiting for transfers between devices, per_device(): lax.all_to_all(sending, ('lvl', 'pcol'), split_axis=0, concat_axis=0, til...  26.8 us
    all_gather x1, waiting for transfers between devices, per_device(): gathered = lax.all_gather(raw, 'prow', axis=0)  20.4 us
    all_to_all x4, starting transfers between devices, per_device(): lax.all_to_all(sending, ('lvl', 'pcol'), split_axis=0, concat_axis=0, til...  13.8 us
    all_to_all x1, waiting for transfers between devices, per_device(): lax.all_to_all(jnp.broadcast_to(meta[None], (devices,) + meta.shape), ('l...  12.4 us
    unnamed x42, local copies, waits for them, and re-layouts  11.6 us
    all_to_all x1, waiting for transfers between devices, per_device(): lax.all_to_all(final, 'prow', split_axis=0, concat_axis=0, tiled=True)  11 us
    ppermute x6, waiting for transfers between devices, level0_shift(): return lax.ppermute(x, all_axes, pairs)  5.61 us
  transfers between devices with their start and end apart: 13, of which 9 were waited for; matrix products, arithmetic and copies ran while one was open for 5% of the time, Pallas kernels for 0%

profile of v23, /device:TPU:0, one launch (start us, length us, event | category | flops | bytes accessed | tf_op | source)
XLA Modules:
  0.0 189.4 jit_solution(11855574053499320210)
XLA Ops:
  7.3 2.3 %pad_maximum_fusion = bf16[512,1024]{1,0:T(8,128)(2,1)} fusion(bf16[256,1024]{1,0:T(8,128)(2,1)} %bitcast.125, bf16[256,1024]{1,0:T(8,128)(2,1)} %bitcast.121), kind=kLoop, calls=%fused_computation.19 | loop fusion | flops 2097152 | bytes 2097152 | tf_op jit(solution)/shard_map/concatenate | solution.py:53
  9.9 1.1 fusion.50
  10.9 6.9 %collective-permute-start.2 = (bf16[256,256]{1,0:T(8,128)(2,1)S(1)}, bf16[256,256]{1,0:T(8,128)(2,1)S(1)}, u32[]{:S(2)}, u32[]{:S(2)}) collective-permute-start(bf16[256,256]{1,0:T(8,128)(2,1)S(1)} %get-tuple-element.37), channel_id=1, source_target_pairs={{0,6},{1,7},{2,0},{3,1},{4,2},{5,3},{6,4},{7,5}} | collective-permute-start | bytes 393224 | tf_op jit(solution)/shard_map/ppermute | solution.py:72
  17.9 1.9 %collective-permute-start.1 = (bf16[256,256]{1,0:T(8,128)(2,1)S(1)}, bf16[256,256]{1,0:T(8,128)(2,1)S(1)}, u32[]{:S(2)}, u32[]{:S(2)}) collective-permute-start(bf16[256,256]{1,0:T(8,128)(2,1)S(1)} %get-tuple-element.37), channel_id=1, source_target_pairs={{0,4},{1,5},{2,6},{3,7},{4,0},{5,1},{6,2},{7,3}} | collective-permute-start | bytes 393224 | tf_op jit(solution)/shard_map/ppermute | solution.py:72
  19.8 2.9 %collective-permute-start = (bf16[256,256]{1,0:T(8,128)(2,1)S(1)}, bf16[256,256]{1,0:T(8,128)(2,1)S(1)}, u32[]{:S(2)}, u32[]{:S(2)}) collective-permute-start(bf16[256,256]{1,0:T(8,128)(2,1)S(1)} %get-tuple-element.37), channel_id=1, source_target_pairs={{0,2},{1,3},{2,4},{3,5},{4,6},{5,7},{6,0},{7,1}} | collective-permute-start | bytes 393224 | tf_op jit(solution)/shard_map/ppermute | solution.py:72
  22.8 0.6 broadcast_in_dim.179
  23.4 3.2 %all-to-all-start = ((s32[32,3,8]{2,1,0:T(4,128)}), s32[32,3,8]{2,1,0:T(4,128)S(1)}, u32[]{:S(2)}, u32[]{:S(2)}) async-start(s32[32,3,8]{2,1,0:T(4,128)} %broadcast_in_dim.179), calls=%async_computation | async-start | bytes 131072 | tf_op jit(solution)/shard_map/all_to_all | solution.py:104
  27.2 12.4 %all-to-all-done = s32[32,3,8]{2,1,0:T(4,128)S(1)} async-done(((s32[32,3,8]{2,1,0:T(4,128)}), s32[32,3,8]{2,1,0:T(4,128)S(1)}, u32[]{:S(2)}, u32[]{:S(2)}) %all-to-all-start) | async-done | bytes 3104 | tf_op jit(solution)/shard_map/all_to_all | solution.py:104
  39.8 0.3 convert_reduce_fusion
  40.1 0.2 fusion.24
  40.3 0.2 select_reduce_fusion
  40.6 0.6 fusion.49
  41.7 0.6 gather_fusion
  42.3 0.3 convolution_convert_fusion.3
  42.7 14.3 %collective-permute-start.5 = (bf16[256,64]{0,1:T(8,128)(2,1)S(1)}, bf16[256,64]{0,1:T(8,128)(2,1)S(1)}, u32[]{:S(2)}, u32[]{:S(2)}) collective-permute-start(bf16[256,64]{0,1:T(8,128)(2,1)S(1)} %get-tuple-element.27), channel_id=1, source_target_pairs={{0,6},{1,7},{2,0},{3,1},{4,2},{5,3},{6,4},{7,5}} | collective-permute-start | bytes 98312 | tf_op jit(solution)/shard_map/ppermute | solution.py:72
  57.0 1.9 %collective-permute-start.4 = (bf16[256,64]{0,1:T(8,128)(2,1)S(1)}, bf16[256,64]{0,1:T(8,128)(2,1)S(1)}, u32[]{:S(2)}, u32[]{:S(2)}) collective-permute-start(bf16[256,64]{0,1:T(8,128)(2,1)S(1)} %get-tuple-element.28), channel_id=1, source_target_pairs={{0,4},{1,5},{2,6},{3,7},{4,0},{5,1},{6,2},{7,3}} | collective-permute-start | bytes 98312 | tf_op jit(solution)/shard_map/ppermute | solution.py:72
  58.9 2.7 %collective-permute-start.3 = (bf16[256,64]{0,1:T(8,128)(2,1)S(1)}, bf16[256,64]{0,1:T(8,128)(2,1)S(1)}, u32[]{:S(2)}, u32[]{:S(2)}) collective-permute-start(bf16[256,64]{0,1:T(8,128)(2,1)S(1)} %get-tuple-element.29), channel_id=1, source_target_pairs={{0,2},{1,3},{2,4},{3,5},{4,6},{5,7},{6,0},{7,1}} | collective-permute-start | bytes 98312 | tf_op jit(solution)/shard_map/ppermute | solution.py:72
  61.7 2.8 %collective-permute-done.4 = bf16[256,64]{0,1:T(8,128)(2,1)S(1)} collective-permute-done((bf16[256,64]{0,1:T(8,128)(2,1)S(1)}, bf16[256,64]{0,1:T(8,128)(2,1)S(1)}, u32[]{:S(2)}, u32[]{:S(2)}) %collective-permute-start.4) | collective-permute-done | bytes 32800 | tf_op jit(solution)/shard_map/ppermute | solution.py:72
  64.4 2.8 %collective-permute-done.3 = bf16[256,64]{0,1:T(8,128)(2,1)S(1)} collective-permute-done((bf16[256,64]{0,1:T(8,128)(2,1)S(1)}, bf16[256,64]{0,1:T(8,128)(2,1)S(1)}, u32[]{:S(2)}, u32[]{:S(2)}) %collective-permute-start.3) | collective-permute-done | bytes 32800 | tf_op jit(solution)/shard_map/ppermute | solution.py:72
  67.3 0.6 gather_fusion.1
  68.1 0.7 gather_fusion.2
  68.8 1.1 reshape.685
  69.9 3.4 %all-to-all-start.1 = ((bf16[8,2,8192]{2,1,0:T(2,128)(2,1)}), bf16[8,2,8192]{2,1,0:T(2,128)(2,1)S(1)}, u32[]{:S(2)}, u32[]{:S(2)}) async-start(bf16[8,2,8192]{2,1,0:T(2,128)(2,1)} %reshape.685), calls=%async_computation.1 | async-start | bytes 524288 | tf_op jit(solution)/shard_map/all_to_all | solution.py:169
  73.5 6.7 %all-to-all-done.1 = bf16[8,2,8192]{2,1,0:T(2,128)(2,1)S(1)} async-done(((bf16[8,2,8192]{2,1,0:T(2,128)(2,1)}), bf16[8,2,8192]{2,1,0:T(2,128)(2,1)S(1)}, u32[]{:S(2)}, u32[]{:S(2)}) %all-to-all-start.1) | async-done | bytes 262176 | tf_op jit(solution)/shard_map/all_to_all | solution.py:169
  80.2 0.3 reshape.686
  80.6 1.2 scatter_fusion
  81.9 20.4 %all-gather.3.cloned.1.call-done = bf16[2048,1024]{1,0:T(8,128)(2,1)} async-done(((bf16[512,1024]{1,0:T(8,128)(2,1)}), bf16[2048,1024]{1,0:T(8,128)(2,1)}) %all-gather.3.cloned.1.call-update) | async-done | bytes 4194320 | tf_op jit(solution)/shard_map/all_gather | solution.py:56
  102.3 2.5 %compare_select_fusion = (bf16[4,256,1024]{2,1,0:T(8,128)(2,1)S(1)}, bf16[4,256,1024]{2,1,0:T(8,128)(2,1)S(1)}) fusion(bf16[4,512,1024]{2,1,0:T(8,128)(2,1)} %bitcast.115, s32[1024]{0:T(1024)S(1)} %select_reduce_fusion.1, s32[4,256]{1,0:T(4,128)S(1)} %eq.225), kind=kLoop, calls=%fused_computation.11 | loop fusion | flops 2097152 | bytes 8396800 | tf_op jit(solution)/shard_map/jit(_where)/select_n | solution.py:58
  104.9 0.3 bitcast_select_fusion
  105.2 0.9 copy-done.4
  106.1 0.8 fusion.11
  106.9 0.8 convolution_convert_fusion.2
  107.8 0.2 copy.62
  107.9 1.5 gather_fusion.3
  109.5 2.1 %reshape.687 = bf16[8,2,8192]{2,1,0:T(2,128)(2,1)} reshape(bf16[64,32,64]{2,1,0:T(8,128)(2,1)} %gather_fusion.3) | data formatting | bytes 524288
  111.6 3.4 %all-to-all-start.2 = ((bf16[8,2,8192]{2,1,0:T(2,128)(2,1)}), bf16[8,2,8192]{2,1,0:T(2,128)(2,1)S(1)}, u32[]{:S(2)}, u32[]{:S(2)}) async-start(bf16[8,2,8192]{2,1,0:T(2,128)(2,1)} %reshape.687), calls=%async_computation.2 | async-start | bytes 524288 | tf_op jit(solution)/shard_map/all_to_all | solution.py:169
  115.2 6.8 %all-to-all-done.2 = bf16[8,2,8192]{2,1,0:T(2,128)(2,1)S(1)} async-done(((bf16[8,2,8192]{2,1,0:T(2,128)(2,1)}), bf16[8,2,8192]{2,1,0:T(2,128)(2,1)S(1)}, u32[]{:S(2)}, u32[]{:S(2)}) %all-to-all-start.2) | async-done | bytes 262176 | tf_op jit(solution)/shard_map/all_to_all | solution.py:169
  121.9 1.2 reshape.688
  123.1 0.9 slice_convert_fusion.3
  124.0 1.2 scatter_fusion.1
  125.3 2.0 %fusion.14 = bf16[1024,64]{0,1:T(8,128)(2,1)S(1)} fusion(bf16[1024,1024]{1,0:T(8,128)(2,1)S(1)} %bitcast.113, f32[1,1,1024,64]{3,2,1,0:T(8,128)S(1)} %bitcast.127, f32[1,1,1024,256]{3,2,1,0:T(8,128)} %param.9, s32[]{:T(128)S(6)} %select_n.259), kind=kOutput, calls=%fused_computation.36 | convolution fusion | flops 134348800 | bytes 3014660 | tf_op jit(solution)/shard_map/dot_general | solution.py:160
  127.3 1.5 convolution_convert_fusion.1
  128.8 1.1 copy.63
  129.9 1.5 gather_fusion.4
  131.4 2.1 %reshape.689 = bf16[8,2,8192]{2,1,0:T(2,128)(2,1)} reshape(bf16[64,32,64]{2,1,0:T(8,128)(2,1)} %gather_fusion.4) | data formatting | bytes 524288
  133.6 3.6 %all-to-all-start.3 = ((bf16[8,2,8192]{2,1,0:T(2,128)(2,1)}), bf16[8,2,8192]{2,1,0:T(2,128)(2,1)S(1)}, u32[]{:S(2)}, u32[]{:S(2)}) async-start(bf16[8,2,8192]{2,1,0:T(2,128)(2,1)} %reshape.689), calls=%async_computation.3 | async-start | bytes 524288 | tf_op jit(solution)/shard_map/all_to_all | solution.py:169
  137.3 6.6 %all-to-all-done.3 = bf16[8,2,8192]{2,1,0:T(2,128)(2,1)S(1)} async-done(((bf16[8,2,8192]{2,1,0:T(2,128)(2,1)}), bf16[8,2,8192]{2,1,0:T(2,128)(2,1)S(1)}, u32[]{:S(2)}, u32[]{:S(2)}) %all-to-all-start.3) | async-done | bytes 262176 | tf_op jit(solution)/shard_map/all_to_all | solution.py:169
  143.9 1.2 reshape.690
  145.0 0.9 slice_convert_fusion.2
  145.9 1.2 scatter_fusion.2
  147.2 2.0 %select_convert_fusion = (bf16[1024,64]{0,1:T(8,128)(2,1)S(1)}, bf16[1024,64]{0,1:T(8,128)(2,1)S(1)}) fusion(bf16[1024,64]{0,1:T(8,128)(2,1)S(1)} %fusion.14, bf16[1024,64]{0,1:T(8,128)(2,1)S(1)} %fusion.11, pred[]{:T(512)S(6)} %eq.257, pred[]{:T(512)S(6)} %eq.256, pred[]{:T(512)S(6)} %eq.224, bf16[1024,1024]{1,0:T(8,128)(2,1)S(1)} %bitcast.114, ...), kind=kOutput, calls=%fused_computation.41 | convolution fusion | flops 134545408 | bytes 3407879 | tf_op jit(solution)/shard_map/dot_general | solution.py:160
  149.3 0.8 convolution_convert_fusion
  150.1 0.2 copy.64
  150.3 0.8 gather_fusion.5
  151.1 1.1 reshape.691
  152.2 3.4 %all-to-all-start.4 = ((bf16[8,2,8192]{2,1,0:T(2,128)(2,1)}), bf16[8,2,8192]{2,1,0:T(2,128)(2,1)S(1)}, u32[]{:S(2)}, u32[]{:S(2)}) async-start(bf16[8,2,8192]{2,1,0:T(2,128)(2,1)} %reshape.691), calls=%async_computation.4 | async-start | bytes 524288 | tf_op jit(solution)/shard_map/all_to_all | solution.py:169
  155.7 6.8 %all-to-all-done.4 = bf16[8,2,8192]{2,1,0:T(2,128)(2,1)S(1)} async-done(((bf16[8,2,8192]{2,1,0:T(2,128)(2,1)}), bf16[8,2,8192]{2,1,0:T(2,128)(2,1)S(1)}, u32[]{:S(2)}, u32[]{:S(2)}) %all-to-all-start.4) | async-done | bytes 262176 | tf_op jit(solution)/shard_map/all_to_all | solution.py:169
  162.5 0.3 reshape.692
  162.8 1.2 scatter_fusion.3
  164.2 0.8 pad_maximum_fusion.2
  165.0 4.6 %all-to-all-start.5 = ((bf16[4,768,64]{1,2,0:T(8,128)(2,1)}), bf16[4,768,64]{1,2,0:T(8,128)(2,1)S(1)}, u32[]{:S(2)}, u32[]{:S(2)}) async-start(bf16[4,768,64]{1,2,0:T(8,128)(2,1)} %pad_maximum_fusion.2), calls=%async_computation.5 | async-start | bytes 786432 | tf_op jit(solution)/shard_map/all_to_all | solution.py:184
  169.6 11.0 %all-to-all-done.5 = bf16[4,768,64]{1,2,0:T(8,128)(2,1)S(1)} async-done(((bf16[4,768,64]{1,2,0:T(8,128)(2,1)}), bf16[4,768,64]{1,2,0:T(8,128)(2,1)S(1)}, u32[]{:S(2)}, u32[]{:S(2)}) %all-to-all-start.5) | async-done | bytes 393248 | tf_op jit(solution)/shard_map/all_to_all | solution.py:184
  180.8 1.0 copy.68
  181.8 0.7 select_bitcast_fusion
  (97 shorter events, 2.7 us)
Async XLA Ops:
  7.2 2.7 %copy-start.5 = (bf16[1,1,256,1024]{3,2,1,0:T(8,128)(2,1)S(1)}, bf16[1,1,256,1024]{3,2,1,0:T(8,128)(2,1)}, u32[]{:S(2)}) copy-start(bf16[1,1,256,1024]{3,2,1,0:T(8,128)(2,1)} %param.10) | copy-start | bytes 1572868
  7.2 2.5 %copy-start.9 = (s32[1,1,8]{2,1,0:T(1,128)S(1)}, s32[1,1,8]{2,1,0:T(1,128)}, u32[]{:S(2)}) copy-start(s32[1,1,8]{2,1,0:T(1,128)} %param.12) | copy-start | bytes 100
  7.2 2.7 %copy-start.3 = (f32[1,1,1024,256]{3,2,1,0:T(8,128)S(1)}, f32[1,1,1024,256]{3,2,1,0:T(8,128)}, u32[]{:S(2)}) copy-start(f32[1,1,1024,256]{3,2,1,0:T(8,128)} %param.9) | copy-start | bytes 3145732
  7.2 95.1 %all-gather.3.cloned.1.call-start = ((), (), s32[]{:S(2)}) async-start(), calls=%async_computation.6 | async-start | bytes 5242880 | tf_op jit(solution)/shard_map/all_gather | solution.py:56
  7.2 15.5 %copy-start.13 = (s32[1,1,8]{2,1,0:T(1,128)S(1)}, s32[1,1,8]{2,1,0:T(1,128)}, u32[]{:S(2)}) copy-start(s32[1,1,8]{2,1,0:T(1,128)} %param.14) | copy-start | bytes 100
  7.3 15.5 %copy-start.14 = (s32[1,1,8]{2,1,0:T(1,128)S(1)}, s32[1,1,8]{2,1,0:T(1,128)}, u32[]{:S(2)}) copy-start(s32[1,1,8]{2,1,0:T(1,128)} %param.13) | copy-start | bytes 100
  7.3 15.5 %copy-start.15 = (s32[1,1,8]{2,1,0:T(1,128)S(1)}, s32[1,1,8]{2,1,0:T(1,128)}, u32[]{:S(2)}) copy-start(s32[1,1,8]{2,1,0:T(1,128)} %param.15) | copy-start | bytes 100
  9.6 17.4 %copy-start.6 = (bf16[1,1,8,32,1024]{4,3,2,1,0:T(8,128)(2,1)S(1)}, bf16[1,1,8,32,1024]{4,3,2,1,0:T(8,128)(2,1)}, u32[]{:S(2)}) copy-start(bf16[1,1,8,32,1024]{4,3,2,1,0:T(8,128)(2,1)} %param.11) | copy-start | bytes 1572868
  10.9 30.6 %collective-permute-start.2 = (bf16[256,256]{1,0:T(8,128)(2,1)S(1)}, bf16[256,256]{1,0:T(8,128)(2,1)S(1)}, u32[]{:S(2)}, u32[]{:S(2)}) collective-permute-start(bf16[256,256]{1,0:T(8,128)(2,1)S(1)} %get-tuple-element.37), channel_id=1, source_target_pairs={{0,6},{1,7},{2,0},{3,1},{4,2},{5,3},{6,4},{7,5}} | collective-permute-start | bytes 393224 | tf_op jit(solution)/shard_map/ppermute | solution.py:72
  17.9 23.7 %collective-permute-start.1 = (bf16[256,256]{1,0:T(8,128)(2,1)S(1)}, bf16[256,256]{1,0:T(8,128)(2,1)S(1)}, u32[]{:S(2)}, u32[]{:S(2)}) collective-permute-start(bf16[256,256]{1,0:T(8,128)(2,1)S(1)} %get-tuple-element.37), channel_id=1, source_target_pairs={{0,4},{1,5},{2,6},{3,7},{4,0},{5,1},{6,2},{7,3}} | collective-permute-start | bytes 393224 | tf_op jit(solution)/shard_map/ppermute | solution.py:72
  19.8 21.8 %collective-permute-start = (bf16[256,256]{1,0:T(8,128)(2,1)S(1)}, bf16[256,256]{1,0:T(8,128)(2,1)S(1)}, u32[]{:S(2)}, u32[]{:S(2)}) collective-permute-start(bf16[256,256]{1,0:T(8,128)(2,1)S(1)} %get-tuple-element.37), channel_id=1, source_target_pairs={{0,2},{1,3},{2,4},{3,5},{4,6},{5,7},{6,0},{7,1}} | collective-permute-start | bytes 393224 | tf_op jit(solution)/shard_map/ppermute | solution.py:72
  23.4 16.1 %all-to-all-start = ((s32[32,3,8]{2,1,0:T(4,128)}), s32[32,3,8]{2,1,0:T(4,128)S(1)}, u32[]{:S(2)}, u32[]{:S(2)}) async-start(s32[32,3,8]{2,1,0:T(4,128)} %broadcast_in_dim.179), calls=%async_computation | async-start | bytes 131072 | tf_op jit(solution)/shard_map/all_to_all | solution.py:104
  41.6 26.5 %copy-start.8 = (s32[1024]{0:T(1024)}, s32[1024]{0:T(1024)S(1)}, u32[]{:S(2)}) copy-start(s32[1024]{0:T(1024)S(1)} %pad_clamp_fusion) | copy-start | bytes 12292
  42.7 19.0 %collective-permute-start.5 = (bf16[256,64]{0,1:T(8,128)(2,1)S(1)}, bf16[256,64]{0,1:T(8,128)(2,1)S(1)}, u32[]{:S(2)}, u32[]{:S(2)}) collective-permute-start(bf16[256,64]{0,1:T(8,128)(2,1)S(1)} %get-tuple-element.27), channel_id=1, source_target_pairs={{0,6},{1,7},{2,0},{3,1},{4,2},{5,3},{6,4},{7,5}} | collective-permute-start | bytes 98312 | tf_op jit(solution)/shard_map/ppermute | solution.py:72
  57.0 7.4 %collective-permute-start.4 = (bf16[256,64]{0,1:T(8,128)(2,1)S(1)}, bf16[256,64]{0,1:T(8,128)(2,1)S(1)}, u32[]{:S(2)}, u32[]{:S(2)}) collective-permute-start(bf16[256,64]{0,1:T(8,128)(2,1)S(1)} %get-tuple-element.28), channel_id=1, source_target_pairs={{0,4},{1,5},{2,6},{3,7},{4,0},{5,1},{6,2},{7,3}} | collective-permute-start | bytes 98312 | tf_op jit(solution)/shard_map/ppermute | solution.py:72
  58.9 8.3 %collective-permute-start.3 = (bf16[256,64]{0,1:T(8,128)(2,1)S(1)}, bf16[256,64]{0,1:T(8,128)(2,1)S(1)}, u32[]{:S(2)}, u32[]{:S(2)}) collective-permute-start(bf16[256,64]{0,1:T(8,128)(2,1)S(1)} %get-tuple-element.29), channel_id=1, source_target_pairs={{0,2},{1,3},{2,4},{3,5},{4,6},{5,7},{6,0},{7,1}} | collective-permute-start | bytes 98312 | tf_op jit(solution)/shard_map/ppermute | solution.py:72
  69.9 10.3 %all-to-all-start.1 = ((bf16[8,2,8192]{2,1,0:T(2,128)(2,1)}), bf16[8,2,8192]{2,1,0:T(2,128)(2,1)S(1)}, u32[]{:S(2)}, u32[]{:S(2)}) async-start(bf16[8,2,8192]{2,1,0:T(2,128)(2,1)} %reshape.685), calls=%async_computation.1 | async-start | bytes 524288 | tf_op jit(solution)/shard_map/all_to_all | solution.py:169
  104.9 1.2 copy-start.4
  105.2 1.7 copy-start
  106.9 8.1 %copy-start.12 = (s32[2,8]{1,0:T(2,128)S(1)}, s32[2,8]{1,0:T(2,128)}, u32[]{:S(2)}) copy-start(s32[2,8]{1,0:T(2,128)} %get-tuple-element.35) | copy-start | bytes 196
  111.6 10.3 %all-to-all-start.2 = ((bf16[8,2,8192]{2,1,0:T(2,128)(2,1)}), bf16[8,2,8192]{2,1,0:T(2,128)(2,1)S(1)}, u32[]{:S(2)}, u32[]{:S(2)}) async-start(bf16[8,2,8192]{2,1,0:T(2,128)(2,1)} %reshape.687), calls=%async_computation.2 | async-start | bytes 524288 | tf_op jit(solution)/shard_map/all_to_all | solution.py:169
  125.2 2.1 %copy-start.1 = (bf16[1024,1024]{1,0:T(8,128)(2,1)S(1)}, bf16[1024,1024]{1,0:T(8,128)(2,1)}, u32[]{:S(2)}) copy-start(bf16[1024,1024]{1,0:T(8,128)(2,1)} %copy-done) | copy-start | bytes 6291460
  127.3 9.9 %copy-start.11 = (s32[2,8]{1,0:T(2,128)S(1)}, s32[2,8]{1,0:T(2,128)}, u32[]{:S(2)}) copy-start(s32[2,8]{1,0:T(2,128)} %get-tuple-element.34) | copy-start | bytes 196
  133.6 10.3 %all-to-all-start.3 = ((bf16[8,2,8192]{2,1,0:T(2,128)(2,1)}), bf16[8,2,8192]{2,1,0:T(2,128)(2,1)S(1)}, u32[]{:S(2)}, u32[]{:S(2)}) async-start(bf16[8,2,8192]{2,1,0:T(2,128)(2,1)} %reshape.689), calls=%async_computation.3 | async-start | bytes 524288 | tf_op jit(solution)/shard_map/all_to_all | solution.py:169
  147.2 2.1 %copy-start.2 = (bf16[1024,1024]{1,0:T(8,128)(2,1)S(1)}, bf16[1024,1024]{1,0:T(8,128)(2,1)}, u32[]{:S(2)}) copy-start(bf16[1024,1024]{1,0:T(8,128)(2,1)} %copy-done) | copy-start | bytes 6291460
  149.3 6.3 %copy-start.10 = (s32[2,8]{1,0:T(2,128)S(1)}, s32[2,8]{1,0:T(2,128)}, u32[]{:S(2)}) copy-start(s32[2,8]{1,0:T(2,128)} %get-tuple-element.33) | copy-start | bytes 196
  152.2 10.3 %all-to-all-start.4 = ((bf16[8,2,8192]{2,1,0:T(2,128)(2,1)}), bf16[8,2,8192]{2,1,0:T(2,128)(2,1)S(1)}, u32[]{:S(2)}, u32[]{:S(2)}) async-start(bf16[8,2,8192]{2,1,0:T(2,128)(2,1)} %reshape.691), calls=%async_computation.4 | async-start | bytes 524288 | tf_op jit(solution)/shard_map/all_to_all | solution.py:169
  165.0 16.8 %copy-start.7 = (f32[256,256]{1,0:T(8,128)S(1)}, f32[256,256]{1,0:T(8,128)}, u32[]{:S(2)}) copy-start(f32[256,256]{1,0:T(8,128)} %get-tuple-element.38) | copy-start | bytes 786436
  165.0 15.6 %all-to-all-start.5 = ((bf16[4,768,64]{1,2,0:T(8,128)(2,1)}), bf16[4,768,64]{1,2,0:T(8,128)(2,1)S(1)}, u32[]{:S(2)}, u32[]{:S(2)}) async-start(bf16[4,768,64]{1,2,0:T(8,128)(2,1)} %pad_maximum_fusion.2), calls=%async_computation.5 | async-start | bytes 786432 | tf_op jit(solution)/shard_map/all_to_all | solution.py:184
Sparse Core Ops, SparseCore 0:
  9.8 92.5 all-gather.2

commit v24 on v17

--- a/solution.py
+++ b/solution.py
@@ -164,12 +164,13 @@
             updates = jnp.dot(
                 tiles_full, solved_now.astype(jnp.bfloat16), preferred_element_type=jnp.float32
             ).astype(jnp.bfloat16)
-        updates = updates.reshape(group_tiles + 1, block_rows, cols)
+        updates = updates.reshape(group_tiles + 1, block_rows // 2, 2 * cols)
         sending = jnp.take(updates, send_index, axis=0, mode="clip")
         incoming = lax.all_to_all(
             sending, ("lvl", "pcol"), split_axis=0, concat_axis=0, tiled=True
         )
-        incoming = incoming.reshape(n_lvl, n_pcol * slots, block_rows, cols)[section]
+        incoming = incoming.reshape(n_lvl, n_pcol * slots, block_rows // 2, 2 * cols)[section]
+        incoming = incoming.reshape(n_pcol * slots, block_rows, cols)
         acc = acc.at[recv_block[section]].add(incoming.astype(jnp.float32), mode="clip")
     outer = acc[window_blocks:NT].reshape(ABOVE, cols)
 

time: 191 us -> 182 us (0.953)
  local copies, waits for them, and re-layouts: 21.2 us -> 14.6 us
    unnamed x42 -> x34, local copies, waits for them, and re-layouts: 11.6 us -> 2.09 us
  transfers between devices with their start and end apart: 13 -> 13, of which waited for: 9 -> 9; matrix products, arithmetic and copies ran while one was open for 5% -> 6% of each run, Pallas kernels for 0% -> 0%
where the time goes in v24:
time: 182 us; the launch traced here: 181 us
  waiting for transfers between devices  76.4 us (42%)
  starting transfers between devices  52.2 us (29%)
  between operations  14.9 us (8%)
  local copies, waits for them, and re-layouts  14.6 us (8%)
  other arithmetic  14.1 us (8%)
  matrix products  8.73 us (5%)
    ppermute x6, starting transfers between devices, level0_shift(): return lax.ppermute(x, all_axes, pairs)  30.8 us
    all_to_all x4, waiting for transfers between devices, per_device(): lax.all_to_all(sending, ('lvl', 'pcol'), split_axis=0, concat_axis=0, til...  26.5 us
    all_gather x1, waiting for transfers between devices, per_device(): gathered = lax.all_gather(raw, 'prow', axis=0)  21 us
    all_to_all x4, starting transfers between devices, per_device(): lax.all_to_all(sending, ('lvl', 'pcol'), split_axis=0, concat_axis=0, til...  13.7 us
    all_to_all x1, waiting for transfers between devices, per_device(): lax.all_to_all(jnp.broadcast_to(meta[None], (devices,) + meta.shape), ('l...  12.4 us
    all_to_all x1, waiting for transfers between devices, per_device(): lax.all_to_all(final, 'prow', split_axis=0, concat_axis=0, tiled=True)  11 us
    gather x4, local copies, waits for them, and re-layouts, per_device(): sending = jnp.take(updates, send_index, axis=0, mode='clip')  5.65 us
    ppermute x6, waiting for transfers between devices, level0_shift(): return lax.ppermute(x, all_axes, pairs)  5.61 us
  transfers between devices with their start and end apart: 13, of which 9 were waited for; matrix products, arithmetic and copies ran while one was open for 6% of the time, Pallas kernels for 0%

profile of v24, /device:TPU:0, one launch (start us, length us, event | category | flops | bytes accessed | tf_op | source)
XLA Modules:
  0.0 181.0 jit_solution(6313202391304462084)
XLA Ops:
  7.3 2.3 %pad_maximum_fusion = bf16[512,1024]{1,0:T(8,128)(2,1)} fusion(bf16[256,1024]{1,0:T(8,128)(2,1)} %bitcast.113, bf16[256,1024]{1,0:T(8,128)(2,1)} %bitcast.109), kind=kLoop, calls=%fused_computation.19 | loop fusion | flops 2097152 | bytes 2097152 | tf_op jit(solution)/shard_map/concatenate | solution.py:53
  9.9 1.1 fusion.53
  10.9 6.9 %collective-permute-start.2 = (bf16[256,256]{1,0:T(8,128)(2,1)S(1)}, bf16[256,256]{1,0:T(8,128)(2,1)S(1)}, u32[]{:S(2)}, u32[]{:S(2)}) collective-permute-start(bf16[256,256]{1,0:T(8,128)(2,1)S(1)} %get-tuple-element.37), channel_id=1, source_target_pairs={{0,6},{1,7},{2,0},{3,1},{4,2},{5,3},{6,4},{7,5}} | collective-permute-start | bytes 393224 | tf_op jit(solution)/shard_map/ppermute | solution.py:72
  17.9 1.9 %collective-permute-start.1 = (bf16[256,256]{1,0:T(8,128)(2,1)S(1)}, bf16[256,256]{1,0:T(8,128)(2,1)S(1)}, u32[]{:S(2)}, u32[]{:S(2)}) collective-permute-start(bf16[256,256]{1,0:T(8,128)(2,1)S(1)} %get-tuple-element.37), channel_id=1, source_target_pairs={{0,4},{1,5},{2,6},{3,7},{4,0},{5,1},{6,2},{7,3}} | collective-permute-start | bytes 393224 | tf_op jit(solution)/shard_map/ppermute | solution.py:72
  19.8 2.9 %collective-permute-start = (bf16[256,256]{1,0:T(8,128)(2,1)S(1)}, bf16[256,256]{1,0:T(8,128)(2,1)S(1)}, u32[]{:S(2)}, u32[]{:S(2)}) collective-permute-start(bf16[256,256]{1,0:T(8,128)(2,1)S(1)} %get-tuple-element.37), channel_id=1, source_target_pairs={{0,2},{1,3},{2,4},{3,5},{4,6},{5,7},{6,0},{7,1}} | collective-permute-start | bytes 393224 | tf_op jit(solution)/shard_map/ppermute | solution.py:72
  22.8 0.6 broadcast_in_dim.180
  23.4 3.2 %all-to-all-start = ((s32[32,3,8]{2,1,0:T(4,128)}), s32[32,3,8]{2,1,0:T(4,128)S(1)}, u32[]{:S(2)}, u32[]{:S(2)}) async-start(s32[32,3,8]{2,1,0:T(4,128)} %broadcast_in_dim.180), calls=%async_computation | async-start | bytes 131072 | tf_op jit(solution)/shard_map/all_to_all | solution.py:104
  26.7 0.2 select_reduce_fusion.5
  27.2 12.4 %all-to-all-done = s32[32,3,8]{2,1,0:T(4,128)S(1)} async-done(((s32[32,3,8]{2,1,0:T(4,128)}), s32[32,3,8]{2,1,0:T(4,128)S(1)}, u32[]{:S(2)}, u32[]{:S(2)}) %all-to-all-start) | async-done | bytes 3104 | tf_op jit(solution)/shard_map/all_to_all | solution.py:104
  39.8 0.3 convert_reduce_fusion
  40.1 0.2 fusion.24
  40.3 0.2 select_reduce_fusion
  40.6 0.6 fusion.52
  41.7 0.6 gather_fusion
  42.3 0.4 convolution_convert_fusion.3
  42.7 14.4 %collective-permute-start.5 = (bf16[256,64]{0,1:T(8,128)(2,1)S(1)}, bf16[256,64]{0,1:T(8,128)(2,1)S(1)}, u32[]{:S(2)}, u32[]{:S(2)}) collective-permute-start(bf16[256,64]{0,1:T(8,128)(2,1)S(1)} %get-tuple-element.27), channel_id=1, source_target_pairs={{0,6},{1,7},{2,0},{3,1},{4,2},{5,3},{6,4},{7,5}} | collective-permute-start | bytes 98312 | tf_op jit(solution)/shard_map/ppermute | solution.py:72
  57.0 1.9 %collective-permute-start.4 = (bf16[256,64]{0,1:T(8,128)(2,1)S(1)}, bf16[256,64]{0,1:T(8,128)(2,1)S(1)}, u32[]{:S(2)}, u32[]{:S(2)}) collective-permute-start(bf16[256,64]{0,1:T(8,128)(2,1)S(1)} %get-tuple-element.28), channel_id=1, source_target_pairs={{0,4},{1,5},{2,6},{3,7},{4,0},{5,1},{6,2},{7,3}} | collective-permute-start | bytes 98312 | tf_op jit(solution)/shard_map/ppermute | solution.py:72
  58.9 2.7 %collective-permute-start.3 = (bf16[256,64]{0,1:T(8,128)(2,1)S(1)}, bf16[256,64]{0,1:T(8,128)(2,1)S(1)}, u32[]{:S(2)}, u32[]{:S(2)}) collective-permute-start(bf16[256,64]{0,1:T(8,128)(2,1)S(1)} %get-tuple-element.29), channel_id=1, source_target_pairs={{0,2},{1,3},{2,4},{3,5},{4,6},{5,7},{6,0},{7,1}} | collective-permute-start | bytes 98312 | tf_op jit(solution)/shard_map/ppermute | solution.py:72
  61.7 2.8 %collective-permute-done.4 = bf16[256,64]{0,1:T(8,128)(2,1)S(1)} collective-permute-done((bf16[256,64]{0,1:T(8,128)(2,1)S(1)}, bf16[256,64]{0,1:T(8,128)(2,1)S(1)}, u32[]{:S(2)}, u32[]{:S(2)}) %collective-permute-start.4) | collective-permute-done | bytes 32800 | tf_op jit(solution)/shard_map/ppermute | solution.py:72
  64.4 2.8 %collective-permute-done.3 = bf16[256,64]{0,1:T(8,128)(2,1)S(1)} collective-permute-done((bf16[256,64]{0,1:T(8,128)(2,1)S(1)}, bf16[256,64]{0,1:T(8,128)(2,1)S(1)}, u32[]{:S(2)}, u32[]{:S(2)}) %collective-permute-start.3) | collective-permute-done | bytes 32800 | tf_op jit(solution)/shard_map/ppermute | solution.py:72
  67.3 0.6 gather_fusion.1
  67.9 0.2 copy.71
  68.1 0.1 reshape.551
  68.3 1.3 gather_fusion.2
  69.6 3.4 %all-to-all-start.1 = ((bf16[64,16,128]{2,1,0:T(8,128)(2,1)}), bf16[64,16,128]{2,1,0:T(8,128)(2,1)S(1)}, u32[]{:S(2)}, u32[]{:S(2)}) async-start(bf16[64,16,128]{2,1,0:T(8,128)(2,1)} %gather_fusion.2), calls=%async_computation.1 | async-start | bytes 524288 | tf_op jit(solution)/shard_map/all_to_all | solution.py:169
  73.2 6.7 %all-to-all-done.1 = bf16[64,16,128]{2,1,0:T(8,128)(2,1)S(1)} async-done(((bf16[64,16,128]{2,1,0:T(8,128)(2,1)}), bf16[64,16,128]{2,1,0:T(8,128)(2,1)S(1)}, u32[]{:S(2)}, u32[]{:S(2)}) %all-to-all-start.1) | async-done | bytes 262176 | tf_op jit(solution)/shard_map/all_to_all | solution.py:169
  79.9 0.1 reshape.672
  80.1 1.2 scatter_fusion
  81.4 21.0 %all-gather.3.cloned.1.call-done = bf16[2048,1024]{1,0:T(8,128)(2,1)} async-done(((bf16[512,1024]{1,0:T(8,128)(2,1)}), bf16[2048,1024]{1,0:T(8,128)(2,1)}) %all-gather.3.cloned.1.call-update) | async-done | bytes 4194320 | tf_op jit(solution)/shard_map/all_gather | solution.py:56
  102.3 2.5 %compare_select_fusion = (bf16[4,256,1024]{2,1,0:T(8,128)(2,1)S(1)}, bf16[4,256,1024]{2,1,0:T(8,128)(2,1)S(1)}) fusion(bf16[4,512,1024]{2,1,0:T(8,128)(2,1)} %bitcast.107, s32[1024]{0:T(1024)S(1)} %select_reduce_fusion.1, s32[4,256]{1,0:T(4,128)S(1)} %eq.225), kind=kLoop, calls=%fused_computation.11 | loop fusion | flops 2097152 | bytes 8396800 | tf_op jit(solution)/shard_map/jit(_where)/select_n | solution.py:58
  104.9 0.3 bitcast_select_fusion
  105.2 0.9 copy-done.4
  106.1 0.8 fusion.11
  106.9 0.8 convolution_convert_fusion.2
  107.8 0.2 copy.63
  107.9 0.2 reshape.554
  108.1 1.4 gather_fusion.3
  109.6 3.4 %all-to-all-start.2 = ((bf16[64,16,128]{2,1,0:T(8,128)(2,1)}), bf16[64,16,128]{2,1,0:T(8,128)(2,1)S(1)}, u32[]{:S(2)}, u32[]{:S(2)}) async-start(bf16[64,16,128]{2,1,0:T(8,128)(2,1)} %gather_fusion.3), calls=%async_computation.2 | async-start | bytes 524288 | tf_op jit(solution)/shard_map/all_to_all | solution.py:169
  113.1 6.8 %all-to-all-done.2 = bf16[64,16,128]{2,1,0:T(8,128)(2,1)S(1)} async-done(((bf16[64,16,128]{2,1,0:T(8,128)(2,1)}), bf16[64,16,128]{2,1,0:T(8,128)(2,1)S(1)}, u32[]{:S(2)}, u32[]{:S(2)}) %all-to-all-start.2) | async-done | bytes 262176 | tf_op jit(solution)/shard_map/all_to_all | solution.py:169
  119.9 0.1 reshape.680
  120.0 1.2 scatter_fusion.1
  121.2 2.0 %fusion.14 = bf16[1024,64]{0,1:T(8,128)(2,1)S(1)} fusion(bf16[1024,1024]{1,0:T(8,128)(2,1)S(1)} %bitcast.105, f32[1,1,1024,64]{3,2,1,0:T(8,128)S(1)} %bitcast.115, f32[1,1,1024,256]{3,2,1,0:T(8,128)} %param.9, s32[]{:T(128)S(6)} %select_n.246), kind=kOutput, calls=%fused_computation.36 | convolution fusion | flops 134348800 | bytes 3014660 | tf_op jit(solution)/shard_map/dot_general | solution.py:160
  123.3 0.8 convolution_convert_fusion.1
  124.1 0.9 copy.64
  125.0 1.1 reshape.556
  126.1 1.4 gather_fusion.4
  127.5 3.4 %all-to-all-start.3 = ((bf16[64,16,128]{2,1,0:T(8,128)(2,1)}), bf16[64,16,128]{2,1,0:T(8,128)(2,1)S(1)}, u32[]{:S(2)}, u32[]{:S(2)}) async-start(bf16[64,16,128]{2,1,0:T(8,128)(2,1)} %gather_fusion.4), calls=%async_computation.3 | async-start | bytes 524288 | tf_op jit(solution)/shard_map/all_to_all | solution.py:169
  131.1 0.5 fusion.44
  131.6 6.3 %all-to-all-done.3 = bf16[64,16,128]{2,1,0:T(8,128)(2,1)S(1)} async-done(((bf16[64,16,128]{2,1,0:T(8,128)(2,1)}), bf16[64,16,128]{2,1,0:T(8,128)(2,1)S(1)}, u32[]{:S(2)}, u32[]{:S(2)}) %all-to-all-start.3) | async-done | bytes 262176 | tf_op jit(solution)/shard_map/all_to_all | solution.py:169
  138.0 1.3 scatter_fusion.2
  139.3 2.0 %select_convert_fusion = (bf16[1024,64]{0,1:T(8,128)(2,1)S(1)}, bf16[1024,64]{0,1:T(8,128)(2,1)S(1)}) fusion(bf16[1024,64]{0,1:T(8,128)(2,1)S(1)} %fusion.14, bf16[1024,64]{0,1:T(8,128)(2,1)S(1)} %fusion.11, pred[]{:T(512)S(6)} %eq.257, pred[]{:T(512)S(6)} %eq.256, pred[]{:T(512)S(6)} %eq.224, bf16[1024,1024]{1,0:T(8,128)(2,1)S(1)} %bitcast.106, ...), kind=kOutput, calls=%fused_computation.41 | convolution fusion | flops 134545408 | bytes 3407879 | tf_op jit(solution)/shard_map/dot_general | solution.py:160
  141.4 0.8 convolution_convert_fusion
  142.2 0.2 copy.65
  142.4 0.2 reshape.558
  142.6 1.4 gather_fusion.5
  144.0 3.4 %all-to-all-start.4 = ((bf16[64,16,128]{2,1,0:T(8,128)(2,1)}), bf16[64,16,128]{2,1,0:T(8,128)(2,1)S(1)}, u32[]{:S(2)}, u32[]{:S(2)}) async-start(bf16[64,16,128]{2,1,0:T(8,128)(2,1)} %gather_fusion.5), calls=%async_computation.4 | async-start | bytes 524288 | tf_op jit(solution)/shard_map/all_to_all | solution.py:169
  147.5 6.8 %all-to-all-done.4 = bf16[64,16,128]{2,1,0:T(8,128)(2,1)S(1)} async-done(((bf16[64,16,128]{2,1,0:T(8,128)(2,1)}), bf16[64,16,128]{2,1,0:T(8,128)(2,1)S(1)}, u32[]{:S(2)}, u32[]{:S(2)}) %all-to-all-start.4) | async-done | bytes 262176 | tf_op jit(solution)/shard_map/all_to_all | solution.py:169
  154.4 1.2 scatter_fusion.3
  155.8 0.8 pad_maximum_fusion.2
  156.6 4.6 %all-to-all-start.5 = ((bf16[4,768,64]{1,2,0:T(8,128)(2,1)}), bf16[4,768,64]{1,2,0:T(8,128)(2,1)S(1)}, u32[]{:S(2)}, u32[]{:S(2)}) async-start(bf16[4,768,64]{1,2,0:T(8,128)(2,1)} %pad_maximum_fusion.2), calls=%async_computation.5 | async-start | bytes 786432 | tf_op jit(solution)/shard_map/all_to_all | solution.py:185
  161.2 11.0 %all-to-all-done.5 = bf16[4,768,64]{1,2,0:T(8,128)(2,1)S(1)} async-done(((bf16[4,768,64]{1,2,0:T(8,128)(2,1)}), bf16[4,768,64]{1,2,0:T(8,128)(2,1)S(1)}, u32[]{:S(2)}, u32[]{:S(2)}) %all-to-all-start.5) | async-done | bytes 393248 | tf_op jit(solution)/shard_map/all_to_all | solution.py:185
  172.2 0.1 copy.68
  172.4 1.0 copy.69
  173.4 0.7 select_bitcast_fusion
  (97 shorter events, 2.4 us)
Async XLA Ops:
  7.2 2.7 %copy-start.5 = (bf16[1,1,256,1024]{3,2,1,0:T(8,128)(2,1)S(1)}, bf16[1,1,256,1024]{3,2,1,0:T(8,128)(2,1)}, u32[]{:S(2)}) copy-start(bf16[1,1,256,1024]{3,2,1,0:T(8,128)(2,1)} %param.10) | copy-start | bytes 1572868
  7.2 2.5 %copy-start.9 = (s32[1,1,8]{2,1,0:T(1,128)S(1)}, s32[1,1,8]{2,1,0:T(1,128)}, u32[]{:S(2)}) copy-start(s32[1,1,8]{2,1,0:T(1,128)} %param.12) | copy-start | bytes 100
  7.2 2.7 %copy-start.3 = (f32[1,1,1024,256]{3,2,1,0:T(8,128)S(1)}, f32[1,1,1024,256]{3,2,1,0:T(8,128)}, u32[]{:S(2)}) copy-start(f32[1,1,1024,256]{3,2,1,0:T(8,128)} %param.9) | copy-start | bytes 3145732
  7.2 95.1 %all-gather.3.cloned.1.call-start = ((), (), s32[]{:S(2)}) async-start(), calls=%async_computation.6 | async-start | bytes 5242880 | tf_op jit(solution)/shard_map/all_gather | solution.py:56
  7.2 15.5 %copy-start.13 = (s32[1,1,8]{2,1,0:T(1,128)S(1)}, s32[1,1,8]{2,1,0:T(1,128)}, u32[]{:S(2)}) copy-start(s32[1,1,8]{2,1,0:T(1,128)} %param.14) | copy-start | bytes 100
  7.3 15.5 %copy-start.14 = (s32[1,1,8]{2,1,0:T(1,128)S(1)}, s32[1,1,8]{2,1,0:T(1,128)}, u32[]{:S(2)}) copy-start(s32[1,1,8]{2,1,0:T(1,128)} %param.13) | copy-start | bytes 100
  7.3 15.5 %copy-start.15 = (s32[1,1,8]{2,1,0:T(1,128)S(1)}, s32[1,1,8]{2,1,0:T(1,128)}, u32[]{:S(2)}) copy-start(s32[1,1,8]{2,1,0:T(1,128)} %param.15) | copy-start | bytes 100
  9.6 17.4 %copy-start.6 = (bf16[1,1,8,32,1024]{4,3,2,1,0:T(8,128)(2,1)S(1)}, bf16[1,1,8,32,1024]{4,3,2,1,0:T(8,128)(2,1)}, u32[]{:S(2)}) copy-start(bf16[1,1,8,32,1024]{4,3,2,1,0:T(8,128)(2,1)} %param.11) | copy-start | bytes 1572868
  10.9 30.6 %collective-permute-start.2 = (bf16[256,256]{1,0:T(8,128)(2,1)S(1)}, bf16[256,256]{1,0:T(8,128)(2,1)S(1)}, u32[]{:S(2)}, u32[]{:S(2)}) collective-permute-start(bf16[256,256]{1,0:T(8,128)(2,1)S(1)} %get-tuple-element.37), channel_id=1, source_target_pairs={{0,6},{1,7},{2,0},{3,1},{4,2},{5,3},{6,4},{7,5}} | collective-permute-start | bytes 393224 | tf_op jit(solution)/shard_map/ppermute | solution.py:72
  17.9 23.7 %collective-permute-start.1 = (bf16[256,256]{1,0:T(8,128)(2,1)S(1)}, bf16[256,256]{1,0:T(8,128)(2,1)S(1)}, u32[]{:S(2)}, u32[]{:S(2)}) collective-permute-start(bf16[256,256]{1,0:T(8,128)(2,1)S(1)} %get-tuple-element.37), channel_id=1, source_target_pairs={{0,4},{1,5},{2,6},{3,7},{4,0},{5,1},{6,2},{7,3}} | collective-permute-start | bytes 393224 | tf_op jit(solution)/shard_map/ppermute | solution.py:72
  19.8 21.8 %collective-permute-start = (bf16[256,256]{1,0:T(8,128)(2,1)S(1)}, bf16[256,256]{1,0:T(8,128)(2,1)S(1)}, u32[]{:S(2)}, u32[]{:S(2)}) collective-permute-start(bf16[256,256]{1,0:T(8,128)(2,1)S(1)} %get-tuple-element.37), channel_id=1, source_target_pairs={{0,2},{1,3},{2,4},{3,5},{4,6},{5,7},{6,0},{7,1}} | collective-permute-start | bytes 393224 | tf_op jit(solution)/shard_map/ppermute | solution.py:72
  23.4 16.1 %all-to-all-start = ((s32[32,3,8]{2,1,0:T(4,128)}), s32[32,3,8]{2,1,0:T(4,128)S(1)}, u32[]{:S(2)}, u32[]{:S(2)}) async-start(s32[32,3,8]{2,1,0:T(4,128)} %broadcast_in_dim.180), calls=%async_computation | async-start | bytes 131072 | tf_op jit(solution)/shard_map/all_to_all | solution.py:104
  41.6 26.7 %copy-start.8 = (s32[1024]{0:T(1024)}, s32[1024]{0:T(1024)S(1)}, u32[]{:S(2)}) copy-start(s32[1024]{0:T(1024)S(1)} %pad_clamp_fusion) | copy-start | bytes 12292
  42.7 19.0 %collective-permute-start.5 = (bf16[256,64]{0,1:T(8,128)(2,1)S(1)}, bf16[256,64]{0,1:T(8,128)(2,1)S(1)}, u32[]{:S(2)}, u32[]{:S(2)}) collective-permute-start(bf16[256,64]{0,1:T(8,128)(2,1)S(1)} %get-tuple-element.27), channel_id=1, source_target_pairs={{0,6},{1,7},{2,0},{3,1},{4,2},{5,3},{6,4},{7,5}} | collective-permute-start | bytes 98312 | tf_op jit(solution)/shard_map/ppermute | solution.py:72
  57.0 7.4 %collective-permute-start.4 = (bf16[256,64]{0,1:T(8,128)(2,1)S(1)}, bf16[256,64]{0,1:T(8,128)(2,1)S(1)}, u32[]{:S(2)}, u32[]{:S(2)}) collective-permute-start(bf16[256,64]{0,1:T(8,128)(2,1)S(1)} %get-tuple-element.28), channel_id=1, source_target_pairs={{0,4},{1,5},{2,6},{3,7},{4,0},{5,1},{6,2},{7,3}} | collective-permute-start | bytes 98312 | tf_op jit(solution)/shard_map/ppermute | solution.py:72
  58.9 8.3 %collective-permute-start.3 = (bf16[256,64]{0,1:T(8,128)(2,1)S(1)}, bf16[256,64]{0,1:T(8,128)(2,1)S(1)}, u32[]{:S(2)}, u32[]{:S(2)}) collective-permute-start(bf16[256,64]{0,1:T(8,128)(2,1)S(1)} %get-tuple-element.29), channel_id=1, source_target_pairs={{0,2},{1,3},{2,4},{3,5},{4,6},{5,7},{6,0},{7,1}} | collective-permute-start | bytes 98312 | tf_op jit(solution)/shard_map/ppermute | solution.py:72
  69.6 10.3 %all-to-all-start.1 = ((bf16[64,16,128]{2,1,0:T(8,128)(2,1)}), bf16[64,16,128]{2,1,0:T(8,128)(2,1)S(1)}, u32[]{:S(2)}, u32[]{:S(2)}) async-start(bf16[64,16,128]{2,1,0:T(8,128)(2,1)} %gather_fusion.2), calls=%async_computation.1 | async-start | bytes 524288 | tf_op jit(solution)/shard_map/all_to_all | solution.py:169
  104.9 1.2 copy-start.4
  105.2 1.7 copy-start
  106.9 6.0 %copy-start.12 = (s32[2,8]{1,0:T(2,128)S(1)}, s32[2,8]{1,0:T(2,128)}, u32[]{:S(2)}) copy-start(s32[2,8]{1,0:T(2,128)} %get-tuple-element.35) | copy-start | bytes 196
  109.6 10.3 %all-to-all-start.2 = ((bf16[64,16,128]{2,1,0:T(8,128)(2,1)}), bf16[64,16,128]{2,1,0:T(8,128)(2,1)S(1)}, u32[]{:S(2)}, u32[]{:S(2)}) async-start(bf16[64,16,128]{2,1,0:T(8,128)(2,1)} %gather_fusion.3), calls=%async_computation.2 | async-start | bytes 524288 | tf_op jit(solution)/shard_map/all_to_all | solution.py:169
  121.2 2.1 %copy-start.1 = (bf16[1024,1024]{1,0:T(8,128)(2,1)S(1)}, bf16[1024,1024]{1,0:T(8,128)(2,1)}, u32[]{:S(2)}) copy-start(bf16[1024,1024]{1,0:T(8,128)(2,1)} %copy-done) | copy-start | bytes 6291460
  123.3 7.7 %copy-start.11 = (s32[2,8]{1,0:T(2,128)S(1)}, s32[2,8]{1,0:T(2,128)}, u32[]{:S(2)}) copy-start(s32[2,8]{1,0:T(2,128)} %get-tuple-element.34) | copy-start | bytes 196
  127.5 10.3 %all-to-all-start.3 = ((bf16[64,16,128]{2,1,0:T(8,128)(2,1)}), bf16[64,16,128]{2,1,0:T(8,128)(2,1)S(1)}, u32[]{:S(2)}, u32[]{:S(2)}) async-start(bf16[64,16,128]{2,1,0:T(8,128)(2,1)} %gather_fusion.4), calls=%async_computation.3 | async-start | bytes 524288 | tf_op jit(solution)/shard_map/all_to_all | solution.py:169
  139.3 2.1 %copy-start.2 = (bf16[1024,1024]{1,0:T(8,128)(2,1)S(1)}, bf16[1024,1024]{1,0:T(8,128)(2,1)}, u32[]{:S(2)}) copy-start(bf16[1024,1024]{1,0:T(8,128)(2,1)} %copy-done) | copy-start | bytes 6291460
  141.4 6.0 %copy-start.10 = (s32[2,8]{1,0:T(2,128)S(1)}, s32[2,8]{1,0:T(2,128)}, u32[]{:S(2)}) copy-start(s32[2,8]{1,0:T(2,128)} %get-tuple-element.33) | copy-start | bytes 196
  144.0 10.3 %all-to-all-start.4 = ((bf16[64,16,128]{2,1,0:T(8,128)(2,1)}), bf16[64,16,128]{2,1,0:T(8,128)(2,1)S(1)}, u32[]{:S(2)}, u32[]{:S(2)}) async-start(bf16[64,16,128]{2,1,0:T(8,128)(2,1)} %gather_fusion.5), calls=%async_computation.4 | async-start | bytes 524288 | tf_op jit(solution)/shard_map/all_to_all | solution.py:169
  156.6 16.8 %copy-start.7 = (f32[256,256]{1,0:T(8,128)S(1)}, f32[256,256]{1,0:T(8,128)}, u32[]{:S(2)}) copy-start(f32[256,256]{1,0:T(8,128)} %get-tuple-element.38) | copy-start | bytes 786436
  156.6 15.6 %all-to-all-start.5 = ((bf16[4,768,64]{1,2,0:T(8,128)(2,1)}), bf16[4,768,64]{1,2,0:T(8,128)(2,1)S(1)}, u32[]{:S(2)}, u32[]{:S(2)}) async-start(bf16[4,768,64]{1,2,0:T(8,128)(2,1)} %pad_maximum_fusion.2), calls=%async_computation.5 | async-start | bytes 786432 | tf_op jit(solution)/shard_map/all_to_all | solution.py:185
Sparse Core Ops, SparseCore 0:
  9.8 92.5 all-gather.2

commit v25 on v24

--- a/solution.py
+++ b/solution.py
@@ -182,7 +182,14 @@
         ],
         axis=1,
     )
-    final = lax.all_to_all(final, "prow", split_axis=0, concat_axis=0, tiled=True)
+    final_shape = final.shape
+    final = lax.all_to_all(
+        final.reshape(n_prow, final_shape[1] // 2, 2 * cols),
+        "prow",
+        split_axis=0,
+        concat_axis=0,
+        tiled=True,
+    ).reshape(final_shape)
     final = final.astype(jnp.float32)
     solution_rows = jnp.transpose(final[:, :rows_out], (1, 0, 2)).reshape(rows_out, columns_all)
     solution_rows = jnp.where(level_index == 0, first_rows, solution_rows)

time: 182 us -> 183 us (level)
  local copies, waits for them, and re-layouts: 14.6 us -> 16.6 us
where the time goes in v25:
time: 183 us; the launch traced here: 182 us
  waiting for transfers between devices  76.1 us (42%)
  starting transfers between devices  52.3 us (29%)
  local copies, waits for them, and re-layouts  16.6 us (9%)
  between operations  14.9 us (8%)
  other arithmetic  13.5 us (7%)
  matrix products  8.73 us (5%)
    ppermute x6, starting transfers between devices, level0_shift(): return lax.ppermute(x, all_axes, pairs)  30.7 us
    all_to_all x4, waiting for transfers between devices, per_device(): lax.all_to_all(sending, ('lvl', 'pcol'), split_axis=0, concat_axis=0, til...  26.1 us
    all_gather x1, waiting for transfers between devices, per_device(): gathered = lax.all_gather(raw, 'prow', axis=0)  21 us
    all_to_all x4, starting transfers between devices, per_device(): lax.all_to_all(sending, ('lvl', 'pcol'), split_axis=0, concat_axis=0, til...  13.8 us
    all_to_all x1, waiting for transfers between devices, per_device(): lax.all_to_all(jnp.broadcast_to(meta[None], (devices,) + meta.shape), ('l...  12.4 us
    all_to_all x1, waiting for transfers between devices, per_device(): lax.all_to_all(final.reshape(n_prow, final_shape[1] // 2, 2 * cols), 'pro...  11 us
    gather x4, local copies, waits for them, and re-layouts, per_device(): sending = jnp.take(updates, send_index, axis=0, mode='clip')  5.65 us
    ppermute x6, waiting for transfers between devices, level0_shift(): return lax.ppermute(x, all_axes, pairs)  5.61 us
  transfers between devices with their start and end apart: 13, of which 9 were waited for; matrix products, arithmetic and copies ran while one was open for 6% of the time, Pallas kernels for 0%

profile of v25, /device:TPU:0, one launch (start us, length us, event | category | flops | bytes accessed | tf_op | source)
XLA Modules:
  0.0 182.1 jit_solution(1387624422002047742)
XLA Ops:
  7.3 2.3 %pad_maximum_fusion = bf16[512,1024]{1,0:T(8,128)(2,1)} fusion(bf16[256,1024]{1,0:T(8,128)(2,1)} %bitcast.110, bf16[256,1024]{1,0:T(8,128)(2,1)} %bitcast.107), kind=kLoop, calls=%fused_computation.20 | loop fusion | flops 2097152 | bytes 2097152 | tf_op jit(solution)/shard_map/concatenate | solution.py:53
  9.9 1.1 fusion.53
  10.9 6.9 %collective-permute-start.2 = (bf16[256,256]{1,0:T(8,128)(2,1)S(1)}, bf16[256,256]{1,0:T(8,128)(2,1)S(1)}, u32[]{:S(2)}, u32[]{:S(2)}) collective-permute-start(bf16[256,256]{1,0:T(8,128)(2,1)S(1)} %get-tuple-element.37), channel_id=1, source_target_pairs={{0,6},{1,7},{2,0},{3,1},{4,2},{5,3},{6,4},{7,5}} | collective-permute-start | bytes 393224 | tf_op jit(solution)/shard_map/ppermute | solution.py:72
  17.9 1.9 %collective-permute-start.1 = (bf16[256,256]{1,0:T(8,128)(2,1)S(1)}, bf16[256,256]{1,0:T(8,128)(2,1)S(1)}, u32[]{:S(2)}, u32[]{:S(2)}) collective-permute-start(bf16[256,256]{1,0:T(8,128)(2,1)S(1)} %get-tuple-element.37), channel_id=1, source_target_pairs={{0,4},{1,5},{2,6},{3,7},{4,0},{5,1},{6,2},{7,3}} | collective-permute-start | bytes 393224 | tf_op jit(solution)/shard_map/ppermute | solution.py:72
  19.8 2.9 %collective-permute-start = (bf16[256,256]{1,0:T(8,128)(2,1)S(1)}, bf16[256,256]{1,0:T(8,128)(2,1)S(1)}, u32[]{:S(2)}, u32[]{:S(2)}) collective-permute-start(bf16[256,256]{1,0:T(8,128)(2,1)S(1)} %get-tuple-element.37), channel_id=1, source_target_pairs={{0,2},{1,3},{2,4},{3,5},{4,6},{5,7},{6,0},{7,1}} | collective-permute-start | bytes 393224 | tf_op jit(solution)/shard_map/ppermute | solution.py:72
  22.8 0.6 broadcast_in_dim.180
  23.4 3.2 %all-to-all-start = ((s32[32,3,8]{2,1,0:T(4,128)}), s32[32,3,8]{2,1,0:T(4,128)S(1)}, u32[]{:S(2)}, u32[]{:S(2)}) async-start(s32[32,3,8]{2,1,0:T(4,128)} %broadcast_in_dim.180), calls=%async_computation | async-start | bytes 131072 | tf_op jit(solution)/shard_map/all_to_all | solution.py:104
  26.7 0.2 select_reduce_fusion.5
  27.2 12.4 %all-to-all-done = s32[32,3,8]{2,1,0:T(4,128)S(1)} async-done(((s32[32,3,8]{2,1,0:T(4,128)}), s32[32,3,8]{2,1,0:T(4,128)S(1)}, u32[]{:S(2)}, u32[]{:S(2)}) %all-to-all-start) | async-done | bytes 3104 | tf_op jit(solution)/shard_map/all_to_all | solution.py:104
  39.8 0.3 convert_reduce_fusion
  40.1 0.2 fusion.24
  40.3 0.2 select_reduce_fusion
  40.6 0.6 fusion.52
  41.7 0.6 gather_fusion
  42.3 0.4 convolution_convert_fusion.3
  42.7 14.3 %collective-permute-start.5 = (bf16[256,64]{0,1:T(8,128)(2,1)S(1)}, bf16[256,64]{0,1:T(8,128)(2,1)S(1)}, u32[]{:S(2)}, u32[]{:S(2)}) collective-permute-start(bf16[256,64]{0,1:T(8,128)(2,1)S(1)} %get-tuple-element.27), channel_id=1, source_target_pairs={{0,6},{1,7},{2,0},{3,1},{4,2},{5,3},{6,4},{7,5}} | collective-permute-start | bytes 98312 | tf_op jit(solution)/shard_map/ppermute | solution.py:72
  57.0 1.9 %collective-permute-start.4 = (bf16[256,64]{0,1:T(8,128)(2,1)S(1)}, bf16[256,64]{0,1:T(8,128)(2,1)S(1)}, u32[]{:S(2)}, u32[]{:S(2)}) collective-permute-start(bf16[256,64]{0,1:T(8,128)(2,1)S(1)} %get-tuple-element.28), channel_id=1, source_target_pairs={{0,4},{1,5},{2,6},{3,7},{4,0},{5,1},{6,2},{7,3}} | collective-permute-start | bytes 98312 | tf_op jit(solution)/shard_map/ppermute | solution.py:72
  58.9 2.7 %collective-permute-start.3 = (bf16[256,64]{0,1:T(8,128)(2,1)S(1)}, bf16[256,64]{0,1:T(8,128)(2,1)S(1)}, u32[]{:S(2)}, u32[]{:S(2)}) collective-permute-start(bf16[256,64]{0,1:T(8,128)(2,1)S(1)} %get-tuple-element.29), channel_id=1, source_target_pairs={{0,2},{1,3},{2,4},{3,5},{4,6},{5,7},{6,0},{7,1}} | collective-permute-start | bytes 98312 | tf_op jit(solution)/shard_map/ppermute | solution.py:72
  61.7 2.8 %collective-permute-done.4 = bf16[256,64]{0,1:T(8,128)(2,1)S(1)} collective-permute-done((bf16[256,64]{0,1:T(8,128)(2,1)S(1)}, bf16[256,64]{0,1:T(8,128)(2,1)S(1)}, u32[]{:S(2)}, u32[]{:S(2)}) %collective-permute-start.4) | collective-permute-done | bytes 32800 | tf_op jit(solution)/shard_map/ppermute | solution.py:72
  64.4 2.8 %collective-permute-done.3 = bf16[256,64]{0,1:T(8,128)(2,1)S(1)} collective-permute-done((bf16[256,64]{0,1:T(8,128)(2,1)S(1)}, bf16[256,64]{0,1:T(8,128)(2,1)S(1)}, u32[]{:S(2)}, u32[]{:S(2)}) %collective-permute-start.3) | collective-permute-done | bytes 32800 | tf_op jit(solution)/shard_map/ppermute | solution.py:72
  67.3 0.6 gather_fusion.1
  67.9 0.2 copy.77
  68.3 1.3 gather_fusion.2
  69.6 3.4 %all-to-all-start.1 = ((bf16[64,16,128]{2,1,0:T(8,128)(2,1)}), bf16[64,16,128]{2,1,0:T(8,128)(2,1)S(1)}, u32[]{:S(2)}, u32[]{:S(2)}) async-start(bf16[64,16,128]{2,1,0:T(8,128)(2,1)} %gather_fusion.2), calls=%async_computation.1 | async-start | bytes 524288 | tf_op jit(solution)/shard_map/all_to_all | solution.py:169
  73.2 6.7 %all-to-all-done.1 = bf16[64,16,128]{2,1,0:T(8,128)(2,1)S(1)} async-done(((bf16[64,16,128]{2,1,0:T(8,128)(2,1)}), bf16[64,16,128]{2,1,0:T(8,128)(2,1)S(1)}, u32[]{:S(2)}, u32[]{:S(2)}) %all-to-all-start.1) | async-done | bytes 262176 | tf_op jit(solution)/shard_map/all_to_all | solution.py:169
  80.1 1.2 scatter_fusion
  81.4 21.0 %all-gather.3.cloned.1.call-done = bf16[2048,1024]{1,0:T(8,128)(2,1)} async-done(((bf16[512,1024]{1,0:T(8,128)(2,1)}), bf16[2048,1024]{1,0:T(8,128)(2,1)}) %all-gather.3.cloned.1.call-update) | async-done | bytes 4194320 | tf_op jit(solution)/shard_map/all_gather | solution.py:56
  102.3 2.5 %compare_select_fusion = (bf16[4,256,1024]{2,1,0:T(8,128)(2,1)S(1)}, bf16[4,256,1024]{2,1,0:T(8,128)(2,1)S(1)}) fusion(bf16[4,512,1024]{2,1,0:T(8,128)(2,1)} %bitcast.104, s32[1024]{0:T(1024)S(1)} %select_reduce_fusion.1, s32[4,256]{1,0:T(4,128)S(1)} %eq.225), kind=kLoop, calls=%fused_computation.11 | loop fusion | flops 2097152 | bytes 8396800 | tf_op jit(solution)/shard_map/jit(_where)/select_n | solution.py:58
  104.9 0.3 bitcast_select_fusion
  105.2 0.9 copy-done.4
  106.1 0.8 fusion.11
  106.9 0.8 convolution_convert_fusion.2
  107.8 0.2 copy.67
  107.9 0.2 reshape.560
  108.1 1.4 gather_fusion.3
  109.6 3.4 %all-to-all-start.2 = ((bf16[64,16,128]{2,1,0:T(8,128)(2,1)}), bf16[64,16,128]{2,1,0:T(8,128)(2,1)S(1)}, u32[]{:S(2)}, u32[]{:S(2)}) async-start(bf16[64,16,128]{2,1,0:T(8,128)(2,1)} %gather_fusion.3), calls=%async_computation.2 | async-start | bytes 524288 | tf_op jit(solution)/shard_map/all_to_all | solution.py:169
  113.1 6.8 %all-to-all-done.2 = bf16[64,16,128]{2,1,0:T(8,128)(2,1)S(1)} async-done(((bf16[64,16,128]{2,1,0:T(8,128)(2,1)}), bf16[64,16,128]{2,1,0:T(8,128)(2,1)S(1)}, u32[]{:S(2)}, u32[]{:S(2)}) %all-to-all-start.2) | async-done | bytes 262176 | tf_op jit(solution)/shard_map/all_to_all | solution.py:169
  120.0 1.2 scatter_fusion.1
  121.2 2.0 %fusion.14 = bf16[1024,64]{0,1:T(8,128)(2,1)S(1)} fusion(bf16[1024,1024]{1,0:T(8,128)(2,1)S(1)} %bitcast.102, f32[1,1,1024,64]{3,2,1,0:T(8,128)S(1)} %bitcast.112, f32[1,1,1024,256]{3,2,1,0:T(8,128)} %param.9, s32[]{:T(128)S(6)} %select_n.246), kind=kOutput, calls=%fused_computation.38 | convolution fusion | flops 134348800 | bytes 3014660 | tf_op jit(solution)/shard_map/dot_general | solution.py:160
  123.3 0.8 convolution_convert_fusion.1
  124.1 0.9 copy.68
  125.0 1.1 reshape.562
  126.1 1.4 gather_fusion.4
  127.5 3.4 %all-to-all-start.3 = ((bf16[64,16,128]{2,1,0:T(8,128)(2,1)}), bf16[64,16,128]{2,1,0:T(8,128)(2,1)S(1)}, u32[]{:S(2)}, u32[]{:S(2)}) async-start(bf16[64,16,128]{2,1,0:T(8,128)(2,1)} %gather_fusion.4), calls=%async_computation.3 | async-start | bytes 524288 | tf_op jit(solution)/shard_map/all_to_all | solution.py:169
  131.1 0.5 fusion.44
  131.6 6.3 %all-to-all-done.3 = bf16[64,16,128]{2,1,0:T(8,128)(2,1)S(1)} async-done(((bf16[64,16,128]{2,1,0:T(8,128)(2,1)}), bf16[64,16,128]{2,1,0:T(8,128)(2,1)S(1)}, u32[]{:S(2)}, u32[]{:S(2)}) %all-to-all-start.3) | async-done | bytes 262176 | tf_op jit(solution)/shard_map/all_to_all | solution.py:169
  138.0 1.3 scatter_fusion.2
  139.3 2.0 %select_convert_fusion = (bf16[1024,64]{0,1:T(8,128)(2,1)S(1)}, bf16[1024,64]{0,1:T(8,128)(2,1)S(1)}) fusion(bf16[1024,64]{0,1:T(8,128)(2,1)S(1)} %fusion.14, bf16[1024,64]{0,1:T(8,128)(2,1)S(1)} %fusion.11, pred[]{:T(512)S(6)} %eq.257, pred[]{:T(512)S(6)} %eq.256, pred[]{:T(512)S(6)} %eq.224, bf16[1024,1024]{1,0:T(8,128)(2,1)S(1)} %bitcast.103, ...), kind=kOutput, calls=%fused_computation.43 | convolution fusion | flops 134545408 | bytes 3407879 | tf_op jit(solution)/shard_map/dot_general | solution.py:160
  141.4 0.8 convolution_convert_fusion
  142.2 0.2 copy.69
  142.6 1.4 gather_fusion.5
  144.0 3.6 %all-to-all-start.4 = ((bf16[64,16,128]{2,1,0:T(8,128)(2,1)}), bf16[64,16,128]{2,1,0:T(8,128)(2,1)S(1)}, u32[]{:S(2)}, u32[]{:S(2)}) async-start(bf16[64,16,128]{2,1,0:T(8,128)(2,1)} %gather_fusion.5), calls=%async_computation.4 | async-start | bytes 524288 | tf_op jit(solution)/shard_map/all_to_all | solution.py:169
  147.7 0.2 copy.75
  147.9 6.4 %all-to-all-done.4 = bf16[64,16,128]{2,1,0:T(8,128)(2,1)S(1)} async-done(((bf16[64,16,128]{2,1,0:T(8,128)(2,1)}), bf16[64,16,128]{2,1,0:T(8,128)(2,1)S(1)}, u32[]{:S(2)}, u32[]{:S(2)}) %all-to-all-start.4) | async-done | bytes 262176 | tf_op jit(solution)/shard_map/all_to_all | solution.py:169
  154.4 1.2 scatter_fusion.3
  155.7 0.2 pad_maximum_fusion.1
  155.9 1.1 reshape.565
  157.0 4.5 %all-to-all-start.5 = ((bf16[4,384,128]{2,1,0:T(8,128)(2,1)}), bf16[4,384,128]{2,1,0:T(8,128)(2,1)S(1)}, u32[]{:S(2)}, u32[]{:S(2)}) async-start(bf16[4,384,128]{2,1,0:T(8,128)(2,1)} %reshape.565), calls=%async_computation.5 | async-start | bytes 786432 | tf_op jit(solution)/shard_map/all_to_all | solution.py:186
  161.5 11.0 %all-to-all-done.5 = bf16[4,384,128]{2,1,0:T(8,128)(2,1)S(1)} async-done(((bf16[4,384,128]{2,1,0:T(8,128)(2,1)}), bf16[4,384,128]{2,1,0:T(8,128)(2,1)S(1)}, u32[]{:S(2)}, u32[]{:S(2)}) %all-to-all-start.5) | async-done | bytes 393248 | tf_op jit(solution)/shard_map/all_to_all | solution.py:186
  172.5 0.3 reshape.618
  172.9 0.2 copy.71
  173.2 0.3 copy.73
  173.5 1.0 copy.74
  174.5 0.7 select_bitcast_fusion
  (100 shorter events, 3.0 us)
Async XLA Ops:
  7.2 2.7 %copy-start.5 = (bf16[1,1,256,1024]{3,2,1,0:T(8,128)(2,1)S(1)}, bf16[1,1,256,1024]{3,2,1,0:T(8,128)(2,1)}, u32[]{:S(2)}) copy-start(bf16[1,1,256,1024]{3,2,1,0:T(8,128)(2,1)} %param.10) | copy-start | bytes 1572868
  7.2 2.5 %copy-start.9 = (s32[1,1,8]{2,1,0:T(1,128)S(1)}, s32[1,1,8]{2,1,0:T(1,128)}, u32[]{:S(2)}) copy-start(s32[1,1,8]{2,1,0:T(1,128)} %param.12) | copy-start | bytes 100
  7.2 2.7 %copy-start.3 = (f32[1,1,1024,256]{3,2,1,0:T(8,128)S(1)}, f32[1,1,1024,256]{3,2,1,0:T(8,128)}, u32[]{:S(2)}) copy-start(f32[1,1,1024,256]{3,2,1,0:T(8,128)} %param.9) | copy-start | bytes 3145732
  7.2 95.1 %all-gather.3.cloned.1.call-start = ((), (), s32[]{:S(2)}) async-start(), calls=%async_computation.6 | async-start | bytes 5242880 | tf_op jit(solution)/shard_map/all_gather | solution.py:56
  7.2 15.5 %copy-start.13 = (s32[1,1,8]{2,1,0:T(1,128)S(1)}, s32[1,1,8]{2,1,0:T(1,128)}, u32[]{:S(2)}) copy-start(s32[1,1,8]{2,1,0:T(1,128)} %param.14) | copy-start | bytes 100
  7.3 15.5 %copy-start.14 = (s32[1,1,8]{2,1,0:T(1,128)S(1)}, s32[1,1,8]{2,1,0:T(1,128)}, u32[]{:S(2)}) copy-start(s32[1,1,8]{2,1,0:T(1,128)} %param.13) | copy-start | bytes 100
  7.3 15.5 %copy-start.15 = (s32[1,1,8]{2,1,0:T(1,128)S(1)}, s32[1,1,8]{2,1,0:T(1,128)}, u32[]{:S(2)}) copy-start(s32[1,1,8]{2,1,0:T(1,128)} %param.15) | copy-start | bytes 100
  9.6 17.4 %copy-start.6 = (bf16[1,1,8,32,1024]{4,3,2,1,0:T(8,128)(2,1)S(1)}, bf16[1,1,8,32,1024]{4,3,2,1,0:T(8,128)(2,1)}, u32[]{:S(2)}) copy-start(bf16[1,1,8,32,1024]{4,3,2,1,0:T(8,128)(2,1)} %param.11) | copy-start | bytes 1572868
  10.9 30.6 %collective-permute-start.2 = (bf16[256,256]{1,0:T(8,128)(2,1)S(1)}, bf16[256,256]{1,0:T(8,128)(2,1)S(1)}, u32[]{:S(2)}, u32[]{:S(2)}) collective-permute-start(bf16[256,256]{1,0:T(8,128)(2,1)S(1)} %get-tuple-element.37), channel_id=1, source_target_pairs={{0,6},{1,7},{2,0},{3,1},{4,2},{5,3},{6,4},{7,5}} | collective-permute-start | bytes 393224 | tf_op jit(solution)/shard_map/ppermute | solution.py:72
  17.9 23.7 %collective-permute-start.1 = (bf16[256,256]{1,0:T(8,128)(2,1)S(1)}, bf16[256,256]{1,0:T(8,128)(2,1)S(1)}, u32[]{:S(2)}, u32[]{:S(2)}) collective-permute-start(bf16[256,256]{1,0:T(8,128)(2,1)S(1)} %get-tuple-element.37), channel_id=1, source_target_pairs={{0,4},{1,5},{2,6},{3,7},{4,0},{5,1},{6,2},{7,3}} | collective-permute-start | bytes 393224 | tf_op jit(solution)/shard_map/ppermute | solution.py:72
  19.8 21.8 %collective-permute-start = (bf16[256,256]{1,0:T(8,128)(2,1)S(1)}, bf16[256,256]{1,0:T(8,128)(2,1)S(1)}, u32[]{:S(2)}, u32[]{:S(2)}) collective-permute-start(bf16[256,256]{1,0:T(8,128)(2,1)S(1)} %get-tuple-element.37), channel_id=1, source_target_pairs={{0,2},{1,3},{2,4},{3,5},{4,6},{5,7},{6,0},{7,1}} | collective-permute-start | bytes 393224 | tf_op jit(solution)/shard_map/ppermute | solution.py:72
  23.4 16.1 %all-to-all-start = ((s32[32,3,8]{2,1,0:T(4,128)}), s32[32,3,8]{2,1,0:T(4,128)S(1)}, u32[]{:S(2)}, u32[]{:S(2)}) async-start(s32[32,3,8]{2,1,0:T(4,128)} %broadcast_in_dim.180), calls=%async_computation | async-start | bytes 131072 | tf_op jit(solution)/shard_map/all_to_all | solution.py:104
  41.6 26.7 %copy-start.8 = (s32[1024]{0:T(1024)}, s32[1024]{0:T(1024)S(1)}, u32[]{:S(2)}) copy-start(s32[1024]{0:T(1024)S(1)} %pad_clamp_fusion) | copy-start | bytes 12292
  42.7 19.0 %collective-permute-start.5 = (bf16[256,64]{0,1:T(8,128)(2,1)S(1)}, bf16[256,64]{0,1:T(8,128)(2,1)S(1)}, u32[]{:S(2)}, u32[]{:S(2)}) collective-permute-start(bf16[256,64]{0,1:T(8,128)(2,1)S(1)} %get-tuple-element.27), channel_id=1, source_target_pairs={{0,6},{1,7},{2,0},{3,1},{4,2},{5,3},{6,4},{7,5}} | collective-permute-start | bytes 98312 | tf_op jit(solution)/shard_map/ppermute | solution.py:72
  57.0 7.4 %collective-permute-start.4 = (bf16[256,64]{0,1:T(8,128)(2,1)S(1)}, bf16[256,64]{0,1:T(8,128)(2,1)S(1)}, u32[]{:S(2)}, u32[]{:S(2)}) collective-permute-start(bf16[256,64]{0,1:T(8,128)(2,1)S(1)} %get-tuple-element.28), channel_id=1, source_target_pairs={{0,4},{1,5},{2,6},{3,7},{4,0},{5,1},{6,2},{7,3}} | collective-permute-start | bytes 98312 | tf_op jit(solution)/shard_map/ppermute | solution.py:72
  58.9 8.3 %collective-permute-start.3 = (bf16[256,64]{0,1:T(8,128)(2,1)S(1)}, bf16[256,64]{0,1:T(8,128)(2,1)S(1)}, u32[]{:S(2)}, u32[]{:S(2)}) collective-permute-start(bf16[256,64]{0,1:T(8,128)(2,1)S(1)} %get-tuple-element.29), channel_id=1, source_target_pairs={{0,2},{1,3},{2,4},{3,5},{4,6},{5,7},{6,0},{7,1}} | collective-permute-start | bytes 98312 | tf_op jit(solution)/shard_map/ppermute | solution.py:72
  69.6 10.3 %all-to-all-start.1 = ((bf16[64,16,128]{2,1,0:T(8,128)(2,1)}), bf16[64,16,128]{2,1,0:T(8,128)(2,1)S(1)}, u32[]{:S(2)}, u32[]{:S(2)}) async-start(bf16[64,16,128]{2,1,0:T(8,128)(2,1)} %gather_fusion.2), calls=%async_computation.1 | async-start | bytes 524288 | tf_op jit(solution)/shard_map/all_to_all | solution.py:169
  104.9 1.2 copy-start.4
  105.2 1.7 copy-start
  106.9 6.0 %copy-start.12 = (s32[2,8]{1,0:T(2,128)S(1)}, s32[2,8]{1,0:T(2,128)}, u32[]{:S(2)}) copy-start(s32[2,8]{1,0:T(2,128)} %get-tuple-element.35) | copy-start | bytes 196
  109.6 10.3 %all-to-all-start.2 = ((bf16[64,16,128]{2,1,0:T(8,128)(2,1)}), bf16[64,16,128]{2,1,0:T(8,128)(2,1)S(1)}, u32[]{:S(2)}, u32[]{:S(2)}) async-start(bf16[64,16,128]{2,1,0:T(8,128)(2,1)} %gather_fusion.3), calls=%async_computation.2 | async-start | bytes 524288 | tf_op jit(solution)/shard_map/all_to_all | solution.py:169
  121.2 2.1 %copy-start.1 = (bf16[1024,1024]{1,0:T(8,128)(2,1)S(1)}, bf16[1024,1024]{1,0:T(8,128)(2,1)}, u32[]{:S(2)}) copy-start(bf16[1024,1024]{1,0:T(8,128)(2,1)} %copy-done) | copy-start | bytes 6291460
  123.3 7.7 %copy-start.11 = (s32[2,8]{1,0:T(2,128)S(1)}, s32[2,8]{1,0:T(2,128)}, u32[]{:S(2)}) copy-start(s32[2,8]{1,0:T(2,128)} %get-tuple-element.34) | copy-start | bytes 196
  127.5 10.3 %all-to-all-start.3 = ((bf16[64,16,128]{2,1,0:T(8,128)(2,1)}), bf16[64,16,128]{2,1,0:T(8,128)(2,1)S(1)}, u32[]{:S(2)}, u32[]{:S(2)}) async-start(bf16[64,16,128]{2,1,0:T(8,128)(2,1)} %gather_fusion.4), calls=%async_computation.3 | async-start | bytes 524288 | tf_op jit(solution)/shard_map/all_to_all | solution.py:169
  139.3 2.1 %copy-start.2 = (bf16[1024,1024]{1,0:T(8,128)(2,1)S(1)}, bf16[1024,1024]{1,0:T(8,128)(2,1)}, u32[]{:S(2)}) copy-start(bf16[1024,1024]{1,0:T(8,128)(2,1)} %copy-done) | copy-start | bytes 6291460
  141.4 6.2 %copy-start.10 = (s32[2,8]{1,0:T(2,128)S(1)}, s32[2,8]{1,0:T(2,128)}, u32[]{:S(2)}) copy-start(s32[2,8]{1,0:T(2,128)} %get-tuple-element.33) | copy-start | bytes 196
  144.0 10.3 %all-to-all-start.4 = ((bf16[64,16,128]{2,1,0:T(8,128)(2,1)}), bf16[64,16,128]{2,1,0:T(8,128)(2,1)S(1)}, u32[]{:S(2)}, u32[]{:S(2)}) async-start(bf16[64,16,128]{2,1,0:T(8,128)(2,1)} %gather_fusion.5), calls=%async_computation.4 | async-start | bytes 524288 | tf_op jit(solution)/shard_map/all_to_all | solution.py:169
  157.0 15.5 %all-to-all-start.5 = ((bf16[4,384,128]{2,1,0:T(8,128)(2,1)}), bf16[4,384,128]{2,1,0:T(8,128)(2,1)S(1)}, u32[]{:S(2)}, u32[]{:S(2)}) async-start(bf16[4,384,128]{2,1,0:T(8,128)(2,1)} %reshape.565), calls=%async_computation.5 | async-start | bytes 786432 | tf_op jit(solution)/shard_map/all_to_all | solution.py:186
  172.9 1.7 copy-start.7
Sparse Core Ops, SparseCore 0:
  9.8 92.5 all-gather.2

commit v26 on v24

--- a/solution.py
+++ b/solution.py
@@ -150,7 +150,7 @@
 
     rhs_cols = lax.dynamic_slice_in_dim(rhs[0, 0], row_index * cols, cols, axis=1)
     window_blocks = width // block_rows
-    acc = jnp.zeros((NT + 1, block_rows, cols), jnp.float32)
+    acc = jnp.zeros((NT + 1, block_rows // 2, 2 * cols), jnp.float32)
     solved = jnp.zeros((width, cols), jnp.float32)
     for section in range(n_lvl):
         if section == 0:
@@ -170,7 +170,6 @@
             sending, ("lvl", "pcol"), split_axis=0, concat_axis=0, tiled=True
         )
         incoming = incoming.reshape(n_lvl, n_pcol * slots, block_rows // 2, 2 * cols)[section]
-        incoming = incoming.reshape(n_pcol * slots, block_rows, cols)
         acc = acc.at[recv_block[section]].add(incoming.astype(jnp.float32), mode="clip")
     outer = acc[window_blocks:NT].reshape(ABOVE, cols)
 

time: 182 us -> 202 us (1.11)
  local copies, waits for them, and re-layouts: 14.6 us -> 28 us
  other arithmetic: 14.1 us -> 18.1 us
    reshape x0 -> x3, local copies, waits for them, and re-layouts: none -> 4.74 us  [per_device(): right = rhs_cols - acc[:window_blocks].reshape(width, cols)]
    convert_element_type x4, other arithmetic: 0.04 us -> 3.03 us  [per_device(): incoming.astype(jnp.float32)]
    convert_element_type x3, local copies, waits for them, and re-layouts: 1.24 us -> 3.72 us  [per_device(): updates = jnp.dot(tiles_full, solved_now.astype(jnp.bfloat16), preferred_...]
    reshape x4, local copies, waits for them, and re-layouts: 1.59 us -> 3.91 us  [per_device(): updates = updates.reshape(group_tiles + 1, block_rows // 2, 2 * cols)]
  transfers between devices with their start and end apart: 13 -> 13, of which waited for: 9 -> 9; matrix products, arithmetic and copies ran while one was open for 6% -> 5% of each run, Pallas kernels for 0% -> 0%
where the time goes in v26:
time: 202 us; the launch traced here: 201 us
  waiting for transfers between devices  75.8 us (38%)
  starting transfers between devices  53.5 us (26%)
  local copies, waits for them, and re-layouts  28 us (14%)
  other arithmetic  18.1 us (9%)
  between operations  14.8 us (7%)
  matrix products  10.7 us (5%)
    ppermute x6, starting transfers between devices, level0_shift(): return lax.ppermute(x, all_axes, pairs)  30.8 us
    all_to_all x4, waiting for transfers between devices, per_device(): lax.all_to_all(sending, ('lvl', 'pcol'), split_axis=0, concat_axis=0, til...  26.5 us
    all_gather x1, waiting for transfers between devices, per_device(): gathered = lax.all_gather(raw, 'prow', axis=0)  20.3 us
    all_to_all x4, starting transfers between devices, per_device(): lax.all_to_all(sending, ('lvl', 'pcol'), split_axis=0, concat_axis=0, til...  14.9 us
    all_to_all x1, waiting for transfers between devices, per_device(): lax.all_to_all(jnp.broadcast_to(meta[None], (devices,) + meta.shape), ('l...  12.4 us
    all_to_all x1, waiting for transfers between devices, per_device(): lax.all_to_all(final, 'prow', split_axis=0, concat_axis=0, tiled=True)  11 us
    gather x4, local copies, waits for them, and re-layouts, per_device(): sending = jnp.take(updates, send_index, axis=0, mode='clip')  7.46 us
    scatter-add x4, other arithmetic, per_device(): acc.at[recv_block[section]].add(incoming.astype(jnp.float32), mode='clip')  5.85 us
  transfers between devices with their start and end apart: 13, of which 9 were waited for; matrix products, arithmetic and copies ran while one was open for 5% of the time, Pallas kernels for 0%

profile of v26, /device:TPU:0, one launch (start us, length us, event | category | flops | bytes accessed | tf_op | source)
XLA Modules:
  0.0 200.9 jit_solution(12728388831279368756)
XLA Ops:
  7.3 2.3 %pad_maximum_fusion = bf16[512,1024]{1,0:T(8,128)(2,1)} fusion(bf16[256,1024]{1,0:T(8,128)(2,1)} %bitcast.108, bf16[256,1024]{1,0:T(8,128)(2,1)} %bitcast.104), kind=kLoop, calls=%fused_computation.19 | loop fusion | flops 2097152 | bytes 2097152 | tf_op jit(solution)/shard_map/concatenate | solution.py:53
  9.9 1.1 fusion.53
  10.9 6.9 %collective-permute-start.2 = (bf16[256,256]{1,0:T(8,128)(2,1)S(1)}, bf16[256,256]{1,0:T(8,128)(2,1)S(1)}, u32[]{:S(2)}, u32[]{:S(2)}) collective-permute-start(bf16[256,256]{1,0:T(8,128)(2,1)S(1)} %get-tuple-element.37), channel_id=1, source_target_pairs={{0,6},{1,7},{2,0},{3,1},{4,2},{5,3},{6,4},{7,5}} | collective-permute-start | bytes 393224 | tf_op jit(solution)/shard_map/ppermute | solution.py:72
  17.9 1.9 collective-permute-start.1
  19.8 2.9 %collective-permute-start = (bf16[256,256]{1,0:T(8,128)(2,1)S(1)}, bf16[256,256]{1,0:T(8,128)(2,1)S(1)}, u32[]{:S(2)}, u32[]{:S(2)}) collective-permute-start(bf16[256,256]{1,0:T(8,128)(2,1)S(1)} %get-tuple-element.37), channel_id=1, source_target_pairs={{0,2},{1,3},{2,4},{3,5},{4,6},{5,7},{6,0},{7,1}} | collective-permute-start | bytes 393224 | tf_op jit(solution)/shard_map/ppermute | solution.py:72
  22.8 0.6 broadcast_in_dim.180
  23.4 3.2 %all-to-all-start = ((s32[32,3,8]{2,1,0:T(4,128)}), s32[32,3,8]{2,1,0:T(4,128)S(1)}, u32[]{:S(2)}, u32[]{:S(2)}) async-start(s32[32,3,8]{2,1,0:T(4,128)} %broadcast_in_dim.180), calls=%async_computation | async-start | bytes 131072 | tf_op jit(solution)/shard_map/all_to_all | solution.py:104
  27.2 12.4 %all-to-all-done = s32[32,3,8]{2,1,0:T(4,128)S(1)} async-done(((s32[32,3,8]{2,1,0:T(4,128)}), s32[32,3,8]{2,1,0:T(4,128)S(1)}, u32[]{:S(2)}, u32[]{:S(2)}) %all-to-all-start) | async-done | bytes 3104 | tf_op jit(solution)/shard_map/all_to_all | solution.py:104
  39.8 0.3 convert_reduce_fusion
  40.3 0.2 select_reduce_fusion
  40.5 0.6 fusion.52
  41.6 0.6 gather_fusion
  42.2 0.3 convolution_convert_fusion.3
  42.6 14.4 %collective-permute-start.5 = (bf16[256,64]{0,1:T(8,128)(2,1)S(1)}, bf16[256,64]{0,1:T(8,128)(2,1)S(1)}, u32[]{:S(2)}, u32[]{:S(2)}) collective-permute-start(bf16[256,64]{0,1:T(8,128)(2,1)S(1)} %get-tuple-element.27), channel_id=1, source_target_pairs={{0,6},{1,7},{2,0},{3,1},{4,2},{5,3},{6,4},{7,5}} | collective-permute-start | bytes 98312 | tf_op jit(solution)/shard_map/ppermute | solution.py:72
  57.0 1.9 collective-permute-start.4
  58.9 2.7 %collective-permute-start.3 = (bf16[256,64]{0,1:T(8,128)(2,1)S(1)}, bf16[256,64]{0,1:T(8,128)(2,1)S(1)}, u32[]{:S(2)}, u32[]{:S(2)}) collective-permute-start(bf16[256,64]{0,1:T(8,128)(2,1)S(1)} %get-tuple-element.29), channel_id=1, source_target_pairs={{0,2},{1,3},{2,4},{3,5},{4,6},{5,7},{6,0},{7,1}} | collective-permute-start | bytes 98312 | tf_op jit(solution)/shard_map/ppermute | solution.py:72
  61.6 2.8 %collective-permute-done.4 = bf16[256,64]{0,1:T(8,128)(2,1)S(1)} collective-permute-done((bf16[256,64]{0,1:T(8,128)(2,1)S(1)}, bf16[256,64]{0,1:T(8,128)(2,1)S(1)}, u32[]{:S(2)}, u32[]{:S(2)}) %collective-permute-start.4) | collective-permute-done | bytes 32800 | tf_op jit(solution)/shard_map/ppermute | solution.py:72
  64.4 2.8 %collective-permute-done.3 = bf16[256,64]{0,1:T(8,128)(2,1)S(1)} collective-permute-done((bf16[256,64]{0,1:T(8,128)(2,1)S(1)}, bf16[256,64]{0,1:T(8,128)(2,1)S(1)}, u32[]{:S(2)}, u32[]{:S(2)}) %collective-permute-start.3) | collective-permute-done | bytes 32800 | tf_op jit(solution)/shard_map/ppermute | solution.py:72
  67.3 0.6 gather_fusion.1
  68.2 1.3 gather_fusion.2
  69.6 3.4 %all-to-all-start.1 = ((bf16[64,16,128]{2,1,0:T(8,128)(2,1)}), bf16[64,16,128]{2,1,0:T(8,128)(2,1)S(1)}, u32[]{:S(2)}, u32[]{:S(2)}) async-start(bf16[64,16,128]{2,1,0:T(8,128)(2,1)} %gather_fusion.2), calls=%async_computation.1 | async-start | bytes 524288 | tf_op jit(solution)/shard_map/all_to_all | solution.py:169
  73.1 0.7 broadcast_compare_fusion
  73.8 6.1 %all-to-all-done.1 = bf16[64,16,128]{2,1,0:T(8,128)(2,1)S(1)} async-done(((bf16[64,16,128]{2,1,0:T(8,128)(2,1)}), bf16[64,16,128]{2,1,0:T(8,128)(2,1)S(1)}, u32[]{:S(2)}, u32[]{:S(2)}) %all-to-all-start.1) | async-done | bytes 262176 | tf_op jit(solution)/shard_map/all_to_all | solution.py:169
  79.9 1.1 scatter_fusion
  81.1 0.9 reshape.545
  82.0 20.3 %all-gather.3.cloned.1.call-done = bf16[2048,1024]{1,0:T(8,128)(2,1)} async-done(((bf16[512,1024]{1,0:T(8,128)(2,1)}), bf16[2048,1024]{1,0:T(8,128)(2,1)}) %all-gather.3.cloned.1.call-update) | async-done | bytes 4194320 | tf_op jit(solution)/shard_map/all_gather | solution.py:56
  102.3 2.5 %compare_select_fusion = (bf16[4,256,1024]{2,1,0:T(8,128)(2,1)S(1)}, bf16[4,256,1024]{2,1,0:T(8,128)(2,1)S(1)}) fusion(bf16[4,512,1024]{2,1,0:T(8,128)(2,1)} %bitcast.103, s32[1024]{0:T(1024)S(1)} %select_reduce_fusion.1, s32[4,256]{1,0:T(4,128)S(1)} %eq.225), kind=kLoop, calls=%fused_computation.11 | loop fusion | flops 2097152 | bytes 8396800 | tf_op jit(solution)/shard_map/jit(_where)/select_n | solution.py:58
  104.9 0.3 bitcast_select_fusion
  105.2 0.7 copy-done.6
  105.9 0.8 fusion.11
  106.8 0.7 copy-done.7
  107.4 1.5 convolution_convert_fusion.2
  108.9 1.8 copy.63
  110.7 1.8 reshape.546
  112.5 2.3 %gather_fusion.3 = bf16[64,16,128]{2,1,0:T(8,128)(2,1)} fusion(bf16[33,16,128]{2,1,0:T(8,128)(2,1)} %reshape.546, s32[1024]{0:T(1024)} %copy-done.12), kind=kCustom, calls=%fused_computation.3 | custom fusion | bytes 524544 | tf_op jit(solution)/shard_map/jit(_take)/gather | solution.py:168
  114.8 4.0 %all-to-all-start.2 = ((bf16[64,16,128]{2,1,0:T(8,128)(2,1)}), bf16[64,16,128]{2,1,0:T(8,128)(2,1)}, u32[]{:S(2)}, u32[]{:S(2)}) async-start(bf16[64,16,128]{2,1,0:T(8,128)(2,1)} %gather_fusion.3), calls=%async_computation.2 | async-start | bytes 524288 | tf_op jit(solution)/shard_map/all_to_all | solution.py:169
  119.0 6.8 %all-to-all-done.2 = bf16[64,16,128]{2,1,0:T(8,128)(2,1)} async-done(((bf16[64,16,128]{2,1,0:T(8,128)(2,1)}), bf16[64,16,128]{2,1,0:T(8,128)(2,1)}, u32[]{:S(2)}, u32[]{:S(2)}) %all-to-all-start.2) | async-done | bytes 262176 | tf_op jit(solution)/shard_map/all_to_all | solution.py:169
  125.8 1.5 slice_convert_fusion.3
  127.3 1.8 scatter_fusion.1
  129.1 0.7 slice.112
  129.8 1.9 reshape.547
  131.7 2.0 %fusion.14 = bf16[1024,64]{0,1:T(8,128)(2,1)S(1)} fusion(bf16[1024,1024]{1,0:T(8,128)(2,1)S(1)} %bitcast.101, f32[1,1,1024,64]{3,2,1,0:T(8,128)} %reshape.547, f32[1,1,1024,256]{3,2,1,0:T(8,128)S(1)} %copy-done.3, s32[]{:T(128)S(6)} %select_n.246), kind=kOutput, calls=%fused_computation.36 | convolution fusion | flops 134348800 | bytes 3014660 | tf_op jit(solution)/shard_map/dot_general | solution.py:160
  133.8 0.6 copy-done.8
  134.4 1.5 convolution_convert_fusion.1
  135.9 1.8 copy.64
  137.6 1.8 reshape.548
  139.4 2.3 %gather_fusion.4 = bf16[64,16,128]{2,1,0:T(8,128)(2,1)} fusion(bf16[33,16,128]{2,1,0:T(8,128)(2,1)} %reshape.548, s32[1024]{0:T(1024)} %copy-done.12), kind=kCustom, calls=%fused_computation.4 | custom fusion | bytes 524544 | tf_op jit(solution)/shard_map/jit(_take)/gather | solution.py:168
  141.8 4.0 %all-to-all-start.3 = ((bf16[64,16,128]{2,1,0:T(8,128)(2,1)}), bf16[64,16,128]{2,1,0:T(8,128)(2,1)}, u32[]{:S(2)}, u32[]{:S(2)}) async-start(bf16[64,16,128]{2,1,0:T(8,128)(2,1)} %gather_fusion.4), calls=%async_computation.3 | async-start | bytes 524288 | tf_op jit(solution)/shard_map/all_to_all | solution.py:169
  145.9 6.8 %all-to-all-done.3 = bf16[64,16,128]{2,1,0:T(8,128)(2,1)} async-done(((bf16[64,16,128]{2,1,0:T(8,128)(2,1)}), bf16[64,16,128]{2,1,0:T(8,128)(2,1)}, u32[]{:S(2)}, u32[]{:S(2)}) %all-to-all-start.3) | async-done | bytes 262176 | tf_op jit(solution)/shard_map/all_to_all | solution.py:169
  152.8 1.5 slice_convert_fusion.2
  154.3 1.8 scatter_fusion.2
  156.1 0.7 slice.114
  156.8 1.9 reshape.549
  158.7 2.7 %select_convert_fusion = (bf16[1024,64]{0,1:T(8,128)(2,1)}, bf16[1024,64]{0,1:T(8,128)(2,1)S(1)}) fusion(bf16[1024,64]{0,1:T(8,128)(2,1)} %copy-done.8, bf16[1024,64]{0,1:T(8,128)(2,1)} %copy-done.7, pred[]{:T(512)S(6)} %eq.257, pred[]{:T(512)S(6)} %eq.256, pred[]{:T(512)S(6)} %eq.224, bf16[1024,1024]{1,0:T(8,128)(2,1)S(1)} %bitcast.102, ...), kind=kOutput, calls=%fused_computation.40 | convolution fusion | flops 134545408 | bytes 3407879 | tf_op jit(solution)/shard_map/dot_general | solution.py:160
  161.4 0.8 convolution_convert_fusion
  162.6 1.4 gather_fusion.5
  164.0 3.4 %all-to-all-start.4 = ((bf16[64,16,128]{2,1,0:T(8,128)(2,1)}), bf16[64,16,128]{2,1,0:T(8,128)(2,1)S(1)}, u32[]{:S(2)}, u32[]{:S(2)}) async-start(bf16[64,16,128]{2,1,0:T(8,128)(2,1)} %gather_fusion.5), calls=%async_computation.4 | async-start | bytes 524288 | tf_op jit(solution)/shard_map/all_to_all | solution.py:169
  167.6 6.7 %all-to-all-done.4 = bf16[64,16,128]{2,1,0:T(8,128)(2,1)S(1)} async-done(((bf16[64,16,128]{2,1,0:T(8,128)(2,1)}), bf16[64,16,128]{2,1,0:T(8,128)(2,1)S(1)}, u32[]{:S(2)}, u32[]{:S(2)}) %all-to-all-start.4) | async-done | bytes 262176 | tf_op jit(solution)/shard_map/all_to_all | solution.py:169
  174.3 1.1 scatter_fusion.3
  175.7 0.8 pad_maximum_fusion.2
  176.5 4.6 %all-to-all-start.5 = ((bf16[4,768,64]{1,2,0:T(8,128)(2,1)}), bf16[4,768,64]{1,2,0:T(8,128)(2,1)S(1)}, u32[]{:S(2)}, u32[]{:S(2)}) async-start(bf16[4,768,64]{1,2,0:T(8,128)(2,1)} %pad_maximum_fusion.2), calls=%async_computation.5 | async-start | bytes 786432 | tf_op jit(solution)/shard_map/all_to_all | solution.py:184
  181.1 11.0 %all-to-all-done.5 = bf16[4,768,64]{1,2,0:T(8,128)(2,1)S(1)} async-done(((bf16[4,768,64]{1,2,0:T(8,128)(2,1)}), bf16[4,768,64]{1,2,0:T(8,128)(2,1)S(1)}, u32[]{:S(2)}, u32[]{:S(2)}) %all-to-all-start.5) | async-done | bytes 393248 | tf_op jit(solution)/shard_map/all_to_all | solution.py:184
  192.4 1.0 copy.69
  193.4 0.7 select_bitcast_fusion
  (105 shorter events, 3.3 us)
Async XLA Ops:
  7.2 2.7 %copy-start.4 = (bf16[1,1,256,1024]{3,2,1,0:T(8,128)(2,1)S(1)}, bf16[1,1,256,1024]{3,2,1,0:T(8,128)(2,1)}, u32[]{:S(2)}) copy-start(bf16[1,1,256,1024]{3,2,1,0:T(8,128)(2,1)} %param.10) | copy-start | bytes 1572868
  7.2 2.5 %copy-start.13 = (s32[1,1,8]{2,1,0:T(1,128)S(1)}, s32[1,1,8]{2,1,0:T(1,128)}, u32[]{:S(2)}) copy-start(s32[1,1,8]{2,1,0:T(1,128)} %param.12) | copy-start | bytes 100
  7.2 2.7 %copy-start.3 = (f32[1,1,1024,256]{3,2,1,0:T(8,128)S(1)}, f32[1,1,1024,256]{3,2,1,0:T(8,128)}, u32[]{:S(2)}) copy-start(f32[1,1,1024,256]{3,2,1,0:T(8,128)} %param.9) | copy-start | bytes 3145732
  7.2 95.1 %all-gather.3.cloned.1.call-start = ((), (), s32[]{:S(2)}) async-start(), calls=%async_computation.6 | async-start | bytes 5242880 | tf_op jit(solution)/shard_map/all_gather | solution.py:56
  7.2 15.5 %copy-start.17 = (s32[1,1,8]{2,1,0:T(1,128)S(1)}, s32[1,1,8]{2,1,0:T(1,128)}, u32[]{:S(2)}) copy-start(s32[1,1,8]{2,1,0:T(1,128)} %param.14) | copy-start | bytes 100
  7.3 15.5 %copy-start.18 = (s32[1,1,8]{2,1,0:T(1,128)S(1)}, s32[1,1,8]{2,1,0:T(1,128)}, u32[]{:S(2)}) copy-start(s32[1,1,8]{2,1,0:T(1,128)} %param.13) | copy-start | bytes 100
  7.3 15.5 %copy-start.19 = (s32[1,1,8]{2,1,0:T(1,128)S(1)}, s32[1,1,8]{2,1,0:T(1,128)}, u32[]{:S(2)}) copy-start(s32[1,1,8]{2,1,0:T(1,128)} %param.15) | copy-start | bytes 100
  9.6 17.4 %copy-start.5 = (bf16[1,1,8,32,1024]{4,3,2,1,0:T(8,128)(2,1)S(1)}, bf16[1,1,8,32,1024]{4,3,2,1,0:T(8,128)(2,1)}, u32[]{:S(2)}) copy-start(bf16[1,1,8,32,1024]{4,3,2,1,0:T(8,128)(2,1)} %param.11) | copy-start | bytes 1572868
  10.9 30.6 %collective-permute-start.2 = (bf16[256,256]{1,0:T(8,128)(2,1)S(1)}, bf16[256,256]{1,0:T(8,128)(2,1)S(1)}, u32[]{:S(2)}, u32[]{:S(2)}) collective-permute-start(bf16[256,256]{1,0:T(8,128)(2,1)S(1)} %get-tuple-element.37), channel_id=1, source_target_pairs={{0,6},{1,7},{2,0},{3,1},{4,2},{5,3},{6,4},{7,5}} | collective-permute-start | bytes 393224 | tf_op jit(solution)/shard_map/ppermute | solution.py:72
  17.9 23.7 %collective-permute-start.1 = (bf16[256,256]{1,0:T(8,128)(2,1)S(1)}, bf16[256,256]{1,0:T(8,128)(2,1)S(1)}, u32[]{:S(2)}, u32[]{:S(2)}) collective-permute-start(bf16[256,256]{1,0:T(8,128)(2,1)S(1)} %get-tuple-element.37), channel_id=1, source_target_pairs={{0,4},{1,5},{2,6},{3,7},{4,0},{5,1},{6,2},{7,3}} | collective-permute-start | bytes 393224 | tf_op jit(solution)/shard_map/ppermute | solution.py:72
  19.8 21.7 %collective-permute-start = (bf16[256,256]{1,0:T(8,128)(2,1)S(1)}, bf16[256,256]{1,0:T(8,128)(2,1)S(1)}, u32[]{:S(2)}, u32[]{:S(2)}) collective-permute-start(bf16[256,256]{1,0:T(8,128)(2,1)S(1)} %get-tuple-element.37), channel_id=1, source_target_pairs={{0,2},{1,3},{2,4},{3,5},{4,6},{5,7},{6,0},{7,1}} | collective-permute-start | bytes 393224 | tf_op jit(solution)/shard_map/ppermute | solution.py:72
  23.4 16.1 %all-to-all-start = ((s32[32,3,8]{2,1,0:T(4,128)}), s32[32,3,8]{2,1,0:T(4,128)S(1)}, u32[]{:S(2)}, u32[]{:S(2)}) async-start(s32[32,3,8]{2,1,0:T(4,128)} %broadcast_in_dim.180), calls=%async_computation | async-start | bytes 131072 | tf_op jit(solution)/shard_map/all_to_all | solution.py:104
  41.5 26.7 %copy-start.12 = (s32[1024]{0:T(1024)}, s32[1024]{0:T(1024)S(1)}, u32[]{:S(2)}) copy-start(s32[1024]{0:T(1024)S(1)} %pad_clamp_fusion) | copy-start | bytes 12292
  42.6 19.0 %collective-permute-start.5 = (bf16[256,64]{0,1:T(8,128)(2,1)S(1)}, bf16[256,64]{0,1:T(8,128)(2,1)S(1)}, u32[]{:S(2)}, u32[]{:S(2)}) collective-permute-start(bf16[256,64]{0,1:T(8,128)(2,1)S(1)} %get-tuple-element.27), channel_id=1, source_target_pairs={{0,6},{1,7},{2,0},{3,1},{4,2},{5,3},{6,4},{7,5}} | collective-permute-start | bytes 98312 | tf_op jit(solution)/shard_map/ppermute | solution.py:72
  57.0 7.4 %collective-permute-start.4 = (bf16[256,64]{0,1:T(8,128)(2,1)S(1)}, bf16[256,64]{0,1:T(8,128)(2,1)S(1)}, u32[]{:S(2)}, u32[]{:S(2)}) collective-permute-start(bf16[256,64]{0,1:T(8,128)(2,1)S(1)} %get-tuple-element.28), channel_id=1, source_target_pairs={{0,4},{1,5},{2,6},{3,7},{4,0},{5,1},{6,2},{7,3}} | collective-permute-start | bytes 98312 | tf_op jit(solution)/shard_map/ppermute | solution.py:72
  58.9 8.3 %collective-permute-start.3 = (bf16[256,64]{0,1:T(8,128)(2,1)S(1)}, bf16[256,64]{0,1:T(8,128)(2,1)S(1)}, u32[]{:S(2)}, u32[]{:S(2)}) collective-permute-start(bf16[256,64]{0,1:T(8,128)(2,1)S(1)} %get-tuple-element.29), channel_id=1, source_target_pairs={{0,2},{1,3},{2,4},{3,5},{4,6},{5,7},{6,0},{7,1}} | collective-permute-start | bytes 98312 | tf_op jit(solution)/shard_map/ppermute | solution.py:72
  69.6 10.3 %all-to-all-start.1 = ((bf16[64,16,128]{2,1,0:T(8,128)(2,1)}), bf16[64,16,128]{2,1,0:T(8,128)(2,1)S(1)}, u32[]{:S(2)}, u32[]{:S(2)}) async-start(bf16[64,16,128]{2,1,0:T(8,128)(2,1)} %gather_fusion.2), calls=%async_computation.1 | async-start | bytes 524288 | tf_op jit(solution)/shard_map/all_to_all | solution.py:169
  102.3 2.6 %copy-start.11 = (pred[32,1024]{1,0:T(8,128)(4,1)S(1)}, pred[32,1024]{1,0:T(8,128)(4,1)}, u32[]{:S(2)}) copy-start(pred[32,1024]{1,0:T(8,128)(4,1)} %broadcast_compare_fusion) | copy-start | bytes 98308
  104.9 1.0 copy-start.6
  105.2 1.5 copy-start
  106.8 0.7 copy-start.7
  107.4 11.4 %copy-start.16 = (s32[2,8]{1,0:T(2,128)S(1)}, s32[2,8]{1,0:T(2,128)}, u32[]{:S(2)}) copy-start(s32[2,8]{1,0:T(2,128)} %get-tuple-element.35) | copy-start | bytes 196
  114.8 11.0 %all-to-all-start.2 = ((bf16[64,16,128]{2,1,0:T(8,128)(2,1)}), bf16[64,16,128]{2,1,0:T(8,128)(2,1)}, u32[]{:S(2)}, u32[]{:S(2)}) async-start(bf16[64,16,128]{2,1,0:T(8,128)(2,1)} %gather_fusion.3), calls=%async_computation.2 | async-start | bytes 524288 | tf_op jit(solution)/shard_map/all_to_all | solution.py:169
  131.7 2.7 %copy-start.1 = (bf16[1024,1024]{1,0:T(8,128)(2,1)S(1)}, bf16[1024,1024]{1,0:T(8,128)(2,1)}, u32[]{:S(2)}) copy-start(bf16[1024,1024]{1,0:T(8,128)(2,1)} %copy-done) | copy-start | bytes 6291460
  133.8 0.7 copy-start.8
  134.4 11.4 %copy-start.15 = (s32[2,8]{1,0:T(2,128)S(1)}, s32[2,8]{1,0:T(2,128)}, u32[]{:S(2)}) copy-start(s32[2,8]{1,0:T(2,128)} %get-tuple-element.34) | copy-start | bytes 196
  141.8 11.0 %all-to-all-start.3 = ((bf16[64,16,128]{2,1,0:T(8,128)(2,1)}), bf16[64,16,128]{2,1,0:T(8,128)(2,1)}, u32[]{:S(2)}, u32[]{:S(2)}) async-start(bf16[64,16,128]{2,1,0:T(8,128)(2,1)} %gather_fusion.4), calls=%async_computation.3 | async-start | bytes 524288 | tf_op jit(solution)/shard_map/all_to_all | solution.py:169
  158.7 2.7 %copy-start.2 = (bf16[1024,1024]{1,0:T(8,128)(2,1)S(1)}, bf16[1024,1024]{1,0:T(8,128)(2,1)}, u32[]{:S(2)}) copy-start(bf16[1024,1024]{1,0:T(8,128)(2,1)} %copy-done) | copy-start | bytes 6291460
  161.4 6.0 %copy-start.14 = (s32[2,8]{1,0:T(2,128)S(1)}, s32[2,8]{1,0:T(2,128)}, u32[]{:S(2)}) copy-start(s32[2,8]{1,0:T(2,128)} %get-tuple-element.33) | copy-start | bytes 196
  161.4 6.1 %copy-start.10 = (bf16[1024,64]{0,1:T(8,128)(2,1)S(1)}, bf16[1024,64]{0,1:T(8,128)(2,1)}, u32[]{:S(2)}) copy-start(bf16[1024,64]{0,1:T(8,128)(2,1)} %get-tuple-element.39) | copy-start | bytes 393220
  164.0 10.3 %all-to-all-start.4 = ((bf16[64,16,128]{2,1,0:T(8,128)(2,1)}), bf16[64,16,128]{2,1,0:T(8,128)(2,1)S(1)}, u32[]{:S(2)}, u32[]{:S(2)}) async-start(bf16[64,16,128]{2,1,0:T(8,128)(2,1)} %gather_fusion.5), calls=%async_computation.4 | async-start | bytes 524288 | tf_op jit(solution)/shard_map/all_to_all | solution.py:169
  176.5 16.9 %copy-start.9 = (f32[256,256]{1,0:T(8,128)S(1)}, f32[256,256]{1,0:T(8,128)}, u32[]{:S(2)}) copy-start(f32[256,256]{1,0:T(8,128)} %get-tuple-element.38) | copy-start | bytes 786436
  176.5 15.6 %all-to-all-start.5 = ((bf16[4,768,64]{1,2,0:T(8,128)(2,1)}), bf16[4,768,64]{1,2,0:T(8,128)(2,1)S(1)}, u32[]{:S(2)}, u32[]{:S(2)}) async-start(bf16[4,768,64]{1,2,0:T(8,128)(2,1)} %pad_maximum_fusion.2), calls=%async_computation.5 | async-start | bytes 786432 | tf_op jit(solution)/shard_map/all_to_all | solution.py:184
Sparse Core Ops, SparseCore 0:
  9.8 92.5 all-gather.2
